TPU v7x, 256 devices: a whole 4x4x8 slice. The times are simulated.
256 devices in a mesh: dp: 8 (over x, core), ev: 32 (over y, z).
Axes of the slice: x: 4, y: 4, z: 8, core: 2. Of those that a mesh axis runs over, the one named last changes fastest.
Arguments:
- events: bfloat16 [8, 4096, 512], P('dp', 'ev'), may hold values from -25 to 25
- cotangent: bfloat16 [8, 4096, 512], P('dp', 'ev'), may hold values from -6 to 6
- intra_gain: float32 [512], replicated, may hold values from 0.25 to 1.75
- intra_proj: bfloat16 [512, 1536], replicated, may hold values from -27 to 27
- intra_out: bfloat16 [512, 512], replicated, may hold values from -0.25 to 0.25
- cross_norm_gain: float32 [512], replicated, may hold values from 0.25 to 1.75
- cross_input_weight: bfloat16 [512, 1536], replicated, may hold values from -27 to 27
- cross_output_weight: bfloat16 [512, 512], replicated, may hold values from -0.25 to 0.25
- owner_map: int32 [8, 4096], P('dp'), may hold values from 0 to 31, as said below
- block_lists: int32 [8, 32, 2, 2], P('dp', 'ev'), may hold values from 0 to 1
Outputs:
- layer_out: bfloat16 [8, 4096, 512], P('dp', 'ev')
- grad_events: bfloat16 [8, 4096, 512], P('dp', 'ev')
- grad_cross_proj: float32 [512, 1536], P('ev')
- grad_cross_out: float32 [512, 512], P('ev')
Inputs may be any that keep to these rules, and one draw needn't show every extreme that they name: `owner_map`: in each replica no device sends more than 8 rows to one owner.
All inputs are finite; a program needn't handle non-finite values.
Results may differ from a plain program's by a relative error of at most 0.033.
The roundings to bfloat16 on the way count: a program that leaves them out, or rounds other values in their place, can miss the bound.
Values may be sent and summed in bfloat16 or wider, within the bound.
No kernel may reach another device: no remote copies, remote signals or barrier semaphores. Data moves between devices by JAX's collectives and lax.ppermute only.
A program may use at most 64 MiB of HBM per device.

v0:
```python
import jax
import jax.numpy as jnp
from jax import lax
from jax.sharding import PartitionSpec as P

HEADS = 8
HEAD_DIM = 64
EVENTS_PER_BLOCK = 128


EPSILON = 1e-05


def layer_norm(values, scale_factors):
    upcast = values.astype(jnp.float32)
    center = upcast - jnp.mean(upcast, axis=-1, keepdims=True)
    spread = jnp.mean(center * center, axis=-1, keepdims=True)
    return center * lax.rsqrt(spread + EPSILON) * scale_factors


def split_heads(matrix, block_groups):
    return matrix.reshape(block_groups, EVENTS_PER_BLOCK, HEADS, HEAD_DIM)


def intra_branch(source, scale_factors, input_weight, output_weight):
    row_total, features = source.shape
    block_groups = row_total // EVENTS_PER_BLOCK
    normed = layer_norm(source, scale_factors).astype(jnp.bfloat16)
    packed_rows = jnp.dot(normed, input_weight, preferred_element_type=jnp.float32).astype(
        jnp.bfloat16
    )
    queries = split_heads(packed_rows[:, :features], block_groups).astype(jnp.float32)
    key_rows = split_heads(packed_rows[:, features : 2 * features], block_groups).astype(
        jnp.float32
    )
    value_rows = split_heads(packed_rows[:, 2 * features :], block_groups).astype(jnp.float32)
    scores = jnp.einsum("bqhd,bkhd->bhqk", queries, key_rows) * HEAD_DIM ** (-0.5)
    highest = jnp.max(scores, axis=-1, keepdims=True)
    weights = jnp.exp(scores - highest)
    attention = (weights / jnp.sum(weights, axis=-1, keepdims=True)).astype(jnp.bfloat16)
    merged_rows = jnp.einsum("bhqk,bkhd->bqhd", attention.astype(jnp.float32), value_rows)
    merged_rows = merged_rows.astype(jnp.bfloat16).reshape(row_total, features)
    branch = jnp.dot(merged_rows, output_weight, preferred_element_type=jnp.float32)
    return (source.astype(jnp.float32) + branch).astype(jnp.bfloat16)


def cross_account_inner(packed_rows, row_presence, block_listing):
    row_total, three_wide = packed_rows.shape
    features = three_wide // 3
    block_groups = row_total // EVENTS_PER_BLOCK
    selected_rows = jnp.concatenate(
        [jnp.arange(block_groups, dtype=jnp.int32)[:, None], block_listing], axis=1
    )
    queries = split_heads(packed_rows[:, :features].astype(jnp.float32), block_groups)
    key_rows = split_heads(
        packed_rows[:, features : 2 * features].astype(jnp.float32), block_groups
    )[selected_rows]
    key_rows = key_rows.reshape(block_groups, -1, HEADS, HEAD_DIM)
    value_rows = split_heads(packed_rows[:, 2 * features :].astype(jnp.float32), block_groups)[
        selected_rows
    ]
    value_rows = value_rows.reshape(block_groups, -1, HEADS, HEAD_DIM)
    key_present = row_presence.reshape(block_groups, EVENTS_PER_BLOCK)[selected_rows].reshape(
        block_groups, -1
    )
    key_total = key_present.shape[1]
    itself = (
        jnp.arange(key_total, dtype=jnp.int32)[None, :]
        == jnp.arange(EVENTS_PER_BLOCK, dtype=jnp.int32)[:, None]
    )
    allowed = key_present[:, None, None, :] | itself[None, None, :, :]
    scores = jnp.einsum("bqhd,bkhd->bhqk", queries, key_rows) * HEAD_DIM ** (-0.5)
    scores = jnp.where(allowed, scores, -1e30)
    highest = jnp.max(scores, axis=-1, keepdims=True)
    weights = jnp.where(allowed, jnp.exp(scores - highest), 0.0)
    attention = (weights / jnp.sum(weights, axis=-1, keepdims=True)).astype(jnp.bfloat16)
    merged_rows = jnp.einsum("bhqk,bkhd->bqhd", attention.astype(jnp.float32), value_rows)
    return merged_rows.astype(jnp.bfloat16).reshape(row_total, features)


def owner_transfer(
    landed_rows,
    landed_cotangent,
    row_presence,
    block_listing,
    scale_factors,
    input_weight,
    output_weight,
):
    normed, norm_pull = jax.vjp(
        lambda input_operand: layer_norm(input_operand, scale_factors), landed_rows
    )
    normed_half = normed.astype(jnp.bfloat16)
    packed_rows = jnp.dot(normed_half, input_weight, preferred_element_type=jnp.float32).astype(
        jnp.bfloat16
    )
    merged_rows, central_gather = jax.vjp(
        lambda input_operand: cross_account_inner(input_operand, row_presence, block_listing),
        packed_rows,
    )
    result = jnp.dot(merged_rows, output_weight, preferred_element_type=jnp.float32).astype(
        jnp.bfloat16
    )
    back_mixed = lax.dot_general(
        landed_cotangent,
        output_weight,
        (((1,), (1,)), ((), ())),
        preferred_element_type=jnp.float32,
    ).astype(jnp.bfloat16)
    back_packed = central_gather(back_mixed)[0]
    back_normed = lax.dot_general(
        back_packed, input_weight, (((1,), (1,)), ((), ())), preferred_element_type=jnp.float32
    )
    back_rows = norm_pull(back_normed)[0]
    return (result, back_rows, normed_half, back_packed, merged_rows)


def contract(left_part, right_part):
    return lax.dot_general(
        left_part, right_part, (((0,), (0,)), ((), ())), preferred_element_type=jnp.float32
    )


def on_device(
    events,
    cotangent,
    intra_gain,
    intra_proj,
    intra_out,
    cross_norm_gain,
    cross_input_weight,
    cross_output_weight,
    owner_map,
    block_lists,
):
    rows_here = events[0]
    upstream = cotangent[0]
    local_rows, features = rows_here.shape
    owners = lax.axis_size("ev")
    replicas = lax.axis_size("dp")
    own_index = lax.axis_index("ev")
    row_capacity = 2 * local_rows // owners
    buffer_rows = owners * row_capacity
    hidden, intra_pull = jax.vjp(
        lambda input_operand: intra_branch(input_operand, intra_gain, intra_proj, intra_out),
        rows_here,
    )
    targets = owner_map[0]
    onehot = (targets[:, None] == jnp.arange(owners, dtype=jnp.int32)[None, :]).astype(jnp.int32)
    row_counts = jnp.sum(onehot.reshape(owners, local_rows, owners), axis=1)
    inbound_rows = lax.dynamic_index_in_dim(row_counts, own_index, axis=1, keepdims=False)
    own_onehot = lax.dynamic_slice_in_dim(onehot, own_index * local_rows, local_rows, 0)
    before = jnp.cumsum(own_onehot, axis=0) - own_onehot
    slot_ids = jnp.sum(before * own_onehot, axis=1)
    own_dest = lax.dynamic_slice_in_dim(targets, own_index * local_rows, local_rows, 0)
    position = own_dest * row_capacity + slot_ids
    outgoing = jnp.zeros((buffer_rows, features), jnp.bfloat16).at[position].set(hidden)
    pending = jnp.zeros((buffer_rows, features), jnp.bfloat16).at[position].set(upstream)
    landed_rows = lax.all_to_all(outgoing, "ev", split_axis=0, concat_axis=0, tiled=True)
    landed_cotangent = lax.all_to_all(pending, "ev", split_axis=0, concat_axis=0, tiled=True)
    row_presence = (
        jnp.arange(row_capacity, dtype=jnp.int32)[None, :] < inbound_rows[:, None]
    ).reshape(buffer_rows)
    block_listing = block_lists[0, 0]
    result, back_rows, normed_half, back_packed, merged_rows = owner_transfer(
        landed_rows,
        landed_cotangent,
        row_presence,
        block_listing,
        cross_norm_gain,
        cross_input_weight,
        cross_output_weight,
    )
    returned = lax.all_to_all(result, "ev", split_axis=0, concat_axis=0, tiled=True)
    sent_back = lax.all_to_all(back_rows, "ev", split_axis=0, concat_axis=0, tiled=True)
    layer_out = (hidden.astype(jnp.float32) + returned[position].astype(jnp.float32)).astype(
        jnp.bfloat16
    )
    grad_hidden = (upstream.astype(jnp.float32) + sent_back[position].astype(jnp.float32)).astype(
        jnp.bfloat16
    )
    grad_rows = intra_pull(grad_hidden)[0]
    factor = (replicas * owners * local_rows) ** (-0.5)
    partial_sum = jnp.concatenate(
        [contract(normed_half, back_packed), contract(merged_rows, landed_cotangent)], axis=1
    )
    summed = lax.psum(partial_sum.astype(jnp.bfloat16), "dp")
    portion = lax.psum_scatter(summed, "ev", scatter_dimension=0, tiled=True).astype(jnp.float32)
    portion = portion * factor
    return (
        layer_out[None],
        grad_rows[None],
        portion[:, : 3 * features],
        portion[:, 3 * features :],
    )


def solution(mesh):
    return jax.shard_map(
        on_device,
        mesh=mesh,
        in_specs=(
            P("dp", "ev", None),
            P("dp", "ev", None),
            P(),
            P(),
            P(),
            P(),
            P(),
            P(),
            P("dp", None),
            P("dp", "ev", None, None),
        ),
        out_specs=(P("dp", "ev", None), P("dp", "ev", None), P("ev", None), P("ev", None)),
        check_vma=False,
    )
```

profile of v0, /device:TPU:1, one launch (start us, length us, event | category | flops | bytes accessed | tf_op | source)
XLA Modules:
  0.0 427.5 jit_solution(11468388101633270498)
XLA Ops:
  10.2 1.1 fusion.50
  12.5 2.0 convolution_convert_fusion.2
  17.0 1.7 scatter_custom_fusion
  18.7 12.0 %all-to-all-start = ((bf16[32,8,512]{2,1,0:T(8,128)(2,1)}), bf16[32,8,512]{2,1,0:T(8,128)(2,1)S(1)}, u32[]{:S(2)}, u32[]{:S(2)}) async-start(bf16[32,8,512]{2,1,0:T(8,128)(2,1)} %bitcast.11), calls=%async_computation | async-start | bytes 524288 | tf_op jit(solution)/shard_map/all_to_all | solution.py:159
  30.7 1.3 convert_reduce_fusion.3
  34.1 1.9 scatter_custom_fusion.1
  36.7 3.7 all-to-all-done
  40.4 6.7 %all-to-all-start.2 = ((bf16[32,8,512]{2,1,0:T(8,128)(2,1)}), bf16[32,8,512]{2,1,0:T(8,128)(2,1)}, u32[]{:S(2)}, u32[]{:S(2)}) async-start(bf16[32,8,512]{2,1,0:T(8,128)(2,1)} %bitcast.20), calls=%async_computation.2 | async-start | bytes 524288 | tf_op jit(solution)/shard_map/all_to_all | solution.py:160
  47.7 1.3 convolution_convert_fusion.1
  50.1 1.0 copy.135
  52.6 1.5 copy.134
  54.1 2.9 reshape.397
  58.5 1.5 copy.130
  60.0 2.2 reshape.394
  62.2 2.3 fusion.107
  64.5 1.7 copy-done.1
  66.2 1.2 fusion.6
  67.4 2.2 convolution_convert_fusion.6
  69.6 1.8 copy.139
  71.4 1.7 reshape.399
  73.2 3.6 fusion.4
  76.8 3.0 fusion.101
  79.8 3.3 fusion.22
  83.1 3.7 fusion.17
  87.6 1.6 convolution_bitcast_fusion
  89.5 1.0 fusion.21
  90.6 9.0 %all-to-all-start.1 = ((bf16[32,8,512]{2,1,0:T(8,128)(2,1)}), bf16[32,8,512]{2,1,0:T(8,128)(2,1)S(1)}, u32[]{:S(2)}, u32[]{:S(2)}) async-start(bf16[32,8,512]{2,1,0:T(8,128)(2,1)} %fusion.21), calls=%async_computation.1 | async-start | bytes 524288 | tf_op jit(solution)/shard_map/all_to_all | solution.py:174
  100.6 3.8 copy.147
  104.4 3.5 reshape.476
  107.8 3.1 copy.148
  111.0 2.8 scatter_fusion.1
  114.8 3.8 copy.141
  118.6 3.5 reshape.468
  122.1 3.0 copy.142
  125.2 2.8 scatter_fusion
  128.4 1.1 copy_bitcast_fusion
  129.5 1.5 convolution_convert_fusion.4
  131.8 1.6 pad_maximum_fusion
  133.5 1.7 fusion.36
  136.4 9.2 %all-to-all-start.3 = ((bf16[32,8,512]{2,1,0:T(8,128)(2,1)}), bf16[32,8,512]{2,1,0:T(8,128)(2,1)S(1)}, u32[]{:S(2)}, u32[]{:S(2)}) async-start(bf16[32,8,512]{2,1,0:T(8,128)(2,1)} %fusion.54), calls=%async_computation.3 | async-start | bytes 524288 | tf_op jit(solution)/shard_map/all_to_all | solution.py:175
  146.6 1.5 gather_fusion.3
  148.1 7.2 %all-to-all-done.3 = bf16[32,8,512]{2,1,0:T(8,128)(2,1)S(1)} async-done(((bf16[32,8,512]{2,1,0:T(8,128)(2,1)}), bf16[32,8,512]{2,1,0:T(8,128)(2,1)S(1)}, u32[]{:S(2)}, u32[]{:S(2)}) %all-to-all-start.3) | async-done | bytes 262176 | tf_op jit(solution)/shard_map/all_to_all | solution.py:175
  156.2 1.4 convolution_convert_fusion.12
  157.7 1.3 multiply_reduce_fusion
  159.6 1.1 convolution_convert_fusion.9
  161.0 1.4 fusion.53
  163.5 186.3 %reduce-scatter.2.cloned.1.call-done = bf16[16,2048]{1,0:T(8,128)(2,1)} async-done(((bf16[512,2048]{1,0:T(8,128)(2,1)}), bf16[16,2048]{1,0:T(8,128)(2,1)}) %reduce-scatter.2.cloned.1.call-update) | async-done | bytes 65552 | tf_op jit(solution)/shard_map/reduce_scatter | solution.py:188
  350.5 68.0 %all-reduce.8.cloned.1.call-done = bf16[16,2048]{1,0:T(8,128)(2,1)} async-done(((bf16[16,2048]{1,0:T(8,128)(2,1)}), bf16[16,2048]{1,0:T(8,128)(2,1)}) %all-reduce.8.cloned.1.call-update) | async-done | bytes 65552 | tf_op jit(solution)/shard_map/psum | solution.py:187
  (181 shorter events, 25.7 us)
Async XLA Ops:
  7.2 40.5 %copy-start = (bf16[512,1536]{1,0:T(8,128)(2,1)S(1)}, bf16[512,1536]{1,0:T(8,128)(2,1)}, u32[]{:S(2)}) copy-start(bf16[512,1536]{1,0:T(8,128)(2,1)} %param.16) | copy-start | bytes 4718596
  9.2 7.8 %copy-start.43 = (s32[128]{0:T(128)}, s32[128]{0:T(128)S(1)}, u32[]{:S(2)}) copy-start(s32[128]{0:T(128)S(1)} %fusion.83) | copy-start | bytes 1540
  12.5 4.2 copy-start.3
  12.5 4.2 copy-start.9
  14.4 19.6 %copy-start.13 = (bf16[1,128,512]{2,1,0:T(8,128)(2,1)S(1)}, bf16[1,128,512]{2,1,0:T(8,128)(2,1)}, u32[]{:S(2)}) copy-start(bf16[1,128,512]{2,1,0:T(8,128)(2,1)} %param.11) | copy-start | bytes 393220
  14.6 4.1 copy-start.19
  14.7 32.5 %copy-start.16 = (bf16[128,512]{0,1:T(8,128)(2,1)}, bf16[128,512]{0,1:T(8,128)(2,1)S(1)}, u32[]{:S(2)}) copy-start(bf16[128,512]{0,1:T(8,128)(2,1)S(1)} %copy.125) | copy-start | bytes 393220
  16.5 32.5 %copy-start.7 = (bf16[8,128,128]{1,2,0:T(8,128)(2,1)}, bf16[8,128,128]{1,2,0:T(8,128)(2,1)S(1)}, u32[]{:S(2)}) copy-start(bf16[8,128,128]{1,2,0:T(8,128)(2,1)S(1)} %get-tuple-element.19) | copy-start | bytes 786436
  17.0 1.7 copy-start.24
  18.7 21.7 %all-to-all-start = ((bf16[32,8,512]{2,1,0:T(8,128)(2,1)}), bf16[32,8,512]{2,1,0:T(8,128)(2,1)S(1)}, u32[]{:S(2)}, u32[]{:S(2)}) async-start(bf16[32,8,512]{2,1,0:T(8,128)(2,1)} %bitcast.11), calls=%async_computation | async-start | bytes 524288 | tf_op jit(solution)/shard_map/all_to_all | solution.py:159
  40.4 27.0 %all-to-all-start.2 = ((bf16[32,8,512]{2,1,0:T(8,128)(2,1)}), bf16[32,8,512]{2,1,0:T(8,128)(2,1)}, u32[]{:S(2)}, u32[]{:S(2)}) async-start(bf16[32,8,512]{2,1,0:T(8,128)(2,1)} %bitcast.20), calls=%async_computation.2 | async-start | bytes 524288 | tf_op jit(solution)/shard_map/all_to_all | solution.py:160
  47.3 2.5 copy-start.38
  47.6 2.2 copy-start.32
  47.7 2.1 copy-start.40
  52.6 4.4 %copy-start.21 = (bf16[256,512]{1,0:T(8,128)(2,1)S(1)}, bf16[256,512]{1,0:T(8,128)(2,1)}, u32[]{:S(2)}) copy-start(bf16[256,512]{1,0:T(8,128)(2,1)} %get-tuple-element.16) | copy-start | bytes 786436
  60.0 6.2 %copy-start.10 = (pred[2,128,384]{2,1,0:T(8,128)(4,1)S(1)}, pred[2,128,384]{2,1,0:T(8,128)(4,1)}, u32[]{:S(2)}) copy-start(pred[2,128,384]{2,1,0:T(8,128)(4,1)} %broadcast_or_fusion) | copy-start | bytes 294916
  62.2 10.9 %copy-start.5 = (bf16[2,384,8,64]{1,0,3,2:T(2,128)(2,1)}, bf16[2,384,8,64]{1,0,3,2:T(2,128)(2,1)S(1)}, u32[]{:S(2)}) copy-start(bf16[2,384,8,64]{1,0,3,2:T(2,128)(2,1)S(1)} %reshape.394) | copy-start | bytes 2359300
  64.5 1.7 copy-start.1
  73.2 3.6 copy-start.2
  76.8 3.0 copy-start.4
  79.8 3.3 copy-start.20
  83.1 3.7 copy-start.6
  83.1 4.5 %copy-start.23 = (bf16[2,128,8,64]{1,0,3,2:T(2,128)(2,1)S(1)}, bf16[2,128,8,64]{1,0,3,2:T(2,128)(2,1)}, u32[]{:S(2)}) copy-start(bf16[2,128,8,64]{1,0,3,2:T(2,128)(2,1)} %reshape.399) | copy-start | bytes 786436
  86.8 2.7 copy-start.27
  87.6 12.0 %copy-start.28 = (bf16[2,128,8,64]{1,3,2,0:T(8,128)(2,1)S(1)}, bf16[2,128,8,64]{1,3,2,0:T(8,128)(2,1)}, u32[]{:S(2)}) copy-start(bf16[2,128,8,64]{1,3,2,0:T(8,128)(2,1)} %fusion.22) | copy-start | bytes 786436
  89.5 18.4 %copy-start.22 = (bf16[2,128,8,64]{1,0,3,2:T(2,128)(2,1)}, bf16[2,128,8,64]{1,0,3,2:T(2,128)(2,1)S(1)}, u32[]{:S(2)}) copy-start(bf16[2,128,8,64]{1,0,3,2:T(2,128)(2,1)S(1)} %copy.138) | copy-start | bytes 786436
  90.6 45.8 %all-to-all-start.1 = ((bf16[32,8,512]{2,1,0:T(8,128)(2,1)}), bf16[32,8,512]{2,1,0:T(8,128)(2,1)S(1)}, u32[]{:S(2)}, u32[]{:S(2)}) async-start(bf16[32,8,512]{2,1,0:T(8,128)(2,1)} %fusion.21), calls=%async_computation.1 | async-start | bytes 524288 | tf_op jit(solution)/shard_map/all_to_all | solution.py:174
  99.5 250.3 %reduce-scatter.2.cloned.1.call-start = ((), (), s32[]{:S(2)}) async-start(), calls=%async_computation.5 | async-start | bytes 2162688 | tf_op jit(solution)/shard_map/reduce_scatter | solution.py:188
  128.0 3.1 copy-start.39
  128.0 3.1 copy-start.41
  128.0 3.1 copy-start.46
  129.5 1.5 copy-start.29
  129.5 1.5 copy-start.30
  133.5 1.8 copy-start.33
  133.5 1.8 copy-start.42
  135.2 20.9 %copy-start.14 = (bf16[1,128,512]{2,1,0:T(8,128)(2,1)S(1)}, bf16[1,128,512]{2,1,0:T(8,128)(2,1)}, u32[]{:S(2)}) copy-start(bf16[1,128,512]{2,1,0:T(8,128)(2,1)} %param.11) | copy-start | bytes 393220
  136.4 18.9 %all-to-all-start.3 = ((bf16[32,8,512]{2,1,0:T(8,128)(2,1)}), bf16[32,8,512]{2,1,0:T(8,128)(2,1)S(1)}, u32[]{:S(2)}, u32[]{:S(2)}) async-start(bf16[32,8,512]{2,1,0:T(8,128)(2,1)} %fusion.54), calls=%async_computation.3 | async-start | bytes 524288 | tf_op jit(solution)/shard_map/all_to_all | solution.py:175
  145.6 272.9 %all-reduce.8.cloned.1.call-start = ((), (), s32[]{:S(2)}) async-start(), calls=%async_computation.6 | async-start | bytes 131072 | tf_op jit(solution)/shard_map/psum | solution.py:187
  146.6 12.7 %copy-start.8 = (bf16[8,128,128]{1,2,0:T(8,128)(2,1)S(1)}, bf16[8,128,128]{1,2,0:T(8,128)(2,1)}, u32[]{:S(2)}) copy-start(bf16[8,128,128]{1,2,0:T(8,128)(2,1)} %copy-done.7) | copy-start | bytes 786436
  148.1 11.5 %copy-start.12 = (pred[8,128,128]{1,2,0:T(32,128)(4,1)S(1)}, pred[8,128,128]{1,2,0:T(32,128)(4,1)}, u32[]{:S(2)}) copy-start(pred[8,128,128]{1,2,0:T(32,128)(4,1)} %get-tuple-element.7) | copy-start | bytes 393220
  156.2 4.5 %copy-start.17 = (bf16[128,512]{0,1:T(8,128)(2,1)S(1)}, bf16[128,512]{0,1:T(8,128)(2,1)}, u32[]{:S(2)}) copy-start(bf16[128,512]{0,1:T(8,128)(2,1)} %copy-done.16) | copy-start | bytes 393220
  157.7 3.3 copy-start.11
  159.1 3.4 copy-start.45
  159.1 3.4 copy-start.35
  159.1 3.4 copy-start.37
  159.2 3.5 copy-start.15
  159.3 190.6 %copy-start.25 = (bf16[128,512]{1,0:T(8,128)(2,1)S(1)}, bf16[128,512]{1,0:T(8,128)(2,1)}, u32[]{:S(2)}) copy-start(bf16[128,512]{1,0:T(8,128)(2,1)} %copy-done.24) | copy-start | bytes 393220
  159.3 190.6 %copy-start.26 = (bf16[128,512]{1,0:T(8,128)(2,1)S(1)}, bf16[128,512]{1,0:T(8,128)(2,1)}, u32[]{:S(2)}) copy-start(bf16[128,512]{1,0:T(8,128)(2,1)} %gather_fusion.3) | copy-start | bytes 393220
  (5 other events, 3.5 us)
Sparse Core Ops, SparseCore 0:
  133.6 216.1 reduce-scatter.1
  352.1 66.3 all-reduce.7
where the time goes:
time: 430 us; the launch traced here: 428 us
  waiting for transfers between devices  265 us (62%)
  local copies, waits for them, and re-layouts  54.3 us (13%)
  starting transfers between devices  37.2 us (9%)
  matrix products  32.3 us (8%)
  other arithmetic  23.3 us (5%)
  between operations  15 us (3%)
    reduce_scatter x1, waiting for transfers between devices, on_device(): lax.psum_scatter(summed, 'ev', scatter_dimension=0, tiled=True)  186 us
    psum x1, waiting for transfers between devices, on_device(): summed = lax.psum(partial_sum.astype(jnp.bfloat16), 'dp')  68 us
    all_to_all x1, starting transfers between devices, on_device(): lax.all_to_all(outgoing, 'ev', split_axis=0, concat_axis=0, tiled=True)  12 us
    reshape x3, local copies, waits for them, and re-layouts, cross_account_inner(): key_rows = key_rows.reshape(block_groups, -1, HEADS, HEAD_DIM)  9.42 us
    dot_general x3, matrix products, cross_account_inner(): jnp.einsum('bqhd,bkhd->bhqk', queries, key_rows) * HEAD_DIM ** (-0.5)  9.3 us
    all_to_all x1, starting transfers between devices, on_device(): lax.all_to_all(back_rows, 'ev', split_axis=0, concat_axis=0, tiled=True)  9.23 us
    all_to_all x1, starting transfers between devices, on_device(): lax.all_to_all(result, 'ev', split_axis=0, concat_axis=0, tiled=True)  8.98 us
    reshape x3, local copies, waits for them, and re-layouts, cross_account_inner(): value_rows = value_rows.reshape(block_groups, -1, HEADS, HEAD_DIM)  8.71 us
  transfers between devices with their start and end apart: 6, of which 4 were waited for; matrix products, arithmetic and copies ran while one was open for 17% of the time, Pallas kernels for 0%

commit v1 on v0

--- a/solution.py
+++ b/solution.py
@@ -119,6 +119,21 @@
     return lax.dot_general(
         left_part, right_part, (((0,), (0,)), ((), ())), preferred_element_type=jnp.float32
     )
+
+
+def reduce_weight_terms(partial, replicas, owners):
+    rows, width = partial.shape
+    per_owner = rows // owners
+    per_device = per_owner // replicas
+    terms = partial.astype(jnp.bfloat16).reshape(owners, replicas, per_device, width)
+    terms = jnp.swapaxes(terms, 0, 1)
+    terms = lax.all_to_all(terms, "dp", 0, 0, tiled=True)
+    terms = jnp.sum(terms.astype(jnp.float32), axis=0).astype(jnp.bfloat16)
+    terms = lax.all_to_all(terms, "ev", 0, 0, tiled=True)
+    piece = jnp.sum(terms.astype(jnp.float32), axis=0)
+    copies = jnp.broadcast_to(piece[None], (replicas, per_device, width))
+    gathered = lax.all_to_all(copies, "dp", 0, 0, tiled=True)
+    return gathered.reshape(per_owner, width)
 
 
 def on_device(
@@ -154,10 +169,14 @@
     slot_ids = jnp.sum(before * own_onehot, axis=1)
     own_dest = lax.dynamic_slice_in_dim(targets, own_index * local_rows, local_rows, 0)
     position = own_dest * row_capacity + slot_ids
-    outgoing = jnp.zeros((buffer_rows, features), jnp.bfloat16).at[position].set(hidden)
-    pending = jnp.zeros((buffer_rows, features), jnp.bfloat16).at[position].set(upstream)
-    landed_rows = lax.all_to_all(outgoing, "ev", split_axis=0, concat_axis=0, tiled=True)
-    landed_cotangent = lax.all_to_all(pending, "ev", split_axis=0, concat_axis=0, tiled=True)
+    placement = (
+        jnp.arange(buffer_rows, dtype=jnp.int32)[:, None] == position[None, :]
+    ).astype(jnp.bfloat16)
+    both = jnp.concatenate([hidden, upstream], axis=1)
+    outgoing = jnp.dot(placement, both, preferred_element_type=jnp.float32).astype(jnp.bfloat16)
+    landed = lax.all_to_all(outgoing, "ev", split_axis=0, concat_axis=0, tiled=True)
+    landed_rows = landed[:, :features]
+    landed_cotangent = landed[:, features:]
     row_presence = (
         jnp.arange(row_capacity, dtype=jnp.int32)[None, :] < inbound_rows[:, None]
     ).reshape(buffer_rows)
@@ -171,22 +190,19 @@
         cross_input_weight,
         cross_output_weight,
     )
-    returned = lax.all_to_all(result, "ev", split_axis=0, concat_axis=0, tiled=True)
-    sent_back = lax.all_to_all(back_rows, "ev", split_axis=0, concat_axis=0, tiled=True)
-    layer_out = (hidden.astype(jnp.float32) + returned[position].astype(jnp.float32)).astype(
-        jnp.bfloat16
-    )
-    grad_hidden = (upstream.astype(jnp.float32) + sent_back[position].astype(jnp.float32)).astype(
-        jnp.bfloat16
-    )
+    going_back = jnp.concatenate([result, back_rows.astype(jnp.bfloat16)], axis=1)
+    came_back = lax.all_to_all(going_back, "ev", split_axis=0, concat_axis=0, tiled=True)
+    picked = lax.dot_general(
+        placement, came_back, (((0,), (0,)), ((), ())), preferred_element_type=jnp.float32
+    )
+    layer_out = (hidden.astype(jnp.float32) + picked[:, :features]).astype(jnp.bfloat16)
+    grad_hidden = (upstream.astype(jnp.float32) + picked[:, features:]).astype(jnp.bfloat16)
     grad_rows = intra_pull(grad_hidden)[0]
     factor = (replicas * owners * local_rows) ** (-0.5)
     partial_sum = jnp.concatenate(
         [contract(normed_half, back_packed), contract(merged_rows, landed_cotangent)], axis=1
     )
-    summed = lax.psum(partial_sum.astype(jnp.bfloat16), "dp")
-    portion = lax.psum_scatter(summed, "ev", scatter_dimension=0, tiled=True).astype(jnp.float32)
-    portion = portion * factor
+    portion = reduce_weight_terms(partial_sum, replicas, owners) * factor
     return (
         layer_out[None],
         grad_rows[None],

time: 430 us -> 215 us (0.50)
  waiting for transfers between devices: 265 us -> 39.6 us
  between operations: 15 us -> 2.15 us
  other arithmetic: 23.3 us -> 31.6 us
  local copies, waits for them, and re-layouts: 54.3 us -> 60 us
  starting transfers between devices: 37.2 us -> 41.8 us
    reduce_scatter x1 -> x0, waiting for transfers between devices: 186 us -> none  [on_device(): lax.psum_scatter(summed, 'ev', scatter_dimension=0, tiled=True)]
    psum x1 -> x0, waiting for transfers between devices: 68 us -> none  [on_device(): summed = lax.psum(partial_sum.astype(jnp.bfloat16), 'dp')]
    all_to_all x3 -> x4, waiting for transfers between devices: 7.25 us -> 29.8 us  [the longest x1 16.6 us: reduce_weight_terms(): terms = lax.all_to_all(terms, 'dp', 0, 0, tiled=True)]
    all_to_all x1, waiting for transfers between devices: 3.75 us -> 9.88 us  [on_device(): lax.all_to_all(outgoing, 'ev', split_axis=0, concat_axis=0, tiled=True)]
    all_to_all x3 -> x4, starting transfers between devices: 24.9 us -> 29.6 us  [the longest x1 9.38 us: reduce_weight_terms(): terms = lax.all_to_all(terms, 'ev', 0, 0, tiled=True)]
    transpose x0 -> x1, other arithmetic: none -> 4.57 us  [reduce_weight_terms(): terms = jnp.swapaxes(terms, 0, 1)]
    concatenate x0 -> x1, local copies, waits for them, and re-layouts: none -> 4.52 us  [on_device(): jnp.concatenate([contract(normed_half, back_packed), contract(merged_rows...]
  transfers between devices with their start and end apart: 6 -> 5, of which waited for: 4 -> 4; matrix products, arithmetic and copies ran while one was open for 17% -> 15% of each run, Pallas kernels for 0% -> 0%
where the time goes in v1:
time: 215 us; the launch traced here: 211 us
  local copies, waits for them, and re-layouts  60 us (28%)
  starting transfers between devices  41.8 us (19%)
  waiting for transfers between devices  39.6 us (18%)
  matrix products  35.8 us (17%)
  other arithmetic  31.6 us (15%)
  between operations  2.15 us (1%)
    all_to_all x1, waiting for transfers between devices, reduce_weight_terms(): terms = lax.all_to_all(terms, 'dp', 0, 0, tiled=True)  16.6 us
    all_to_all x1, starting transfers between devices, on_device(): lax.all_to_all(outgoing, 'ev', split_axis=0, concat_axis=0, tiled=True)  12.2 us
    all_to_all x1, waiting for transfers between devices, on_device(): lax.all_to_all(outgoing, 'ev', split_axis=0, concat_axis=0, tiled=True)  9.88 us
    all_to_all x1, starting transfers between devices, reduce_weight_terms(): terms = lax.all_to_all(terms, 'ev', 0, 0, tiled=True)  9.38 us
    reshape x3, local copies, waits for them, and re-layouts, cross_account_inner(): key_rows = key_rows.reshape(block_groups, -1, HEADS, HEAD_DIM)  8.72 us
    reshape x3, local copies, waits for them, and re-layouts, cross_account_inner(): value_rows = value_rows.reshape(block_groups, -1, HEADS, HEAD_DIM)  8.7 us
    all_to_all x1, waiting for transfers between devices, reduce_weight_terms(): terms = lax.all_to_all(terms, 'ev', 0, 0, tiled=True)  8.6 us
    all_to_all x1, starting transfers between devices, on_device(): lax.all_to_all(going_back, 'ev', split_axis=0, concat_axis=0, tiled=True)  7.23 us
  transfers between devices with their start and end apart: 5, of which 4 were waited for; matrix products, arithmetic and copies ran while one was open for 15% of the time, Pallas kernels for 0%

profile of v1, /device:TPU:1, one launch (start us, length us, event | category | flops | bytes accessed | tf_op | source)
XLA Modules:
  0.0 211.0 jit_solution(2530116676671360514)
XLA Ops:
  4.0 2.0 convolution_convert_fusion.2
  6.8 1.4 convert_reduce_fusion.3
  10.6 2.0 fusion.18
  12.6 12.2 %all-to-all-start = ((bf16[32,8,1024]{2,1,0:T(8,128)(2,1)}), bf16[32,8,1024]{2,1,0:T(8,128)(2,1)S(1)}, u32[]{:S(2)}, u32[]{:S(2)}) async-start(bf16[32,8,1024]{2,1,0:T(8,128)(2,1)} %fusion.18), calls=%async_computation | async-start | bytes 1048576 | tf_op jit(solution)/shard_map/all_to_all | solution.py:177
  25.7 1.3 convert_reduce_fusion.4
  29.5 9.9 %all-to-all-done = bf16[32,8,1024]{2,1,0:T(8,128)(2,1)S(1)} async-done(((bf16[32,8,1024]{2,1,0:T(8,128)(2,1)}), bf16[32,8,1024]{2,1,0:T(8,128)(2,1)S(1)}, u32[]{:S(2)}, u32[]{:S(2)}) %all-to-all-start) | async-done | bytes 524320 | tf_op jit(solution)/shard_map/all_to_all | solution.py:177
  39.8 1.3 convolution_convert_fusion.1
  42.0 1.3 reshape.417
  46.7 1.5 copy.244
  48.2 2.2 %reshape.354 = bf16[2,384,8,64]{1,0,3,2:T(2,128)(2,1)S(1)} reshape(bf16[6,128,8,64]{1,0,3,2:T(8,128)(2,1)} %copy.244) | data formatting | bytes 1572864 | tf_op jit(solution)/shard_map/jvp()/reshape | solution.py:58
  50.5 2.1 fusion.112
  52.5 1.7 copy-done.1
  58.5 1.5 copy.240
  60.0 2.2 %reshape.351 = bf16[2,384,8,64]{1,0,3,2:T(2,128)(2,1)S(1)} reshape(bf16[6,128,8,64]{1,0,3,2:T(8,128)(2,1)} %copy.240) | data formatting | bytes 1572864 | tf_op jit(solution)/shard_map/jvp()/reshape | solution.py:62
  62.2 2.5 %convolution_convert_fusion.7 = bf16[256,512]{1,0:T(8,128)(2,1)} fusion(bf16[512,512]{1,0:T(8,128)(2,1)} %param.17, bf16[256,1024]{1,0:T(8,128)(2,1)} %bitcast.168), kind=kOutput, calls=%fused_computation.45 | convolution fusion | flops 134348800 | bytes 1048576 | tf_op jit(solution)/shard_map/dot_general | solution.py:104
  64.7 1.8 copy.249
  66.5 1.7 reshape.356
  68.2 3.6 %fusion.4 = (f32[2,8,128]{2,1,0:T(8,128)S(1)}, bf16[2,8,128,384]{3,2,1,0:T(8,128)(2,1)S(1)}) fusion(f32[2,8,128,384]{3,2,1,0:T(8,128)} %copy-done.1, f32[2,8,128]{2,1,0:T(8,128)S(1)} %copy-done.46, f32[2,8,128]{2,1,0:T(8,128)S(1)} %get-tuple-element.25, pred[2,128,384]{2,1,0:T(8,128)(4,1)S(1)} %copy-done.15, bf16[2,384,8,64]{1,0,3,2:T(2,128)(2,1)S(1)} %reshape.351, ...), kind=kOutput, calls=%fused_computation.11 | convolution fusion | flops 106166272 | bytes 5890048 | tf_op jit(solution)/shard_map/transpose(jvp(bhqk,bkhd->bqhd))/dot_general | solution.py:77
  71.9 3.0 %divide_convert_fusion = (bf16[2,8,128,384]{3,2,1,0:T(8,128)(2,1)S(1)}, f32[2,8,128]{2,1,0:T(8,128)S(1)}, f32[2,8,128]{2,1,0:T(8,128)S(1)}, pred[2,8,128,384]{3,2,1,0:T(32,128)(4,1)S(1)}) fusion(f32[2,8,128,384]{3,2,1,0:T(8,128)S(1)} %copy-done.2, f32[2,8,128]{2,1,0:T(8,128)S(1)} %copy-done.34, f32[2,8,128]{2,1,0:T(8,128)S(1)} %get-tuple-element.25, ...), kind=kLoop, calls=%fused_computation.14 | loop fusion | flops 10219520 | bytes 7217152 | tf_op jit(solution)/shard_map/jvp()/convert_element_type | solution.py:76
  75.0 2.5 %fusion.22 = bf16[2,128,8,64]{1,3,2,0:T(8,128)(2,1)S(1)} fusion(pred[2,8,128,384]{3,2,1,0:T(32,128)(4,1)S(1)} %get-tuple-element.15, f32[2,8,128]{2,1,0:T(8,128)S(1)} %negate_divide_fusion, pred[2,128,384]{2,1,0:T(8,128)(4,1)S(1)} %copy-done.15, bf16[2,384,8,64]{1,0,3,2:T(2,128)(2,1)S(1)} %copy-done.7, bf16[2,8,128,384]{3,2,1,0:T(8,128)(2,1)S(1)} %get-tuple-element.28, ...), kind=kOutput, calls=%fused_computation.49 | convolution fusion | flops 108658688 | bytes 6684672 | tf_op jit(solution)/shard_map/transpose(jvp(bqhd,bkhd->bhqk))/dot_general | solution.py:72
  77.4 2.2 %fusion.17 = f32[2,384,8,64]{1,3,2,0:T(8,128)S(1)} fusion(bf16[2,128,8,64]{1,3,2,0:T(8,128)(2,1)S(1)} %copy-done.26, pred[2,8,128,384]{3,2,1,0:T(32,128)(4,1)S(1)} %get-tuple-element.15, f32[2,8,128]{2,1,0:T(8,128)S(1)} %negate_divide_fusion, pred[2,128,384]{2,1,0:T(8,128)(4,1)S(1)} %copy-done.15, bf16[2,8,128,384]{3,2,1,0:T(8,128)(2,1)S(1)} %get-tuple-element.28, ...), kind=kOutput, calls=%fused_computation.35 | convolution fusion | flops 108527616 | bytes 7471104 | tf_op jit(solution)/shard_map/transpose(jvp(bqhd,bkhd->bhqk))/dot_general | solution.py:72
  79.7 1.6 convolution_bitcast_fusion
  85.2 2.4 %copy.257 = f32[2,384,8,64]{1,0,3,2:T(2,128)} copy(f32[2,384,8,64]{1,3,2,0:T(8,128)S(1)} %fusion.17) | data formatting | bytes 3145728 | tf_op jit(solution)/shard_map/transpose(jvp(bqhd,bkhd->bhqk))/transpose | solution.py:72
  87.6 3.5 %reshape.400 = f32[6,128,8,64]{1,0,3,2:T(8,128)} reshape(f32[2,384,8,64]{1,0,3,2:T(2,128)} %copy.257) | data formatting | bytes 3145728 | tf_op jit(solution)/shard_map/transpose(jvp())/reshape | solution.py:58
  91.0 3.1 %copy.258 = f32[6,128,8,64]{1,3,2,0:T(8,128)} copy(f32[6,128,8,64]{1,0,3,2:T(8,128)} %reshape.400) | data formatting | bytes 3145728 | tf_op jit(solution)/shard_map/transpose(jvp())/reshape | solution.py:58
  94.2 2.8 %scatter_fusion.1 = f32[2,128,8,64]{1,3,2,0:T(8,128)S(1)} fusion(f32[2,128,8,64]{1,3,2,0:T(8,128)S(1)} %broadcast.181.clone, s32[6]{0:T(128)S(1)} %copy-done.38, f32[6,128,8,64]{1,3,2,0:T(8,128)} %copy.258), kind=kCustom, calls=%fused_computation.4 | custom fusion | flops 393216 | bytes 4718616 | tf_op jit(solution)/shard_map/transpose(jvp())/scatter-add | solution.py:55
  98.0 3.8 %copy.251 = f32[2,384,8,64]{1,0,3,2:T(2,128)} copy(f32[2,384,8,64]{1,3,2,0:T(8,128)} %convolution_bitcast_fusion) | data formatting | bytes 3145728 | tf_op jit(solution)/shard_map/transpose(jvp(bhqk,bkhd->bqhd))/transpose | solution.py:77
  101.8 3.5 %reshape.392 = f32[6,128,8,64]{1,0,3,2:T(8,128)} reshape(f32[2,384,8,64]{1,0,3,2:T(2,128)} %copy.251) | data formatting | bytes 3145728 | tf_op jit(solution)/shard_map/transpose(jvp())/reshape | solution.py:62
  105.2 3.0 %copy.252 = f32[6,128,8,64]{1,3,2,0:T(8,128)} copy(f32[6,128,8,64]{1,0,3,2:T(8,128)} %reshape.392) | data formatting | bytes 3145728 | tf_op jit(solution)/shard_map/transpose(jvp())/reshape | solution.py:62
  108.4 3.1 %scatter_fusion = f32[2,128,8,64]{1,3,2,0:T(8,128)S(1)} fusion(f32[2,128,8,64]{1,3,2,0:T(8,128)S(1)} %broadcast.181.clone.1, s32[6]{0:T(128)S(1)} %copy-done.38, f32[6,128,8,64]{1,3,2,0:T(8,128)} %copy.252), kind=kCustom, calls=%fused_computation.3 | custom fusion | flops 393216 | bytes 4718616 | tf_op jit(solution)/shard_map/transpose(jvp())/scatter-add | solution.py:59
  113.1 1.5 fusion.37
  115.9 7.2 %all-to-all-start.1 = ((bf16[32,8,1024]{2,1,0:T(8,128)(2,1)}), bf16[32,8,1024]{2,1,0:T(8,128)(2,1)S(1)}, u32[]{:S(2)}, u32[]{:S(2)}) async-start(bf16[32,8,1024]{2,1,0:T(8,128)(2,1)} %maximum_bitcast_fusion.1), calls=%async_computation.1 | async-start | bytes 1048576 | tf_op jit(solution)/shard_map/all_to_all | solution.py:194
  123.2 1.8 dot_general.100
  127.4 3.0 %convolution_convert_fusion = bf16[512,1536]{1,0:T(8,128)(2,1)} fusion(bf16[256,512]{0,1:T(8,128)(2,1)} %copy-done.31, bf16[256,512]{0,1:T(8,128)(2,1)} %copy-done.32, bf16[256,512]{0,1:T(8,128)(2,1)} %bitcast.192, f32[512]{0:T(512)} %param.15, f32[256]{0:T(256)S(1)} %copy-done.52, f32[256]{0:T(256)S(1)} %copy-done.41, bf16[256,1024]{1,0:T(8,128)(2,1)S(1)} %bitcast.172), kind=kOutput, calls=%fused_computation.17 | convolution fusion | flops 406454272 | bytes 2625536 | tf_op jit(solution)/shard_map/dot_general | solution.py:119
  130.4 4.5 %concatenate.41 = bf16[32,8,2,1536]{3,2,1,0:T(2,128)(2,1)} reshape(bf16[512,1536]{1,0:T(8,128)(2,1)} %convolution_convert_fusion) | data formatting | bytes 3145728 | tf_op jit(solution)/shard_map/concatenate | solution.py:202
  135.0 4.6 %maximum_bitcast_fusion = bf16[8,32,2,2048]{3,2,1,0:T(2,128)(2,1)} fusion(bf16[32,8,2,512]{3,2,0,1:T(2,128)(2,1)S(1)} %copy-done.13, bf16[32,8,2,1536]{3,2,1,0:T(2,128)(2,1)} %concatenate.41), kind=kLoop, calls=%fused_computation.21 | loop fusion | flops 4194304 | bytes 4194304 | tf_op jit(solution)/shard_map/transpose | solution.py:129
  140.3 6.1 %all-to-all-start.2 = ((bf16[8,32,2,2048]{3,2,1,0:T(2,128)(2,1)}), bf16[8,32,2,2048]{3,2,1,0:T(2,128)(2,1)}, u32[]{:S(2)}, u32[]{:S(2)}) async-start(bf16[8,32,2,2048]{3,2,1,0:T(2,128)(2,1)} %maximum_bitcast_fusion), calls=%async_computation.2 | async-start | bytes 4194304 | tf_op jit(solution)/shard_map/all_to_all | solution.py:130
  146.4 1.3 fusion.38
  147.7 1.9 convolution_convert_fusion.13
  149.6 1.7 copy.262
  151.3 1.4 multiply_reduce_fusion
  154.7 1.5 fusion.54
  156.2 16.6 %all-to-all-done.2 = bf16[8,32,2,2048]{3,2,1,0:T(2,128)(2,1)} async-done(((bf16[8,32,2,2048]{3,2,1,0:T(2,128)(2,1)}), bf16[8,32,2,2048]{3,2,1,0:T(2,128)(2,1)}, u32[]{:S(2)}, u32[]{:S(2)}) %all-to-all-start.2) | async-done | bytes 2097184 | tf_op jit(solution)/shard_map/all_to_all | solution.py:130
  172.7 4.3 %reduce_sum.236 = bf16[32,2,2048]{2,1,0:T(2,128)(2,1)} reduce(bf16[8,32,2,2048]{3,2,1,0:T(2,128)(2,1)} %all-to-all-done.2, bf16[]{:T(256)} %constant.60.clone.1), dimensions={0}, to_apply=%region_23.24 | reduce | flops 917504 | bytes 2359298 | tf_op jit(solution)/shard_map/reduce_sum | solution.py:131
  177.1 9.4 %all-to-all-start.3 = ((bf16[32,2,2048]{2,1,0:T(2,128)(2,1)}), bf16[32,2,2048]{2,1,0:T(2,128)(2,1)S(1)}, u32[]{:S(2)}, u32[]{:S(2)}) async-start(bf16[32,2,2048]{2,1,0:T(2,128)(2,1)} %reduce_sum.236), calls=%async_computation.3 | async-start | bytes 524288 | tf_op jit(solution)/shard_map/all_to_all | solution.py:132
  187.5 8.6 %all-to-all-done.3 = bf16[32,2,2048]{2,1,0:T(2,128)(2,1)S(1)} async-done(((bf16[32,2,2048]{2,1,0:T(2,128)(2,1)}), bf16[32,2,2048]{2,1,0:T(2,128)(2,1)S(1)}, u32[]{:S(2)}, u32[]{:S(2)}) %all-to-all-start.3) | async-done | bytes 262176 | tf_op jit(solution)/shard_map/all_to_all | solution.py:132
  196.9 6.9 %all-to-all-start.4 = ((f32[8,2,2048]{2,1,0:T(2,128)}), f32[8,2,2048]{2,1,0:T(2,128)S(1)}, u32[]{:S(2)}, u32[]{:S(2)}) async-start(f32[8,2,2048]{2,1,0:T(2,128)} %broadcast_in_dim.102), calls=%async_computation.4 | async-start | bytes 262144 | tf_op jit(solution)/shard_map/all_to_all | solution.py:135
  204.5 4.6 %all-to-all-done.4 = f32[8,2,2048]{2,1,0:T(2,128)S(1)} async-done(((f32[8,2,2048]{2,1,0:T(2,128)}), f32[8,2,2048]{2,1,0:T(2,128)S(1)}, u32[]{:S(2)}, u32[]{:S(2)}) %all-to-all-start.4) | async-done | bytes 131104 | tf_op jit(solution)/shard_map/all_to_all | solution.py:135
  (196 shorter events, 35.5 us)
Async XLA Ops:
  0.6 39.1 %copy-start = (bf16[512,1536]{1,0:T(8,128)(2,1)S(1)}, bf16[512,1536]{1,0:T(8,128)(2,1)}, u32[]{:S(2)}) copy-start(bf16[512,1536]{1,0:T(8,128)(2,1)} %param.16) | copy-start | bytes 4718596
  4.0 6.3 %copy-start.5 = (bf16[1,128,512]{2,1,0:T(8,128)(2,1)S(1)}, bf16[1,128,512]{2,1,0:T(8,128)(2,1)}, u32[]{:S(2)}) copy-start(bf16[1,128,512]{2,1,0:T(8,128)(2,1)} %param.10) | copy-start | bytes 393220
  4.0 6.3 %copy-start.10 = (bf16[512,512]{1,0:T(8,128)(2,1)S(1)}, bf16[512,512]{1,0:T(8,128)(2,1)}, u32[]{:S(2)}) copy-start(bf16[512,512]{1,0:T(8,128)(2,1)} %param.14) | copy-start | bytes 1572868
  6.1 6.5 %copy-start.22 = (bf16[128,512]{0,1:T(8,128)(2,1)}, bf16[128,512]{0,1:T(8,128)(2,1)S(1)}, u32[]{:S(2)}) copy-start(bf16[128,512]{0,1:T(8,128)(2,1)S(1)} %copy.234) | copy-start | bytes 393220
  6.3 23.2 %copy-start.18 = (bf16[128,512]{0,1:T(8,128)(2,1)}, bf16[128,512]{0,1:T(8,128)(2,1)S(1)}, u32[]{:S(2)}) copy-start(bf16[128,512]{0,1:T(8,128)(2,1)S(1)} %copy.235) | copy-start | bytes 393220
  6.4 33.1 %copy-start.20 = (bf16[128,512]{0,1:T(8,128)(2,1)}, bf16[128,512]{0,1:T(8,128)(2,1)S(1)}, u32[]{:S(2)}) copy-start(bf16[128,512]{0,1:T(8,128)(2,1)S(1)} %copy.236) | copy-start | bytes 393220
  10.1 17.3 %copy-start.49 = (s32[128]{0:T(128)}, s32[128]{0:T(128)S(1)}, u32[]{:S(2)}) copy-start(s32[128]{0:T(128)S(1)} %fusion.86) | copy-start | bytes 1540
  10.6 31.5 %copy-start.23 = (bf16[128,512]{1,0:T(8,128)(2,1)}, bf16[128,512]{1,0:T(8,128)(2,1)S(1)}, u32[]{:S(2)}) copy-start(bf16[128,512]{1,0:T(8,128)(2,1)S(1)} %fusion.23) | copy-start | bytes 393220
  12.6 26.7 %all-to-all-start = ((bf16[32,8,1024]{2,1,0:T(8,128)(2,1)}), bf16[32,8,1024]{2,1,0:T(8,128)(2,1)S(1)}, u32[]{:S(2)}, u32[]{:S(2)}) async-start(bf16[32,8,1024]{2,1,0:T(8,128)(2,1)} %fusion.18), calls=%async_computation | async-start | bytes 1048576 | tf_op jit(solution)/shard_map/all_to_all | solution.py:177
  25.7 2.5 %copy-start.37 = (s32[6]{0:T(128)}, s32[6]{0:T(128)S(1)}, u32[]{:S(2)}) copy-start(s32[6]{0:T(128)S(1)} %reshape.366) | copy-start | bytes 76
  27.6 18.4 %copy-start.39 = (s32[1024]{0:T(1024)}, s32[1024]{0:T(1024)S(1)}, u32[]{:S(2)}) copy-start(s32[1024]{0:T(1024)S(1)} %pad_clamp_fusion) | copy-start | bytes 12292
  39.4 5.0 %copy-start.3 = (bf16[32,8,1024]{2,1,0:T(8,128)(2,1)}, bf16[32,8,1024]{2,1,0:T(8,128)(2,1)S(1)}, u32[]{:S(2)}) copy-start(bf16[32,8,1024]{2,1,0:T(8,128)(2,1)S(1)} %all-to-all-done) | copy-start | bytes 1572868
  39.5 6.1 %copy-start.40 = (f32[256]{0:T(256)}, f32[256]{0:T(256)S(1)}, u32[]{:S(2)}) copy-start(f32[256]{0:T(256)S(1)} %broadcast_multiply_fusion.1) | copy-start | bytes 3076
  39.7 2.3 %copy-start.42 = (f32[256]{0:T(256)}, f32[256]{0:T(256)S(1)}, u32[]{:S(2)}) copy-start(f32[256]{0:T(256)S(1)} %fusion.34) | copy-start | bytes 3076
  48.2 6.0 %copy-start.14 = (pred[2,128,384]{2,1,0:T(8,128)(4,1)S(1)}, pred[2,128,384]{2,1,0:T(8,128)(4,1)}, u32[]{:S(2)}) copy-start(pred[2,128,384]{2,1,0:T(8,128)(4,1)} %broadcast_or_fusion) | copy-start | bytes 294916
  50.4 5.0 %copy-start.6 = (bf16[2,384,8,64]{1,0,3,2:T(2,128)(2,1)}, bf16[2,384,8,64]{1,0,3,2:T(2,128)(2,1)S(1)}, u32[]{:S(2)}) copy-start(bf16[2,384,8,64]{1,0,3,2:T(2,128)(2,1)S(1)} %reshape.354) | copy-start | bytes 2359300
  60.0 8.2 %copy-start.15 = (pred[2,128,384]{2,1,0:T(8,128)(4,1)S(1)}, pred[2,128,384]{2,1,0:T(8,128)(4,1)}, u32[]{:S(2)}) copy-start(pred[2,128,384]{2,1,0:T(8,128)(4,1)} %broadcast_or_fusion) | copy-start | bytes 294916
  60.0 8.2 %copy-start.46 = (f32[2,8,128]{2,1,0:T(8,128)S(1)}, f32[2,8,128]{2,1,0:T(8,128)}, u32[]{:S(2)}) copy-start(f32[2,8,128]{2,1,0:T(8,128)} %multiply_divide_fusion) | copy-start | bytes 24580
  62.2 9.6 %copy-start.8 = (bf16[2,384,8,64]{1,0,3,2:T(2,128)(2,1)}, bf16[2,384,8,64]{1,0,3,2:T(2,128)(2,1)S(1)}, u32[]{:S(2)}) copy-start(bf16[2,384,8,64]{1,0,3,2:T(2,128)(2,1)S(1)} %reshape.351) | copy-start | bytes 2359300
  68.2 3.6 %copy-start.2 = (f32[2,8,128,384]{3,2,1,0:T(8,128)S(1)}, f32[2,8,128,384]{3,2,1,0:T(8,128)}, u32[]{:S(2)}) copy-start(f32[2,8,128,384]{3,2,1,0:T(8,128)} %copy-done.1) | copy-start | bytes 9437188
  68.2 3.7 %copy-start.34 = (f32[2,8,128]{2,1,0:T(8,128)S(1)}, f32[2,8,128]{2,1,0:T(8,128)}, u32[]{:S(2)}) copy-start(f32[2,8,128]{2,1,0:T(8,128)} %copy-done.33) | copy-start | bytes 24580
  71.9 3.0 %copy-start.7 = (bf16[2,384,8,64]{1,0,3,2:T(2,128)(2,1)S(1)}, bf16[2,384,8,64]{1,0,3,2:T(2,128)(2,1)}, u32[]{:S(2)}) copy-start(bf16[2,384,8,64]{1,0,3,2:T(2,128)(2,1)} %copy-done.6) | copy-start | bytes 2359300
  74.9 2.5 %copy-start.26 = (bf16[2,128,8,64]{1,3,2,0:T(8,128)(2,1)S(1)}, bf16[2,128,8,64]{1,3,2,0:T(8,128)(2,1)}, u32[]{:S(2)}) copy-start(bf16[2,128,8,64]{1,3,2,0:T(8,128)(2,1)} %copy.245) | copy-start | bytes 786436
  79.7 2.7 %copy-start.28 = (bf16[512,512]{1,0:T(8,128)(2,1)S(1)}, bf16[512,512]{1,0:T(8,128)(2,1)}, u32[]{:S(2)}) copy-start(bf16[512,512]{1,0:T(8,128)(2,1)} %param.17) | copy-start | bytes 1572868
  87.6 6.6 %copy-start.38 = (s32[6]{0:T(128)S(1)}, s32[6]{0:T(128)}, u32[]{:S(2)}) copy-start(s32[6]{0:T(128)} %copy-done.37) | copy-start | bytes 76
  108.3 4.7 %copy-start.4 = (bf16[32,8,1024]{2,1,0:T(8,128)(2,1)S(1)}, bf16[32,8,1024]{2,1,0:T(8,128)(2,1)}, u32[]{:S(2)}) copy-start(bf16[32,8,1024]{2,1,0:T(8,128)(2,1)} %copy-done.3) | copy-start | bytes 1572868
  108.3 4.7 %copy-start.41 = (f32[256]{0:T(256)S(1)}, f32[256]{0:T(256)}, u32[]{:S(2)}) copy-start(f32[256]{0:T(256)} %copy-done.40) | copy-start | bytes 3076
  111.7 2.8 %copy-start.43 = (f32[256]{0:T(256)S(1)}, f32[256]{0:T(256)}, u32[]{:S(2)}) copy-start(f32[256]{0:T(256)} %copy-done.42) | copy-start | bytes 3076
  111.8 2.9 %copy-start.51 = (f32[256]{0:T(256)S(1)}, f32[256]{0:T(256)}, u32[]{:S(2)}) copy-start(f32[256]{0:T(256)} %copy-done.50) | copy-start | bytes 3076
  111.8 2.8 %copy-start.29 = (bf16[64,8,2,128]{3,1,2,0:T(8,128)(2,1)}, bf16[64,8,2,128]{3,1,2,0:T(8,128)(2,1)S(1)}, u32[]{:S(2)}) copy-start(bf16[64,8,2,128]{3,1,2,0:T(8,128)(2,1)S(1)} %copy.316) | copy-start | bytes 786436
  114.6 12.8 %copy-start.52 = (f32[256]{0:T(256)S(1)}, f32[256]{0:T(256)}, u32[]{:S(2)}) copy-start(f32[256]{0:T(256)} %copy-done.50) | copy-start | bytes 3076
  115.9 23.6 %all-to-all-start.1 = ((bf16[32,8,1024]{2,1,0:T(8,128)(2,1)}), bf16[32,8,1024]{2,1,0:T(8,128)(2,1)S(1)}, u32[]{:S(2)}, u32[]{:S(2)}) async-start(bf16[32,8,1024]{2,1,0:T(8,128)(2,1)} %maximum_bitcast_fusion.1), calls=%async_computation.1 | async-start | bytes 1048576 | tf_op jit(solution)/shard_map/all_to_all | solution.py:194
  130.4 4.5 %copy-start.13 = (bf16[32,8,2,512]{3,2,0,1:T(2,128)(2,1)S(1)}, bf16[32,8,2,512]{3,2,0,1:T(2,128)(2,1)}, u32[]{:S(2)}) copy-start(bf16[32,8,2,512]{3,2,0,1:T(2,128)(2,1)} %copy.268) | copy-start | bytes 1572868
  139.5 8.2 %copy-start.11 = (bf16[512,512]{1,0:T(8,128)(2,1)S(1)}, bf16[512,512]{1,0:T(8,128)(2,1)}, u32[]{:S(2)}) copy-start(bf16[512,512]{1,0:T(8,128)(2,1)} %param.14) | copy-start | bytes 1572868
  139.5 11.7 %copy-start.36 = (f32[8,128]{1,0:T(8,128)S(1)}, f32[8,128]{1,0:T(8,128)}, u32[]{:S(2)}) copy-start(f32[8,128]{1,0:T(8,128)} %multiply_divide_fusion.1) | copy-start | bytes 12292
  140.3 32.4 %all-to-all-start.2 = ((bf16[8,32,2,2048]{3,2,1,0:T(2,128)(2,1)}), bf16[8,32,2,2048]{3,2,1,0:T(2,128)(2,1)}, u32[]{:S(2)}, u32[]{:S(2)}) async-start(bf16[8,32,2,2048]{3,2,1,0:T(2,128)(2,1)} %maximum_bitcast_fusion), calls=%async_computation.2 | async-start | bytes 4194304 | tf_op jit(solution)/shard_map/all_to_all | solution.py:130
  146.4 6.5 %copy-start.35 = (f32[8,128]{1,0:T(8,128)S(1)}, f32[8,128]{1,0:T(8,128)}, u32[]{:S(2)}) copy-start(f32[8,128]{1,0:T(8,128)} %get-tuple-element.6) | copy-start | bytes 12292
  151.3 2.8 %copy-start.17 = (pred[8,128,128]{1,2,0:T(32,128)(4,1)S(1)}, pred[8,128,128]{1,2,0:T(32,128)(4,1)}, u32[]{:S(2)}) copy-start(pred[8,128,128]{1,2,0:T(32,128)(4,1)} %get-tuple-element.7) | copy-start | bytes 393220
  151.3 2.8 %copy-start.21 = (bf16[128,512]{0,1:T(8,128)(2,1)S(1)}, bf16[128,512]{0,1:T(8,128)(2,1)}, u32[]{:S(2)}) copy-start(bf16[128,512]{0,1:T(8,128)(2,1)} %copy-done.20) | copy-start | bytes 393220
  151.3 3.0 %copy-start.19 = (bf16[128,512]{0,1:T(8,128)(2,1)S(1)}, bf16[128,512]{0,1:T(8,128)(2,1)}, u32[]{:S(2)}) copy-start(bf16[128,512]{0,1:T(8,128)(2,1)} %copy-done.18) | copy-start | bytes 393220
  151.3 3.4 %copy-start.16 = (bf16[512,1536]{1,0:T(8,128)(2,1)S(1)}, bf16[512,1536]{1,0:T(8,128)(2,1)}, u32[]{:S(2)}) copy-start(bf16[512,1536]{1,0:T(8,128)(2,1)} %param.13) | copy-start | bytes 4718596
  152.7 3.4 %copy-start.54 = (f32[128]{0:T(128)S(1)}, f32[128]{0:T(128)}, u32[]{:S(2)}) copy-start(f32[128]{0:T(128)} %copy-done.53) | copy-start | bytes 1540
  154.3 32.1 %copy-start.45 = (f32[128]{0:T(128)S(1)}, f32[128]{0:T(128)}, u32[]{:S(2)}) copy-start(f32[128]{0:T(128)} %copy-done.44) | copy-start | bytes 1540
  154.3 32.1 %copy-start.48 = (f32[128]{0:T(128)S(1)}, f32[128]{0:T(128)}, u32[]{:S(2)}) copy-start(f32[128]{0:T(128)} %copy-done.47) | copy-start | bytes 1540
  154.6 32.1 %copy-start.25 = (bf16[1,128,512]{2,1,0:T(8,128)(2,1)S(1)}, bf16[1,128,512]{2,1,0:T(8,128)(2,1)}, u32[]{:S(2)}) copy-start(bf16[1,128,512]{2,1,0:T(8,128)(2,1)} %param.11) | copy-start | bytes 393220
  154.7 49.2 %copy-start.24 = (bf16[128,512]{1,0:T(8,128)(2,1)S(1)}, bf16[128,512]{1,0:T(8,128)(2,1)}, u32[]{:S(2)}) copy-start(bf16[128,512]{1,0:T(8,128)(2,1)} %copy-done.23) | copy-start | bytes 393220
  177.1 19.0 %all-to-all-start.3 = ((bf16[32,2,2048]{2,1,0:T(2,128)(2,1)}), bf16[32,2,2048]{2,1,0:T(2,128)(2,1)S(1)}, u32[]{:S(2)}, u32[]{:S(2)}) async-start(bf16[32,2,2048]{2,1,0:T(2,128)(2,1)} %reduce_sum.236), calls=%async_computation.3 | async-start | bytes 524288 | tf_op jit(solution)/shard_map/all_to_all | solution.py:132
  196.9 12.2 %all-to-all-start.4 = ((f32[8,2,2048]{2,1,0:T(2,128)}), f32[8,2,2048]{2,1,0:T(2,128)S(1)}, u32[]{:S(2)}, u32[]{:S(2)}) async-start(f32[8,2,2048]{2,1,0:T(2,128)} %broadcast_in_dim.102), calls=%async_computation.4 | async-start | bytes 262144 | tf_op jit(solution)/shard_map/all_to_all | solution.py:135
  (12 other events, 18.9 us)

commit v2 on v1

--- a/solution.py
+++ b/solution.py
@@ -44,6 +44,13 @@
     return (source.astype(jnp.float32) + branch).astype(jnp.bfloat16)
 
 
+def pick_blocks(blocks, chosen):
+    picked = blocks[0]
+    for index in range(1, blocks.shape[0]):
+        picked = jnp.where(chosen == index, blocks[index], picked)
+    return picked
+
+
 def cross_account_inner(packed_rows, row_presence, block_listing):
     row_total, three_wide = packed_rows.shape
     features = three_wide // 3
@@ -51,18 +58,20 @@
     selected_rows = jnp.concatenate(
         [jnp.arange(block_groups, dtype=jnp.int32)[:, None], block_listing], axis=1
     )
+    segments = selected_rows.shape[1]
+    chosen = selected_rows[:, :, None, None, None]
     queries = split_heads(packed_rows[:, :features].astype(jnp.float32), block_groups)
-    key_rows = split_heads(
+    key_blocks = split_heads(
         packed_rows[:, features : 2 * features].astype(jnp.float32), block_groups
-    )[selected_rows]
-    key_rows = key_rows.reshape(block_groups, -1, HEADS, HEAD_DIM)
-    value_rows = split_heads(packed_rows[:, 2 * features :].astype(jnp.float32), block_groups)[
-        selected_rows
-    ]
-    value_rows = value_rows.reshape(block_groups, -1, HEADS, HEAD_DIM)
-    key_present = row_presence.reshape(block_groups, EVENTS_PER_BLOCK)[selected_rows].reshape(
-        block_groups, -1
-    )
+    )
+    key_rows = pick_blocks(key_blocks[:, None], chosen)
+    key_rows = key_rows.reshape(block_groups, segments * EVENTS_PER_BLOCK, HEADS, HEAD_DIM)
+    value_blocks = split_heads(packed_rows[:, 2 * features :].astype(jnp.float32), block_groups)
+    value_rows = pick_blocks(value_blocks[:, None], chosen)
+    value_rows = value_rows.reshape(block_groups, segments * EVENTS_PER_BLOCK, HEADS, HEAD_DIM)
+    presence_blocks = row_presence.reshape(block_groups, EVENTS_PER_BLOCK)
+    key_present = pick_blocks(presence_blocks[:, None], selected_rows[:, :, None])
+    key_present = key_present.reshape(block_groups, -1)
     key_total = key_present.shape[1]
     itself = (
         jnp.arange(key_total, dtype=jnp.int32)[None, :]

time: 215 us -> 198 us (0.921); the launches traced: 211 us -> 196 us
  local copies, waits for them, and re-layouts: 60 us -> 43.7 us
  matrix products: 35.8 us -> 32.2 us
  other arithmetic: 31.6 us -> 34.9 us
  waiting for transfers between devices: 39.6 us -> 42.9 us
    reshape x6 -> x0, local copies, waits for them, and re-layouts: 17.4 us -> none  [the longest x3 8.72 us: cross_account_inner(): key_rows = key_rows.reshape(block_groups, -1, HEADS, HEAD_DIM)]
    reduce_sum x0 -> x4, other arithmetic: none -> 9.55 us  [pick_blocks(): picked = jnp.where(chosen == index, blocks[index], picked)]
    broadcast_in_dim x0 -> x9, local copies, waits for them, and re-layouts: none -> 8.63 us  [pick_blocks(): picked = jnp.where(chosen == index, blocks[index], picked)]
    reduce_sum x0 -> x4, local copies, waits for them, and re-layouts: none -> 8.18 us  [pick_blocks(): picked = jnp.where(chosen == index, blocks[index], picked)]
    slice x0 -> x6, local copies, waits for them, and re-layouts: none -> 7.42 us  [the longest x4 4.1 us: pick_blocks(): picked = jnp.where(chosen == index, blocks[index], picked)]
    transpose x2 -> x0, local copies, waits for them, and re-layouts: 6.17 us -> none  [the longest x1 3.79 us: cross_account_inner(): jnp.einsum('bhqk,bkhd->bqhd', attention.astype(jnp.float32), value_rows)]
    scatter-add x2 -> x0, other arithmetic: 5.86 us -> none  [the longest x1 3.06 us: cross_account_inner(): split_heads(packed_rows[:, 2 * features:].astype(jnp.float32), block_groups)]
    gather x5 -> x0, local copies, waits for them, and re-layouts: 5.16 us -> none  [the longest x2 2.36 us: cross_account_inner(): split_heads(packed_rows[:, 2 * features:].astype(jnp.float32), block_groups)]
  transfers between devices with their start and end apart: 5 -> 5, of which waited for: 4 -> 5; matrix products, arithmetic and copies ran while one was open for 15% -> 13% of each run, Pallas kernels for 0% -> 0%
where the time goes in v2:
time: 198 us; the launch traced here: 196 us
  local copies, waits for them, and re-layouts  43.7 us (22%)
  waiting for transfers between devices  42.9 us (22%)
  starting transfers between devices  41 us (21%)
  other arithmetic  34.9 us (18%)
  matrix products  32.2 us (16%)
    all_to_all x1, waiting for transfers between devices, reduce_weight_terms(): terms = lax.all_to_all(terms, 'dp', 0, 0, tiled=True)  16.9 us
    all_to_all x1, starting transfers between devices, on_device(): lax.all_to_all(outgoing, 'ev', split_axis=0, concat_axis=0, tiled=True)  12.2 us
    all_to_all x1, waiting for transfers between devices, on_device(): lax.all_to_all(outgoing, 'ev', split_axis=0, concat_axis=0, tiled=True)  11.7 us
    reduce_sum x4, other arithmetic, pick_blocks(): picked = jnp.where(chosen == index, blocks[index], picked)  9.55 us
    all_to_all x1, starting transfers between devices, reduce_weight_terms(): terms = lax.all_to_all(terms, 'dp', 0, 0, tiled=True)  8.65 us
    broadcast_in_dim x9, local copies, waits for them, and re-layouts, pick_blocks(): picked = jnp.where(chosen == index, blocks[index], picked)  8.63 us
    all_to_all x1, waiting for transfers between devices, reduce_weight_terms(): terms = lax.all_to_all(terms, 'ev', 0, 0, tiled=True)  8.61 us
    dot_general x3, matrix products, cross_account_inner(): jnp.einsum('bqhd,bkhd->bhqk', queries, key_rows) * HEAD_DIM ** (-0.5)  8.38 us
  transfers between devices with their start and end apart: 5, of which 5 were waited for; matrix products, arithmetic and copies ran while one was open for 13% of the time, Pallas kernels for 0%

profile of v2, /device:TPU:1, one launch (start us, length us, event | category | flops | bytes accessed | tf_op | source)
XLA Modules:
  0.0 196.3 jit_solution(5486674596430928689)
XLA Ops:
  0.6 1.1 convert_reduce_fusion.5
  1.8 1.1 fusion.79
  5.3 2.0 %convolution_convert_fusion.2 = bf16[128,1536]{1,0:T(8,128)(2,1)S(1)} fusion(bf16[512,1536]{1,0:T(8,128)(2,1)} %param.13, bf16[1,128,512]{2,1,0:T(8,128)(2,1)} %param.10, f32[512]{0:T(512)} %param.12, f32[128]{0:T(128)S(1)} %fusion.116, f32[128]{0:T(128)S(1)} %broadcast_multiply_fusion.2), kind=kOutput, calls=%fused_computation.15 | convolution fusion | flops 201850880 | bytes 2100224 | tf_op jit(solution)/shard_map/jvp()/dot_general | solution.py:29
  10.9 1.1 fusion.29
  11.9 12.2 %all-to-all-start = ((bf16[32,8,1024]{2,1,0:T(8,128)(2,1)}), bf16[32,8,1024]{2,1,0:T(8,128)(2,1)S(1)}, u32[]{:S(2)}, u32[]{:S(2)}) async-start(bf16[32,8,1024]{2,1,0:T(8,128)(2,1)} %fusion.29), calls=%async_computation | async-start | bytes 1048576 | tf_op jit(solution)/shard_map/all_to_all | solution.py:186
  26.8 11.7 %all-to-all-done = bf16[32,8,1024]{2,1,0:T(8,128)(2,1)S(1)} async-done(((bf16[32,8,1024]{2,1,0:T(8,128)(2,1)}), bf16[32,8,1024]{2,1,0:T(8,128)(2,1)S(1)}, u32[]{:S(2)}, u32[]{:S(2)}) %all-to-all-start) | async-done | bytes 524320 | tf_op jit(solution)/shard_map/all_to_all | solution.py:186
  39.4 1.4 convolution_convert_fusion.6
  43.2 1.7 copy.175
  44.9 1.7 copy.176
  46.6 1.7 copy.179
  48.2 1.6 copy.178
  50.9 1.1 broadcast_in_dim.219
  55.3 1.1 broadcast_in_dim.209
  57.4 1.1 broadcast_in_dim.206
  59.9 2.1 %fusion.144 = (f32[2,8,128]{2,1,0:T(8,128)S(1)}, f32[2,8,128,384]{3,2,1,0:T(8,128)S(1)}) fusion(bf16[2,128,8,64]{1,3,2,0:T(8,128)(2,1)} %copy.180, bf16[384,8,64]{0,2,1:T(8,128)(2,1)} %broadcast_in_dim.222, bf16[384,8,64]{0,2,1:T(8,128)(2,1)} %broadcast_in_dim.219, pred[2,384]{1,0:T(4,128)(4,1)} %bitcast.241, pred[2,128,384]{2,1,0:T(8,128)(4,1)} %broadcast_or_fusion), kind=kOutput, calls=%fused_computation.213 | convolution fusion | flops 103413760 | bytes 4301568 | tf_op jit(solution)/shard_map/jvp(bqhd,bkhd->bhqk)/dot_general | solution.py:81
  62.0 1.2 fusion.14
  63.3 1.8 fusion.4
  65.1 3.0 %divide_convert_fusion = (bf16[2,8,128,384]{3,2,1,0:T(8,128)(2,1)S(1)}, f32[2,8,128]{2,1,0:T(8,128)S(1)}, f32[2,8,128]{2,1,0:T(8,128)S(1)}, pred[2,8,128,384]{3,2,1,0:T(32,128)(4,1)S(1)}) fusion(f32[2,8,128,384]{3,2,1,0:T(8,128)S(1)} %get-tuple-element.36, f32[2,8,128]{2,1,0:T(8,128)S(1)} %fusion.14, f32[2,8,128]{2,1,0:T(8,128)S(1)} %get-tuple-element.35, ...), kind=kLoop, calls=%fused_computation.9 | loop fusion | flops 10219520 | bytes 7217152 | tf_op jit(solution)/shard_map/jvp()/convert_element_type | solution.py:85
  68.2 2.4 %fusion.40 = bf16[2,128,8,64]{1,3,2,0:T(8,128)(2,1)S(1)} fusion(pred[2,8,128,384]{3,2,1,0:T(32,128)(4,1)S(1)} %get-tuple-element.19, f32[2,8,128]{2,1,0:T(8,128)S(1)} %negate_divide_fusion, pred[2,128,384]{2,1,0:T(8,128)(4,1)S(1)} %copy-done.15, bf16[384,8,64]{0,2,1:T(8,128)(2,1)S(1)} %copy-done.20, bf16[384,8,64]{0,2,1:T(8,128)(2,1)S(1)} %copy-done.19, ...), kind=kOutput, calls=%fused_computation.54 | convolution fusion | flops 108920832 | bytes 6685440 | tf_op jit(solution)/shard_map/transpose(jvp(bqhd,bkhd->bhqk))/dot_general | solution.py:81
  70.5 3.9 %select_reduce_fusion.1 = (f32[8,384,64]{1,2,0:T(8,128)}, f32[8,384,64]{1,2,0:T(8,128)}) fusion(pred[2,384]{1,0:T(4,128)(4,1)S(1)} %bitcast.244, bf16[2,128,8,64]{1,3,2,0:T(8,128)(2,1)S(1)} %copy-done.21, pred[2,8,128,384]{3,2,1,0:T(32,128)(4,1)S(1)} %get-tuple-element.19, f32[2,8,128]{2,1,0:T(8,128)S(1)} %negate_divide_fusion, ...), kind=kOutput, calls=%fused_computation.29 | convolution fusion | flops 109707264 | bytes 7471872 | tf_op jit(solution)/shard_map/transpose(jvp(bqhd,bkhd->bhqk))/dot_general | solution.py:81
  75.3 1.4 select_reduce_fusion.3
  79.7 2.3 %reduce_sum.319 = f32[3,128,8,64]{1,0,3,2:T(4,128)} reshape(f32[384,8,64]{0,2,1:T(8,128)} %bitcast.224) | data formatting | bytes 1572864 | tf_op jit(solution)/shard_map/transpose(jvp(jit(_where)))/reduce_sum | solution.py:50
  82.0 2.3 %reduce_sum.315 = f32[3,128,8,64]{1,0,3,2:T(4,128)} reshape(f32[384,8,64]{0,2,1:T(8,128)} %bitcast.223) | data formatting | bytes 1572864 | tf_op jit(solution)/shard_map/transpose(jvp(jit(_where)))/reduce_sum | solution.py:50
  84.3 2.5 %reduce_sum.320 = f32[128,8,64]{0,2,1:T(8,128)} reduce(f32[3,128,8,64]{1,0,3,2:T(4,128)} %reduce_sum.319, f32[]{:T(128)} %constant.23.clone.1), dimensions={0}, to_apply=%region_21.22 | reduce | flops 131072 | bytes 1048580 | tf_op jit(solution)/shard_map/transpose(jvp(jit(_where)))/reduce_sum | solution.py:50
  86.8 2.6 %reduce_sum.316 = f32[128,8,64]{0,2,1:T(8,128)} reduce(f32[3,128,8,64]{1,0,3,2:T(4,128)} %reduce_sum.315, f32[]{:T(128)} %constant.23.clone.1), dimensions={0}, to_apply=%region_19.20 | reduce | flops 131072 | bytes 1048580 | tf_op jit(solution)/shard_map/transpose(jvp(jit(_where)))/reduce_sum | solution.py:50
  89.4 1.4 add_convert_fusion.1
  91.6 2.3 %reduce_sum.308 = f32[3,128,8,64]{1,0,3,2:T(4,128)} reshape(f32[384,8,64]{0,2,1:T(8,128)} %bitcast.201) | data formatting | bytes 1572864 | tf_op jit(solution)/shard_map/transpose(jvp(jit(_where)))/reduce_sum | solution.py:50
  93.9 2.5 %reduce_sum.309 = f32[128,8,64]{0,2,1:T(8,128)} reduce(f32[3,128,8,64]{1,0,3,2:T(4,128)} %reduce_sum.308, f32[]{:T(128)} %constant.23.clone.1), dimensions={0}, to_apply=%region_14.15 | reduce | flops 131072 | bytes 1048580 | tf_op jit(solution)/shard_map/transpose(jvp(jit(_where)))/reduce_sum | solution.py:50
  96.4 1.3 reduce_sum.304
  97.7 1.9 reduce_sum.305
  99.6 1.4 add_convert_fusion.2
  102.9 1.7 fusion.65
  105.9 7.4 %all-to-all-start.1 = ((bf16[32,8,1024]{2,1,0:T(8,128)(2,1)}), bf16[32,8,1024]{2,1,0:T(8,128)(2,1)}, u32[]{:S(2)}, u32[]{:S(2)}) async-start(bf16[32,8,1024]{2,1,0:T(8,128)(2,1)} %maximum_bitcast_fusion.1), calls=%async_computation.1 | async-start | bytes 1048576 | tf_op jit(solution)/shard_map/all_to_all | solution.py:203
  114.0 3.0 %convolution_convert_fusion = bf16[512,1536]{1,0:T(8,128)(2,1)} fusion(bf16[256,512]{0,1:T(8,128)(2,1)S(1)} %bitcast.231, bf16[256,512]{0,1:T(8,128)(2,1)} %bitcast.232, bf16[256,512]{0,1:T(8,128)(2,1)} %bitcast.235, f32[512]{0:T(512)} %param.15, f32[256]{0:T(256)} %copy-done.36, f32[256]{0:T(256)} %copy-done.26, bf16[256,1024]{1,0:T(8,128)(2,1)S(1)} %bitcast.199), kind=kOutput, calls=%fused_computation.12 | convolution fusion | flops 406454272 | bytes 2625536 | tf_op jit(solution)/shard_map/dot_general | solution.py:128
  117.0 4.5 %concatenate.30 = bf16[32,8,2,1536]{3,2,1,0:T(2,128)(2,1)} reshape(bf16[512,1536]{1,0:T(8,128)(2,1)} %convolution_convert_fusion) | data formatting | bytes 3145728 | tf_op jit(solution)/shard_map/concatenate | solution.py:211
  121.4 4.6 %maximum_bitcast_fusion = bf16[8,32,2,2048]{3,2,1,0:T(2,128)(2,1)} fusion(bf16[32,8,2,512]{3,2,0,1:T(2,128)(2,1)S(1)} %copy.193, bf16[32,8,2,1536]{3,2,1,0:T(2,128)(2,1)} %concatenate.30), kind=kLoop, calls=%fused_computation.24 | loop fusion | flops 4194304 | bytes 4194304 | tf_op jit(solution)/shard_map/transpose | solution.py:138
  127.1 8.7 %all-to-all-start.2 = ((bf16[8,32,2,2048]{3,2,1,0:T(2,128)(2,1)}), bf16[8,32,2,2048]{3,2,1,0:T(2,128)(2,1)}, u32[]{:S(2)}, u32[]{:S(2)}) async-start(bf16[8,32,2,2048]{3,2,1,0:T(2,128)(2,1)} %maximum_bitcast_fusion), calls=%async_computation.2 | async-start | bytes 4194304 | tf_op jit(solution)/shard_map/all_to_all | solution.py:139
  135.7 1.4 fusion.66
  137.1 1.9 convolution_convert_fusion.11
  140.0 1.3 multiply_reduce_fusion
  141.8 1.2 convolution_convert_fusion.8
  143.0 1.3 convolution_convert_fusion.9
  145.1 16.9 %all-to-all-done.2 = bf16[8,32,2,2048]{3,2,1,0:T(2,128)(2,1)} async-done(((bf16[8,32,2,2048]{3,2,1,0:T(2,128)(2,1)}), bf16[8,32,2,2048]{3,2,1,0:T(2,128)(2,1)}, u32[]{:S(2)}, u32[]{:S(2)}) %all-to-all-start.2) | async-done | bytes 2097184 | tf_op jit(solution)/shard_map/all_to_all | solution.py:139
  162.0 4.3 %reduce_sum.328 = bf16[32,2,2048]{2,1,0:T(2,128)(2,1)} reduce(bf16[8,32,2,2048]{3,2,1,0:T(2,128)(2,1)} %all-to-all-done.2, bf16[]{:T(256)} %constant.65.clone.1), dimensions={0}, to_apply=%region_29.30 | reduce | flops 917504 | bytes 2359298 | tf_op jit(solution)/shard_map/reduce_sum | solution.py:140
  166.4 5.8 %all-to-all-start.3 = ((bf16[32,2,2048]{2,1,0:T(2,128)(2,1)}), bf16[32,2,2048]{2,1,0:T(2,128)(2,1)S(1)}, u32[]{:S(2)}, u32[]{:S(2)}) async-start(bf16[32,2,2048]{2,1,0:T(2,128)(2,1)} %reduce_sum.328), calls=%async_computation.3 | async-start | bytes 524288 | tf_op jit(solution)/shard_map/all_to_all | solution.py:141
  173.2 8.6 %all-to-all-done.3 = bf16[32,2,2048]{2,1,0:T(2,128)(2,1)S(1)} async-done(((bf16[32,2,2048]{2,1,0:T(2,128)(2,1)}), bf16[32,2,2048]{2,1,0:T(2,128)(2,1)S(1)}, u32[]{:S(2)}, u32[]{:S(2)}) %all-to-all-start.3) | async-done | bytes 262176 | tf_op jit(solution)/shard_map/all_to_all | solution.py:141
  182.6 6.9 %all-to-all-start.4 = ((f32[8,2,2048]{2,1,0:T(2,128)}), f32[8,2,2048]{2,1,0:T(2,128)S(1)}, u32[]{:S(2)}, u32[]{:S(2)}) async-start(f32[8,2,2048]{2,1,0:T(2,128)} %broadcast_in_dim.246), calls=%async_computation.4 | async-start | bytes 262144 | tf_op jit(solution)/shard_map/all_to_all | solution.py:144
  190.2 4.6 %all-to-all-done.4 = f32[8,2,2048]{2,1,0:T(2,128)S(1)} async-done(((f32[8,2,2048]{2,1,0:T(2,128)}), f32[8,2,2048]{2,1,0:T(2,128)S(1)}, u32[]{:S(2)}, u32[]{:S(2)}) %all-to-all-start.4) | async-done | bytes 131104 | tf_op jit(solution)/shard_map/all_to_all | solution.py:144
  (170 shorter events, 33.9 us)
Async XLA Ops:
  0.6 41.1 %copy-start = (bf16[512,1536]{1,0:T(8,128)(2,1)S(1)}, bf16[512,1536]{1,0:T(8,128)(2,1)}, u32[]{:S(2)}) copy-start(bf16[512,1536]{1,0:T(8,128)(2,1)} %param.16) | copy-start | bytes 4718596
  1.8 3.5 %copy-start.30 = (f32[128]{0:T(128)}, f32[128]{0:T(128)S(1)}, u32[]{:S(2)}) copy-start(f32[128]{0:T(128)S(1)} %broadcast_multiply_fusion.2) | copy-start | bytes 1540
  2.9 0.5 copy-start.40
  3.4 1.9 copy-start.33
  5.3 4.9 %copy-start.35 = (s32[128]{0:T(128)}, s32[128]{0:T(128)S(1)}, u32[]{:S(2)}) copy-start(s32[128]{0:T(128)S(1)} %fusion.115) | copy-start | bytes 1540
  5.3 4.6 %copy-start.1 = (bf16[1,128,512]{2,1,0:T(8,128)(2,1)S(1)}, bf16[1,128,512]{2,1,0:T(8,128)(2,1)}, u32[]{:S(2)}) copy-start(bf16[1,128,512]{2,1,0:T(8,128)(2,1)} %param.10) | copy-start | bytes 393220
  5.3 4.6 %copy-start.4 = (bf16[512,512]{1,0:T(8,128)(2,1)S(1)}, bf16[512,512]{1,0:T(8,128)(2,1)}, u32[]{:S(2)}) copy-start(bf16[512,512]{1,0:T(8,128)(2,1)} %param.14) | copy-start | bytes 1572868
  7.3 3.6 %copy-start.12 = (bf16[1,128,512]{2,1,0:T(8,128)(2,1)S(1)}, bf16[1,128,512]{2,1,0:T(8,128)(2,1)}, u32[]{:S(2)}) copy-start(bf16[1,128,512]{2,1,0:T(8,128)(2,1)} %param.11) | copy-start | bytes 393220
  7.3 16.8 %copy-start.25 = (s32[1,4096]{1,0:T(1,128)S(1)}, s32[1,4096]{1,0:T(1,128)}, u32[]{:S(2)}) copy-start(s32[1,4096]{1,0:T(1,128)} %param.18) | copy-start | bytes 49156
  7.4 17.7 %copy-start.39 = (s32[1,1,2,2]{3,2,1,0:T(2,128)S(1)}, s32[1,1,2,2]{3,2,1,0:T(2,128)}, u32[]{:S(2)}) copy-start(s32[1,1,2,2]{3,2,1,0:T(2,128)} %param.19) | copy-start | bytes 52
  7.5 19.3 %copy-start.7 = (bf16[128,512]{0,1:T(8,128)(2,1)}, bf16[128,512]{0,1:T(8,128)(2,1)S(1)}, u32[]{:S(2)}) copy-start(bf16[128,512]{0,1:T(8,128)(2,1)S(1)} %copy.173) | copy-start | bytes 393220
  7.6 31.0 %copy-start.8 = (bf16[128,512]{0,1:T(8,128)(2,1)}, bf16[128,512]{0,1:T(8,128)(2,1)S(1)}, u32[]{:S(2)}) copy-start(bf16[128,512]{0,1:T(8,128)(2,1)S(1)} %copy.172) | copy-start | bytes 393220
  7.8 31.1 %copy-start.9 = (bf16[128,512]{0,1:T(8,128)(2,1)}, bf16[128,512]{0,1:T(8,128)(2,1)S(1)}, u32[]{:S(2)}) copy-start(bf16[128,512]{0,1:T(8,128)(2,1)S(1)} %copy.171) | copy-start | bytes 393220
  9.0 0.7 copy-start.2
  9.0 32.7 %copy-start.42 = (f32[512]{0:T(512)S(1)}, f32[512]{0:T(512)}, u32[]{:S(2)}) copy-start(f32[512]{0:T(512)} %param.15) | copy-start | bytes 6148
  10.2 0.7 copy-start.10
  11.9 26.6 %all-to-all-start = ((bf16[32,8,1024]{2,1,0:T(8,128)(2,1)}), bf16[32,8,1024]{2,1,0:T(8,128)(2,1)S(1)}, u32[]{:S(2)}, u32[]{:S(2)}) async-start(bf16[32,8,1024]{2,1,0:T(8,128)(2,1)} %fusion.29), calls=%async_computation | async-start | bytes 1048576 | tf_op jit(solution)/shard_map/all_to_all | solution.py:186
  38.6 3.1 %copy-start.26 = (f32[256]{0:T(256)}, f32[256]{0:T(256)S(1)}, u32[]{:S(2)}) copy-start(f32[256]{0:T(256)S(1)} %broadcast_multiply_fusion.1) | copy-start | bytes 3076
  38.9 0.5 copy-start.28
  39.4 2.3 %copy-start.36 = (f32[256]{0:T(256)}, f32[256]{0:T(256)S(1)}, u32[]{:S(2)}) copy-start(f32[256]{0:T(256)S(1)} %fusion.114) | copy-start | bytes 3076
  58.8 3.2 %copy-start.15 = (pred[2,128,384]{2,1,0:T(8,128)(4,1)S(1)}, pred[2,128,384]{2,1,0:T(8,128)(4,1)}, u32[]{:S(2)}) copy-start(pred[2,128,384]{2,1,0:T(8,128)(4,1)} %broadcast_or_fusion) | copy-start | bytes 294916
  59.8 3.4 %copy-start.14 = (bf16[2,128,8,64]{1,0,3,2:T(2,128)(2,1)S(1)}, bf16[2,128,8,64]{1,0,3,2:T(2,128)(2,1)}, u32[]{:S(2)}) copy-start(bf16[2,128,8,64]{1,0,3,2:T(2,128)(2,1)} %reshape.364) | copy-start | bytes 786436
  59.8 3.4 %copy-start.17 = (bf16[384,8,64]{0,2,1:T(8,128)(2,1)S(1)}, bf16[384,8,64]{0,2,1:T(8,128)(2,1)}, u32[]{:S(2)}) copy-start(bf16[384,8,64]{0,2,1:T(8,128)(2,1)} %broadcast_in_dim.209) | copy-start | bytes 1179652
  59.9 3.4 %copy-start.18 = (bf16[384,8,64]{0,2,1:T(8,128)(2,1)S(1)}, bf16[384,8,64]{0,2,1:T(8,128)(2,1)}, u32[]{:S(2)}) copy-start(bf16[384,8,64]{0,2,1:T(8,128)(2,1)} %broadcast_in_dim.206) | copy-start | bytes 1179652
  59.9 3.4 %copy-start.32 = (pred[1,2,3,128]{3,1,2,0:T(4,128)(4,1)S(1)}, pred[1,2,3,128]{3,1,2,0:T(4,128)(4,1)}, u32[]{:S(2)}) copy-start(pred[1,2,3,128]{3,1,2,0:T(4,128)(4,1)} %copy.235) | copy-start | bytes 2308
  65.1 3.0 %copy-start.19 = (bf16[384,8,64]{0,2,1:T(8,128)(2,1)S(1)}, bf16[384,8,64]{0,2,1:T(8,128)(2,1)}, u32[]{:S(2)}) copy-start(bf16[384,8,64]{0,2,1:T(8,128)(2,1)} %broadcast_in_dim.219) | copy-start | bytes 1179652
  65.1 3.0 %copy-start.20 = (bf16[384,8,64]{0,2,1:T(8,128)(2,1)S(1)}, bf16[384,8,64]{0,2,1:T(8,128)(2,1)}, u32[]{:S(2)}) copy-start(bf16[384,8,64]{0,2,1:T(8,128)(2,1)} %broadcast_in_dim.222) | copy-start | bytes 1179652
  68.2 2.4 %copy-start.21 = (bf16[2,128,8,64]{1,3,2,0:T(8,128)(2,1)S(1)}, bf16[2,128,8,64]{1,3,2,0:T(8,128)(2,1)}, u32[]{:S(2)}) copy-start(bf16[2,128,8,64]{1,3,2,0:T(8,128)(2,1)} %copy.180) | copy-start | bytes 786436
  74.4 3.2 %copy-start.16 = (bf16[512,512]{1,0:T(8,128)(2,1)S(1)}, bf16[512,512]{1,0:T(8,128)(2,1)}, u32[]{:S(2)}) copy-start(bf16[512,512]{1,0:T(8,128)(2,1)} %param.17) | copy-start | bytes 1572868
  97.7 5.1 %copy-start.22 = (bf16[64,8,2,128]{3,1,2,0:T(8,128)(2,1)S(1)}, bf16[64,8,2,128]{3,1,2,0:T(8,128)(2,1)}, u32[]{:S(2)}) copy-start(bf16[64,8,2,128]{3,1,2,0:T(8,128)(2,1)} %copy.231) | copy-start | bytes 786436
  97.7 5.1 %copy-start.23 = (bf16[64,8,2,128]{3,1,2,0:T(8,128)(2,1)S(1)}, bf16[64,8,2,128]{3,1,2,0:T(8,128)(2,1)}, u32[]{:S(2)}) copy-start(bf16[64,8,2,128]{3,1,2,0:T(8,128)(2,1)} %copy.232) | copy-start | bytes 786436
  102.8 1.8 copy-start.29
  102.8 1.8 copy-start.27
  102.8 1.8 copy-start.37
  102.8 2.2 %copy-start.24 = (bf16[256,512]{1,0:T(8,128)(2,1)S(1)}, bf16[256,512]{1,0:T(8,128)(2,1)}, u32[]{:S(2)}) copy-start(bf16[256,512]{1,0:T(8,128)(2,1)} %convolution_convert_fusion.7) | copy-start | bytes 786436
  105.9 21.2 %all-to-all-start.1 = ((bf16[32,8,1024]{2,1,0:T(8,128)(2,1)}), bf16[32,8,1024]{2,1,0:T(8,128)(2,1)}, u32[]{:S(2)}, u32[]{:S(2)}) async-start(bf16[32,8,1024]{2,1,0:T(8,128)(2,1)} %maximum_bitcast_fusion.1), calls=%async_computation.1 | async-start | bytes 1048576 | tf_op jit(solution)/shard_map/all_to_all | solution.py:203
  126.0 11.1 %copy-start.5 = (bf16[512,512]{1,0:T(8,128)(2,1)S(1)}, bf16[512,512]{1,0:T(8,128)(2,1)}, u32[]{:S(2)}) copy-start(bf16[512,512]{1,0:T(8,128)(2,1)} %param.14) | copy-start | bytes 1572868
  127.1 35.0 %all-to-all-start.2 = ((bf16[8,32,2,2048]{3,2,1,0:T(2,128)(2,1)}), bf16[8,32,2,2048]{3,2,1,0:T(2,128)(2,1)}, u32[]{:S(2)}, u32[]{:S(2)}) async-start(bf16[8,32,2,2048]{3,2,1,0:T(2,128)(2,1)} %maximum_bitcast_fusion), calls=%async_computation.2 | async-start | bytes 4194304 | tf_op jit(solution)/shard_map/all_to_all | solution.py:139
  135.7 5.8 %copy-start.3 = (bf16[8,128,128]{1,2,0:T(8,128)(2,1)S(1)}, bf16[8,128,128]{1,2,0:T(8,128)(2,1)}, u32[]{:S(2)}) copy-start(bf16[8,128,128]{1,2,0:T(8,128)(2,1)} %copy-done.2) | copy-start | bytes 786436
  139.0 5.3 %copy-start.31 = (f32[128]{0:T(128)S(1)}, f32[128]{0:T(128)}, u32[]{:S(2)}) copy-start(f32[128]{0:T(128)} %copy-done.30) | copy-start | bytes 1540
  139.0 5.3 %copy-start.38 = (f32[512]{0:T(512)S(1)}, f32[512]{0:T(512)}, u32[]{:S(2)}) copy-start(f32[512]{0:T(512)} %param.12) | copy-start | bytes 6148
  140.0 4.3 %copy-start.6 = (bf16[512,1536]{1,0:T(8,128)(2,1)S(1)}, bf16[512,1536]{1,0:T(8,128)(2,1)}, u32[]{:S(2)}) copy-start(bf16[512,1536]{1,0:T(8,128)(2,1)} %param.13) | copy-start | bytes 4718596
  141.3 3.7 %copy-start.41 = (f32[128]{0:T(128)S(1)}, f32[128]{0:T(128)}, u32[]{:S(2)}) copy-start(f32[128]{0:T(128)} %copy-done.40) | copy-start | bytes 1540
  143.0 29.2 %copy-start.34 = (f32[128]{0:T(128)S(1)}, f32[128]{0:T(128)}, u32[]{:S(2)}) copy-start(f32[128]{0:T(128)} %copy-done.33) | copy-start | bytes 1540
  144.3 28.1 %copy-start.13 = (bf16[1,128,512]{2,1,0:T(8,128)(2,1)S(1)}, bf16[1,128,512]{2,1,0:T(8,128)(2,1)}, u32[]{:S(2)}) copy-start(bf16[1,128,512]{2,1,0:T(8,128)(2,1)} %param.11) | copy-start | bytes 393220
  144.3 45.2 %copy-start.11 = (bf16[128,512]{1,0:T(8,128)(2,1)S(1)}, bf16[128,512]{1,0:T(8,128)(2,1)}, u32[]{:S(2)}) copy-start(bf16[128,512]{1,0:T(8,128)(2,1)} %copy-done.10) | copy-start | bytes 393220
  166.4 15.5 %all-to-all-start.3 = ((bf16[32,2,2048]{2,1,0:T(2,128)(2,1)}), bf16[32,2,2048]{2,1,0:T(2,128)(2,1)S(1)}, u32[]{:S(2)}, u32[]{:S(2)}) async-start(bf16[32,2,2048]{2,1,0:T(2,128)(2,1)} %reduce_sum.328), calls=%async_computation.3 | async-start | bytes 524288 | tf_op jit(solution)/shard_map/all_to_all | solution.py:141
  182.6 12.2 %all-to-all-start.4 = ((f32[8,2,2048]{2,1,0:T(2,128)}), f32[8,2,2048]{2,1,0:T(2,128)S(1)}, u32[]{:S(2)}, u32[]{:S(2)}) async-start(f32[8,2,2048]{2,1,0:T(2,128)} %broadcast_in_dim.246), calls=%async_computation.4 | async-start | bytes 262144 | tf_op jit(solution)/shard_map/all_to_all | solution.py:144

commit v3 on v2

--- a/solution.py
+++ b/solution.py
@@ -44,11 +44,25 @@
     return (source.astype(jnp.float32) + branch).astype(jnp.bfloat16)
 
 
-def pick_blocks(blocks, chosen):
+def pick_block(blocks, chosen):
     picked = blocks[0]
     for index in range(1, blocks.shape[0]):
         picked = jnp.where(chosen == index, blocks[index], picked)
     return picked
+
+
+def gather_segments(blocks, selected_rows):
+    block_groups, segments = selected_rows.shape
+    return jnp.stack(
+        [
+            jnp.concatenate(
+                [pick_block(blocks, selected_rows[group, segment]) for segment in range(segments)],
+                axis=0,
+            )
+            for group in range(block_groups)
+        ],
+        axis=0,
+    )
 
 
 def cross_account_inner(packed_rows, row_presence, block_listing):
@@ -58,20 +72,15 @@
     selected_rows = jnp.concatenate(
         [jnp.arange(block_groups, dtype=jnp.int32)[:, None], block_listing], axis=1
     )
-    segments = selected_rows.shape[1]
-    chosen = selected_rows[:, :, None, None, None]
     queries = split_heads(packed_rows[:, :features].astype(jnp.float32), block_groups)
     key_blocks = split_heads(
         packed_rows[:, features : 2 * features].astype(jnp.float32), block_groups
     )
-    key_rows = pick_blocks(key_blocks[:, None], chosen)
-    key_rows = key_rows.reshape(block_groups, segments * EVENTS_PER_BLOCK, HEADS, HEAD_DIM)
+    key_rows = gather_segments(key_blocks, selected_rows)
     value_blocks = split_heads(packed_rows[:, 2 * features :].astype(jnp.float32), block_groups)
-    value_rows = pick_blocks(value_blocks[:, None], chosen)
-    value_rows = value_rows.reshape(block_groups, segments * EVENTS_PER_BLOCK, HEADS, HEAD_DIM)
+    value_rows = gather_segments(value_blocks, selected_rows)
     presence_blocks = row_presence.reshape(block_groups, EVENTS_PER_BLOCK)
-    key_present = pick_blocks(presence_blocks[:, None], selected_rows[:, :, None])
-    key_present = key_present.reshape(block_groups, -1)
+    key_present = gather_segments(presence_blocks, selected_rows)
     key_total = key_present.shape[1]
     itself = (
         jnp.arange(key_total, dtype=jnp.int32)[None, :]

time: 198 us -> 204 us (1.030)
  waiting for transfers between devices: 42.9 us -> 28.6 us
  local copies, waits for them, and re-layouts: 43.7 us -> 55.4 us
  between operations: 1.54 us -> 5.42 us
  starting transfers between devices: 41 us -> 43.6 us
  matrix products: 32.2 us -> 34.8 us
    select_n x0 -> x18, local copies, waits for them, and re-layouts: none -> 26.9 us  [pick_block(): picked = jnp.where(chosen == index, blocks[index], picked)]
    all_to_all x1, waiting for transfers between devices: 11.7 us -> 0.01 us  [on_device(): lax.all_to_all(outgoing, 'ev', split_axis=0, concat_axis=0, tiled=True)]
    reduce_sum x4 -> x0, other arithmetic: 9.55 us -> none  [pick_blocks(): picked = jnp.where(chosen == index, blocks[index], picked)]
    broadcast_in_dim x9 -> x0, local copies, waits for them, and re-layouts: 8.63 us -> none  [pick_blocks(): picked = jnp.where(chosen == index, blocks[index], picked)]
    reduce_sum x4 -> x0, local copies, waits for them, and re-layouts: 8.18 us -> none  [pick_blocks(): picked = jnp.where(chosen == index, blocks[index], picked)]
    select_n x1 -> x5, other arithmetic: 0.01 us -> 6.53 us  [pick_block(): picked = jnp.where(chosen == index, blocks[index], picked)]
    slice x6 -> x2, local copies, waits for them, and re-layouts: 7.42 us -> 1.12 us  [gather_segments(): selected_rows[group, segment]]
    reshape x2, local copies, waits for them, and re-layouts: 1.3 us -> 4.06 us  [split_heads(): return matrix.reshape(block_groups, EVENTS_PER_BLOCK, HEADS, HEAD_DIM)]
  transfers between devices with their start and end apart: 5 -> 5, of which waited for: 5 -> 3; matrix products, arithmetic and copies ran while one was open for 13% -> 20% of each run, Pallas kernels for 0% -> 0%
where the time goes in v3:
time: 204 us; the launch traced here: 202 us
  local copies, waits for them, and re-layouts  55.4 us (27%)
  starting transfers between devices  43.6 us (21%)
  matrix products  34.8 us (17%)
  other arithmetic  34.2 us (17%)
  waiting for transfers between devices  28.6 us (14%)
  between operations  5.42 us (3%)
    select_n x18, local copies, waits for them, and re-layouts, pick_block(): picked = jnp.where(chosen == index, blocks[index], picked)  26.9 us
    all_to_all x1, waiting for transfers between devices, reduce_weight_terms(): terms = lax.all_to_all(terms, 'dp', 0, 0, tiled=True)  15.4 us
    all_to_all x1, starting transfers between devices, on_device(): lax.all_to_all(outgoing, 'ev', split_axis=0, concat_axis=0, tiled=True)  12 us
    all_to_all x1, starting transfers between devices, on_device(): lax.all_to_all(going_back, 'ev', split_axis=0, concat_axis=0, tiled=True)  9.35 us
    all_to_all x1, waiting for transfers between devices, reduce_weight_terms(): terms = lax.all_to_all(terms, 'ev', 0, 0, tiled=True)  8.6 us
    dot_general x3, matrix products, cross_account_inner(): jnp.einsum('bqhd,bkhd->bhqk', queries, key_rows) * HEAD_DIM ** (-0.5)  7.84 us
    all_to_all x1, starting transfers between devices, reduce_weight_terms(): terms = lax.all_to_all(terms, 'dp', 0, 0, tiled=True)  7.72 us
    all_to_all x1, starting transfers between devices, reduce_weight_terms(): terms = lax.all_to_all(terms, 'ev', 0, 0, tiled=True)  7.53 us
  transfers between devices with their start and end apart: 5, of which 3 were waited for; matrix products, arithmetic and copies ran while one was open for 20% of the time, Pallas kernels for 0%

profile of v3, /device:TPU:1, one launch (start us, length us, event | category | flops | bytes accessed | tf_op | source)
XLA Modules:
  0.0 202.0 jit_solution(13406751582521105023)
XLA Ops:
  5.3 2.0 convolution_convert_fusion.2
  11.4 12.0 %all-to-all-start = ((bf16[32,8,1024]{2,1,0:T(8,128)(2,1)}), bf16[32,8,1024]{2,1,0:T(8,128)(2,1)S(1)}, u32[]{:S(2)}, u32[]{:S(2)}) async-start(bf16[32,8,1024]{2,1,0:T(8,128)(2,1)} %fusion.19), calls=%async_computation | async-start | bytes 1048576 | tf_op jit(solution)/shard_map/all_to_all | solution.py:195
  28.5 1.9 convert_reduce_fusion.4
  33.2 1.3 select_n.340
  43.2 2.1 %convolution_convert_fusion.7 = bf16[256,512]{1,0:T(8,128)(2,1)} fusion(bf16[512,512]{1,0:T(8,128)(2,1)} %param.17, bf16[256,1024]{1,0:T(8,128)(2,1)S(1)} %bitcast.185), kind=kOutput, calls=%fused_computation.44 | convolution fusion | flops 134348800 | bytes 1048576 | tf_op jit(solution)/shard_map/dot_general | solution.py:122
  45.2 1.8 copy.225
  47.0 1.7 reshape.337
  48.7 1.3 convolution_convert_fusion.1
  51.0 2.0 %reshape.344 = bf16[2,128,8,64]{3,2,1,0:T(8,128)(2,1)} reshape(bf16[256,512]{1,0:T(8,128)(2,1)} %get-tuple-element.42) | data formatting | bytes 524288 | tf_op jit(solution)/shard_map/jvp()/reshape | solution.py:22
  53.0 2.0 copy.223
  55.0 1.9 slice_select_fusion.35
  56.9 1.7 copy.210
  58.6 1.6 copy.212
  60.2 1.7 copy.213
  61.9 1.6 copy.214
  63.5 1.7 copy.215
  65.2 1.7 copy.211
  66.8 1.9 slice_select_fusion.29
  68.7 1.7 copy.217
  70.4 1.7 copy.219
  72.0 1.7 copy.220
  73.7 1.6 copy.221
  75.3 1.7 copy.222
  77.0 1.7 copy.218
  78.7 1.3 maximum_bitcast_fusion.3
  80.1 1.9 fusion.116
  83.4 1.8 fusion.4
  85.3 3.0 %divide_convert_fusion = (bf16[2,8,128,384]{3,2,1,0:T(8,128)(2,1)S(1)}, f32[2,8,128]{2,1,0:T(8,128)S(1)}, f32[2,8,128]{2,1,0:T(8,128)S(1)}, pred[2,8,128,384]{3,2,1,0:T(32,128)(4,1)S(1)}) fusion(f32[2,8,128,384]{3,2,1,0:T(8,128)S(1)} %get-tuple-element.74, f32[2,8,128]{2,1,0:T(8,128)S(1)} %fusion.6, f32[2,8,128]{2,1,0:T(8,128)S(1)} %get-tuple-element.73, ...), kind=kLoop, calls=%fused_computation.9 | loop fusion | flops 10219520 | bytes 7217152 | tf_op jit(solution)/shard_map/jvp()/convert_element_type | solution.py:94
  88.3 2.5 %fusion.23 = bf16[2,128,8,64]{1,3,2,0:T(8,128)(2,1)S(1)} fusion(bf16[1,384,8,64]{1,3,2,0:T(8,128)(2,1)S(1)} %get-tuple-element.84, bf16[1,384,8,64]{1,3,2,0:T(8,128)(2,1)S(1)} %get-tuple-element.83, pred[2,8,128,384]{3,2,1,0:T(32,128)(4,1)S(1)} %get-tuple-element.15, f32[2,8,128]{2,1,0:T(8,128)S(1)} %negate_divide_fusion, ...), kind=kOutput, calls=%fused_computation.47 | convolution fusion | flops 108920832 | bytes 6684672 | tf_op jit(solution)/shard_map/transpose(jvp(bqhd,bkhd->bhqk))/dot_general | solution.py:90
  90.8 3.5 %fusion.17 = f32[2,384,8,64]{1,3,2,0:T(8,128)} fusion(bf16[2,128,8,64]{1,3,2,0:T(8,128)(2,1)S(1)} %copy-done.23, pred[2,8,128,384]{3,2,1,0:T(32,128)(4,1)S(1)} %get-tuple-element.15, f32[2,8,128]{2,1,0:T(8,128)S(1)} %negate_divide_fusion, pred[2,128,384]{2,1,0:T(8,128)(4,1)S(1)} %copy-done.15, bf16[2,8,128,384]{3,2,1,0:T(8,128)(2,1)S(1)} %get-tuple-element.76, ...), kind=kOutput, calls=%fused_computation.32 | convolution fusion | flops 108527616 | bytes 7471104 | tf_op jit(solution)/shard_map/transpose(jvp(bqhd,bkhd->bhqk))/dot_general | solution.py:90
  97.1 1.6 convolution_bitcast_fusion
  99.7 1.7 dot_general.100
  101.4 1.7 slice_select_fusion.23
  108.0 9.4 %all-to-all-start.1 = ((bf16[32,8,1024]{2,1,0:T(8,128)(2,1)}), bf16[32,8,1024]{2,1,0:T(8,128)(2,1)}, u32[]{:S(2)}, u32[]{:S(2)}) async-start(bf16[32,8,1024]{2,1,0:T(8,128)(2,1)} %maximum_bitcast_fusion.5), calls=%async_computation.1 | async-start | bytes 1048576 | tf_op jit(solution)/shard_map/all_to_all | solution.py:212
  119.8 3.1 %convolution_convert_fusion = bf16[512,1536]{1,0:T(8,128)(2,1)} fusion(bf16[256,512]{0,1:T(8,128)(2,1)} %bitcast.221, bf16[256,512]{0,1:T(8,128)(2,1)} %bitcast.226, bf16[256,512]{0,1:T(8,128)(2,1)} %bitcast.224, f32[512]{0:T(512)} %param.15, f32[256]{0:T(256)} %fusion.83, f32[256]{0:T(256)} %copy-done.28, bf16[256,1024]{1,0:T(8,128)(2,1)S(1)} %bitcast.190), kind=kOutput, calls=%fused_computation.12 | convolution fusion | flops 406454272 | bytes 2625536 | tf_op jit(solution)/shard_map/dot_general | solution.py:137
  122.9 4.5 %concatenate.39 = bf16[32,8,2,1536]{3,2,1,0:T(2,128)(2,1)} reshape(bf16[512,1536]{1,0:T(8,128)(2,1)} %convolution_convert_fusion) | data formatting | bytes 3145728 | tf_op jit(solution)/shard_map/concatenate | solution.py:220
  127.4 4.6 %maximum_bitcast_fusion = bf16[8,32,2,2048]{3,2,1,0:T(2,128)(2,1)} fusion(bf16[32,8,2,512]{3,2,0,1:T(2,128)(2,1)S(1)} %copy-done.3, bf16[32,8,2,1536]{3,2,1,0:T(2,128)(2,1)} %concatenate.39), kind=kLoop, calls=%fused_computation.16 | loop fusion | flops 4194304 | bytes 4194304 | tf_op jit(solution)/shard_map/transpose | solution.py:147
  132.0 7.7 %all-to-all-start.2 = ((bf16[8,32,2,2048]{3,2,1,0:T(2,128)(2,1)}), bf16[8,32,2,2048]{3,2,1,0:T(2,128)(2,1)}, u32[]{:S(2)}, u32[]{:S(2)}) async-start(bf16[8,32,2,2048]{3,2,1,0:T(2,128)(2,1)} %maximum_bitcast_fusion), calls=%async_computation.2 | async-start | bytes 4194304 | tf_op jit(solution)/shard_map/all_to_all | solution.py:148
  139.7 1.3 fusion.36
  141.0 1.9 convolution_convert_fusion.12
  143.9 1.3 multiply_reduce_fusion
  149.1 1.5 fusion.52
  150.6 15.4 %all-to-all-done.2 = bf16[8,32,2,2048]{3,2,1,0:T(2,128)(2,1)} async-done(((bf16[8,32,2,2048]{3,2,1,0:T(2,128)(2,1)}), bf16[8,32,2,2048]{3,2,1,0:T(2,128)(2,1)}, u32[]{:S(2)}, u32[]{:S(2)}) %all-to-all-start.2) | async-done | bytes 2097184 | tf_op jit(solution)/shard_map/all_to_all | solution.py:148
  166.0 4.3 %reduce_sum.236 = bf16[32,2,2048]{2,1,0:T(2,128)(2,1)} reduce(bf16[8,32,2,2048]{3,2,1,0:T(2,128)(2,1)} %all-to-all-done.2, bf16[]{:T(256)} %constant.77.clone.1), dimensions={0}, to_apply=%region_21.22 | reduce | flops 917504 | bytes 2359298 | tf_op jit(solution)/shard_map/reduce_sum | solution.py:149
  170.3 7.5 %all-to-all-start.3 = ((bf16[32,2,2048]{2,1,0:T(2,128)(2,1)}), bf16[32,2,2048]{2,1,0:T(2,128)(2,1)S(1)}, u32[]{:S(2)}, u32[]{:S(2)}) async-start(bf16[32,2,2048]{2,1,0:T(2,128)(2,1)} %reduce_sum.236), calls=%async_computation.3 | async-start | bytes 524288 | tf_op jit(solution)/shard_map/all_to_all | solution.py:150
  178.9 8.6 %all-to-all-done.3 = bf16[32,2,2048]{2,1,0:T(2,128)(2,1)S(1)} async-done(((bf16[32,2,2048]{2,1,0:T(2,128)(2,1)}), bf16[32,2,2048]{2,1,0:T(2,128)(2,1)S(1)}, u32[]{:S(2)}, u32[]{:S(2)}) %all-to-all-start.3) | async-done | bytes 262176 | tf_op jit(solution)/shard_map/all_to_all | solution.py:150
  188.3 6.9 %all-to-all-start.4 = ((f32[8,2,2048]{2,1,0:T(2,128)}), f32[8,2,2048]{2,1,0:T(2,128)S(1)}, u32[]{:S(2)}, u32[]{:S(2)}) async-start(f32[8,2,2048]{2,1,0:T(2,128)} %broadcast_in_dim.140), calls=%async_computation.4 | async-start | bytes 262144 | tf_op jit(solution)/shard_map/all_to_all | solution.py:153
  196.0 4.6 %all-to-all-done.4 = f32[8,2,2048]{2,1,0:T(2,128)S(1)} async-done(((f32[8,2,2048]{2,1,0:T(2,128)}), f32[8,2,2048]{2,1,0:T(2,128)S(1)}, u32[]{:S(2)}, u32[]{:S(2)}) %all-to-all-start.4) | async-done | bytes 131104 | tf_op jit(solution)/shard_map/all_to_all | solution.py:153
  (173 shorter events, 43.1 us)
Async XLA Ops:
  0.6 48.1 %copy-start = (bf16[512,1536]{1,0:T(8,128)(2,1)S(1)}, bf16[512,1536]{1,0:T(8,128)(2,1)}, u32[]{:S(2)}) copy-start(bf16[512,1536]{1,0:T(8,128)(2,1)} %param.16) | copy-start | bytes 4718596
  1.8 3.5 %copy-start.32 = (f32[128]{0:T(128)}, f32[128]{0:T(128)S(1)}, u32[]{:S(2)}) copy-start(f32[128]{0:T(128)S(1)} %broadcast_multiply_fusion.2) | copy-start | bytes 1540
  2.9 0.5 copy-start.39
  3.4 1.9 copy-start.34
  5.3 4.4 %copy-start.36 = (s32[128]{0:T(128)}, s32[128]{0:T(128)S(1)}, u32[]{:S(2)}) copy-start(s32[128]{0:T(128)S(1)} %fusion.84) | copy-start | bytes 1540
  5.3 4.1 %copy-start.1 = (bf16[1,128,512]{2,1,0:T(8,128)(2,1)S(1)}, bf16[1,128,512]{2,1,0:T(8,128)(2,1)}, u32[]{:S(2)}) copy-start(bf16[1,128,512]{2,1,0:T(8,128)(2,1)} %param.10) | copy-start | bytes 393220
  5.3 4.1 %copy-start.2 = (bf16[512,512]{1,0:T(8,128)(2,1)S(1)}, bf16[512,512]{1,0:T(8,128)(2,1)}, u32[]{:S(2)}) copy-start(bf16[512,512]{1,0:T(8,128)(2,1)} %param.14) | copy-start | bytes 1572868
  7.3 3.0 %copy-start.12 = (bf16[1,128,512]{2,1,0:T(8,128)(2,1)S(1)}, bf16[1,128,512]{2,1,0:T(8,128)(2,1)}, u32[]{:S(2)}) copy-start(bf16[1,128,512]{2,1,0:T(8,128)(2,1)} %param.11) | copy-start | bytes 393220
  7.3 17.9 %copy-start.38 = (s32[1,1,2,2]{3,2,1,0:T(2,128)S(1)}, s32[1,1,2,2]{3,2,1,0:T(2,128)}, u32[]{:S(2)}) copy-start(s32[1,1,2,2]{3,2,1,0:T(2,128)} %param.19) | copy-start | bytes 52
  7.5 0.6 copy-start.6
  7.6 0.6 copy-start.7
  7.7 3.7 %copy-start.8 = (bf16[128,512]{0,1:T(8,128)(2,1)}, bf16[128,512]{0,1:T(8,128)(2,1)S(1)}, u32[]{:S(2)}) copy-start(bf16[128,512]{0,1:T(8,128)(2,1)S(1)} %copy.206) | copy-start | bytes 393220
  9.7 0.7 copy-start.10
  11.4 29.7 %all-to-all-start = ((bf16[32,8,1024]{2,1,0:T(8,128)(2,1)}), bf16[32,8,1024]{2,1,0:T(8,128)(2,1)S(1)}, u32[]{:S(2)}, u32[]{:S(2)}) async-start(bf16[32,8,1024]{2,1,0:T(8,128)(2,1)} %fusion.19), calls=%async_computation | async-start | bytes 1048576 | tf_op jit(solution)/shard_map/all_to_all | solution.py:195
  41.3 0.6 copy-start.28
  42.0 0.6 copy-start.30
  78.7 3.3 %copy-start.15 = (pred[2,128,384]{2,1,0:T(8,128)(4,1)S(1)}, pred[2,128,384]{2,1,0:T(8,128)(4,1)}, u32[]{:S(2)}) copy-start(pred[2,128,384]{2,1,0:T(8,128)(4,1)} %broadcast_or_fusion) | copy-start | bytes 294916
  80.0 3.2 %copy-start.16 = (bf16[128,512]{0,1:T(8,128)(2,1)S(1)}, bf16[128,512]{0,1:T(8,128)(2,1)}, u32[]{:S(2)}) copy-start(bf16[128,512]{0,1:T(8,128)(2,1)} %copy.210) | copy-start | bytes 393220
  80.0 3.2 %copy-start.17 = (bf16[128,512]{0,1:T(8,128)(2,1)S(1)}, bf16[128,512]{0,1:T(8,128)(2,1)}, u32[]{:S(2)}) copy-start(bf16[128,512]{0,1:T(8,128)(2,1)} %copy.212) | copy-start | bytes 393220
  80.0 3.2 %copy-start.18 = (bf16[128,512]{0,1:T(8,128)(2,1)S(1)}, bf16[128,512]{0,1:T(8,128)(2,1)}, u32[]{:S(2)}) copy-start(bf16[128,512]{0,1:T(8,128)(2,1)} %copy.213) | copy-start | bytes 393220
  80.0 3.2 %copy-start.19 = (bf16[128,512]{0,1:T(8,128)(2,1)S(1)}, bf16[128,512]{0,1:T(8,128)(2,1)}, u32[]{:S(2)}) copy-start(bf16[128,512]{0,1:T(8,128)(2,1)} %copy.214) | copy-start | bytes 393220
  80.0 3.2 %copy-start.20 = (bf16[128,512]{0,1:T(8,128)(2,1)S(1)}, bf16[128,512]{0,1:T(8,128)(2,1)}, u32[]{:S(2)}) copy-start(bf16[128,512]{0,1:T(8,128)(2,1)} %copy.215) | copy-start | bytes 393220
  80.1 3.2 %copy-start.21 = (bf16[128,512]{0,1:T(8,128)(2,1)S(1)}, bf16[128,512]{0,1:T(8,128)(2,1)}, u32[]{:S(2)}) copy-start(bf16[128,512]{0,1:T(8,128)(2,1)} %copy.211) | copy-start | bytes 393220
  82.0 1.5 copy-start.14
  88.3 2.5 %copy-start.23 = (bf16[2,128,8,64]{1,3,2,0:T(8,128)(2,1)S(1)}, bf16[2,128,8,64]{1,3,2,0:T(8,128)(2,1)}, u32[]{:S(2)}) copy-start(bf16[2,128,8,64]{1,3,2,0:T(8,128)(2,1)} %copy.223) | copy-start | bytes 786436
  94.3 1.8 copy-start.22
  103.2 1.4 copy-start.5
  104.6 1.1 copy-start.25
  105.0 1.0 copy-start.24
  105.0 0.9 copy-start.29
  105.0 0.9 copy-start.41
  105.4 1.3 copy-start.31
  105.4 1.4 copy-start.37
  105.7 1.4 copy-start.26
  106.0 1.1 copy-start.27
  108.0 24.0 %all-to-all-start.1 = ((bf16[32,8,1024]{2,1,0:T(8,128)(2,1)}), bf16[32,8,1024]{2,1,0:T(8,128)(2,1)}, u32[]{:S(2)}, u32[]{:S(2)}) async-start(bf16[32,8,1024]{2,1,0:T(8,128)(2,1)} %maximum_bitcast_fusion.5), calls=%async_computation.1 | async-start | bytes 1048576 | tf_op jit(solution)/shard_map/all_to_all | solution.py:212
  122.9 4.5 %copy-start.3 = (bf16[32,8,2,512]{3,2,0,1:T(2,128)(2,1)S(1)}, bf16[32,8,2,512]{3,2,0,1:T(2,128)(2,1)}, u32[]{:S(2)}) copy-start(bf16[32,8,2,512]{3,2,0,1:T(2,128)(2,1)} %copy.238) | copy-start | bytes 1572868
  132.0 34.0 %all-to-all-start.2 = ((bf16[8,32,2,2048]{3,2,1,0:T(2,128)(2,1)}), bf16[8,32,2,2048]{3,2,1,0:T(2,128)(2,1)}, u32[]{:S(2)}, u32[]{:S(2)}) async-start(bf16[8,32,2,2048]{3,2,1,0:T(2,128)(2,1)} %maximum_bitcast_fusion), calls=%async_computation.2 | async-start | bytes 4194304 | tf_op jit(solution)/shard_map/all_to_all | solution.py:148
  143.9 1.4 copy-start.9
  143.9 5.2 %copy-start.4 = (bf16[512,1536]{1,0:T(8,128)(2,1)S(1)}, bf16[512,1536]{1,0:T(8,128)(2,1)}, u32[]{:S(2)}) copy-start(bf16[512,1536]{1,0:T(8,128)(2,1)} %param.13) | copy-start | bytes 4718596
  145.3 5.3 %copy-start.40 = (f32[128]{0:T(128)S(1)}, f32[128]{0:T(128)}, u32[]{:S(2)}) copy-start(f32[128]{0:T(128)} %copy-done.39) | copy-start | bytes 1540
  147.8 30.1 %copy-start.33 = (f32[128]{0:T(128)S(1)}, f32[128]{0:T(128)}, u32[]{:S(2)}) copy-start(f32[128]{0:T(128)} %copy-done.32) | copy-start | bytes 1540
  147.8 30.1 %copy-start.35 = (f32[128]{0:T(128)S(1)}, f32[128]{0:T(128)}, u32[]{:S(2)}) copy-start(f32[128]{0:T(128)} %copy-done.34) | copy-start | bytes 1540
  149.1 29.0 %copy-start.13 = (bf16[1,128,512]{2,1,0:T(8,128)(2,1)S(1)}, bf16[1,128,512]{2,1,0:T(8,128)(2,1)}, u32[]{:S(2)}) copy-start(bf16[1,128,512]{2,1,0:T(8,128)(2,1)} %param.11) | copy-start | bytes 393220
  149.1 46.1 %copy-start.11 = (bf16[128,512]{1,0:T(8,128)(2,1)S(1)}, bf16[128,512]{1,0:T(8,128)(2,1)}, u32[]{:S(2)}) copy-start(bf16[128,512]{1,0:T(8,128)(2,1)} %copy-done.10) | copy-start | bytes 393220
  170.3 17.2 %all-to-all-start.3 = ((bf16[32,2,2048]{2,1,0:T(2,128)(2,1)}), bf16[32,2,2048]{2,1,0:T(2,128)(2,1)S(1)}, u32[]{:S(2)}, u32[]{:S(2)}) async-start(bf16[32,2,2048]{2,1,0:T(2,128)(2,1)} %reduce_sum.236), calls=%async_computation.3 | async-start | bytes 524288 | tf_op jit(solution)/shard_map/all_to_all | solution.py:150
  188.3 12.2 %all-to-all-start.4 = ((f32[8,2,2048]{2,1,0:T(2,128)}), f32[8,2,2048]{2,1,0:T(2,128)S(1)}, u32[]{:S(2)}, u32[]{:S(2)}) async-start(f32[8,2,2048]{2,1,0:T(2,128)} %broadcast_in_dim.140), calls=%async_computation.4 | async-start | bytes 262144 | tf_op jit(solution)/shard_map/all_to_all | solution.py:153

commit v4 on v3

--- a/solution.py
+++ b/solution.py
@@ -20,6 +20,15 @@
 
 def split_heads(matrix, block_groups):
     return matrix.reshape(block_groups, EVENTS_PER_BLOCK, HEADS, HEAD_DIM)
+
+
+def heads_first(packed_rows, block_groups):
+    parts = packed_rows.reshape(block_groups, EVENTS_PER_BLOCK, 3, HEADS, HEAD_DIM)
+    return jnp.transpose(parts, (2, 0, 3, 1, 4)).astype(jnp.float32)
+
+
+def rows_first(merged, row_total):
+    return jnp.transpose(merged, (0, 2, 1, 3)).astype(jnp.bfloat16).reshape(row_total, -1)
 
 
 def intra_branch(source, scale_factors, input_weight, output_weight):
@@ -29,17 +38,14 @@
     packed_rows = jnp.dot(normed, input_weight, preferred_element_type=jnp.float32).astype(
         jnp.bfloat16
     )
-    queries = split_heads(packed_rows[:, :features], block_groups).astype(jnp.float32)
-    key_rows = split_heads(packed_rows[:, features : 2 * features], block_groups).astype(
-        jnp.float32
-    )
-    value_rows = split_heads(packed_rows[:, 2 * features :], block_groups).astype(jnp.float32)
-    scores = jnp.einsum("bqhd,bkhd->bhqk", queries, key_rows) * HEAD_DIM ** (-0.5)
+    parts = heads_first(packed_rows, block_groups)
+    queries, key_rows, value_rows = parts[0], parts[1], parts[2]
+    scores = jnp.einsum("bhqd,bhkd->bhqk", queries, key_rows) * HEAD_DIM ** (-0.5)
     highest = jnp.max(scores, axis=-1, keepdims=True)
     weights = jnp.exp(scores - highest)
     attention = (weights / jnp.sum(weights, axis=-1, keepdims=True)).astype(jnp.bfloat16)
-    merged_rows = jnp.einsum("bhqk,bkhd->bqhd", attention.astype(jnp.float32), value_rows)
-    merged_rows = merged_rows.astype(jnp.bfloat16).reshape(row_total, features)
+    merged_rows = jnp.einsum("bhqk,bhkd->bhqd", attention.astype(jnp.float32), value_rows)
+    merged_rows = rows_first(merged_rows, row_total)
     branch = jnp.dot(merged_rows, output_weight, preferred_element_type=jnp.float32)
     return (source.astype(jnp.float32) + branch).astype(jnp.bfloat16)
 
@@ -51,13 +57,13 @@
     return picked
 
 
-def gather_segments(blocks, selected_rows):
+def gather_segments(blocks, selected_rows, axis):
     block_groups, segments = selected_rows.shape
     return jnp.stack(
         [
             jnp.concatenate(
                 [pick_block(blocks, selected_rows[group, segment]) for segment in range(segments)],
-                axis=0,
+                axis=axis,
             )
             for group in range(block_groups)
         ],
@@ -67,33 +73,29 @@
 
 def cross_account_inner(packed_rows, row_presence, block_listing):
     row_total, three_wide = packed_rows.shape
-    features = three_wide // 3
     block_groups = row_total // EVENTS_PER_BLOCK
     selected_rows = jnp.concatenate(
         [jnp.arange(block_groups, dtype=jnp.int32)[:, None], block_listing], axis=1
     )
-    queries = split_heads(packed_rows[:, :features].astype(jnp.float32), block_groups)
-    key_blocks = split_heads(
-        packed_rows[:, features : 2 * features].astype(jnp.float32), block_groups
-    )
-    key_rows = gather_segments(key_blocks, selected_rows)
-    value_blocks = split_heads(packed_rows[:, 2 * features :].astype(jnp.float32), block_groups)
-    value_rows = gather_segments(value_blocks, selected_rows)
+    parts = heads_first(packed_rows, block_groups)
+    queries = parts[0]
+    key_rows = gather_segments(parts[1], selected_rows, 1)
+    value_rows = gather_segments(parts[2], selected_rows, 1)
     presence_blocks = row_presence.reshape(block_groups, EVENTS_PER_BLOCK)
-    key_present = gather_segments(presence_blocks, selected_rows)
+    key_present = gather_segments(presence_blocks, selected_rows, 0)
     key_total = key_present.shape[1]
     itself = (
         jnp.arange(key_total, dtype=jnp.int32)[None, :]
         == jnp.arange(EVENTS_PER_BLOCK, dtype=jnp.int32)[:, None]
     )
     allowed = key_present[:, None, None, :] | itself[None, None, :, :]
-    scores = jnp.einsum("bqhd,bkhd->bhqk", queries, key_rows) * HEAD_DIM ** (-0.5)
+    scores = jnp.einsum("bhqd,bhkd->bhqk", queries, key_rows) * HEAD_DIM ** (-0.5)
     scores = jnp.where(allowed, scores, -1e30)
     highest = jnp.max(scores, axis=-1, keepdims=True)
     weights = jnp.where(allowed, jnp.exp(scores - highest), 0.0)
     attention = (weights / jnp.sum(weights, axis=-1, keepdims=True)).astype(jnp.bfloat16)
-    merged_rows = jnp.einsum("bhqk,bkhd->bqhd", attention.astype(jnp.float32), value_rows)
-    return merged_rows.astype(jnp.bfloat16).reshape(row_total, features)
+    merged_rows = jnp.einsum("bhqk,bhkd->bhqd", attention.astype(jnp.float32), value_rows)
+    return rows_first(merged_rows, row_total)
 
 
 def owner_transfer(

time: 204 us -> 166 us (0.81)
  local copies, waits for them, and re-layouts: 55.4 us -> 27.8 us
  waiting for transfers between devices: 28.6 us -> 39.7 us
  other arithmetic: 34.2 us -> 24.7 us
  matrix products: 34.8 us -> 25.6 us
    select_n x18 -> x6, local copies, waits for them, and re-layouts: 26.9 us -> 0.58 us  [pick_block(): picked = jnp.where(chosen == index, blocks[index], picked)]
    all_to_all x1, waiting for transfers between devices: 0.01 us -> 6.92 us  [on_device(): lax.all_to_all(outgoing, 'ev', split_axis=0, concat_axis=0, tiled=True)]
    dot_general x12, matrix products: 17.5 us -> 10.8 us  [the longest x3 6.25 us: cross_account_inner(): jnp.einsum('bhqd,bhkd->bhqk', queries, key_rows) * HEAD_DIM ** (-0.5)]
    select_n x5 -> x3, other arithmetic: 6.53 us -> 1.9 us  [pick_block(): picked = jnp.where(chosen == index, blocks[index], picked)]
    concatenate x1 -> x0, local copies, waits for them, and re-layouts: 4.52 us -> none  [on_device(): jnp.concatenate([contract(normed_half, back_packed), contract(merged_rows...]
    transpose x1, other arithmetic: 4.55 us -> 0.24 us  [reduce_weight_terms(): terms = jnp.swapaxes(terms, 0, 1)]
    transpose x0 -> x2, local copies, waits for them, and re-layouts: none -> 4.27 us  [the longest x1 3.46 us: reduce_weight_terms(): terms = jnp.swapaxes(terms, 0, 1)]
    all_to_all x1, waiting for transfers between devices: 15.4 us -> 19.4 us  [reduce_weight_terms(): terms = lax.all_to_all(terms, 'dp', 0, 0, tiled=True)]
  transfers between devices with their start and end apart: 5 -> 5, of which waited for: 3 -> 5; matrix products, arithmetic and copies ran while one was open for 20% -> 15% of each run, Pallas kernels for 0% -> 0%
where the time goes in v4:
time: 166 us; the launch traced here: 165 us
  starting transfers between devices  41.8 us (25%)
  waiting for transfers between devices  39.7 us (24%)
  local copies, waits for them, and re-layouts  27.8 us (17%)
  matrix products  25.6 us (15%)
  other arithmetic  24.7 us (15%)
  between operations  5.59 us (3%)
    all_to_all x1, waiting for transfers between devices, reduce_weight_terms(): terms = lax.all_to_all(terms, 'dp', 0, 0, tiled=True)  19.4 us
    all_to_all x1, starting transfers between devices, on_device(): lax.all_to_all(outgoing, 'ev', split_axis=0, concat_axis=0, tiled=True)  12.2 us
    all_to_all x1, starting transfers between devices, reduce_weight_terms(): terms = lax.all_to_all(terms, 'dp', 0, 0, tiled=True)  8.65 us
    all_to_all x1, waiting for transfers between devices, reduce_weight_terms(): terms = lax.all_to_all(terms, 'ev', 0, 0, tiled=True)  8.59 us
    all_to_all x1, starting transfers between devices, on_device(): lax.all_to_all(going_back, 'ev', split_axis=0, concat_axis=0, tiled=True)  7.36 us
    all_to_all x1, starting transfers between devices, reduce_weight_terms(): gathered = lax.all_to_all(copies, 'dp', 0, 0, tiled=True)  6.94 us
    all_to_all x1, waiting for transfers between devices, on_device(): lax.all_to_all(outgoing, 'ev', split_axis=0, concat_axis=0, tiled=True)  6.92 us
    all_to_all x1, starting transfers between devices, reduce_weight_terms(): terms = lax.all_to_all(terms, 'ev', 0, 0, tiled=True)  6.67 us
  transfers between devices with their start and end apart: 5, of which 5 were waited for; matrix products, arithmetic and copies ran while one was open for 15% of the time, Pallas kernels for 0%

profile of v4, /device:TPU:1, one launch (start us, length us, event | category | flops | bytes accessed | tf_op | source)
XLA Modules:
  0.0 165.2 jit_solution(3518923087214866740)
XLA Ops:
  0.7 1.2 convert_reduce_fusion.5
  1.9 1.1 fusion.46
  3.0 0.8 dynamic-slice.1
  4.9 1.9 %convolution_convert_fusion.2 = bf16[128,1536]{1,0:T(8,128)(2,1)S(1)} fusion(bf16[512,1536]{1,0:T(8,128)(2,1)} %param.13, bf16[1,128,512]{2,1,0:T(8,128)(2,1)} %param.10, f32[512]{0:T(512)} %param.12, f32[128]{0:T(128)S(1)} %fusion.84, f32[128]{0:T(128)S(1)} %broadcast_multiply_fusion.2), kind=kOutput, calls=%fused_computation.15 | convolution fusion | flops 201850880 | bytes 2100224 | tf_op jit(solution)/shard_map/jvp()/dot_general | solution.py:38
  7.5 0.8 convert_reduce_fusion.3
  9.6 1.1 fusion.18
  10.6 12.2 %all-to-all-start = ((bf16[32,8,1024]{2,1,0:T(8,128)(2,1)}), bf16[32,8,1024]{2,1,0:T(8,128)(2,1)S(1)}, u32[]{:S(2)}, u32[]{:S(2)}) async-start(bf16[32,8,1024]{2,1,0:T(8,128)(2,1)} %fusion.18), calls=%async_computation | async-start | bytes 1048576 | tf_op jit(solution)/shard_map/all_to_all | solution.py:197
  30.3 6.9 %all-to-all-done = bf16[32,8,1024]{2,1,0:T(8,128)(2,1)S(1)} async-done(((bf16[32,8,1024]{2,1,0:T(8,128)(2,1)}), bf16[32,8,1024]{2,1,0:T(8,128)(2,1)S(1)}, u32[]{:S(2)}, u32[]{:S(2)}) %all-to-all-start) | async-done | bytes 524320 | tf_op jit(solution)/shard_map/all_to_all | solution.py:197
  38.7 1.3 convolution_convert_fusion.1
  40.0 1.8 %reshape.321 = bf16[2,128,3,8,64]{4,3,2,1,0:T(8,128)(2,1)} reshape(bf16[256,1536]{1,0:T(8,128)(2,1)S(1)} %convolution_convert_fusion.1) | data formatting | bytes 1572864 | tf_op jit(solution)/shard_map/jvp()/reshape | solution.py:26
  41.9 2.0 %copy.122 = bf16[2,128,3,8,64]{1,4,3,0,2:T(8,128)(2,1)S(1)} copy(bf16[2,128,3,8,64]{4,3,2,1,0:T(8,128)(2,1)} %reshape.321) | data formatting | bytes 1572864 | tf_op jit(solution)/shard_map/jvp()/reshape | solution.py:26
  43.9 0.9 select_bitcast_fusion.28
  44.8 1.0 select_bitcast_fusion.29
  45.7 2.1 %convolution_convert_fusion.7 = bf16[256,512]{1,0:T(8,128)(2,1)} fusion(bf16[512,512]{1,0:T(8,128)(2,1)} %param.17, bf16[256,1024]{1,0:T(8,128)(2,1)S(1)} %bitcast.271), kind=kOutput, calls=%fused_computation.43 | convolution fusion | flops 134348800 | bytes 1048576 | tf_op jit(solution)/shard_map/dot_general | solution.py:124
  47.8 1.8 %copy.124 = bf16[256,512]{0,1:T(8,128)(2,1)} copy(bf16[256,512]{1,0:T(8,128)(2,1)} %convolution_convert_fusion.7) | data formatting | bytes 524288 | tf_op jit(solution)/shard_map/convert_element_type | solution.py:129
  49.6 1.7 %reshape.314 = bf16[2,128,8,64]{1,0,3,2:T(2,128)(2,1)} reshape(bf16[256,512]{0,1:T(8,128)(2,1)} %copy.124) | data formatting | bytes 524288 | tf_op jit(solution)/shard_map/transpose(jvp())/reshape | solution.py:31
  51.3 1.1 maximum_bitcast_fusion.1
  52.4 1.1 maximum_bitcast_fusion.2
  53.6 1.8 %fusion.110 = (f32[2,8,128]{2,1,0:T(8,128)S(1)}, f32[2,8,128,384]{3,2,1,0:T(8,128)S(1)}) fusion(bf16[1,8,384,64]{2,3,1,0:T(8,128)(2,1)S(1)} %maximum_bitcast_fusion.2, bf16[1,8,384,64]{2,3,1,0:T(8,128)(2,1)S(1)} %maximum_bitcast_fusion.1, bf16[3,2,8,128,64]{3,4,2,1,0:T(8,128)(2,1)S(1)} %bitcast.277, pred[2,128,384]{2,1,0:T(8,128)(4,1)} %broadcast_or_fusion), kind=kOutput, calls=%fused_computation.240 | convolution fusion | flops 103413760 | bytes 4300800 | tf_op jit(solution)/shard_map/jvp(bhqd,bhkd->bhqk)/dot_general | solution.py:92
  55.4 1.2 fusion.6
  56.8 1.8 %fusion.4 = (f32[2,8,128]{2,1,0:T(8,128)S(1)}, bf16[2,8,128,384]{3,2,1,0:T(8,128)(2,1)S(1)}) fusion(f32[2,8,128,384]{3,2,1,0:T(8,128)S(1)} %get-tuple-element.73, f32[2,8,128]{2,1,0:T(8,128)S(1)} %multiply_divide_fusion, f32[2,8,128]{2,1,0:T(8,128)S(1)} %get-tuple-element.72, pred[2,128,384]{2,1,0:T(8,128)(4,1)S(1)} %copy-done.18, ...), kind=kOutput, calls=%fused_computation.6 | convolution fusion | flops 105773056 | bytes 5890048 | tf_op jit(solution)/shard_map/transpose(jvp(bhqk,bhkd->bhqd))/dot_general | solution.py:97
  58.7 3.0 %divide_convert_fusion = (bf16[2,8,128,384]{3,2,1,0:T(8,128)(2,1)S(1)}, f32[2,8,128]{2,1,0:T(8,128)S(1)}, f32[2,8,128]{2,1,0:T(8,128)S(1)}, pred[2,8,128,384]{3,2,1,0:T(32,128)(4,1)S(1)}) fusion(f32[2,8,128,384]{3,2,1,0:T(8,128)S(1)} %get-tuple-element.73, f32[2,8,128]{2,1,0:T(8,128)S(1)} %fusion.6, f32[2,8,128]{2,1,0:T(8,128)S(1)} %get-tuple-element.72, ...), kind=kLoop, calls=%fused_computation.9 | loop fusion | flops 10219520 | bytes 7217152 | tf_op jit(solution)/shard_map/jvp()/convert_element_type | solution.py:96
  61.7 2.0 %fusion.19 = f32[1,2,8,128,64]{3,4,2,1,0:T(8,128)S(1)} fusion(bf16[1,8,384,64]{2,3,1,0:T(8,128)(2,1)S(1)} %maximum_bitcast_fusion.2, bf16[1,8,384,64]{2,3,1,0:T(8,128)(2,1)S(1)} %maximum_bitcast_fusion.1, pred[2,8,128,384]{3,2,1,0:T(32,128)(4,1)S(1)} %get-tuple-element.15, f32[2,8,128]{2,1,0:T(8,128)S(1)} %negate_divide_fusion, ...), kind=kOutput, calls=%fused_computation.37 | convolution fusion | flops 108920832 | bytes 6946816 | tf_op jit(solution)/shard_map/transpose(jvp(bhqd,bhkd->bhqk))/dot_general | solution.py:92
  63.7 2.5 %fusion.8 = f32[2,8,384,64]{2,3,1,0:T(8,128)S(1)} fusion(pred[2,8,128,384]{3,2,1,0:T(32,128)(4,1)S(1)} %get-tuple-element.15, f32[2,8,128]{2,1,0:T(8,128)S(1)} %negate_divide_fusion, pred[2,128,384]{2,1,0:T(8,128)(4,1)S(1)} %copy-done.18, bf16[3,2,8,128,64]{3,4,2,1,0:T(8,128)(2,1)S(1)} %bitcast.278, bf16[2,8,128,384]{3,2,1,0:T(8,128)(2,1)S(1)} %get-tuple-element.75, ...), kind=kOutput, calls=%fused_computation.19 | convolution fusion | flops 108527616 | bytes 7471104 | tf_op jit(solution)/shard_map/transpose(jvp(bhqd,bhkd->bhqk))/dot_general | solution.py:92
  66.2 0.8 fusion.22
  70.4 0.8 copy.127
  72.0 1.0 fusion.106
  73.1 0.9 maximum_bitcast_fusion.5
  73.9 7.4 %all-to-all-start.1 = ((bf16[32,8,1024]{2,1,0:T(8,128)(2,1)}), bf16[32,8,1024]{2,1,0:T(8,128)(2,1)}, u32[]{:S(2)}, u32[]{:S(2)}) async-start(bf16[32,8,1024]{2,1,0:T(8,128)(2,1)} %maximum_bitcast_fusion.5), calls=%async_computation.1 | async-start | bytes 1048576 | tf_op jit(solution)/shard_map/all_to_all | solution.py:214
  81.3 1.7 %copy.175 = bf16[64,8,2,128]{3,1,2,0:T(8,128)(2,1)} copy(bf16[64,8,2,128]{3,2,1,0:T(2,128)(2,1)} %bitcast.291) | data formatting | bytes 524288
  83.0 1.8 %dot_general.109 = bf16[32,8,2,256]{3,2,1,0:T(2,128)(2,1)} reshape(bf16[512,256]{1,0:T(8,128)(2,1)} %bitcast.292) | data formatting | bytes 524288 | tf_op jit(solution)/shard_map/dot_general | solution.py:139
  84.8 1.8 %copy.132 = bf16[512,256]{1,0:T(8,128)(2,1)} copy(bf16[512,256]{0,1:T(8,128)(2,1)} %get-tuple-element.57) | data formatting | bytes 524288 | tf_op jit(solution)/shard_map/dot_general | solution.py:139
  86.6 1.8 %dot_general.106 = bf16[32,8,2,256]{3,2,1,0:T(2,128)(2,1)} reshape(bf16[512,256]{1,0:T(8,128)(2,1)} %copy.132) | data formatting | bytes 524288 | tf_op jit(solution)/shard_map/dot_general | solution.py:139
  88.3 1.3 convolution_convert_fusion.4
  89.6 1.6 convolution_convert_fusion
  91.4 3.5 %copy.136 = bf16[8,32,2,2048]{3,2,1,0:T(2,128)(2,1)} copy(bf16[8,32,2,2048]{3,0,2,1:T(8,128)(2,1)S(1)} %maximum_bitcast_fusion) | data formatting | bytes 4194304 | tf_op jit(solution)/shard_map/transpose | solution.py:149
  95.1 8.7 %all-to-all-start.2 = ((bf16[8,32,2,2048]{3,2,1,0:T(2,128)(2,1)}), bf16[8,32,2,2048]{3,2,1,0:T(2,128)(2,1)}, u32[]{:S(2)}, u32[]{:S(2)}) async-start(bf16[8,32,2,2048]{3,2,1,0:T(2,128)(2,1)} %copy.136), calls=%async_computation.2 | async-start | bytes 4194304 | tf_op jit(solution)/shard_map/all_to_all | solution.py:150
  103.7 1.3 fusion.38
  105.1 2.2 %convolution_convert_fusion.10 = bf16[128,512]{1,0:T(8,128)(2,1)} fusion(bf16[512,512]{1,0:T(8,128)(2,1)} %param.14, f32[128,1024]{1,0:T(8,128)S(1)} %fusion.38, bf16[1,128,512]{2,1,0:T(8,128)(2,1)S(1)} %copy-done.13), kind=kOutput, calls=%fused_computation.52 | convolution fusion | flops 67371008 | bytes 1048576 | tf_op jit(solution)/shard_map/transpose(jvp())/dot_general | solution.py:49
  107.3 1.0 copy.128
  109.9 0.7 fusion.49
  110.6 19.4 %all-to-all-done.2 = bf16[8,32,2,2048]{3,2,1,0:T(2,128)(2,1)} async-done(((bf16[8,32,2,2048]{3,2,1,0:T(2,128)(2,1)}), bf16[8,32,2,2048]{3,2,1,0:T(2,128)(2,1)}, u32[]{:S(2)}, u32[]{:S(2)}) %all-to-all-start.2) | async-done | bytes 2097184 | tf_op jit(solution)/shard_map/all_to_all | solution.py:150
  130.0 4.4 %reduce_sum.236 = bf16[32,2,2048]{2,1,0:T(2,128)(2,1)} reduce(bf16[8,32,2,2048]{3,2,1,0:T(2,128)(2,1)} %all-to-all-done.2, bf16[]{:T(256)} %constant.78.clone.1), dimensions={0}, to_apply=%region_21.22 | reduce | flops 917504 | bytes 2359298 | tf_op jit(solution)/shard_map/reduce_sum | solution.py:151
  134.4 6.7 %all-to-all-start.3 = ((bf16[32,2,2048]{2,1,0:T(2,128)(2,1)}), bf16[32,2,2048]{2,1,0:T(2,128)(2,1)S(1)}, u32[]{:S(2)}, u32[]{:S(2)}) async-start(bf16[32,2,2048]{2,1,0:T(2,128)(2,1)} %reduce_sum.236), calls=%async_computation.3 | async-start | bytes 524288 | tf_op jit(solution)/shard_map/all_to_all | solution.py:152
  141.4 0.8 fusion.72
  142.2 8.6 %all-to-all-done.3 = bf16[32,2,2048]{2,1,0:T(2,128)(2,1)S(1)} async-done(((bf16[32,2,2048]{2,1,0:T(2,128)(2,1)}), bf16[32,2,2048]{2,1,0:T(2,128)(2,1)S(1)}, u32[]{:S(2)}, u32[]{:S(2)}) %all-to-all-start.3) | async-done | bytes 262176 | tf_op jit(solution)/shard_map/all_to_all | solution.py:152
  151.5 6.9 %all-to-all-start.4 = ((f32[8,2,2048]{2,1,0:T(2,128)}), f32[8,2,2048]{2,1,0:T(2,128)S(1)}, u32[]{:S(2)}, u32[]{:S(2)}) async-start(f32[8,2,2048]{2,1,0:T(2,128)} %broadcast_in_dim.236), calls=%async_computation.4 | async-start | bytes 262144 | tf_op jit(solution)/shard_map/all_to_all | solution.py:155
  159.2 4.6 %all-to-all-done.4 = f32[8,2,2048]{2,1,0:T(2,128)S(1)} async-done(((f32[8,2,2048]{2,1,0:T(2,128)}), f32[8,2,2048]{2,1,0:T(2,128)S(1)}, u32[]{:S(2)}, u32[]{:S(2)}) %all-to-all-start.4) | async-done | bytes 131104 | tf_op jit(solution)/shard_map/all_to_all | solution.py:155
  (159 shorter events, 17.1 us)
Async XLA Ops:
  0.6 38.1 %copy-start = (bf16[512,1536]{1,0:T(8,128)(2,1)S(1)}, bf16[512,1536]{1,0:T(8,128)(2,1)}, u32[]{:S(2)}) copy-start(bf16[512,1536]{1,0:T(8,128)(2,1)} %param.16) | copy-start | bytes 4718596
  0.6 8.6 %copy-start.1 = (bf16[1,128,512]{2,1,0:T(8,128)(2,1)S(1)}, bf16[1,128,512]{2,1,0:T(8,128)(2,1)}, u32[]{:S(2)}) copy-start(bf16[1,128,512]{2,1,0:T(8,128)(2,1)} %param.10) | copy-start | bytes 393220
  0.7 8.6 %copy-start.9 = (bf16[512,512]{1,0:T(8,128)(2,1)S(1)}, bf16[512,512]{1,0:T(8,128)(2,1)}, u32[]{:S(2)}) copy-start(bf16[512,512]{1,0:T(8,128)(2,1)} %param.14) | copy-start | bytes 1572868
  1.8 5.2 %copy-start.27 = (f32[128]{0:T(128)}, f32[128]{0:T(128)S(1)}, u32[]{:S(2)}) copy-start(f32[128]{0:T(128)S(1)} %broadcast_multiply_fusion.2) | copy-start | bytes 1540
  2.9 0.8 copy-start.40
  3.0 4.1 %copy-start.33 = (f32[128]{0:T(128)}, f32[128]{0:T(128)S(1)}, u32[]{:S(2)}) copy-start(f32[128]{0:T(128)S(1)} %fusion.84) | copy-start | bytes 1540
  4.9 4.7 %copy-start.35 = (s32[128]{0:T(128)}, s32[128]{0:T(128)S(1)}, u32[]{:S(2)}) copy-start(s32[128]{0:T(128)S(1)} %fusion.83) | copy-start | bytes 1540
  4.9 4.7 %copy-start.12 = (bf16[1,128,512]{2,1,0:T(8,128)(2,1)S(1)}, bf16[1,128,512]{2,1,0:T(8,128)(2,1)}, u32[]{:S(2)}) copy-start(bf16[1,128,512]{2,1,0:T(8,128)(2,1)} %param.11) | copy-start | bytes 393220
  6.8 17.9 %copy-start.38 = (s32[1,1,2,2]{3,2,1,0:T(2,128)S(1)}, s32[1,1,2,2]{3,2,1,0:T(2,128)}, u32[]{:S(2)}) copy-start(s32[1,1,2,2]{3,2,1,0:T(2,128)} %param.19) | copy-start | bytes 52
  6.8 21.2 %copy-start.26 = (s32[1,4096]{1,0:T(1,128)S(1)}, s32[1,4096]{1,0:T(1,128)}, u32[]{:S(2)}) copy-start(s32[1,4096]{1,0:T(1,128)} %param.18) | copy-start | bytes 49156
  7.1 3.5 %copy-start.3 = (bf16[128,1536]{0,1:T(8,128)(2,1)}, bf16[128,1536]{0,1:T(8,128)(2,1)S(1)}, u32[]{:S(2)}) copy-start(bf16[128,1536]{0,1:T(8,128)(2,1)S(1)} %copy.118) | copy-start | bytes 1179652
  8.3 0.7 copy-start.7
  9.5 1.1 copy-start.10
  10.6 26.6 %all-to-all-start = ((bf16[32,8,1024]{2,1,0:T(8,128)(2,1)}), bf16[32,8,1024]{2,1,0:T(8,128)(2,1)S(1)}, u32[]{:S(2)}, u32[]{:S(2)}) async-start(bf16[32,8,1024]{2,1,0:T(8,128)(2,1)} %fusion.18), calls=%async_computation | async-start | bytes 1048576 | tf_op jit(solution)/shard_map/all_to_all | solution.py:197
  37.6 0.6 copy-start.30
  38.1 0.6 copy-start.36
  51.3 4.1 %copy-start.18 = (pred[2,128,384]{2,1,0:T(8,128)(4,1)S(1)}, pred[2,128,384]{2,1,0:T(8,128)(4,1)}, u32[]{:S(2)}) copy-start(pred[2,128,384]{2,1,0:T(8,128)(4,1)} %broadcast_or_fusion) | copy-start | bytes 294916
  53.5 3.1 %copy-start.22 = (bf16[8,128,64]{1,2,0:T(8,128)(2,1)S(1)}, bf16[8,128,64]{1,2,0:T(8,128)(2,1)}, u32[]{:S(2)}) copy-start(bf16[8,128,64]{1,2,0:T(8,128)(2,1)} %get-tuple-element.51) | copy-start | bytes 393220
  53.5 3.1 %copy-start.24 = (bf16[8,128,64]{1,2,0:T(8,128)(2,1)S(1)}, bf16[8,128,64]{1,2,0:T(8,128)(2,1)}, u32[]{:S(2)}) copy-start(bf16[8,128,64]{1,2,0:T(8,128)(2,1)} %get-tuple-element.44) | copy-start | bytes 393220
  53.5 3.1 %copy-start.25 = (bf16[8,128,64]{1,2,0:T(8,128)(2,1)S(1)}, bf16[8,128,64]{1,2,0:T(8,128)(2,1)}, u32[]{:S(2)}) copy-start(bf16[8,128,64]{1,2,0:T(8,128)(2,1)} %get-tuple-element.49) | copy-start | bytes 393220
  55.3 1.4 copy-start.20
  55.3 1.4 copy-start.21
  55.3 1.4 copy-start.23
  55.4 1.5 copy-start.17
  67.0 1.4 copy-start.19
  67.7 0.7 copy-start.16
  70.0 1.3 copy-start.39
  70.4 1.6 copy-start.31
  70.4 1.6 copy-start.37
  73.9 21.1 %all-to-all-start.1 = ((bf16[32,8,1024]{2,1,0:T(8,128)(2,1)}), bf16[32,8,1024]{2,1,0:T(8,128)(2,1)}, u32[]{:S(2)}, u32[]{:S(2)}) async-start(bf16[32,8,1024]{2,1,0:T(8,128)(2,1)} %maximum_bitcast_fusion.5), calls=%async_computation.1 | async-start | bytes 1048576 | tf_op jit(solution)/shard_map/all_to_all | solution.py:214
  94.9 10.2 %copy-start.13 = (bf16[1,128,512]{2,1,0:T(8,128)(2,1)S(1)}, bf16[1,128,512]{2,1,0:T(8,128)(2,1)}, u32[]{:S(2)}) copy-start(bf16[1,128,512]{2,1,0:T(8,128)(2,1)} %param.11) | copy-start | bytes 393220
  94.9 13.4 %copy-start.4 = (bf16[128,1536]{0,1:T(8,128)(2,1)S(1)}, bf16[128,1536]{0,1:T(8,128)(2,1)}, u32[]{:S(2)}) copy-start(bf16[128,1536]{0,1:T(8,128)(2,1)} %copy-done.3) | copy-start | bytes 1179652
  94.9 13.8 %copy-start.8 = (bf16[8,128,128]{1,2,0:T(8,128)(2,1)S(1)}, bf16[8,128,128]{1,2,0:T(8,128)(2,1)}, u32[]{:S(2)}) copy-start(bf16[8,128,128]{1,2,0:T(8,128)(2,1)} %copy-done.7) | copy-start | bytes 786436
  95.1 35.0 %all-to-all-start.2 = ((bf16[8,32,2,2048]{3,2,1,0:T(2,128)(2,1)}), bf16[8,32,2,2048]{3,2,1,0:T(2,128)(2,1)}, u32[]{:S(2)}, u32[]{:S(2)}) async-start(bf16[8,32,2,2048]{3,2,1,0:T(2,128)(2,1)} %copy.136), calls=%async_computation.2 | async-start | bytes 4194304 | tf_op jit(solution)/shard_map/all_to_all | solution.py:150
  105.1 3.9 %copy-start.5 = (f32[128,1024]{1,0:T(8,128)}, f32[128,1024]{1,0:T(8,128)S(1)}, u32[]{:S(2)}) copy-start(f32[128,1024]{1,0:T(8,128)S(1)} %fusion.38) | copy-start | bytes 1572868
  108.3 0.9 copy-start.15
  108.3 1.5 copy-start.2
  108.3 1.5 copy-start.28
  108.3 1.5 copy-start.32
  109.1 1.5 copy-start.41
  109.7 31.4 %copy-start.29 = (f32[128]{0:T(128)S(1)}, f32[128]{0:T(128)}, u32[]{:S(2)}) copy-start(f32[128]{0:T(128)} %copy-done.27) | copy-start | bytes 1540
  109.7 31.4 %copy-start.34 = (f32[128]{0:T(128)S(1)}, f32[128]{0:T(128)}, u32[]{:S(2)}) copy-start(f32[128]{0:T(128)} %copy-done.33) | copy-start | bytes 1540
  109.7 31.6 %copy-start.6 = (f32[128,1024]{1,0:T(8,128)S(1)}, f32[128,1024]{1,0:T(8,128)}, u32[]{:S(2)}) copy-start(f32[128,1024]{1,0:T(8,128)} %copy-done.5) | copy-start | bytes 1572868
  109.7 31.6 %copy-start.14 = (bf16[1,128,512]{2,1,0:T(8,128)(2,1)S(1)}, bf16[1,128,512]{2,1,0:T(8,128)(2,1)}, u32[]{:S(2)}) copy-start(bf16[1,128,512]{2,1,0:T(8,128)(2,1)} %param.11) | copy-start | bytes 393220
  109.9 48.6 %copy-start.11 = (bf16[128,512]{1,0:T(8,128)(2,1)S(1)}, bf16[128,512]{1,0:T(8,128)(2,1)}, u32[]{:S(2)}) copy-start(bf16[128,512]{1,0:T(8,128)(2,1)} %copy-done.10) | copy-start | bytes 393220
  134.4 16.3 %all-to-all-start.3 = ((bf16[32,2,2048]{2,1,0:T(2,128)(2,1)}), bf16[32,2,2048]{2,1,0:T(2,128)(2,1)S(1)}, u32[]{:S(2)}, u32[]{:S(2)}) async-start(bf16[32,2,2048]{2,1,0:T(2,128)(2,1)} %reduce_sum.236), calls=%async_computation.3 | async-start | bytes 524288 | tf_op jit(solution)/shard_map/all_to_all | solution.py:152
  151.5 12.2 %all-to-all-start.4 = ((f32[8,2,2048]{2,1,0:T(2,128)}), f32[8,2,2048]{2,1,0:T(2,128)S(1)}, u32[]{:S(2)}, u32[]{:S(2)}) async-start(f32[8,2,2048]{2,1,0:T(2,128)} %broadcast_in_dim.236), calls=%async_computation.4 | async-start | bytes 262144 | tf_op jit(solution)/shard_map/all_to_all | solution.py:155

commit v5 on v4

--- a/solution.py
+++ b/solution.py
@@ -141,19 +141,26 @@
     )
 
 
-def reduce_weight_terms(partial, replicas, owners):
+def sum_leading(stacked):
+    total = stacked[0].astype(jnp.float32)
+    for index in range(1, stacked.shape[0]):
+        total = total + stacked[index].astype(jnp.float32)
+    return total
+
+
+def replica_sums(partial, replicas, owners):
     rows, width = partial.shape
-    per_owner = rows // owners
-    per_device = per_owner // replicas
+    per_device = rows // owners // replicas
     terms = partial.astype(jnp.bfloat16).reshape(owners, replicas, per_device, width)
     terms = jnp.swapaxes(terms, 0, 1)
     terms = lax.all_to_all(terms, "dp", 0, 0, tiled=True)
-    terms = jnp.sum(terms.astype(jnp.float32), axis=0).astype(jnp.bfloat16)
-    terms = lax.all_to_all(terms, "ev", 0, 0, tiled=True)
-    piece = jnp.sum(terms.astype(jnp.float32), axis=0)
-    copies = jnp.broadcast_to(piece[None], (replicas, per_device, width))
+    return sum_leading(terms).astype(jnp.bfloat16)
+
+
+def gather_replicas(piece, replicas):
+    copies = jnp.broadcast_to(piece[None], (replicas,) + piece.shape)
     gathered = lax.all_to_all(copies, "dp", 0, 0, tiled=True)
-    return gathered.reshape(per_owner, width)
+    return gathered.reshape(-1, piece.shape[-1])
 
 
 def on_device(
@@ -210,19 +217,26 @@
         cross_input_weight,
         cross_output_weight,
     )
+    factor = (replicas * owners * local_rows) ** (-0.5)
+    partial_sum = jnp.concatenate(
+        [contract(normed_half, back_packed), contract(merged_rows, landed_cotangent)], axis=1
+    )
+    weight_terms = replica_sums(partial_sum, replicas, owners)
     going_back = jnp.concatenate([result, back_rows.astype(jnp.bfloat16)], axis=1)
-    came_back = lax.all_to_all(going_back, "ev", split_axis=0, concat_axis=0, tiled=True)
+    payload = jnp.concatenate(
+        [going_back.reshape(owners, -1), weight_terms.reshape(owners, -1)], axis=1
+    )
+    arrived = lax.all_to_all(payload, "ev", split_axis=0, concat_axis=0, tiled=True)
+    split_at = going_back.size // owners
+    came_back = arrived[:, :split_at].reshape(going_back.shape)
+    owner_terms = arrived[:, split_at:].reshape((owners,) + weight_terms.shape[1:])
+    portion = gather_replicas(sum_leading(owner_terms), replicas) * factor
     picked = lax.dot_general(
         placement, came_back, (((0,), (0,)), ((), ())), preferred_element_type=jnp.float32
     )
     layer_out = (hidden.astype(jnp.float32) + picked[:, :features]).astype(jnp.bfloat16)
     grad_hidden = (upstream.astype(jnp.float32) + picked[:, features:]).astype(jnp.bfloat16)
     grad_rows = intra_pull(grad_hidden)[0]
-    factor = (replicas * owners * local_rows) ** (-0.5)
-    partial_sum = jnp.concatenate(
-        [contract(normed_half, back_packed), contract(merged_rows, landed_cotangent)], axis=1
-    )
-    portion = reduce_weight_terms(partial_sum, replicas, owners) * factor
     return (
         layer_out[None],
         grad_rows[None],

time: 166 us -> 203 us (1.22)
  local copies, waits for them, and re-layouts: 27.8 us -> 49.2 us
  waiting for transfers between devices: 39.7 us -> 52.7 us
  starting transfers between devices: 41.8 us -> 33 us
  matrix products: 25.6 us -> 31.4 us
  other arithmetic: 24.7 us -> 28.8 us
    all_to_all x4 -> x3, waiting for transfers between devices: 32.8 us -> 45.4 us  [the longest x1 25.5 us: replica_sums(): terms = lax.all_to_all(terms, 'dp', 0, 0, tiled=True)]
    convert_element_type x0 -> x17, local copies, waits for them, and re-layouts: none -> 12.5 us  [sum_leading(): total = total + stacked[index].astype(jnp.float32)]
    all_to_all x4 -> x3, starting transfers between devices: 29.6 us -> 21 us  [the longest x1 7.93 us: gather_replicas(): gathered = lax.all_to_all(copies, 'dp', 0, 0, tiled=True)]
    unnamed x85 -> x95, local copies, waits for them, and re-layouts: 4.41 us -> 11 us
    dot_general x3, local copies, waits for them, and re-layouts: 5.32 us -> 2.94 us  [contract(): lax.dot_general(left_part, right_part, (((0,), (0,)), ((), ())), preferre...]
    another operation x4, local copies, waits for them, and re-layouts: 0.24 us -> 2.53 us  [gather_segments(): jnp.stack([jnp.concatenate([pick_block(blocks, selected_rows[group, segme...]
    convert_element_type x1 -> x3, other arithmetic: 3.01 us -> 4.75 us  [the longest x1 2.59 us: replica_sums(): return sum_leading(terms).astype(jnp.bfloat16)]
    reduce_sum x2 -> x1, other arithmetic: 4.49 us -> 2.97 us  [cross_account_inner(): weights = jnp.where(allowed, jnp.exp(scores - highest), 0.0)]
  transfers between devices with their start and end apart: 5 -> 4, of which waited for: 5 -> 4; matrix products, arithmetic and copies ran while one was open for 15% -> 4% of each run, Pallas kernels for 0% -> 0%
where the time goes in v5:
time: 203 us; the launch traced here: 201 us
  waiting for transfers between devices  52.7 us (26%)
  local copies, waits for them, and re-layouts  49.2 us (24%)
  starting transfers between devices  33 us (16%)
  matrix products  31.4 us (15%)
  other arithmetic  28.8 us (14%)
  between operations  5.49 us (3%)
    all_to_all x1, waiting for transfers between devices, replica_sums(): terms = lax.all_to_all(terms, 'dp', 0, 0, tiled=True)  25.5 us
    all_to_all x1, waiting for transfers between devices, on_device(): lax.all_to_all(payload, 'ev', split_axis=0, concat_axis=0, tiled=True)  19.7 us
    convert_element_type x17, local copies, waits for them, and re-layouts, sum_leading(): total = total + stacked[index].astype(jnp.float32)  12.5 us
    all_to_all x1, starting transfers between devices, on_device(): lax.all_to_all(outgoing, 'ev', split_axis=0, concat_axis=0, tiled=True)  12 us
    unnamed x95, local copies, waits for them, and re-layouts  11 us
    all_to_all x1, starting transfers between devices, gather_replicas(): gathered = lax.all_to_all(copies, 'dp', 0, 0, tiled=True)  7.93 us
    all_to_all x1, starting transfers between devices, replica_sums(): terms = lax.all_to_all(terms, 'dp', 0, 0, tiled=True)  7.55 us
    dot_general x3, matrix products, cross_account_inner(): jnp.einsum('bhqd,bhkd->bhqk', queries, key_rows) * HEAD_DIM ** (-0.5)  7.34 us
  transfers between devices with their start and end apart: 4, of which 4 were waited for; matrix products, arithmetic and copies ran while one was open for 4% of the time, Pallas kernels for 0%

profile of v5, /device:TPU:1, one launch (start us, length us, event | category | flops | bytes accessed | tf_op | source)
XLA Modules:
  0.0 200.6 jit_solution(8379531517941195501)
XLA Ops:
  0.7 1.2 convert_reduce_fusion.4
  1.9 1.1 fusion.44
  4.9 1.9 convolution_convert_fusion.2
  9.6 1.1 fusion.18
  10.6 12.0 %all-to-all-start = ((bf16[32,8,1024]{2,1,0:T(8,128)(2,1)}), bf16[32,8,1024]{2,1,0:T(8,128)(2,1)S(1)}, u32[]{:S(2)}, u32[]{:S(2)}) async-start(bf16[32,8,1024]{2,1,0:T(8,128)(2,1)} %fusion.18), calls=%async_computation | async-start | bytes 1048576 | tf_op jit(solution)/shard_map/all_to_all | solution.py:204
  29.9 7.3 %all-to-all-done = bf16[32,8,1024]{2,1,0:T(8,128)(2,1)S(1)} async-done(((bf16[32,8,1024]{2,1,0:T(8,128)(2,1)}), bf16[32,8,1024]{2,1,0:T(8,128)(2,1)S(1)}, u32[]{:S(2)}, u32[]{:S(2)}) %all-to-all-start) | async-done | bytes 524320 | tf_op jit(solution)/shard_map/all_to_all | solution.py:204
  38.7 1.3 convolution_convert_fusion.1
  40.0 1.8 reshape.719
  41.9 2.0 copy.104
  45.7 2.1 %convolution_convert_fusion.7 = bf16[256,512]{1,0:T(8,128)(2,1)} fusion(bf16[512,512]{1,0:T(8,128)(2,1)} %param.17, bf16[256,1024]{1,0:T(8,128)(2,1)S(1)} %bitcast.275), kind=kOutput, calls=%fused_computation.43 | convolution fusion | flops 134348800 | bytes 1048576 | tf_op jit(solution)/shard_map/dot_general | solution.py:124
  47.8 1.8 copy.106
  49.5 1.7 reshape.662
  51.3 1.1 maximum_bitcast_fusion.1
  52.4 1.1 maximum_bitcast_fusion.2
  53.5 1.8 fusion.141
  55.3 1.2 fusion.6
  56.8 1.8 fusion.4
  58.6 3.0 %fusion.135 = (f32[2,8,128]{2,1,0:T(8,128)S(1)}, bf16[2,8,128,384]{3,2,1,0:T(8,128)(2,1)S(1)}, f32[2,8,128]{2,1,0:T(8,128)S(1)}, pred[2,8,128,384]{3,2,1,0:T(32,128)(4,1)S(1)}) fusion(f32[2,8,128,384]{3,2,1,0:T(8,128)S(1)} %get-tuple-element.91, f32[2,8,128]{2,1,0:T(8,128)S(1)} %get-tuple-element.90, f32[2,8,128]{2,1,0:T(8,128)S(1)} %neg.25, ...), kind=kLoop, calls=%fused_computation.300 | loop fusion | flops 10219520 | bytes 7217152 | tf_op jit(solution)/shard_map/transpose(jvp())/reduce_sum | solution.py:95
  61.6 3.2 %fusion.19 = f32[1,2,8,128,64]{3,4,2,1,0:T(8,128)} fusion(bf16[1,8,384,64]{2,3,1,0:T(8,128)(2,1)S(1)} %maximum_bitcast_fusion.2, bf16[1,8,384,64]{2,3,1,0:T(8,128)(2,1)S(1)} %maximum_bitcast_fusion.1, pred[2,8,128,384]{3,2,1,0:T(32,128)(4,1)S(1)} %get-tuple-element.33, f32[2,8,128]{2,1,0:T(8,128)S(1)} %negate_divide_fusion, ...), kind=kOutput, calls=%fused_computation.37 | convolution fusion | flops 108920832 | bytes 6946816 | tf_op jit(solution)/shard_map/transpose(jvp(bhqd,bhkd->bhqk))/dot_general | solution.py:92
  64.8 2.4 %fusion.8 = f32[2,8,384,64]{2,3,1,0:T(8,128)S(1)} fusion(pred[2,8,128,384]{3,2,1,0:T(32,128)(4,1)S(1)} %get-tuple-element.33, f32[2,8,128]{2,1,0:T(8,128)S(1)} %negate_divide_fusion, pred[2,128,384]{2,1,0:T(8,128)(4,1)S(1)} %copy-done.21, bf16[3,2,8,128,64]{3,4,2,1,0:T(8,128)(2,1)S(1)} %bitcast.285, bf16[2,8,128,384]{3,2,1,0:T(8,128)(2,1)S(1)} %get-tuple-element.93, ...), kind=kOutput, calls=%fused_computation.19 | convolution fusion | flops 108527616 | bytes 7471104 | tf_op jit(solution)/shard_map/transpose(jvp(bhqd,bhkd->bhqk))/dot_general | solution.py:92
  68.0 1.6 fusion.67
  69.9 1.0 slice_bitcast_fusion.1
  71.6 1.8 dot_general.101
  73.4 2.1 %convolution_convert_fusion.4 = bf16[32,8,2,512]{3,1,2,0:T(8,128)(2,1)} fusion(bf16[32,8,2,256]{3,2,1,0:T(2,128)(2,1)} %dot_general.101, bf16[256,1024]{1,0:T(8,128)(2,1)S(1)} %bitcast.276), kind=kOutput, calls=%fused_computation.33 | convolution fusion | flops 134479872 | bytes 1048576 | tf_op jit(solution)/shard_map/dot_general | solution.py:139
  75.5 1.5 slice_bitcast_fusion.3
  80.7 1.7 fusion.137
  82.3 1.1 copy.110
  84.2 1.3 maximum_bitcast_fusion
  85.4 3.5 %copy.114 = bf16[8,32,2,2048]{3,2,1,0:T(2,128)(2,1)} copy(bf16[8,32,2,2048]{3,0,2,1:T(8,128)(2,1)S(1)} %maximum_bitcast_fusion) | data formatting | bytes 4194304 | tf_op jit(solution)/shard_map/transpose | solution.py:155
  88.9 7.6 %all-to-all-start.1 = ((bf16[8,32,2,2048]{3,2,1,0:T(2,128)(2,1)}), bf16[8,32,2,2048]{3,2,1,0:T(2,128)(2,1)}, u32[]{:S(2)}, u32[]{:S(2)}) async-start(bf16[8,32,2,2048]{3,2,1,0:T(2,128)(2,1)} %copy.114), calls=%async_computation.1 | async-start | bytes 4194304 | tf_op jit(solution)/shard_map/all_to_all | solution.py:156
  97.3 25.5 %all-to-all-done.1 = bf16[8,32,2,2048]{3,2,1,0:T(2,128)(2,1)} async-done(((bf16[8,32,2,2048]{3,2,1,0:T(2,128)(2,1)}), bf16[8,32,2,2048]{3,2,1,0:T(2,128)(2,1)}, u32[]{:S(2)}, u32[]{:S(2)}) %all-to-all-start.1) | async-done | bytes 2097184 | tf_op jit(solution)/shard_map/all_to_all | solution.py:156
  122.8 2.6 %add_convert_fusion.2 = bf16[1,32,2,2048]{3,2,1,0:T(2,128)(2,1)S(1)} fusion(bf16[8,32,2,2048]{3,2,1,0:T(2,128)(2,1)} %all-to-all-done.1), kind=kLoop, calls=%fused_computation.84 | loop fusion | flops 2097152 | bytes 2359296 | tf_op jit(solution)/shard_map/convert_element_type | solution.py:157
  126.0 1.9 reduce.85
  127.9 3.3 %reshape.813 = bf16[32,2,6144]{2,1,0:T(2,128)(2,1)} reshape(bf16[32,12288]{1,0:T(8,128)(2,1)} %reduce.85) | data formatting | bytes 1572864
  131.1 5.5 %all-to-all-start.2 = ((bf16[32,2,6144]{2,1,0:T(2,128)(2,1)}), bf16[32,2,6144]{2,1,0:T(2,128)(2,1)S(1)}, u32[]{:S(2)}, u32[]{:S(2)}) async-start(bf16[32,2,6144]{2,1,0:T(2,128)(2,1)} %reshape.813), calls=%async_computation.2 | async-start | bytes 1572864 | tf_op jit(solution)/shard_map/all_to_all | solution.py:229
  136.7 19.7 %all-to-all-done.2 = bf16[32,2,6144]{2,1,0:T(2,128)(2,1)S(1)} async-done(((bf16[32,2,6144]{2,1,0:T(2,128)(2,1)}), bf16[32,2,6144]{2,1,0:T(2,128)(2,1)S(1)}, u32[]{:S(2)}, u32[]{:S(2)}) %all-to-all-start.2) | async-done | bytes 786464 | tf_op jit(solution)/shard_map/all_to_all | solution.py:229
  156.3 2.1 %reshape.814 = bf16[32,1,12288]{2,1,0:T(2,128)(2,1)} reshape(bf16[32,2,6144]{2,1,0:T(2,128)(2,1)S(1)} %all-to-all-done.2) | data formatting | bytes 1572864
  158.4 2.3 %copy.159 = bf16[32,1,12288]{2,0,1:T(8,128)(2,1)S(1)} copy(bf16[32,1,12288]{2,1,0:T(2,128)(2,1)} %reshape.814) | data formatting | bytes 1572864
  161.7 1.2 fusion.94
  162.9 1.0 reshape.665
  163.9 1.3 fusion.73
  165.3 2.2 %convolution_convert_fusion.10 = bf16[128,512]{1,0:T(8,128)(2,1)} fusion(bf16[512,512]{1,0:T(8,128)(2,1)} %param.14, f32[128,1024]{1,0:T(8,128)S(1)} %fusion.73, bf16[1,128,512]{2,1,0:T(8,128)(2,1)S(1)} %copy-done.14), kind=kOutput, calls=%fused_computation.52 | convolution fusion | flops 67371008 | bytes 1048576 | tf_op jit(solution)/shard_map/transpose(jvp())/dot_general | solution.py:49
  167.5 1.0 copy.116
  168.5 1.0 convolution_bitcast_fusion.2
  171.0 1.0 convolution_bitcast_fusion.1
  185.9 7.9 %all-to-all-start.3 = ((f32[8,2,2048]{2,1,0:T(2,128)}), f32[8,2,2048]{2,1,0:T(2,128)S(1)}, u32[]{:S(2)}, u32[]{:S(2)}) async-start(f32[8,2,2048]{2,1,0:T(2,128)} %broadcast_in_dim.236), calls=%async_computation.3 | async-start | bytes 262144 | tf_op jit(solution)/shard_map/all_to_all | solution.py:162
  193.9 1.1 add_convert_fusion.1
  195.0 2.1 %fusion.47 = (f32[128]{0:T(128)S(1)}, f32[128,512]{1,0:T(8,128)S(1)}) fusion(bf16[1,128,512]{2,1,0:T(8,128)(2,1)S(1)} %copy-done.1, f32[128]{0:T(128)S(1)} %copy-done.32, f32[512]{0:T(512)} %param.12, bf16[128,1536]{0,1:T(8,128)(2,1)S(1)} %bitcast.293, bf16[512,1536]{1,0:T(8,128)(2,1)} %param.13), kind=kOutput, calls=%fused_computation.108 | convolution fusion | flops 201785216 | bytes 2362368 | tf_op jit(solution)/shard_map/transpose(jvp())/dot_general | solution.py:38
  (193 shorter events, 38.5 us)
Async XLA Ops:
  0.6 38.1 %copy-start = (bf16[512,1536]{1,0:T(8,128)(2,1)S(1)}, bf16[512,1536]{1,0:T(8,128)(2,1)}, u32[]{:S(2)}) copy-start(bf16[512,1536]{1,0:T(8,128)(2,1)} %param.16) | copy-start | bytes 4718596
  0.6 8.6 %copy-start.1 = (bf16[1,128,512]{2,1,0:T(8,128)(2,1)S(1)}, bf16[1,128,512]{2,1,0:T(8,128)(2,1)}, u32[]{:S(2)}) copy-start(bf16[1,128,512]{2,1,0:T(8,128)(2,1)} %param.10) | copy-start | bytes 393220
  0.7 8.6 %copy-start.9 = (bf16[512,512]{1,0:T(8,128)(2,1)S(1)}, bf16[512,512]{1,0:T(8,128)(2,1)}, u32[]{:S(2)}) copy-start(bf16[512,512]{1,0:T(8,128)(2,1)} %param.14) | copy-start | bytes 1572868
  1.8 5.2 %copy-start.31 = (f32[128]{0:T(128)}, f32[128]{0:T(128)S(1)}, u32[]{:S(2)}) copy-start(f32[128]{0:T(128)S(1)} %broadcast_multiply_fusion.2) | copy-start | bytes 1540
  2.9 0.8 copy-start.43
  3.0 4.1 %copy-start.35 = (f32[128]{0:T(128)}, f32[128]{0:T(128)S(1)}, u32[]{:S(2)}) copy-start(f32[128]{0:T(128)S(1)} %fusion.115) | copy-start | bytes 1540
  4.9 4.7 %copy-start.37 = (s32[128]{0:T(128)}, s32[128]{0:T(128)S(1)}, u32[]{:S(2)}) copy-start(s32[128]{0:T(128)S(1)} %fusion.114) | copy-start | bytes 1540
  4.9 4.7 %copy-start.13 = (bf16[1,128,512]{2,1,0:T(8,128)(2,1)S(1)}, bf16[1,128,512]{2,1,0:T(8,128)(2,1)}, u32[]{:S(2)}) copy-start(bf16[1,128,512]{2,1,0:T(8,128)(2,1)} %param.11) | copy-start | bytes 393220
  6.8 17.7 %copy-start.41 = (s32[1,1,2,2]{3,2,1,0:T(2,128)S(1)}, s32[1,1,2,2]{3,2,1,0:T(2,128)}, u32[]{:S(2)}) copy-start(s32[1,1,2,2]{3,2,1,0:T(2,128)} %param.19) | copy-start | bytes 52
  6.8 20.8 %copy-start.30 = (s32[1,4096]{1,0:T(1,128)S(1)}, s32[1,4096]{1,0:T(1,128)}, u32[]{:S(2)}) copy-start(s32[1,4096]{1,0:T(1,128)} %param.18) | copy-start | bytes 49156
  7.1 3.5 %copy-start.2 = (bf16[128,1536]{0,1:T(8,128)(2,1)}, bf16[128,1536]{0,1:T(8,128)(2,1)S(1)}, u32[]{:S(2)}) copy-start(bf16[128,1536]{0,1:T(8,128)(2,1)S(1)} %copy.100) | copy-start | bytes 1179652
  8.3 0.7 copy-start.7
  9.5 1.1 copy-start.11
  10.6 26.6 %all-to-all-start = ((bf16[32,8,1024]{2,1,0:T(8,128)(2,1)}), bf16[32,8,1024]{2,1,0:T(8,128)(2,1)S(1)}, u32[]{:S(2)}, u32[]{:S(2)}) async-start(bf16[32,8,1024]{2,1,0:T(8,128)(2,1)} %fusion.18), calls=%async_computation | async-start | bytes 1048576 | tf_op jit(solution)/shard_map/all_to_all | solution.py:204
  38.1 0.6 copy-start.38
  51.3 4.1 %copy-start.21 = (pred[2,128,384]{2,1,0:T(8,128)(4,1)S(1)}, pred[2,128,384]{2,1,0:T(8,128)(4,1)}, u32[]{:S(2)}) copy-start(pred[2,128,384]{2,1,0:T(8,128)(4,1)} %broadcast_or_fusion) | copy-start | bytes 294916
  53.5 3.1 %copy-start.25 = (bf16[8,128,64]{1,2,0:T(8,128)(2,1)S(1)}, bf16[8,128,64]{1,2,0:T(8,128)(2,1)}, u32[]{:S(2)}) copy-start(bf16[8,128,64]{1,2,0:T(8,128)(2,1)} %get-tuple-element.69) | copy-start | bytes 393220
  53.5 3.1 %copy-start.28 = (bf16[8,128,64]{1,2,0:T(8,128)(2,1)S(1)}, bf16[8,128,64]{1,2,0:T(8,128)(2,1)}, u32[]{:S(2)}) copy-start(bf16[8,128,64]{1,2,0:T(8,128)(2,1)} %get-tuple-element.62) | copy-start | bytes 393220
  53.5 3.1 %copy-start.29 = (bf16[8,128,64]{1,2,0:T(8,128)(2,1)S(1)}, bf16[8,128,64]{1,2,0:T(8,128)(2,1)}, u32[]{:S(2)}) copy-start(bf16[8,128,64]{1,2,0:T(8,128)(2,1)} %get-tuple-element.67) | copy-start | bytes 393220
  55.3 1.4 copy-start.23
  55.3 1.4 copy-start.24
  55.3 1.4 copy-start.27
  55.3 1.5 copy-start.20
  69.8 1.0 copy-start.17
  73.4 3.7 %copy-start.6 = (f32[8,384,64]{1,2,0:T(8,128)S(1)}, f32[8,384,64]{1,2,0:T(8,128)}, u32[]{:S(2)}) copy-start(f32[8,384,64]{1,2,0:T(8,128)} %get-tuple-element.36) | copy-start | bytes 2359300
  77.9 1.0 copy-start.26
  78.2 1.7 copy-start.42
  79.1 1.6 copy-start.34
  79.1 1.6 copy-start.39
  88.9 7.6 %copy-start.40 = (f32[256]{0:T(256)S(1)}, f32[256]{0:T(256)}, u32[]{:S(2)}) copy-start(f32[256]{0:T(256)} %get-tuple-element.26) | copy-start | bytes 3076
  88.9 7.6 %copy-start.10 = (f32[256,512]{1,0:T(8,128)S(1)}, f32[256,512]{1,0:T(8,128)}, u32[]{:S(2)}) copy-start(f32[256,512]{1,0:T(8,128)} %get-tuple-element.27) | copy-start | bytes 1572868
  88.9 7.7 %copy-start.18 = (bf16[2,128,8,64]{1,0,3,2:T(2,128)(2,1)S(1)}, bf16[2,128,8,64]{1,0,3,2:T(2,128)(2,1)}, u32[]{:S(2)}) copy-start(bf16[2,128,8,64]{1,0,3,2:T(2,128)(2,1)} %copy-done.17) | copy-start | bytes 786436
  88.9 7.7 %copy-start.22 = (bf16[512,512]{1,0:T(8,128)(2,1)S(1)}, bf16[512,512]{1,0:T(8,128)(2,1)}, u32[]{:S(2)}) copy-start(bf16[512,512]{1,0:T(8,128)(2,1)} %param.17) | copy-start | bytes 1572868
  88.9 33.9 %all-to-all-start.1 = ((bf16[8,32,2,2048]{3,2,1,0:T(2,128)(2,1)}), bf16[8,32,2,2048]{3,2,1,0:T(2,128)(2,1)}, u32[]{:S(2)}, u32[]{:S(2)}) async-start(bf16[8,32,2,2048]{3,2,1,0:T(2,128)(2,1)} %copy.114), calls=%async_computation.1 | async-start | bytes 4194304 | tf_op jit(solution)/shard_map/all_to_all | solution.py:156
  131.1 25.2 %all-to-all-start.2 = ((bf16[32,2,6144]{2,1,0:T(2,128)(2,1)}), bf16[32,2,6144]{2,1,0:T(2,128)(2,1)S(1)}, u32[]{:S(2)}, u32[]{:S(2)}) async-start(bf16[32,2,6144]{2,1,0:T(2,128)(2,1)} %reshape.813), calls=%async_computation.2 | async-start | bytes 1572864 | tf_op jit(solution)/shard_map/all_to_all | solution.py:229
  158.4 6.9 %copy-start.14 = (bf16[1,128,512]{2,1,0:T(8,128)(2,1)S(1)}, bf16[1,128,512]{2,1,0:T(8,128)(2,1)}, u32[]{:S(2)}) copy-start(bf16[1,128,512]{2,1,0:T(8,128)(2,1)} %param.11) | copy-start | bytes 393220
  160.7 7.8 %copy-start.8 = (bf16[8,128,128]{1,2,0:T(8,128)(2,1)S(1)}, bf16[8,128,128]{1,2,0:T(8,128)(2,1)}, u32[]{:S(2)}) copy-start(bf16[8,128,128]{1,2,0:T(8,128)(2,1)} %copy-done.7) | copy-start | bytes 786436
  160.7 8.8 %copy-start.3 = (bf16[128,1536]{0,1:T(8,128)(2,1)S(1)}, bf16[128,1536]{0,1:T(8,128)(2,1)}, u32[]{:S(2)}) copy-start(bf16[128,1536]{0,1:T(8,128)(2,1)} %copy-done.2) | copy-start | bytes 1179652
  165.3 4.6 %copy-start.4 = (f32[128,1024]{1,0:T(8,128)}, f32[128,1024]{1,0:T(8,128)S(1)}, u32[]{:S(2)}) copy-start(f32[128,1024]{1,0:T(8,128)S(1)} %fusion.73) | copy-start | bytes 1572868
  168.5 1.5 copy-start.16
  169.8 24.1 %copy-start.19 = (f32[1,1,8,128,64]{3,4,2,1,0:T(8,128)S(1)}, f32[1,1,8,128,64]{3,4,2,1,0:T(8,128)}, u32[]{:S(2)}) copy-start(f32[1,1,8,128,64]{3,4,2,1,0:T(8,128)} %convolution_bitcast_fusion.2) | copy-start | bytes 786436
  169.8 25.2 %copy-start.32 = (f32[128]{0:T(128)S(1)}, f32[128]{0:T(128)}, u32[]{:S(2)}) copy-start(f32[128]{0:T(128)} %copy-done.31) | copy-start | bytes 1540
  171.0 26.2 %copy-start.44 = (f32[128]{0:T(128)S(1)}, f32[128]{0:T(128)}, u32[]{:S(2)}) copy-start(f32[128]{0:T(128)} %copy-done.43) | copy-start | bytes 1540
  171.0 26.2 %copy-start.36 = (f32[128]{0:T(128)S(1)}, f32[128]{0:T(128)}, u32[]{:S(2)}) copy-start(f32[128]{0:T(128)} %copy-done.35) | copy-start | bytes 1540
  171.0 26.4 %copy-start.5 = (f32[128,1024]{1,0:T(8,128)S(1)}, f32[128,1024]{1,0:T(8,128)}, u32[]{:S(2)}) copy-start(f32[128,1024]{1,0:T(8,128)} %copy-done.4) | copy-start | bytes 1572868
  171.0 26.4 %copy-start.15 = (bf16[1,128,512]{2,1,0:T(8,128)(2,1)S(1)}, bf16[1,128,512]{2,1,0:T(8,128)(2,1)}, u32[]{:S(2)}) copy-start(bf16[1,128,512]{2,1,0:T(8,128)(2,1)} %param.11) | copy-start | bytes 393220
  172.0 26.2 %copy-start.12 = (bf16[128,512]{1,0:T(8,128)(2,1)S(1)}, bf16[128,512]{1,0:T(8,128)(2,1)}, u32[]{:S(2)}) copy-start(bf16[128,512]{1,0:T(8,128)(2,1)} %copy-done.11) | copy-start | bytes 393220
  185.9 13.2 %all-to-all-start.3 = ((f32[8,2,2048]{2,1,0:T(2,128)}), f32[8,2,2048]{2,1,0:T(2,128)S(1)}, u32[]{:S(2)}, u32[]{:S(2)}) async-start(f32[8,2,2048]{2,1,0:T(2,128)} %broadcast_in_dim.236), calls=%async_computation.3 | async-start | bytes 262144 | tf_op jit(solution)/shard_map/all_to_all | solution.py:162
  (1 other events, 0.6 us)

commit v6 on v4

--- a/solution.py
+++ b/solution.py
@@ -141,19 +141,26 @@
     )
 
 
+def feature_order(left_part, replicas, owners):
+    rows, features = left_part.shape
+    per_device = features // owners // replicas
+    split = left_part.reshape(rows, owners, replicas, per_device)
+    return jnp.swapaxes(split, 1, 2).reshape(rows, features)
+
+
 def reduce_weight_terms(partial, replicas, owners):
     rows, width = partial.shape
-    per_owner = rows // owners
-    per_device = per_owner // replicas
-    terms = partial.astype(jnp.bfloat16).reshape(owners, replicas, per_device, width)
-    terms = jnp.swapaxes(terms, 0, 1)
+    per_replica = rows // replicas
+    per_device = per_replica // owners
+    terms = partial.astype(jnp.bfloat16).reshape(replicas, per_replica, width)
     terms = lax.all_to_all(terms, "dp", 0, 0, tiled=True)
     terms = jnp.sum(terms.astype(jnp.float32), axis=0).astype(jnp.bfloat16)
+    terms = terms.reshape(owners, per_device, width)
     terms = lax.all_to_all(terms, "ev", 0, 0, tiled=True)
     piece = jnp.sum(terms.astype(jnp.float32), axis=0)
     copies = jnp.broadcast_to(piece[None], (replicas, per_device, width))
     gathered = lax.all_to_all(copies, "dp", 0, 0, tiled=True)
-    return gathered.reshape(per_owner, width)
+    return gathered.reshape(replicas * per_device, width)
 
 
 def on_device(
@@ -220,7 +227,11 @@
     grad_rows = intra_pull(grad_hidden)[0]
     factor = (replicas * owners * local_rows) ** (-0.5)
     partial_sum = jnp.concatenate(
-        [contract(normed_half, back_packed), contract(merged_rows, landed_cotangent)], axis=1
+        [
+            contract(feature_order(normed_half, replicas, owners), back_packed),
+            contract(feature_order(merged_rows, replicas, owners), landed_cotangent),
+        ],
+        axis=1,
     )
     portion = reduce_weight_terms(partial_sum, replicas, owners) * factor
     return (

time: 166 us -> 168 us (1.012)
  local copies, waits for them, and re-layouts: 27.8 us -> 31.4 us
    reshape x0 -> x5, local copies, waits for them, and re-layouts: none -> 7.98 us  [the longest x2 3.58 us: feature_order(): split = left_part.reshape(rows, owners, replicas, per_device)]
    dot_general x3 -> x0, local copies, waits for them, and re-layouts: 5.32 us -> none  [contract(): lax.dot_general(left_part, right_part, (((0,), (0,)), ((), ())), preferre...]
    all_to_all x1, starting transfers between devices: 6.67 us -> 9.43 us  [reduce_weight_terms(): terms = lax.all_to_all(terms, 'ev', 0, 0, tiled=True)]
    all_to_all x1, starting transfers between devices: 8.65 us -> 6.1 us  [reduce_weight_terms(): terms = lax.all_to_all(terms, 'dp', 0, 0, tiled=True)]
    reduce_sum x1, other arithmetic: 4.38 us -> 1.96 us  [reduce_weight_terms(): terms = jnp.sum(terms.astype(jnp.float32), axis=0).astype(jnp.bfloat16)]
    convert_element_type x0 -> x1, local copies, waits for them, and re-layouts: none -> 1.81 us  [owner_transfer(): normed_half = normed.astype(jnp.bfloat16)]
    unnamed x85 -> x88, local copies, waits for them, and re-layouts: 4.41 us -> 3.35 us
    transpose x1 -> x2, local copies, waits for them, and re-layouts: 3.46 us -> 3.66 us  [feature_order(): return jnp.swapaxes(split, 1, 2).reshape(rows, features)]
  transfers between devices with their start and end apart: 5 -> 5, of which waited for: 5 -> 4; matrix products, arithmetic and copies ran while one was open for 15% -> 17% of each run, Pallas kernels for 0% -> 0%
where the time goes in v6:
time: 168 us; the launch traced here: 166 us
  starting transfers between devices  42.1 us (25%)
  waiting for transfers between devices  39.5 us (24%)
  local copies, waits for them, and re-layouts  31.4 us (19%)
  matrix products  24.8 us (15%)
  other arithmetic  23.1 us (14%)
  between operations  5.56 us (3%)
    all_to_all x1, waiting for transfers between devices, reduce_weight_terms(): terms = lax.all_to_all(terms, 'dp', 0, 0, tiled=True)  19.4 us
    all_to_all x1, starting transfers between devices, on_device(): lax.all_to_all(outgoing, 'ev', split_axis=0, concat_axis=0, tiled=True)  12.2 us
    all_to_all x1, starting transfers between devices, reduce_weight_terms(): terms = lax.all_to_all(terms, 'ev', 0, 0, tiled=True)  9.43 us
    all_to_all x1, waiting for transfers between devices, reduce_weight_terms(): terms = lax.all_to_all(terms, 'ev', 0, 0, tiled=True)  8.59 us
    all_to_all x1, starting transfers between devices, on_device(): lax.all_to_all(going_back, 'ev', split_axis=0, concat_axis=0, tiled=True)  7.39 us
    all_to_all x1, waiting for transfers between devices, on_device(): lax.all_to_all(outgoing, 'ev', split_axis=0, concat_axis=0, tiled=True)  6.96 us
    all_to_all x1, starting transfers between devices, reduce_weight_terms(): gathered = lax.all_to_all(copies, 'dp', 0, 0, tiled=True)  6.94 us
    dot_general x3, matrix products, cross_account_inner(): jnp.einsum('bhqd,bhkd->bhqk', queries, key_rows) * HEAD_DIM ** (-0.5)  6.25 us
  transfers between devices with their start and end apart: 5, of which 4 were waited for; matrix products, arithmetic and copies ran while one was open for 17% of the time, Pallas kernels for 0%

profile of v6, /device:TPU:1, one launch (start us, length us, event | category | flops | bytes accessed | tf_op | source)
XLA Modules:
  0.0 166.5 jit_solution(6047202248649003501)
XLA Ops:
  0.7 1.2 convert_reduce_fusion.5
  1.9 1.1 fusion.46
  4.9 1.9 %convolution_convert_fusion.2 = bf16[128,1536]{1,0:T(8,128)(2,1)S(1)} fusion(bf16[512,1536]{1,0:T(8,128)(2,1)} %param.13, bf16[1,128,512]{2,1,0:T(8,128)(2,1)} %param.10, f32[512]{0:T(512)} %param.12, f32[128]{0:T(128)S(1)} %fusion.82, f32[128]{0:T(128)S(1)} %broadcast_multiply_fusion.2), kind=kOutput, calls=%fused_computation.15 | convolution fusion | flops 201850880 | bytes 2100224 | tf_op jit(solution)/shard_map/jvp()/dot_general | solution.py:38
  7.5 0.8 convert_reduce_fusion.3
  9.6 1.1 fusion.18
  10.6 12.2 %all-to-all-start = ((bf16[32,8,1024]{2,1,0:T(8,128)(2,1)}), bf16[32,8,1024]{2,1,0:T(8,128)(2,1)S(1)}, u32[]{:S(2)}, u32[]{:S(2)}) async-start(bf16[32,8,1024]{2,1,0:T(8,128)(2,1)} %fusion.18), calls=%async_computation | async-start | bytes 1048576 | tf_op jit(solution)/shard_map/all_to_all | solution.py:204
  30.2 7.0 %all-to-all-done = bf16[32,8,1024]{2,1,0:T(8,128)(2,1)S(1)} async-done(((bf16[32,8,1024]{2,1,0:T(8,128)(2,1)}), bf16[32,8,1024]{2,1,0:T(8,128)(2,1)S(1)}, u32[]{:S(2)}, u32[]{:S(2)}) %all-to-all-start) | async-done | bytes 524320 | tf_op jit(solution)/shard_map/all_to_all | solution.py:204
  40.1 1.8 %reshape.341 = bf16[2,128,3,8,64]{4,3,2,1,0:T(8,128)(2,1)} reshape(bf16[256,1536]{1,0:T(8,128)(2,1)S(1)} %convolution_convert_fusion.1) | data formatting | bytes 1572864 | tf_op jit(solution)/shard_map/jvp()/reshape | solution.py:26
  41.9 2.0 %copy.122 = bf16[2,128,3,8,64]{1,4,3,0,2:T(8,128)(2,1)S(1)} copy(bf16[2,128,3,8,64]{4,3,2,1,0:T(8,128)(2,1)} %reshape.341) | data formatting | bytes 1572864 | tf_op jit(solution)/shard_map/jvp()/reshape | solution.py:26
  43.9 0.9 select_bitcast_fusion.28
  44.8 0.9 select_bitcast_fusion.29
  45.8 2.1 %convolution_convert_fusion.7 = bf16[256,512]{1,0:T(8,128)(2,1)} fusion(bf16[512,512]{1,0:T(8,128)(2,1)} %param.17, bf16[256,1024]{1,0:T(8,128)(2,1)S(1)} %bitcast.279), kind=kOutput, calls=%fused_computation.43 | convolution fusion | flops 134348800 | bytes 1048576 | tf_op jit(solution)/shard_map/dot_general | solution.py:124
  47.8 1.8 %copy.124 = bf16[256,512]{0,1:T(8,128)(2,1)} copy(bf16[256,512]{1,0:T(8,128)(2,1)} %convolution_convert_fusion.7) | data formatting | bytes 524288 | tf_op jit(solution)/shard_map/convert_element_type | solution.py:129
  49.6 1.7 %reshape.329 = bf16[2,128,8,64]{1,0,3,2:T(2,128)(2,1)} reshape(bf16[256,512]{0,1:T(8,128)(2,1)} %copy.124) | data formatting | bytes 524288 | tf_op jit(solution)/shard_map/transpose(jvp())/reshape | solution.py:31
  51.3 1.1 maximum_bitcast_fusion
  52.4 1.1 maximum_bitcast_fusion.1
  53.6 1.8 %fusion.106 = (f32[2,8,128]{2,1,0:T(8,128)S(1)}, f32[2,8,128,384]{3,2,1,0:T(8,128)S(1)}) fusion(bf16[1,8,384,64]{2,3,1,0:T(8,128)(2,1)S(1)} %maximum_bitcast_fusion.1, bf16[1,8,384,64]{2,3,1,0:T(8,128)(2,1)S(1)} %maximum_bitcast_fusion, bf16[3,2,8,128,64]{3,4,2,1,0:T(8,128)(2,1)S(1)} %bitcast.285, pred[2,128,384]{2,1,0:T(8,128)(4,1)} %broadcast_or_fusion), kind=kOutput, calls=%fused_computation.236 | convolution fusion | flops 103413760 | bytes 4300800 | tf_op jit(solution)/shard_map/jvp(bhqd,bhkd->bhqk)/dot_general | solution.py:92
  55.4 1.2 fusion.6
  56.8 1.8 %fusion.4 = (f32[2,8,128]{2,1,0:T(8,128)S(1)}, bf16[2,8,128,384]{3,2,1,0:T(8,128)(2,1)S(1)}) fusion(f32[2,8,128,384]{3,2,1,0:T(8,128)S(1)} %get-tuple-element.72, f32[2,8,128]{2,1,0:T(8,128)S(1)} %multiply_divide_fusion, f32[2,8,128]{2,1,0:T(8,128)S(1)} %get-tuple-element.71, pred[2,128,384]{2,1,0:T(8,128)(4,1)S(1)} %copy-done.19, ...), kind=kOutput, calls=%fused_computation.6 | convolution fusion | flops 105773056 | bytes 5890048 | tf_op jit(solution)/shard_map/transpose(jvp(bhqk,bhkd->bhqd))/dot_general | solution.py:97
  58.7 3.0 %divide_convert_fusion = (bf16[2,8,128,384]{3,2,1,0:T(8,128)(2,1)S(1)}, f32[2,8,128]{2,1,0:T(8,128)S(1)}, f32[2,8,128]{2,1,0:T(8,128)S(1)}, pred[2,8,128,384]{3,2,1,0:T(32,128)(4,1)S(1)}) fusion(f32[2,8,128,384]{3,2,1,0:T(8,128)S(1)} %get-tuple-element.72, f32[2,8,128]{2,1,0:T(8,128)S(1)} %fusion.6, f32[2,8,128]{2,1,0:T(8,128)S(1)} %get-tuple-element.71, ...), kind=kLoop, calls=%fused_computation.9 | loop fusion | flops 10219520 | bytes 7217152 | tf_op jit(solution)/shard_map/jvp()/convert_element_type | solution.py:96
  61.7 2.0 %fusion.19 = f32[1,2,8,128,64]{3,4,2,1,0:T(8,128)S(1)} fusion(bf16[1,8,384,64]{2,3,1,0:T(8,128)(2,1)S(1)} %maximum_bitcast_fusion.1, bf16[1,8,384,64]{2,3,1,0:T(8,128)(2,1)S(1)} %maximum_bitcast_fusion, pred[2,8,128,384]{3,2,1,0:T(32,128)(4,1)S(1)} %get-tuple-element.15, f32[2,8,128]{2,1,0:T(8,128)S(1)} %negate_divide_fusion, ...), kind=kOutput, calls=%fused_computation.37 | convolution fusion | flops 108920832 | bytes 6946816 | tf_op jit(solution)/shard_map/transpose(jvp(bhqd,bhkd->bhqk))/dot_general | solution.py:92
  63.7 2.5 %fusion.8 = f32[2,8,384,64]{2,3,1,0:T(8,128)S(1)} fusion(pred[2,8,128,384]{3,2,1,0:T(32,128)(4,1)S(1)} %get-tuple-element.15, f32[2,8,128]{2,1,0:T(8,128)S(1)} %negate_divide_fusion, pred[2,128,384]{2,1,0:T(8,128)(4,1)S(1)} %copy-done.19, bf16[3,2,8,128,64]{3,4,2,1,0:T(8,128)(2,1)S(1)} %bitcast.286, bf16[2,8,128,384]{3,2,1,0:T(8,128)(2,1)S(1)} %get-tuple-element.74, ...), kind=kOutput, calls=%fused_computation.19 | convolution fusion | flops 108527616 | bytes 7471104 | tf_op jit(solution)/shard_map/transpose(jvp(bhqd,bhkd->bhqk))/dot_general | solution.py:92
  66.2 0.8 fusion.22
  70.4 0.8 copy.127
  72.4 0.9 maximum_bitcast_fusion.4
  73.3 7.4 %all-to-all-start.1 = ((bf16[32,8,1024]{2,1,0:T(8,128)(2,1)}), bf16[32,8,1024]{2,1,0:T(8,128)(2,1)}, u32[]{:S(2)}, u32[]{:S(2)}) async-start(bf16[32,8,1024]{2,1,0:T(8,128)(2,1)} %maximum_bitcast_fusion.4), calls=%async_computation.1 | async-start | bytes 1048576 | tf_op jit(solution)/shard_map/all_to_all | solution.py:221
  80.7 1.8 %copy.132 = bf16[256,512]{0,1:T(8,128)(2,1)} copy(bf16[256,512]{1,0:T(8,128)(2,1)} %copy-done.9) | data formatting | bytes 524288 | tf_op jit(solution)/shard_map/convert_element_type | solution.py:113
  82.5 1.8 %reshape.336 = bf16[256,32,8,2]{0,3,2,1:T(2,128)(2,1)} reshape(bf16[2,128,8,64]{1,0,3,2:T(2,128)(2,1)} %copy-done.17) | data formatting | bytes 524288 | tf_op jit(solution)/shard_map/reshape;jvp()/reshape | solution.py:147
  84.3 1.7 %reshape.334 = bf16[256,32,8,2]{0,3,2,1:T(2,128)(2,1)} reshape(bf16[256,512]{0,1:T(8,128)(2,1)} %copy.132) | data formatting | bytes 524288 | tf_op jit(solution)/shard_map/reshape | solution.py:147
  86.1 1.8 %copy.133 = bf16[256,8,32,2]{0,3,2,1:T(2,128)(2,1)} copy(bf16[256,8,32,2]{0,3,1,2:T(2,128)(2,1)} %bitcast.301) | data formatting | bytes 524288 | tf_op jit(solution)/shard_map/transpose | solution.py:148
  87.9 1.8 %reshape.335 = bf16[256,512]{0,1:T(8,128)(2,1)} reshape(bf16[256,8,32,2]{0,3,2,1:T(2,128)(2,1)} %copy.133) | data formatting | bytes 524288 | tf_op jit(solution)/shard_map/reshape | solution.py:148
  89.7 1.8 %copy.136 = bf16[256,8,32,2]{0,3,2,1:T(2,128)(2,1)} copy(bf16[256,8,32,2]{0,3,1,2:T(2,128)(2,1)} %bitcast.300) | data formatting | bytes 524288 | tf_op jit(solution)/shard_map/transpose | solution.py:148
  91.5 1.8 %reshape.337 = bf16[256,512]{0,1:T(8,128)(2,1)} reshape(bf16[256,8,32,2]{0,3,2,1:T(2,128)(2,1)} %copy.136) | data formatting | bytes 524288 | tf_op jit(solution)/shard_map/reshape | solution.py:148
  93.3 1.2 convolution_convert_fusion.4
  94.5 1.6 convolution_convert_fusion
  96.1 1.6 pad_maximum_fusion
  97.7 6.1 %all-to-all-start.2 = ((bf16[8,64,2048]{2,1,0:T(8,128)(2,1)}), bf16[8,64,2048]{2,1,0:T(8,128)(2,1)}, u32[]{:S(2)}, u32[]{:S(2)}) async-start(bf16[8,64,2048]{2,1,0:T(8,128)(2,1)} %pad_maximum_fusion), calls=%async_computation.2 | async-start | bytes 4194304 | tf_op jit(solution)/shard_map/all_to_all | solution.py:156
  103.8 1.3 fusion.38
  105.1 2.2 %convolution_convert_fusion.10 = bf16[128,512]{1,0:T(8,128)(2,1)} fusion(bf16[512,512]{1,0:T(8,128)(2,1)} %param.14, f32[128,1024]{1,0:T(8,128)S(1)} %fusion.38, bf16[1,128,512]{2,1,0:T(8,128)(2,1)S(1)} %copy-done.14), kind=kOutput, calls=%fused_computation.52 | convolution fusion | flops 67371008 | bytes 1048576 | tf_op jit(solution)/shard_map/transpose(jvp())/dot_general | solution.py:49
  107.3 1.0 copy.128
  110.7 19.4 %all-to-all-done.2 = bf16[8,64,2048]{2,1,0:T(8,128)(2,1)} async-done(((bf16[8,64,2048]{2,1,0:T(8,128)(2,1)}), bf16[8,64,2048]{2,1,0:T(8,128)(2,1)}, u32[]{:S(2)}, u32[]{:S(2)}) %all-to-all-start.2) | async-done | bytes 2097184 | tf_op jit(solution)/shard_map/all_to_all | solution.py:156
  130.1 2.0 %reduce_sum.236 = bf16[64,2048]{1,0:T(8,128)(2,1)S(1)} reduce(bf16[8,64,2048]{2,1,0:T(8,128)(2,1)} %all-to-all-done.2, bf16[]{:T(256)} %constant.78.clone.1), dimensions={0}, to_apply=%region_21.22 | reduce | flops 917504 | bytes 2359298 | tf_op jit(solution)/shard_map/reduce_sum | solution.py:157
  132.1 0.9 reshape.338
  132.9 9.4 %all-to-all-start.3 = ((bf16[32,2,2048]{2,1,0:T(2,128)(2,1)}), bf16[32,2,2048]{2,1,0:T(2,128)(2,1)S(1)}, u32[]{:S(2)}, u32[]{:S(2)}) async-start(bf16[32,2,2048]{2,1,0:T(2,128)(2,1)} %reshape.338), calls=%async_computation.3 | async-start | bytes 524288 | tf_op jit(solution)/shard_map/all_to_all | solution.py:159
  142.6 0.8 fusion.70
  143.4 8.6 %all-to-all-done.3 = bf16[32,2,2048]{2,1,0:T(2,128)(2,1)S(1)} async-done(((bf16[32,2,2048]{2,1,0:T(2,128)(2,1)}), bf16[32,2,2048]{2,1,0:T(2,128)(2,1)S(1)}, u32[]{:S(2)}, u32[]{:S(2)}) %all-to-all-start.3) | async-done | bytes 262176 | tf_op jit(solution)/shard_map/all_to_all | solution.py:159
  152.8 6.9 %all-to-all-start.4 = ((f32[8,2,2048]{2,1,0:T(2,128)}), f32[8,2,2048]{2,1,0:T(2,128)S(1)}, u32[]{:S(2)}, u32[]{:S(2)}) async-start(f32[8,2,2048]{2,1,0:T(2,128)} %broadcast_in_dim.236), calls=%async_computation.4 | async-start | bytes 262144 | tf_op jit(solution)/shard_map/all_to_all | solution.py:162
  160.4 4.6 %all-to-all-done.4 = f32[8,2,2048]{2,1,0:T(2,128)S(1)} async-done(((f32[8,2,2048]{2,1,0:T(2,128)}), f32[8,2,2048]{2,1,0:T(2,128)S(1)}, u32[]{:S(2)}, u32[]{:S(2)}) %all-to-all-start.4) | async-done | bytes 131104 | tf_op jit(solution)/shard_map/all_to_all | solution.py:162
  (167 shorter events, 19.8 us)
Async XLA Ops:
  0.6 38.9 %copy-start = (bf16[512,1536]{1,0:T(8,128)(2,1)S(1)}, bf16[512,1536]{1,0:T(8,128)(2,1)}, u32[]{:S(2)}) copy-start(bf16[512,1536]{1,0:T(8,128)(2,1)} %param.16) | copy-start | bytes 4718596
  0.6 8.6 %copy-start.1 = (bf16[1,128,512]{2,1,0:T(8,128)(2,1)S(1)}, bf16[1,128,512]{2,1,0:T(8,128)(2,1)}, u32[]{:S(2)}) copy-start(bf16[1,128,512]{2,1,0:T(8,128)(2,1)} %param.10) | copy-start | bytes 393220
  0.7 8.6 %copy-start.10 = (bf16[512,512]{1,0:T(8,128)(2,1)S(1)}, bf16[512,512]{1,0:T(8,128)(2,1)}, u32[]{:S(2)}) copy-start(bf16[512,512]{1,0:T(8,128)(2,1)} %param.14) | copy-start | bytes 1572868
  1.8 5.2 %copy-start.28 = (f32[128]{0:T(128)}, f32[128]{0:T(128)S(1)}, u32[]{:S(2)}) copy-start(f32[128]{0:T(128)S(1)} %broadcast_multiply_fusion.2) | copy-start | bytes 1540
  2.9 0.8 copy-start.42
  3.0 4.1 %copy-start.36 = (f32[128]{0:T(128)}, f32[128]{0:T(128)S(1)}, u32[]{:S(2)}) copy-start(f32[128]{0:T(128)S(1)} %fusion.82) | copy-start | bytes 1540
  4.9 4.7 %copy-start.38 = (s32[128]{0:T(128)}, s32[128]{0:T(128)S(1)}, u32[]{:S(2)}) copy-start(s32[128]{0:T(128)S(1)} %fusion.81) | copy-start | bytes 1540
  4.9 4.7 %copy-start.13 = (bf16[1,128,512]{2,1,0:T(8,128)(2,1)S(1)}, bf16[1,128,512]{2,1,0:T(8,128)(2,1)}, u32[]{:S(2)}) copy-start(bf16[1,128,512]{2,1,0:T(8,128)(2,1)} %param.11) | copy-start | bytes 393220
  6.8 17.9 %copy-start.39 = (s32[1,1,2,2]{3,2,1,0:T(2,128)S(1)}, s32[1,1,2,2]{3,2,1,0:T(2,128)}, u32[]{:S(2)}) copy-start(s32[1,1,2,2]{3,2,1,0:T(2,128)} %param.19) | copy-start | bytes 52
  6.8 21.1 %copy-start.27 = (s32[1,4096]{1,0:T(1,128)S(1)}, s32[1,4096]{1,0:T(1,128)}, u32[]{:S(2)}) copy-start(s32[1,4096]{1,0:T(1,128)} %param.18) | copy-start | bytes 49156
  7.1 3.5 %copy-start.3 = (bf16[128,1536]{0,1:T(8,128)(2,1)}, bf16[128,1536]{0,1:T(8,128)(2,1)S(1)}, u32[]{:S(2)}) copy-start(bf16[128,1536]{0,1:T(8,128)(2,1)S(1)} %copy.118) | copy-start | bytes 1179652
  7.1 31.6 %copy-start.40 = (f32[512]{0:T(512)S(1)}, f32[512]{0:T(512)}, u32[]{:S(2)}) copy-start(f32[512]{0:T(512)} %param.15) | copy-start | bytes 6148
  8.3 0.7 copy-start.7
  9.5 1.1 copy-start.11
  10.6 26.6 %all-to-all-start = ((bf16[32,8,1024]{2,1,0:T(8,128)(2,1)}), bf16[32,8,1024]{2,1,0:T(8,128)(2,1)S(1)}, u32[]{:S(2)}, u32[]{:S(2)}) async-start(bf16[32,8,1024]{2,1,0:T(8,128)(2,1)} %fusion.18), calls=%async_computation | async-start | bytes 1048576 | tf_op jit(solution)/shard_map/all_to_all | solution.py:204
  38.1 0.6 copy-start.31
  38.8 0.7 copy-start.9
  51.3 4.1 %copy-start.19 = (pred[2,128,384]{2,1,0:T(8,128)(4,1)S(1)}, pred[2,128,384]{2,1,0:T(8,128)(4,1)}, u32[]{:S(2)}) copy-start(pred[2,128,384]{2,1,0:T(8,128)(4,1)} %broadcast_or_fusion) | copy-start | bytes 294916
  53.5 3.1 %copy-start.23 = (bf16[8,128,64]{1,2,0:T(8,128)(2,1)S(1)}, bf16[8,128,64]{1,2,0:T(8,128)(2,1)}, u32[]{:S(2)}) copy-start(bf16[8,128,64]{1,2,0:T(8,128)(2,1)} %get-tuple-element.51) | copy-start | bytes 393220
  53.5 3.1 %copy-start.25 = (bf16[8,128,64]{1,2,0:T(8,128)(2,1)S(1)}, bf16[8,128,64]{1,2,0:T(8,128)(2,1)}, u32[]{:S(2)}) copy-start(bf16[8,128,64]{1,2,0:T(8,128)(2,1)} %get-tuple-element.44) | copy-start | bytes 393220
  53.5 3.1 %copy-start.26 = (bf16[8,128,64]{1,2,0:T(8,128)(2,1)S(1)}, bf16[8,128,64]{1,2,0:T(8,128)(2,1)}, u32[]{:S(2)}) copy-start(bf16[8,128,64]{1,2,0:T(8,128)(2,1)} %get-tuple-element.49) | copy-start | bytes 393220
  55.3 1.4 copy-start.21
  55.3 1.4 copy-start.22
  55.3 1.4 copy-start.24
  55.4 1.5 copy-start.18
  67.0 1.4 copy-start.20
  67.7 0.7 copy-start.17
  70.0 1.3 copy-start.41
  70.4 1.6 copy-start.34
  70.4 1.6 copy-start.32
  73.3 24.4 %all-to-all-start.1 = ((bf16[32,8,1024]{2,1,0:T(8,128)(2,1)}), bf16[32,8,1024]{2,1,0:T(8,128)(2,1)}, u32[]{:S(2)}, u32[]{:S(2)}) async-start(bf16[32,8,1024]{2,1,0:T(8,128)(2,1)} %maximum_bitcast_fusion.4), calls=%async_computation.1 | async-start | bytes 1048576 | tf_op jit(solution)/shard_map/all_to_all | solution.py:221
  97.7 7.4 %copy-start.14 = (bf16[1,128,512]{2,1,0:T(8,128)(2,1)S(1)}, bf16[1,128,512]{2,1,0:T(8,128)(2,1)}, u32[]{:S(2)}) copy-start(bf16[1,128,512]{2,1,0:T(8,128)(2,1)} %param.11) | copy-start | bytes 393220
  97.7 10.7 %copy-start.4 = (bf16[128,1536]{0,1:T(8,128)(2,1)S(1)}, bf16[128,1536]{0,1:T(8,128)(2,1)}, u32[]{:S(2)}) copy-start(bf16[128,1536]{0,1:T(8,128)(2,1)} %copy-done.3) | copy-start | bytes 1179652
  97.7 11.0 %copy-start.8 = (bf16[8,128,128]{1,2,0:T(8,128)(2,1)S(1)}, bf16[8,128,128]{1,2,0:T(8,128)(2,1)}, u32[]{:S(2)}) copy-start(bf16[8,128,128]{1,2,0:T(8,128)(2,1)} %copy-done.7) | copy-start | bytes 786436
  97.7 32.4 %all-to-all-start.2 = ((bf16[8,64,2048]{2,1,0:T(8,128)(2,1)}), bf16[8,64,2048]{2,1,0:T(8,128)(2,1)}, u32[]{:S(2)}, u32[]{:S(2)}) async-start(bf16[8,64,2048]{2,1,0:T(8,128)(2,1)} %pad_maximum_fusion), calls=%async_computation.2 | async-start | bytes 4194304 | tf_op jit(solution)/shard_map/all_to_all | solution.py:156
  105.1 3.9 %copy-start.5 = (f32[128,1024]{1,0:T(8,128)}, f32[128,1024]{1,0:T(8,128)S(1)}, u32[]{:S(2)}) copy-start(f32[128,1024]{1,0:T(8,128)S(1)} %fusion.38) | copy-start | bytes 1572868
  108.4 0.9 copy-start.16
  108.4 1.5 copy-start.2
  108.4 1.5 copy-start.29
  108.4 1.5 copy-start.35
  109.2 1.5 copy-start.43
  109.9 32.5 %copy-start.30 = (f32[128]{0:T(128)S(1)}, f32[128]{0:T(128)}, u32[]{:S(2)}) copy-start(f32[128]{0:T(128)} %copy-done.28) | copy-start | bytes 1540
  109.9 32.5 %copy-start.37 = (f32[128]{0:T(128)S(1)}, f32[128]{0:T(128)}, u32[]{:S(2)}) copy-start(f32[128]{0:T(128)} %copy-done.36) | copy-start | bytes 1540
  109.9 32.7 %copy-start.6 = (f32[128,1024]{1,0:T(8,128)S(1)}, f32[128,1024]{1,0:T(8,128)}, u32[]{:S(2)}) copy-start(f32[128,1024]{1,0:T(8,128)} %copy-done.5) | copy-start | bytes 1572868
  109.9 32.7 %copy-start.15 = (bf16[1,128,512]{2,1,0:T(8,128)(2,1)S(1)}, bf16[1,128,512]{2,1,0:T(8,128)(2,1)}, u32[]{:S(2)}) copy-start(bf16[1,128,512]{2,1,0:T(8,128)(2,1)} %param.11) | copy-start | bytes 393220
  110.7 49.1 %copy-start.12 = (bf16[128,512]{1,0:T(8,128)(2,1)S(1)}, bf16[128,512]{1,0:T(8,128)(2,1)}, u32[]{:S(2)}) copy-start(bf16[128,512]{1,0:T(8,128)(2,1)} %copy-done.11) | copy-start | bytes 393220
  132.9 19.1 %all-to-all-start.3 = ((bf16[32,2,2048]{2,1,0:T(2,128)(2,1)}), bf16[32,2,2048]{2,1,0:T(2,128)(2,1)S(1)}, u32[]{:S(2)}, u32[]{:S(2)}) async-start(bf16[32,2,2048]{2,1,0:T(2,128)(2,1)} %reshape.338), calls=%async_computation.3 | async-start | bytes 524288 | tf_op jit(solution)/shard_map/all_to_all | solution.py:159
  152.8 12.2 %all-to-all-start.4 = ((f32[8,2,2048]{2,1,0:T(2,128)}), f32[8,2,2048]{2,1,0:T(2,128)S(1)}, u32[]{:S(2)}, u32[]{:S(2)}) async-start(f32[8,2,2048]{2,1,0:T(2,128)} %broadcast_in_dim.236), calls=%async_computation.4 | async-start | bytes 262144 | tf_op jit(solution)/shard_map/all_to_all | solution.py:162
  (1 other events, 0.6 us)

commit v7 on v6

--- a/solution.py
+++ b/solution.py
@@ -22,9 +22,14 @@
     return matrix.reshape(block_groups, EVENTS_PER_BLOCK, HEADS, HEAD_DIM)
 
 
-def heads_first(packed_rows, block_groups):
-    parts = packed_rows.reshape(block_groups, EVENTS_PER_BLOCK, 3, HEADS, HEAD_DIM)
-    return jnp.transpose(parts, (2, 0, 3, 1, 4)).astype(jnp.float32)
+def project_heads(normed, input_weight):
+    row_total, features = normed.shape
+    block_groups = row_total // EVENTS_PER_BLOCK
+    weight = input_weight.reshape(features, 3, HEADS, HEAD_DIM)
+    blocks = normed.reshape(block_groups, EVENTS_PER_BLOCK, features)
+    return jnp.einsum(
+        "bqf,fphd->pbhqd", blocks, weight, preferred_element_type=jnp.float32
+    ).astype(jnp.bfloat16)
 
 
 def rows_first(merged, row_total):
@@ -35,10 +40,7 @@
     row_total, features = source.shape
     block_groups = row_total // EVENTS_PER_BLOCK
     normed = layer_norm(source, scale_factors).astype(jnp.bfloat16)
-    packed_rows = jnp.dot(normed, input_weight, preferred_element_type=jnp.float32).astype(
-        jnp.bfloat16
-    )
-    parts = heads_first(packed_rows, block_groups)
+    parts = project_heads(normed, input_weight).astype(jnp.float32)
     queries, key_rows, value_rows = parts[0], parts[1], parts[2]
     scores = jnp.einsum("bhqd,bhkd->bhqk", queries, key_rows) * HEAD_DIM ** (-0.5)
     highest = jnp.max(scores, axis=-1, keepdims=True)
@@ -71,13 +73,13 @@
     )
 
 
-def cross_account_inner(packed_rows, row_presence, block_listing):
-    row_total, three_wide = packed_rows.shape
-    block_groups = row_total // EVENTS_PER_BLOCK
+def cross_account_inner(packed_heads, row_presence, block_listing):
+    block_groups = packed_heads.shape[1]
+    row_total = block_groups * EVENTS_PER_BLOCK
     selected_rows = jnp.concatenate(
         [jnp.arange(block_groups, dtype=jnp.int32)[:, None], block_listing], axis=1
     )
-    parts = heads_first(packed_rows, block_groups)
+    parts = packed_heads.astype(jnp.float32)
     queries = parts[0]
     key_rows = gather_segments(parts[1], selected_rows, 1)
     value_rows = gather_segments(parts[2], selected_rows, 1)
@@ -111,12 +113,10 @@
         lambda input_operand: layer_norm(input_operand, scale_factors), landed_rows
     )
     normed_half = normed.astype(jnp.bfloat16)
-    packed_rows = jnp.dot(normed_half, input_weight, preferred_element_type=jnp.float32).astype(
-        jnp.bfloat16
-    )
+    packed_heads = project_heads(normed_half, input_weight)
     merged_rows, central_gather = jax.vjp(
         lambda input_operand: cross_account_inner(input_operand, row_presence, block_listing),
-        packed_rows,
+        packed_heads,
     )
     result = jnp.dot(merged_rows, output_weight, preferred_element_type=jnp.float32).astype(
         jnp.bfloat16
@@ -128,9 +128,13 @@
         preferred_element_type=jnp.float32,
     ).astype(jnp.bfloat16)
     back_packed = central_gather(back_mixed)[0]
-    back_normed = lax.dot_general(
-        back_packed, input_weight, (((1,), (1,)), ((), ())), preferred_element_type=jnp.float32
-    )
+    features = normed_half.shape[1]
+    back_normed = jnp.einsum(
+        "pbhqd,fphd->bqf",
+        back_packed,
+        input_weight.reshape(features, 3, HEADS, HEAD_DIM),
+        preferred_element_type=jnp.float32,
+    ).reshape(normed_half.shape)
     back_rows = norm_pull(back_normed)[0]
     return (result, back_rows, normed_half, back_packed, merged_rows)
 
@@ -228,7 +232,12 @@
     factor = (replicas * owners * local_rows) ** (-0.5)
     partial_sum = jnp.concatenate(
         [
-            contract(feature_order(normed_half, replicas, owners), back_packed),
+            jnp.einsum(
+                "bqf,pbhqd->fphd",
+                feature_order(normed_half, replicas, owners).reshape(back_packed.shape[1], -1, features),
+                back_packed,
+                preferred_element_type=jnp.float32,
+            ).reshape(features, -1),
             contract(feature_order(merged_rows, replicas, owners), landed_cotangent),
         ],
         axis=1,

time: 168 us -> 186 us (1.11)
  other arithmetic: 23.1 us -> 34 us
  local copies, waits for them, and re-layouts: 31.4 us -> 42.1 us
  waiting for transfers between devices: 39.5 us -> 28.8 us
  matrix products: 24.8 us -> 31.7 us
    all_to_all x1, waiting for transfers between devices: 6.96 us -> 0.01 us  [on_device(): lax.all_to_all(outgoing, 'ev', split_axis=0, concat_axis=0, tiled=True)]
    dot_general x0 -> x4, local copies, waits for them, and re-layouts: none -> 5.9 us  [the longest x2 4.86 us: owner_transfer(): jnp.einsum('pbhqd,fphd->bqf', back_packed, input_weight.reshape(features,...]
    select_n x6, local copies, waits for them, and re-layouts: 0.58 us -> 6.05 us  [pick_block(): picked = jnp.where(chosen == index, blocks[index], picked)]
    unnamed x88 -> x94, local copies, waits for them, and re-layouts: 3.35 us -> 8.77 us
    reshape x2 -> x0, local copies, waits for them, and re-layouts: 3.8 us -> none  [heads_first(): packed_rows.reshape(block_groups, EVENTS_PER_BLOCK, 3, HEADS, HEAD_DIM)]
    all_to_all x1, starting transfers between devices: 9.43 us -> 5.96 us  [reduce_weight_terms(): terms = lax.all_to_all(terms, 'ev', 0, 0, tiled=True)]
    all_to_all x1, waiting for transfers between devices: 19.4 us -> 16.4 us  [reduce_weight_terms(): terms = lax.all_to_all(terms, 'dp', 0, 0, tiled=True)]
    reshape x2 -> x1, local copies, waits for them, and re-layouts: 3.53 us -> 0.8 us  [feature_order(): return jnp.swapaxes(split, 1, 2).reshape(rows, features)]
  transfers between devices with their start and end apart: 5 -> 5, of which waited for: 4 -> 4; matrix products, arithmetic and copies ran while one was open for 17% -> 23% of each run, Pallas kernels for 0% -> 0%
where the time goes in v7:
time: 186 us; the launch traced here: 185 us
  starting transfers between devices  42.5 us (23%)
  local copies, waits for them, and re-layouts  42.1 us (23%)
  other arithmetic  34 us (18%)
  matrix products  31.7 us (17%)
  waiting for transfers between devices  28.8 us (15%)
  between operations  5.44 us (3%)
    all_to_all x1, waiting for transfers between devices, reduce_weight_terms(): terms = lax.all_to_all(terms, 'dp', 0, 0, tiled=True)  16.4 us
    all_to_all x1, starting transfers between devices, on_device(): lax.all_to_all(outgoing, 'ev', split_axis=0, concat_axis=0, tiled=True)  12.2 us
    all_to_all x1, starting transfers between devices, on_device(): lax.all_to_all(going_back, 'ev', split_axis=0, concat_axis=0, tiled=True)  9.05 us
    unnamed x94, local copies, waits for them, and re-layouts  8.77 us
    all_to_all x1, starting transfers between devices, reduce_weight_terms(): terms = lax.all_to_all(terms, 'dp', 0, 0, tiled=True)  8.33 us
    all_to_all x1, waiting for transfers between devices, reduce_weight_terms(): terms = lax.all_to_all(terms, 'ev', 0, 0, tiled=True)  7.7 us
    all_to_all x1, starting transfers between devices, reduce_weight_terms(): gathered = lax.all_to_all(copies, 'dp', 0, 0, tiled=True)  6.94 us
    dot_general x3, matrix products, cross_account_inner(): jnp.einsum('bhqd,bhkd->bhqk', queries, key_rows) * HEAD_DIM ** (-0.5)  6.25 us
  transfers between devices with their start and end apart: 5, of which 4 were waited for; matrix products, arithmetic and copies ran while one was open for 23% of the time, Pallas kernels for 0%

profile of v7, /device:TPU:1, one launch (start us, length us, event | category | flops | bytes accessed | tf_op | source)
XLA Modules:
  0.0 184.5 jit_solution(3501442835916975685)
XLA Ops:
  3.3 2.3 %fusion.87 = f32[128,1536]{0,1:S(1)} fusion(bf16[512,1536]{1,0:T(8,128)(2,1)} %param.13, bf16[1,128,512]{2,1,0:T(8,128)(2,1)} %param.10, f32[512]{0:T(512)} %param.12, f32[128]{0:T(128)S(1)} %fusion.98, f32[128]{0:T(128)S(1)} %broadcast_multiply_fusion.2), kind=kOutput, calls=%fused_computation.185 | convolution fusion | flops 201654272 | bytes 2493440
  6.2 1.4 convert_reduce_fusion.3
  10.0 1.6 reduce_window_sum.11
  13.3 1.2 fusion.33
  15.1 2.0 %fusion.25 = bf16[32,8,1024]{2,1,0:T(8,128)(2,1)} fusion(bf16[128,512]{1,0:T(8,128)(2,1)} %bitcast.374, bf16[128,512]{1,0:T(8,128)(2,1)S(1)} %fusion.33, s32[128]{0:T(128)S(1)} %fusion.97), kind=kOutput, calls=%fused_computation.40 | convolution fusion | flops 67928064 | bytes 786944 | tf_op jit(solution)/shard_map/dot_general | solution.py:207
  17.1 12.2 %all-to-all-start = ((bf16[32,8,1024]{2,1,0:T(8,128)(2,1)}), bf16[32,8,1024]{2,1,0:T(8,128)(2,1)S(1)}, u32[]{:S(2)}, u32[]{:S(2)}) async-start(bf16[32,8,1024]{2,1,0:T(8,128)(2,1)} %fusion.25), calls=%async_computation | async-start | bytes 1048576 | tf_op jit(solution)/shard_map/all_to_all | solution.py:208
  29.3 1.6 copy.182
  30.9 1.7 copy.184
  37.7 1.9 %convert_reduce_fusion.4 = s32[32,32]{1,0:T(8,128)} fusion(s32[32,128]{1,0:T(8,128)} %bitcast.385), kind=kLoop, calls=%fused_computation.92 | loop fusion | flops 392192 | bytes 20480 | tf_op jit(solution)/shard_map/reduce_sum | solution.py:196
  42.0 1.3 select_n.304
  43.3 1.3 select_n.301
  46.6 1.3 select_n.295
  56.4 1.6 copy-done.1
  58.0 1.2 fusion.7
  60.9 1.8 copy.196
  62.7 1.7 reshape.363
  64.4 1.1 maximum_bitcast_fusion.3
  65.5 1.1 maximum_bitcast_fusion.2
  66.6 3.6 %fusion.4 = (f32[2,8,128]{2,1,0:T(8,128)S(1)}, bf16[2,8,128,384]{3,2,1,0:T(8,128)(2,1)S(1)}) fusion(f32[2,8,128,384]{3,2,1,0:T(8,128)} %copy-done.1, f32[2,8,128]{2,1,0:T(8,128)} %multiply_divide_fusion, f32[2,8,128]{2,1,0:T(8,128)} %copy-done.27, pred[2,128,384]{2,1,0:T(8,128)(4,1)} %broadcast_or_fusion, ...), kind=kOutput, calls=%fused_computation.7 | convolution fusion | flops 105773056 | bytes 5890048 | tf_op jit(solution)/shard_map/transpose(jvp(bhqk,bhkd->bhqd))/dot_general | solution.py:99
  70.3 3.0 %divide_convert_fusion = (bf16[2,8,128,384]{3,2,1,0:T(8,128)(2,1)S(1)}, f32[2,8,128]{2,1,0:T(8,128)S(1)}, f32[2,8,128]{2,1,0:T(8,128)S(1)}, pred[2,8,128,384]{3,2,1,0:T(32,128)(4,1)S(1)}) fusion(f32[2,8,128,384]{3,2,1,0:T(8,128)S(1)} %copy-done.2, f32[2,8,128]{2,1,0:T(8,128)S(1)} %fusion.7, f32[2,8,128]{2,1,0:T(8,128)S(1)} %copy-done.28, ...), kind=kLoop, calls=%fused_computation.10 | loop fusion | flops 10219520 | bytes 7217152 | tf_op jit(solution)/shard_map/jvp()/convert_element_type | solution.py:98
  73.4 2.0 %fusion.26 = f32[1,2,8,128,64]{3,4,2,1,0:T(8,128)S(1)} fusion(bf16[1,8,384,64]{2,3,1,0:T(8,128)(2,1)S(1)} %copy-done.23, bf16[1,8,384,64]{2,3,1,0:T(8,128)(2,1)S(1)} %copy-done.25, pred[2,8,128,384]{3,2,1,0:T(32,128)(4,1)S(1)} %get-tuple-element.15, f32[2,8,128]{2,1,0:T(8,128)S(1)} %negate_divide_fusion, pred[2,128,384]{2,1,0:T(8,128)(4,1)S(1)} %copy-done.21, ...), kind=kOutput, calls=%fused_computation.41 | convolution fusion | flops 108920832 | bytes 6946816 | tf_op jit(solution)/shard_map/transpose(jvp(bhqd,bhkd->bhqk))/dot_general | solution.py:94
  75.4 3.4 %fusion.9 = f32[2,8,384,64]{2,3,1,0:T(8,128)S(1)} fusion(pred[2,8,128,384]{3,2,1,0:T(32,128)(4,1)S(1)} %get-tuple-element.15, f32[2,8,128]{2,1,0:T(8,128)S(1)} %negate_divide_fusion, pred[2,128,384]{2,1,0:T(8,128)(4,1)S(1)} %copy-done.21, bf16[3,2,8,128,64]{3,4,2,0,1:T(8,128)(2,1)} %copy-done.6, bf16[2,8,128,384]{3,2,1,0:T(8,128)(2,1)S(1)} %get-tuple-element.75, ...), kind=kOutput, calls=%fused_computation.18 | convolution fusion | flops 108527616 | bytes 7471104 | tf_op jit(solution)/shard_map/transpose(jvp(bhqd,bhkd->bhqk))/dot_general | solution.py:94
  79.2 1.5 fusion.32
  82.4 1.1 fusion.115
  83.5 1.7 copy.199
  85.2 3.1 %dot_general.105 = bf16[256,64,8,3]{0,2,3,1:T(8,128)(2,1)} reshape(bf16[2,128,64,8,3]{1,0,3,4,2:T(2,128)(2,1)} %copy.199) | data formatting | bytes 1572864 | tf_op jit(solution)/shard_map/pbhqd,fphd->bqf/dot_general | solution.py:132
  88.4 2.4 %fusion.44 = (f32[256]{0:T(256)S(1)}, f32[256,512]{1,0:T(8,128)S(1)}) fusion(f32[256]{0:T(256)S(1)} %copy-done.30, bf16[256,1024]{1,0:T(8,128)(2,1)S(1)} %bitcast.363, f32[512]{0:T(512)} %param.15, bf16[256,64,8,3]{0,2,3,1:T(8,128)(2,1)} %dot_general.105, bf16[512,3,8,64]{0,3,2,1:T(8,128)(2,1)S(1)} %bitcast.368), kind=kOutput, calls=%fused_computation.80 | convolution fusion | flops 403308288 | bytes 3149824 | tf_op jit(solution)/shard_map/pbhqd,fphd->bqf/dot_general | solution.py:132
  93.2 9.1 %all-to-all-start.1 = ((bf16[32,8,1024]{2,1,0:T(8,128)(2,1)}), bf16[32,8,1024]{2,1,0:T(8,128)(2,1)S(1)}, u32[]{:S(2)}, u32[]{:S(2)}) async-start(bf16[32,8,1024]{2,1,0:T(8,128)(2,1)} %maximum_bitcast_fusion.4), calls=%async_computation.1 | async-start | bytes 1048576 | tf_op jit(solution)/shard_map/all_to_all | solution.py:225
  102.2 1.8 reshape.368
  104.9 1.1 copy.210
  108.8 1.8 reshape_reshape.4
  111.7 1.2 convolution_convert_fusion.2
  113.6 1.6 pad_maximum_fusion
  117.0 8.3 %all-to-all-start.2 = ((bf16[8,64,2048]{2,1,0:T(8,128)(2,1)}), bf16[8,64,2048]{2,1,0:T(8,128)(2,1)S(1)}, u32[]{:S(2)}, u32[]{:S(2)}) async-start(bf16[8,64,2048]{2,1,0:T(8,128)(2,1)} %pad_maximum_fusion), calls=%async_computation.2 | async-start | bytes 4194304 | tf_op jit(solution)/shard_map/all_to_all | solution.py:160
  125.3 1.3 fusion.45
  127.5 2.1 %convolution_convert_fusion.8 = bf16[128,512]{1,0:T(8,128)(2,1)} fusion(bf16[512,512]{1,0:T(8,128)(2,1)} %param.14, f32[128,1024]{1,0:T(8,128)S(1)} %fusion.45, bf16[1,128,512]{2,1,0:T(8,128)(2,1)} %param.11), kind=kOutput, calls=%fused_computation.57 | convolution fusion | flops 67371008 | bytes 1048576 | tf_op jit(solution)/shard_map/transpose(jvp())/dot_general | solution.py:51
  129.5 1.7 copy.201
  131.2 1.4 multiply_reduce_fusion
  132.6 1.2 convolution_bitcast_fusion.3
  135.1 16.4 %all-to-all-done.2 = bf16[8,64,2048]{2,1,0:T(8,128)(2,1)S(1)} async-done(((bf16[8,64,2048]{2,1,0:T(8,128)(2,1)}), bf16[8,64,2048]{2,1,0:T(8,128)(2,1)S(1)}, u32[]{:S(2)}, u32[]{:S(2)}) %all-to-all-start.2) | async-done | bytes 2097184 | tf_op jit(solution)/shard_map/all_to_all | solution.py:160
  151.5 1.1 reduce_sum.236
  152.6 1.8 reshape.370
  154.5 6.0 %all-to-all-start.3 = ((bf16[32,2,2048]{2,1,0:T(2,128)(2,1)}), bf16[32,2,2048]{2,1,0:T(2,128)(2,1)S(1)}, u32[]{:S(2)}, u32[]{:S(2)}) async-start(bf16[32,2,2048]{2,1,0:T(2,128)(2,1)} %reshape.370), calls=%async_computation.3 | async-start | bytes 524288 | tf_op jit(solution)/shard_map/all_to_all | solution.py:163
  160.7 1.7 fusion.84
  162.4 7.7 %all-to-all-done.3 = bf16[32,2,2048]{2,1,0:T(2,128)(2,1)S(1)} async-done(((bf16[32,2,2048]{2,1,0:T(2,128)(2,1)}), bf16[32,2,2048]{2,1,0:T(2,128)(2,1)S(1)}, u32[]{:S(2)}, u32[]{:S(2)}) %all-to-all-start.3) | async-done | bytes 262176 | tf_op jit(solution)/shard_map/all_to_all | solution.py:163
  170.9 6.9 %all-to-all-start.4 = ((f32[8,2,2048]{2,1,0:T(2,128)}), f32[8,2,2048]{2,1,0:T(2,128)S(1)}, u32[]{:S(2)}, u32[]{:S(2)}) async-start(f32[8,2,2048]{2,1,0:T(2,128)} %broadcast_in_dim.236), calls=%async_computation.4 | async-start | bytes 262144 | tf_op jit(solution)/shard_map/all_to_all | solution.py:166
  177.8 1.6 fusion.85
  179.4 3.7 %all-to-all-done.4 = f32[8,2,2048]{2,1,0:T(2,128)S(1)} async-done(((f32[8,2,2048]{2,1,0:T(2,128)}), f32[8,2,2048]{2,1,0:T(2,128)S(1)}, u32[]{:S(2)}, u32[]{:S(2)}) %all-to-all-start.4) | async-done | bytes 131104 | tf_op jit(solution)/shard_map/all_to_all | solution.py:166
  (174 shorter events, 39.1 us)
Async XLA Ops:
  0.6 59.2 %copy-start = (bf16[512,512]{1,0:T(8,128)(2,1)S(1)}, bf16[512,512]{1,0:T(8,128)(2,1)}, u32[]{:S(2)}) copy-start(bf16[512,512]{1,0:T(8,128)(2,1)} %param.17) | copy-start | bytes 1572868
  1.7 4.0 %copy-start.32 = (f32[128]{0:T(128)}, f32[128]{0:T(128)S(1)}, u32[]{:S(2)}) copy-start(f32[128]{0:T(128)S(1)} %broadcast_multiply_fusion.2) | copy-start | bytes 1540
  3.3 2.4 %copy-start.41 = (f32[128]{0:T(128)}, f32[128]{0:T(128)S(1)}, u32[]{:S(2)}) copy-start(f32[128]{0:T(128)S(1)} %fusion.98) | copy-start | bytes 1540
  3.3 9.9 %copy-start.3 = (bf16[1,128,512]{2,1,0:T(8,128)(2,1)S(1)}, bf16[1,128,512]{2,1,0:T(8,128)(2,1)}, u32[]{:S(2)}) copy-start(bf16[1,128,512]{2,1,0:T(8,128)(2,1)} %param.10) | copy-start | bytes 393220
  3.3 9.9 %copy-start.14 = (bf16[512,512]{1,0:T(8,128)(2,1)S(1)}, bf16[512,512]{1,0:T(8,128)(2,1)}, u32[]{:S(2)}) copy-start(bf16[512,512]{1,0:T(8,128)(2,1)} %param.14) | copy-start | bytes 1572868
  5.8 1.8 copy-start.7
  5.8 23.5 %copy-start.5 = (bf16[512,1536]{1,0:T(8,128)(2,1)S(1)}, bf16[512,1536]{1,0:T(8,128)(2,1)}, u32[]{:S(2)}) copy-start(bf16[512,1536]{1,0:T(8,128)(2,1)} %param.13) | copy-start | bytes 4718596
  13.2 19.4 %copy-start.40 = (s32[128]{0:T(128)}, s32[128]{0:T(128)S(1)}, u32[]{:S(2)}) copy-start(s32[128]{0:T(128)S(1)} %fusion.97) | copy-start | bytes 1540
  17.1 33.5 %all-to-all-start = ((bf16[32,8,1024]{2,1,0:T(8,128)(2,1)}), bf16[32,8,1024]{2,1,0:T(8,128)(2,1)S(1)}, u32[]{:S(2)}, u32[]{:S(2)}) async-start(bf16[32,8,1024]{2,1,0:T(8,128)(2,1)} %fusion.25), calls=%async_computation | async-start | bytes 1048576 | tf_op jit(solution)/shard_map/all_to_all | solution.py:208
  29.3 3.3 %copy-start.43 = (s32[1,1,2,2]{3,2,1,0:T(2,128)S(1)}, s32[1,1,2,2]{3,2,1,0:T(2,128)}, u32[]{:S(2)}) copy-start(s32[1,1,2,2]{3,2,1,0:T(2,128)} %param.19) | copy-start | bytes 52
  50.7 4.6 %copy-start.29 = (f32[256]{0:T(256)}, f32[256]{0:T(256)S(1)}, u32[]{:S(2)}) copy-start(f32[256]{0:T(256)S(1)} %broadcast_multiply_fusion.1) | copy-start | bytes 3076
  51.6 3.9 %copy-start.35 = (f32[256]{0:T(256)}, f32[256]{0:T(256)S(1)}, u32[]{:S(2)}) copy-start(f32[256]{0:T(256)S(1)} %fusion.96) | copy-start | bytes 3076
  52.4 3.0 %copy-start.12 = (bf16[256,512]{1,0:T(8,128)(2,1)}, bf16[256,512]{1,0:T(8,128)(2,1)S(1)}, u32[]{:S(2)}) copy-start(bf16[256,512]{1,0:T(8,128)(2,1)S(1)} %fusion.43) | copy-start | bytes 786436
  52.4 3.1 %copy-start.20 = (pred[2,128,384]{2,1,0:T(8,128)(4,1)S(1)}, pred[2,128,384]{2,1,0:T(8,128)(4,1)}, u32[]{:S(2)}) copy-start(pred[2,128,384]{2,1,0:T(8,128)(4,1)} %broadcast_or_fusion) | copy-start | bytes 294916
  53.0 3.3 %copy-start.6 = (bf16[3,2,8,128,64]{3,4,2,0,1:T(8,128)(2,1)}, bf16[3,2,8,128,64]{3,4,2,0,1:T(8,128)(2,1)S(1)}, u32[]{:S(2)}) copy-start(bf16[3,2,8,128,64]{3,4,2,0,1:T(8,128)(2,1)S(1)} %fusion.20) | copy-start | bytes 2359300
  55.4 1.0 copy-start.22
  55.5 0.9 copy-start.24
  56.4 1.6 copy-start.1
  56.4 2.9 %copy-start.27 = (f32[2,8,128]{2,1,0:T(8,128)}, f32[2,8,128]{2,1,0:T(8,128)S(1)}, u32[]{:S(2)}) copy-start(f32[2,8,128]{2,1,0:T(8,128)S(1)} %get-tuple-element.72) | copy-start | bytes 24580
  66.6 3.7 %copy-start.2 = (f32[2,8,128,384]{3,2,1,0:T(8,128)S(1)}, f32[2,8,128,384]{3,2,1,0:T(8,128)}, u32[]{:S(2)}) copy-start(f32[2,8,128,384]{3,2,1,0:T(8,128)} %copy-done.1) | copy-start | bytes 9437188
  66.6 3.7 %copy-start.21 = (pred[2,128,384]{2,1,0:T(8,128)(4,1)S(1)}, pred[2,128,384]{2,1,0:T(8,128)(4,1)}, u32[]{:S(2)}) copy-start(pred[2,128,384]{2,1,0:T(8,128)(4,1)} %broadcast_or_fusion) | copy-start | bytes 294916
  66.6 3.6 %copy-start.28 = (f32[2,8,128]{2,1,0:T(8,128)S(1)}, f32[2,8,128]{2,1,0:T(8,128)}, u32[]{:S(2)}) copy-start(f32[2,8,128]{2,1,0:T(8,128)} %copy-done.27) | copy-start | bytes 24580
  70.3 3.1 %copy-start.23 = (bf16[1,8,384,64]{2,3,1,0:T(8,128)(2,1)S(1)}, bf16[1,8,384,64]{2,3,1,0:T(8,128)(2,1)}, u32[]{:S(2)}) copy-start(bf16[1,8,384,64]{2,3,1,0:T(8,128)(2,1)} %copy-done.22) | copy-start | bytes 1179652
  70.3 3.1 %copy-start.25 = (bf16[1,8,384,64]{2,3,1,0:T(8,128)(2,1)S(1)}, bf16[1,8,384,64]{2,3,1,0:T(8,128)(2,1)}, u32[]{:S(2)}) copy-start(bf16[1,8,384,64]{2,3,1,0:T(8,128)(2,1)} %copy-done.24) | copy-start | bytes 1179652
  75.4 3.4 %copy-start.19 = (bf16[2,128,8,64]{1,0,3,2:T(2,128)(2,1)S(1)}, bf16[2,128,8,64]{1,0,3,2:T(2,128)(2,1)}, u32[]{:S(2)}) copy-start(bf16[2,128,8,64]{1,0,3,2:T(2,128)(2,1)} %reshape.363) | copy-start | bytes 786436
  82.4 6.0 %copy-start.30 = (f32[256]{0:T(256)S(1)}, f32[256]{0:T(256)}, u32[]{:S(2)}) copy-start(f32[256]{0:T(256)} %copy-done.29) | copy-start | bytes 3076
  88.4 2.5 %copy-start.38 = (f32[256]{0:T(256)S(1)}, f32[256]{0:T(256)}, u32[]{:S(2)}) copy-start(f32[256]{0:T(256)} %copy-done.37) | copy-start | bytes 3076
  88.4 2.5 %copy-start.36 = (f32[256]{0:T(256)S(1)}, f32[256]{0:T(256)}, u32[]{:S(2)}) copy-start(f32[256]{0:T(256)} %copy-done.35) | copy-start | bytes 3076
  88.4 2.8 %copy-start.26 = (bf16[2,128,8,64]{1,3,2,0:T(8,128)(2,1)S(1)}, bf16[2,128,8,64]{1,3,2,0:T(8,128)(2,1)}, u32[]{:S(2)}) copy-start(bf16[2,128,8,64]{1,3,2,0:T(8,128)(2,1)} %fusion.32) | copy-start | bytes 786436
  90.9 13.2 %copy-start.13 = (bf16[256,512]{1,0:T(8,128)(2,1)S(1)}, bf16[256,512]{1,0:T(8,128)(2,1)}, u32[]{:S(2)}) copy-start(bf16[256,512]{1,0:T(8,128)(2,1)} %copy-done.12) | copy-start | bytes 786436
  91.5 0.7 copy-start.18
  92.3 19.4 %copy-start.11 = (bf16[3,8,64,2,128]{4,2,1,3,0:T(8,128)(2,1)S(1)}, bf16[3,8,64,2,128]{4,2,1,3,0:T(8,128)(2,1)}, u32[]{:S(2)}) copy-start(bf16[3,8,64,2,128]{4,2,1,3,0:T(8,128)(2,1)} %get-tuple-element.16) | copy-start | bytes 2359300
  93.2 23.0 %all-to-all-start.1 = ((bf16[32,8,1024]{2,1,0:T(8,128)(2,1)}), bf16[32,8,1024]{2,1,0:T(8,128)(2,1)S(1)}, u32[]{:S(2)}, u32[]{:S(2)}) async-start(bf16[32,8,1024]{2,1,0:T(8,128)(2,1)} %maximum_bitcast_fusion.4), calls=%async_computation.1 | async-start | bytes 1048576 | tf_op jit(solution)/shard_map/all_to_all | solution.py:225
  116.2 0.8 copy-start.15
  117.0 34.5 %all-to-all-start.2 = ((bf16[8,64,2048]{2,1,0:T(8,128)(2,1)}), bf16[8,64,2048]{2,1,0:T(8,128)(2,1)S(1)}, u32[]{:S(2)}, u32[]{:S(2)}) async-start(bf16[8,64,2048]{2,1,0:T(8,128)(2,1)} %pad_maximum_fusion), calls=%async_computation.2 | async-start | bytes 4194304 | tf_op jit(solution)/shard_map/all_to_all | solution.py:160
  125.3 8.6 %copy-start.31 = (f32[8,128]{1,0:T(8,128)S(1)}, f32[8,128]{1,0:T(8,128)}, u32[]{:S(2)}) copy-start(f32[8,128]{1,0:T(8,128)} %get-tuple-element.6) | copy-start | bytes 12292
  126.7 0.8 copy-start.9
  131.2 2.8 %copy-start.8 = (bf16[3,1,8,128,64]{3,4,2,0,1:T(8,128)(2,1)S(1)}, bf16[3,1,8,128,64]{3,4,2,0,1:T(8,128)(2,1)}, u32[]{:S(2)}) copy-start(bf16[3,1,8,128,64]{3,4,2,0,1:T(8,128)(2,1)} %copy-done.7) | copy-start | bytes 1179652
  131.2 2.8 %copy-start.17 = (pred[8,128,128]{1,2,0:T(32,128)(4,1)S(1)}, pred[8,128,128]{1,2,0:T(32,128)(4,1)}, u32[]{:S(2)}) copy-start(pred[8,128,128]{1,2,0:T(32,128)(4,1)} %get-tuple-element.7) | copy-start | bytes 393220
  131.2 3.3 %copy-start.4 = (bf16[512,1536]{0,1:T(8,128)(2,1)S(1)}, bf16[512,1536]{0,1:T(8,128)(2,1)}, u32[]{:S(2)}) copy-start(bf16[512,1536]{0,1:T(8,128)(2,1)} %copy.182) | copy-start | bytes 4718596
  131.2 3.3 %copy-start.33 = (f32[128]{0:T(128)S(1)}, f32[128]{0:T(128)}, u32[]{:S(2)}) copy-start(f32[128]{0:T(128)} %copy-done.32) | copy-start | bytes 1540
  131.2 3.4 %copy-start.39 = (f32[512]{0:T(512)S(1)}, f32[512]{0:T(512)}, u32[]{:S(2)}) copy-start(f32[512]{0:T(512)} %param.12) | copy-start | bytes 6148
  133.8 1.3 copy-start.45
  134.5 25.9 %copy-start.34 = (f32[128]{0:T(128)S(1)}, f32[128]{0:T(128)}, u32[]{:S(2)}) copy-start(f32[128]{0:T(128)} %copy-done.32) | copy-start | bytes 1540
  134.5 25.9 %copy-start.42 = (f32[128]{0:T(128)S(1)}, f32[128]{0:T(128)}, u32[]{:S(2)}) copy-start(f32[128]{0:T(128)} %copy-done.41) | copy-start | bytes 1540
  134.6 26.1 %copy-start.10 = (f32[128,1024]{1,0:T(8,128)S(1)}, f32[128,1024]{1,0:T(8,128)}, u32[]{:S(2)}) copy-start(f32[128,1024]{1,0:T(8,128)} %copy-done.9) | copy-start | bytes 1572868
  154.5 15.6 %all-to-all-start.3 = ((bf16[32,2,2048]{2,1,0:T(2,128)(2,1)}), bf16[32,2,2048]{2,1,0:T(2,128)(2,1)S(1)}, u32[]{:S(2)}, u32[]{:S(2)}) async-start(bf16[32,2,2048]{2,1,0:T(2,128)(2,1)} %reshape.370), calls=%async_computation.3 | async-start | bytes 524288 | tf_op jit(solution)/shard_map/all_to_all | solution.py:163
  170.9 12.2 %all-to-all-start.4 = ((f32[8,2,2048]{2,1,0:T(2,128)}), f32[8,2,2048]{2,1,0:T(2,128)S(1)}, u32[]{:S(2)}, u32[]{:S(2)}) async-start(f32[8,2,2048]{2,1,0:T(2,128)} %broadcast_in_dim.236), calls=%async_computation.4 | async-start | bytes 262144 | tf_op jit(solution)/shard_map/all_to_all | solution.py:166
  (3 other events, 1.7 us)

commit v8 on v6

--- a/solution.py
+++ b/solution.py
@@ -71,16 +71,22 @@
     )
 
 
+def head_mask(features):
+    lanes = jnp.arange(features, dtype=jnp.int32) // HEAD_DIM
+    return (lanes[None, :] == jnp.arange(HEADS, dtype=jnp.int32)[:, None]).astype(jnp.float32)
+
+
 def cross_account_inner(packed_rows, row_presence, block_listing):
     row_total, three_wide = packed_rows.shape
+    features = three_wide // 3
     block_groups = row_total // EVENTS_PER_BLOCK
     selected_rows = jnp.concatenate(
         [jnp.arange(block_groups, dtype=jnp.int32)[:, None], block_listing], axis=1
     )
-    parts = heads_first(packed_rows, block_groups)
-    queries = parts[0]
-    key_rows = gather_segments(parts[1], selected_rows, 1)
-    value_rows = gather_segments(parts[2], selected_rows, 1)
+    by_block = packed_rows.astype(jnp.float32).reshape(block_groups, EVENTS_PER_BLOCK, three_wide)
+    queries = by_block[:, :, :features]
+    key_rows = gather_segments(by_block[:, :, features : 2 * features], selected_rows, 0)
+    value_rows = gather_segments(by_block[:, :, 2 * features :], selected_rows, 0)
     presence_blocks = row_presence.reshape(block_groups, EVENTS_PER_BLOCK)
     key_present = gather_segments(presence_blocks, selected_rows, 0)
     key_total = key_present.shape[1]
@@ -89,13 +95,16 @@
         == jnp.arange(EVENTS_PER_BLOCK, dtype=jnp.int32)[:, None]
     )
     allowed = key_present[:, None, None, :] | itself[None, None, :, :]
-    scores = jnp.einsum("bhqd,bhkd->bhqk", queries, key_rows) * HEAD_DIM ** (-0.5)
+    mask = head_mask(features)
+    masked_queries = queries[:, None, :, :] * mask[None, :, None, :]
+    scores = jnp.einsum("bhqf,bkf->bhqk", masked_queries, key_rows) * HEAD_DIM ** (-0.5)
     scores = jnp.where(allowed, scores, -1e30)
     highest = jnp.max(scores, axis=-1, keepdims=True)
     weights = jnp.where(allowed, jnp.exp(scores - highest), 0.0)
     attention = (weights / jnp.sum(weights, axis=-1, keepdims=True)).astype(jnp.bfloat16)
-    merged_rows = jnp.einsum("bhqk,bhkd->bhqd", attention.astype(jnp.float32), value_rows)
-    return rows_first(merged_rows, row_total)
+    per_head = jnp.einsum("bhqk,bkf->bhqf", attention.astype(jnp.float32), value_rows)
+    merged_rows = jnp.sum(per_head * mask[None, :, None, :], axis=1)
+    return merged_rows.astype(jnp.bfloat16).reshape(row_total, features)
 
 
 def owner_transfer(

time: 168 us -> 164 us (0.976)
  waiting for transfers between devices: 39.5 us -> 32.6 us
    all_to_all x1, waiting for transfers between devices: 6.96 us -> 0.01 us  [on_device(): lax.all_to_all(outgoing, 'ev', split_axis=0, concat_axis=0, tiled=True)]
    select_n x6, local copies, waits for them, and re-layouts: 0.58 us -> 7.2 us  [pick_block(): picked = jnp.where(chosen == index, blocks[index], picked)]
    reshape x3 -> x0, local copies, waits for them, and re-layouts: 5.5 us -> none  [the longest x2 3.8 us: heads_first(): packed_rows.reshape(block_groups, EVENTS_PER_BLOCK, 3, HEADS, HEAD_DIM)]
    another operation x5 -> x3, other arithmetic: 2.33 us -> 0.12 us  [gather_segments(): jnp.stack([jnp.concatenate([pick_block(blocks, selected_rows[group, segme...]
    dot_general x6, matrix products: 9.29 us -> 11.4 us  [the longest x3 7.13 us: cross_account_inner(): jnp.einsum('bhqf,bkf->bhqk', masked_queries, key_rows) * HEAD_DIM ** (-0.5)]
    all_to_all x1, starting transfers between devices: 7.39 us -> 9.4 us  [on_device(): lax.all_to_all(going_back, 'ev', split_axis=0, concat_axis=0, tiled=True)]
    reshape x2 -> x1, local copies, waits for them, and re-layouts: 3.58 us -> 1.76 us  [feature_order(): split = left_part.reshape(rows, owners, replicas, per_device)]
    dot_general x1, matrix products: 2.06 us -> 0.33 us  [owner_transfer(): lax.dot_general(landed_cotangent, output_weight, (((1,), (1,)), ((), ()))...]
  transfers between devices with their start and end apart: 5 -> 5, of which waited for: 4 -> 3; matrix products, arithmetic and copies ran while one was open for 17% -> 26% of each run, Pallas kernels for 0% -> 0%
where the time goes in v8:
time: 164 us; the launch traced here: 162 us
  starting transfers between devices  43.6 us (27%)
  waiting for transfers between devices  32.6 us (20%)
  local copies, waits for them, and re-layouts  31.6 us (19%)
  matrix products  25.4 us (15%)
  other arithmetic  23.7 us (14%)
  between operations  5.27 us (3%)
    all_to_all x1, waiting for transfers between devices, reduce_weight_terms(): terms = lax.all_to_all(terms, 'dp', 0, 0, tiled=True)  19.4 us
    all_to_all x1, starting transfers between devices, on_device(): lax.all_to_all(outgoing, 'ev', split_axis=0, concat_axis=0, tiled=True)  12 us
    all_to_all x1, starting transfers between devices, reduce_weight_terms(): terms = lax.all_to_all(terms, 'ev', 0, 0, tiled=True)  9.43 us
    all_to_all x1, starting transfers between devices, on_device(): lax.all_to_all(going_back, 'ev', split_axis=0, concat_axis=0, tiled=True)  9.4 us
    all_to_all x1, waiting for transfers between devices, reduce_weight_terms(): terms = lax.all_to_all(terms, 'ev', 0, 0, tiled=True)  8.59 us
    select_n x6, local copies, waits for them, and re-layouts, pick_block(): picked = jnp.where(chosen == index, blocks[index], picked)  7.2 us
    dot_general x3, matrix products, cross_account_inner(): jnp.einsum('bhqf,bkf->bhqk', masked_queries, key_rows) * HEAD_DIM ** (-0.5)  7.13 us
    all_to_all x1, starting transfers between devices, reduce_weight_terms(): gathered = lax.all_to_all(copies, 'dp', 0, 0, tiled=True)  6.94 us
  transfers between devices with their start and end apart: 5, of which 3 were waited for; matrix products, arithmetic and copies ran while one was open for 26% of the time, Pallas kernels for 0%

profile of v8, /device:TPU:1, one launch (start us, length us, event | category | flops | bytes accessed | tf_op | source)
XLA Modules:
  0.0 162.3 jit_solution(8352764769977515310)
XLA Ops:
  0.7 1.2 convert_reduce_fusion.5
  1.9 1.1 fusion.63
  4.9 1.9 %convolution_convert_fusion.2 = bf16[128,1536]{1,0:T(8,128)(2,1)S(1)} fusion(bf16[512,1536]{1,0:T(8,128)(2,1)} %param.13, bf16[1,128,512]{2,1,0:T(8,128)(2,1)} %param.10, f32[512]{0:T(512)} %param.12, f32[128]{0:T(128)S(1)} %fusion.98, f32[128]{0:T(128)S(1)} %broadcast_multiply_fusion.2), kind=kOutput, calls=%fused_computation.25 | convolution fusion | flops 201850880 | bytes 2100224 | tf_op jit(solution)/shard_map/jvp()/dot_general | solution.py:38
  7.5 0.8 convert_reduce_fusion.3
  9.4 1.1 fusion.42
  10.5 12.0 %all-to-all-start = ((bf16[32,8,1024]{2,1,0:T(8,128)(2,1)}), bf16[32,8,1024]{2,1,0:T(8,128)(2,1)S(1)}, u32[]{:S(2)}, u32[]{:S(2)}) async-start(bf16[32,8,1024]{2,1,0:T(8,128)(2,1)} %fusion.42), calls=%async_computation | async-start | bytes 1048576 | tf_op jit(solution)/shard_map/all_to_all | solution.py:213
  24.4 1.5 fusion.120
  28.4 1.9 %convert_reduce_fusion.4 = s32[32,32]{1,0:T(8,128)} fusion(s32[32,128]{1,0:T(8,128)} %bitcast.241), kind=kLoop, calls=%fused_computation.97 | loop fusion | flops 392192 | bytes 20480 | tf_op jit(solution)/shard_map/reduce_sum | solution.py:201
  30.4 0.9 dynamic-slice_reduce_fusion
  32.0 1.3 select_n.319
  33.2 1.3 select_n.325
  34.6 1.4 select_n.328
  35.9 1.3 select_n.331
  37.2 1.3 select_n.334
  42.3 0.8 fusion.53
  44.8 1.4 fusion.122
  46.2 1.2 fusion.22
  47.4 2.0 %fusion.12 = (f32[2,8,128]{2,1,0:T(8,128)S(1)}, bf16[2,8,128,384]{3,2,1,0:T(8,128)(2,1)S(1)}) fusion(f32[2,8,128,384]{3,2,1,0:T(8,128)S(1)} %get-tuple-element.68, f32[2,8,128]{2,1,0:T(8,128)S(1)} %multiply_divide_fusion, f32[2,8,128]{2,1,0:T(8,128)S(1)} %get-tuple-element.67, pred[2,128,384]{2,1,0:T(8,128)(4,1)S(1)} %copy-done.15, ...), kind=kOutput, calls=%fused_computation.16 | convolution fusion | flops 811464704 | bytes 6168576 | tf_op jit(solution)/shard_map/transpose(jvp(bhqk,bkf->bhqf))/dot_general | solution.py:105
  49.4 3.0 %divide_convert_fusion = (bf16[2,8,128,384]{3,2,1,0:T(8,128)(2,1)S(1)}, f32[2,8,128]{2,1,0:T(8,128)S(1)}, f32[2,8,128]{2,1,0:T(8,128)S(1)}, pred[2,8,128,384]{3,2,1,0:T(32,128)(4,1)S(1)}) fusion(f32[2,8,128,384]{3,2,1,0:T(8,128)S(1)} %get-tuple-element.68, f32[2,8,128]{2,1,0:T(8,128)S(1)} %fusion.22, f32[2,8,128]{2,1,0:T(8,128)S(1)} %get-tuple-element.67, ...), kind=kLoop, calls=%fused_computation.19 | loop fusion | flops 10219520 | bytes 7217152 | tf_op jit(solution)/shard_map/jvp()/convert_element_type | solution.py:104
  52.5 3.0 %multiply_reduce_fusion = f32[2,128,512]{2,1,0:T(8,128)S(1)} fusion(f32[8,512]{1,0:T(8,128)S(1)} %copy-done.16, pred[2,8,128,384]{3,2,1,0:T(32,128)(4,1)S(1)} %get-tuple-element.15, f32[2,8,128]{2,1,0:T(8,128)S(1)} %negate_divide_fusion, pred[2,128,384]{2,1,0:T(8,128)(4,1)S(1)} %copy-done.15, bf16[1,384,512]{2,1,0:T(8,128)(2,1)S(1)} %get-tuple-element.77, ...), kind=kOutput, calls=%fused_computation.8 | convolution fusion | flops 815529984 | bytes 6963200 | tf_op jit(solution)/shard_map/transpose(jvp(bhqf,bkf->bhqk))/dot_general | solution.py:100
  55.5 2.8 %fusion.36 = f32[2,384,512]{2,1,0:T(8,128)S(1)} fusion(f32[8,512]{1,0:T(8,128)S(1)} %copy-done.16, f32[2,128,512]{2,1,0:T(8,128)S(1)} %slice.168, pred[2,8,128,384]{3,2,1,0:T(32,128)(4,1)S(1)} %get-tuple-element.15, f32[2,8,128]{2,1,0:T(8,128)S(1)} %negate_divide_fusion, pred[2,128,384]{2,1,0:T(8,128)(4,1)S(1)} %copy-done.15, ...), kind=kOutput, calls=%fused_computation.49 | convolution fusion | flops 814219264 | bytes 7749632 | tf_op jit(solution)/shard_map/transpose(jvp(bhqf,bkf->bhqk))/dot_general | solution.py:100
  58.2 1.3 multiply_reduce_fusion.1
  59.5 1.1 fusion.39
  62.4 0.9 copy-done.5
  64.4 0.9 maximum_bitcast_fusion.10
  65.2 9.4 %all-to-all-start.1 = ((bf16[32,8,1024]{2,1,0:T(8,128)(2,1)}), bf16[32,8,1024]{2,1,0:T(8,128)(2,1)}, u32[]{:S(2)}, u32[]{:S(2)}) async-start(bf16[32,8,1024]{2,1,0:T(8,128)(2,1)} %maximum_bitcast_fusion.10), calls=%async_computation.1 | async-start | bytes 1048576 | tf_op jit(solution)/shard_map/all_to_all | solution.py:230
  74.7 1.8 %copy.108 = bf16[256,512]{0,1:T(8,128)(2,1)} copy(bf16[256,512]{1,0:T(8,128)(2,1)} %copy-done.6) | data formatting | bytes 524288 | tf_op jit(solution)/shard_map/convert_element_type | solution.py:122
  76.5 1.8 %copy.110 = bf16[2,128,512]{1,0,2:T(2,128)(2,1)} copy(bf16[2,128,512]{2,1,0:T(8,128)(2,1)} %copy-done.14) | data formatting | bytes 524288 | tf_op jit(solution)/shard_map/jvp()/convert_element_type | solution.py:107
  78.3 1.8 %reshape.377 = bf16[256,32,8,2]{0,3,2,1:T(2,128)(2,1)} reshape(bf16[256,512]{0,1:T(8,128)(2,1)} %copy.108) | data formatting | bytes 524288 | tf_op jit(solution)/shard_map/reshape | solution.py:156
  80.1 1.8 %copy.109 = bf16[256,8,32,2]{0,3,2,1:T(2,128)(2,1)} copy(bf16[256,8,32,2]{0,3,1,2:T(2,128)(2,1)} %bitcast.235) | data formatting | bytes 524288 | tf_op jit(solution)/shard_map/transpose | solution.py:157
  81.9 1.8 %reshape.378 = bf16[256,512]{0,1:T(8,128)(2,1)} reshape(bf16[256,8,32,2]{0,3,2,1:T(2,128)(2,1)} %copy.109) | data formatting | bytes 524288 | tf_op jit(solution)/shard_map/reshape | solution.py:157
  83.7 1.8 %convert_element_type.201 = bf16[256,32,8,2]{0,3,2,1:T(2,128)(2,1)} reshape(bf16[2,128,512]{1,0,2:T(2,128)(2,1)} %copy.110) | data formatting | bytes 524288 | tf_op jit(solution)/shard_map/jvp()/convert_element_type | solution.py:107
  85.5 1.8 %copy.111 = bf16[256,8,32,2]{0,3,2,1:T(2,128)(2,1)} copy(bf16[256,8,32,2]{0,3,1,2:T(2,128)(2,1)} %bitcast.236) | data formatting | bytes 524288 | tf_op jit(solution)/shard_map/transpose | solution.py:157
  87.4 1.8 %reshape.379 = bf16[256,512]{0,1:T(8,128)(2,1)} reshape(bf16[256,8,32,2]{0,3,2,1:T(2,128)(2,1)} %copy.111) | data formatting | bytes 524288 | tf_op jit(solution)/shard_map/reshape | solution.py:157
  89.1 1.2 convolution_convert_fusion.3
  90.4 1.8 %convolution_convert_fusion = bf16[8,64,1536]{2,1,0:T(8,128)(2,1)S(1)} fusion(bf16[8,64,256]{2,1,0:T(8,128)(2,1)} %bitcast.234, bf16[256,1536,1]{1,0,2:T(8,128)(2,1)} %bitcast.229), kind=kOutput, calls=%fused_computation.22 | convolution fusion | flops 403439616 | bytes 2621440 | tf_op jit(solution)/shard_map/dot_general | solution.py:148
  92.2 1.6 pad_maximum_fusion
  93.8 5.8 %all-to-all-start.2 = ((bf16[8,64,2048]{2,1,0:T(8,128)(2,1)}), bf16[8,64,2048]{2,1,0:T(8,128)(2,1)}, u32[]{:S(2)}, u32[]{:S(2)}) async-start(bf16[8,64,2048]{2,1,0:T(8,128)(2,1)} %pad_maximum_fusion), calls=%async_computation.2 | async-start | bytes 4194304 | tf_op jit(solution)/shard_map/all_to_all | solution.py:165
  99.6 1.3 fusion.55
  101.0 2.2 %convolution_convert_fusion.9 = bf16[128,512]{1,0:T(8,128)(2,1)} fusion(bf16[512,512]{1,0:T(8,128)(2,1)} %param.14, f32[128,1024]{1,0:T(8,128)S(1)} %fusion.55, bf16[1,128,512]{2,1,0:T(8,128)(2,1)S(1)} %copy-done.11), kind=kOutput, calls=%fused_computation.66 | convolution fusion | flops 67371008 | bytes 1048576 | tf_op jit(solution)/shard_map/transpose(jvp())/dot_general | solution.py:49
  103.1 1.0 copy.104
  106.5 19.4 %all-to-all-done.2 = bf16[8,64,2048]{2,1,0:T(8,128)(2,1)} async-done(((bf16[8,64,2048]{2,1,0:T(8,128)(2,1)}), bf16[8,64,2048]{2,1,0:T(8,128)(2,1)}, u32[]{:S(2)}, u32[]{:S(2)}) %all-to-all-start.2) | async-done | bytes 2097184 | tf_op jit(solution)/shard_map/all_to_all | solution.py:165
  125.9 2.0 %reduce_sum.260 = bf16[64,2048]{1,0:T(8,128)(2,1)S(1)} reduce(bf16[8,64,2048]{2,1,0:T(8,128)(2,1)} %all-to-all-done.2, bf16[]{:T(256)} %constant.95.clone.1), dimensions={0}, to_apply=%region_23.24 | reduce | flops 917504 | bytes 2359298 | tf_op jit(solution)/shard_map/reduce_sum | solution.py:166
  127.9 0.9 reshape.380
  128.8 9.4 %all-to-all-start.3 = ((bf16[32,2,2048]{2,1,0:T(2,128)(2,1)}), bf16[32,2,2048]{2,1,0:T(2,128)(2,1)S(1)}, u32[]{:S(2)}, u32[]{:S(2)}) async-start(bf16[32,2,2048]{2,1,0:T(2,128)(2,1)} %reshape.380), calls=%async_computation.3 | async-start | bytes 524288 | tf_op jit(solution)/shard_map/all_to_all | solution.py:168
  139.3 8.6 %all-to-all-done.3 = bf16[32,2,2048]{2,1,0:T(2,128)(2,1)S(1)} async-done(((bf16[32,2,2048]{2,1,0:T(2,128)(2,1)}), bf16[32,2,2048]{2,1,0:T(2,128)(2,1)S(1)}, u32[]{:S(2)}, u32[]{:S(2)}) %all-to-all-start.3) | async-done | bytes 262176 | tf_op jit(solution)/shard_map/all_to_all | solution.py:168
  148.7 6.9 %all-to-all-start.4 = ((f32[8,2,2048]{2,1,0:T(2,128)}), f32[8,2,2048]{2,1,0:T(2,128)S(1)}, u32[]{:S(2)}, u32[]{:S(2)}) async-start(f32[8,2,2048]{2,1,0:T(2,128)} %broadcast_in_dim.161), calls=%async_computation.4 | async-start | bytes 262144 | tf_op jit(solution)/shard_map/all_to_all | solution.py:171
  156.3 4.6 %all-to-all-done.4 = f32[8,2,2048]{2,1,0:T(2,128)S(1)} async-done(((f32[8,2,2048]{2,1,0:T(2,128)}), f32[8,2,2048]{2,1,0:T(2,128)S(1)}, u32[]{:S(2)}, u32[]{:S(2)}) %all-to-all-start.4) | async-done | bytes 131104 | tf_op jit(solution)/shard_map/all_to_all | solution.py:171
  (127 shorter events, 19.1 us)
Async XLA Ops:
  0.6 42.5 %copy-start = (bf16[512,1536]{1,0:T(8,128)(2,1)S(1)}, bf16[512,1536]{1,0:T(8,128)(2,1)}, u32[]{:S(2)}) copy-start(bf16[512,1536]{1,0:T(8,128)(2,1)} %param.16) | copy-start | bytes 4718596
  0.6 7.9 %copy-start.1 = (bf16[1,128,512]{2,1,0:T(8,128)(2,1)S(1)}, bf16[1,128,512]{2,1,0:T(8,128)(2,1)}, u32[]{:S(2)}) copy-start(bf16[1,128,512]{2,1,0:T(8,128)(2,1)} %param.10) | copy-start | bytes 393220
  0.7 7.9 %copy-start.7 = (bf16[512,512]{1,0:T(8,128)(2,1)S(1)}, bf16[512,512]{1,0:T(8,128)(2,1)}, u32[]{:S(2)}) copy-start(bf16[512,512]{1,0:T(8,128)(2,1)} %param.14) | copy-start | bytes 1572868
  1.8 3.0 %copy-start.17 = (f32[128]{0:T(128)}, f32[128]{0:T(128)S(1)}, u32[]{:S(2)}) copy-start(f32[128]{0:T(128)S(1)} %broadcast_multiply_fusion.2) | copy-start | bytes 1540
  2.9 0.8 copy-start.25
  3.0 1.9 %copy-start.21 = (f32[128]{0:T(128)}, f32[128]{0:T(128)S(1)}, u32[]{:S(2)}) copy-start(f32[128]{0:T(128)S(1)} %fusion.98) | copy-start | bytes 1540
  4.9 3.9 %copy-start.23 = (s32[128]{0:T(128)}, s32[128]{0:T(128)S(1)}, u32[]{:S(2)}) copy-start(s32[128]{0:T(128)S(1)} %fusion.97) | copy-start | bytes 1540
  4.9 4.6 %copy-start.11 = (bf16[1,128,512]{2,1,0:T(8,128)(2,1)S(1)}, bf16[1,128,512]{2,1,0:T(8,128)(2,1)}, u32[]{:S(2)}) copy-start(bf16[1,128,512]{2,1,0:T(8,128)(2,1)} %param.11) | copy-start | bytes 393220
  8.8 0.7 copy-start.9
  10.5 31.4 %all-to-all-start = ((bf16[32,8,1024]{2,1,0:T(8,128)(2,1)}), bf16[32,8,1024]{2,1,0:T(8,128)(2,1)S(1)}, u32[]{:S(2)}, u32[]{:S(2)}) async-start(bf16[32,8,1024]{2,1,0:T(8,128)(2,1)} %fusion.42), calls=%async_computation | async-start | bytes 1048576 | tf_op jit(solution)/shard_map/all_to_all | solution.py:213
  43.1 0.8 copy-start.6
  43.2 1.1 copy-start.8
  43.9 0.9 copy-start.15
  43.9 0.9 copy-start.16
  59.5 1.1 copy-start.14
  61.9 1.4 copy-start.24
  62.4 0.9 copy-start.5
  65.2 28.6 %all-to-all-start.1 = ((bf16[32,8,1024]{2,1,0:T(8,128)(2,1)}), bf16[32,8,1024]{2,1,0:T(8,128)(2,1)}, u32[]{:S(2)}, u32[]{:S(2)}) async-start(bf16[32,8,1024]{2,1,0:T(8,128)(2,1)} %maximum_bitcast_fusion.10), calls=%async_computation.1 | async-start | bytes 1048576 | tf_op jit(solution)/shard_map/all_to_all | solution.py:230
  93.8 32.1 %all-to-all-start.2 = ((bf16[8,64,2048]{2,1,0:T(8,128)(2,1)}), bf16[8,64,2048]{2,1,0:T(8,128)(2,1)}, u32[]{:S(2)}, u32[]{:S(2)}) async-start(bf16[8,64,2048]{2,1,0:T(8,128)(2,1)} %pad_maximum_fusion), calls=%async_computation.2 | async-start | bytes 4194304 | tf_op jit(solution)/shard_map/all_to_all | solution.py:165
  100.9 3.9 %copy-start.3 = (f32[128,1024]{1,0:T(8,128)}, f32[128,1024]{1,0:T(8,128)S(1)}, u32[]{:S(2)}) copy-start(f32[128,1024]{1,0:T(8,128)S(1)} %fusion.55) | copy-start | bytes 1572868
  104.2 0.9 copy-start.13
  104.2 1.5 copy-start.2
  104.2 1.5 copy-start.18
  104.2 1.5 copy-start.20
  105.0 1.5 copy-start.26
  105.7 32.5 %copy-start.19 = (f32[128]{0:T(128)S(1)}, f32[128]{0:T(128)}, u32[]{:S(2)}) copy-start(f32[128]{0:T(128)} %copy-done.17) | copy-start | bytes 1540
  105.7 32.5 %copy-start.22 = (f32[128]{0:T(128)S(1)}, f32[128]{0:T(128)}, u32[]{:S(2)}) copy-start(f32[128]{0:T(128)} %copy-done.21) | copy-start | bytes 1540
  105.7 32.8 %copy-start.4 = (f32[128,1024]{1,0:T(8,128)S(1)}, f32[128,1024]{1,0:T(8,128)}, u32[]{:S(2)}) copy-start(f32[128,1024]{1,0:T(8,128)} %copy-done.3) | copy-start | bytes 1572868
  105.7 32.8 %copy-start.12 = (bf16[1,128,512]{2,1,0:T(8,128)(2,1)S(1)}, bf16[1,128,512]{2,1,0:T(8,128)(2,1)}, u32[]{:S(2)}) copy-start(bf16[1,128,512]{2,1,0:T(8,128)(2,1)} %param.11) | copy-start | bytes 393220
  106.5 49.1 %copy-start.10 = (bf16[128,512]{1,0:T(8,128)(2,1)S(1)}, bf16[128,512]{1,0:T(8,128)(2,1)}, u32[]{:S(2)}) copy-start(bf16[128,512]{1,0:T(8,128)(2,1)} %copy-done.9) | copy-start | bytes 393220
  128.8 19.1 %all-to-all-start.3 = ((bf16[32,2,2048]{2,1,0:T(2,128)(2,1)}), bf16[32,2,2048]{2,1,0:T(2,128)(2,1)S(1)}, u32[]{:S(2)}, u32[]{:S(2)}) async-start(bf16[32,2,2048]{2,1,0:T(2,128)(2,1)} %reshape.380), calls=%async_computation.3 | async-start | bytes 524288 | tf_op jit(solution)/shard_map/all_to_all | solution.py:168
  148.7 12.2 %all-to-all-start.4 = ((f32[8,2,2048]{2,1,0:T(2,128)}), f32[8,2,2048]{2,1,0:T(2,128)S(1)}, u32[]{:S(2)}, u32[]{:S(2)}) async-start(f32[8,2,2048]{2,1,0:T(2,128)} %broadcast_in_dim.161), calls=%async_computation.4 | async-start | bytes 262144 | tf_op jit(solution)/shard_map/all_to_all | solution.py:171

commit v9 on v8

--- a/solution.py
+++ b/solution.py
@@ -150,11 +150,12 @@
     )
 
 
-def feature_order(left_part, replicas, owners):
+def ordered_contract(left_part, right_part, replicas, owners):
     rows, features = left_part.shape
     per_device = features // owners // replicas
-    split = left_part.reshape(rows, owners, replicas, per_device)
-    return jnp.swapaxes(split, 1, 2).reshape(rows, features)
+    flipped = jnp.transpose(left_part).reshape(owners, replicas, per_device * rows)
+    flipped = jnp.swapaxes(flipped, 0, 1).reshape(features, rows)
+    return jnp.dot(flipped, right_part, preferred_element_type=jnp.float32)
 
 
 def reduce_weight_terms(partial, replicas, owners):
@@ -237,8 +238,8 @@
     factor = (replicas * owners * local_rows) ** (-0.5)
     partial_sum = jnp.concatenate(
         [
-            contract(feature_order(normed_half, replicas, owners), back_packed),
-            contract(feature_order(merged_rows, replicas, owners), landed_cotangent),
+            ordered_contract(normed_half, back_packed, replicas, owners),
+            ordered_contract(merged_rows, landed_cotangent, replicas, owners),
         ],
         axis=1,
     )

time: 164 us -> 164 us (level)
    dot_general x0 -> x2, local copies, waits for them, and re-layouts: none -> 3.51 us  [ordered_contract(): return jnp.dot(flipped, right_part, preferred_element_type=jnp.float32)]
    convert_element_type x2 -> x1, local copies, waits for them, and re-layouts: 3.67 us -> 1.81 us  [cross_account_inner(): return merged_rows.astype(jnp.bfloat16).reshape(row_total, features)]
    convert_element_type x1 -> x0, local copies, waits for them, and re-layouts: 1.81 us -> none  [owner_transfer(): normed_half = normed.astype(jnp.bfloat16)]
    reshape x3 -> x2, local copies, waits for them, and re-layouts: 5.29 us -> 3.51 us  [ordered_contract(): jnp.transpose(left_part).reshape(owners, replicas, per_device * rows)]
    transpose x2 -> x3, local copies, waits for them, and re-layouts: 3.69 us -> 5.29 us  [the longest x2 3.49 us: ordered_contract(): flipped = jnp.swapaxes(flipped, 0, 1).reshape(features, rows)]
where the time goes in v9:
time: 164 us; the launch traced here: 162 us
  starting transfers between devices  43.5 us (27%)
  waiting for transfers between devices  32.6 us (20%)
  local copies, waits for them, and re-layouts  31.2 us (19%)
  matrix products  26.3 us (16%)
  other arithmetic  23.6 us (14%)
  between operations  5.25 us (3%)
    all_to_all x1, waiting for transfers between devices, reduce_weight_terms(): terms = lax.all_to_all(terms, 'dp', 0, 0, tiled=True)  19.4 us
    all_to_all x1, starting transfers between devices, on_device(): lax.all_to_all(outgoing, 'ev', split_axis=0, concat_axis=0, tiled=True)  12 us
    all_to_all x1, starting transfers between devices, reduce_weight_terms(): terms = lax.all_to_all(terms, 'ev', 0, 0, tiled=True)  9.44 us
    all_to_all x1, starting transfers between devices, on_device(): lax.all_to_all(going_back, 'ev', split_axis=0, concat_axis=0, tiled=True)  9.34 us
    all_to_all x1, waiting for transfers between devices, reduce_weight_terms(): terms = lax.all_to_all(terms, 'ev', 0, 0, tiled=True)  8.59 us
    select_n x6, local copies, waits for them, and re-layouts, pick_block(): picked = jnp.where(chosen == index, blocks[index], picked)  7.2 us
    dot_general x3, matrix products, cross_account_inner(): jnp.einsum('bhqf,bkf->bhqk', masked_queries, key_rows) * HEAD_DIM ** (-0.5)  7.17 us
    all_to_all x1, starting transfers between devices, reduce_weight_terms(): gathered = lax.all_to_all(copies, 'dp', 0, 0, tiled=True)  6.94 us
  transfers between devices with their start and end apart: 5, of which 3 were waited for; matrix products, arithmetic and copies ran while one was open for 26% of the time, Pallas kernels for 0%

profile of v9, /device:TPU:1, one launch (start us, length us, event | category | flops | bytes accessed | tf_op | source)
XLA Modules:
  0.0 162.5 jit_solution(1398611476025274492)
XLA Ops:
  0.7 1.2 convert_reduce_fusion.5
  1.9 1.1 fusion.63
  4.9 1.9 %convolution_convert_fusion.2 = bf16[128,1536]{1,0:T(8,128)(2,1)S(1)} fusion(bf16[512,1536]{1,0:T(8,128)(2,1)} %param.13, bf16[1,128,512]{2,1,0:T(8,128)(2,1)} %param.10, f32[512]{0:T(512)} %param.12, f32[128]{0:T(128)S(1)} %fusion.98, f32[128]{0:T(128)S(1)} %broadcast_multiply_fusion.2), kind=kOutput, calls=%fused_computation.25 | convolution fusion | flops 201850880 | bytes 2100224 | tf_op jit(solution)/shard_map/jvp()/dot_general | solution.py:38
  9.4 1.1 fusion.42
  10.5 12.0 %all-to-all-start = ((bf16[32,8,1024]{2,1,0:T(8,128)(2,1)}), bf16[32,8,1024]{2,1,0:T(8,128)(2,1)S(1)}, u32[]{:S(2)}, u32[]{:S(2)}) async-start(bf16[32,8,1024]{2,1,0:T(8,128)(2,1)} %fusion.42), calls=%async_computation | async-start | bytes 1048576 | tf_op jit(solution)/shard_map/all_to_all | solution.py:214
  24.4 1.5 fusion.122
  28.4 1.9 %convert_reduce_fusion.4 = s32[32,32]{1,0:T(8,128)} fusion(s32[32,128]{1,0:T(8,128)} %bitcast.229), kind=kLoop, calls=%fused_computation.97 | loop fusion | flops 392192 | bytes 20480 | tf_op jit(solution)/shard_map/reduce_sum | solution.py:202
  30.4 0.9 dynamic-slice_reduce_fusion
  32.0 1.3 select_n.319
  33.2 1.3 select_n.325
  34.6 1.4 select_n.328
  35.9 1.3 select_n.331
  37.2 1.3 select_n.334
  42.3 1.4 convolution_convert_fusion.1
  44.7 1.4 fusion.124
  46.1 1.2 fusion.22
  47.3 2.0 %fusion.12 = (f32[2,8,128]{2,1,0:T(8,128)S(1)}, bf16[2,8,128,384]{3,2,1,0:T(8,128)(2,1)S(1)}) fusion(f32[2,8,128,384]{3,2,1,0:T(8,128)S(1)} %get-tuple-element.69, f32[2,8,128]{2,1,0:T(8,128)S(1)} %multiply_divide_fusion, f32[2,8,128]{2,1,0:T(8,128)S(1)} %get-tuple-element.68, pred[2,128,384]{2,1,0:T(8,128)(4,1)S(1)} %copy-done.14, ...), kind=kOutput, calls=%fused_computation.16 | convolution fusion | flops 811464704 | bytes 6168576 | tf_op jit(solution)/shard_map/transpose(jvp(bhqk,bkf->bhqf))/dot_general | solution.py:105
  49.3 3.0 %divide_convert_fusion = (bf16[2,8,128,384]{3,2,1,0:T(8,128)(2,1)S(1)}, f32[2,8,128]{2,1,0:T(8,128)S(1)}, f32[2,8,128]{2,1,0:T(8,128)S(1)}, pred[2,8,128,384]{3,2,1,0:T(32,128)(4,1)S(1)}) fusion(f32[2,8,128,384]{3,2,1,0:T(8,128)S(1)} %get-tuple-element.69, f32[2,8,128]{2,1,0:T(8,128)S(1)} %fusion.22, f32[2,8,128]{2,1,0:T(8,128)S(1)} %get-tuple-element.68, ...), kind=kLoop, calls=%fused_computation.19 | loop fusion | flops 10219520 | bytes 7217152 | tf_op jit(solution)/shard_map/jvp()/convert_element_type | solution.py:104
  52.4 3.0 %multiply_reduce_fusion = f32[2,128,512]{2,1,0:T(8,128)S(1)} fusion(f32[8,512]{1,0:T(8,128)S(1)} %copy-done.15, pred[2,8,128,384]{3,2,1,0:T(32,128)(4,1)S(1)} %get-tuple-element.15, f32[2,8,128]{2,1,0:T(8,128)S(1)} %negate_divide_fusion, pred[2,128,384]{2,1,0:T(8,128)(4,1)S(1)} %copy-done.14, bf16[1,384,512]{2,1,0:T(8,128)(2,1)S(1)} %get-tuple-element.78, ...), kind=kOutput, calls=%fused_computation.8 | convolution fusion | flops 815529984 | bytes 6963200 | tf_op jit(solution)/shard_map/transpose(jvp(bhqf,bkf->bhqk))/dot_general | solution.py:100
  55.4 2.8 %fusion.36 = f32[2,384,512]{2,1,0:T(8,128)S(1)} fusion(f32[8,512]{1,0:T(8,128)S(1)} %copy-done.15, f32[2,128,512]{2,1,0:T(8,128)S(1)} %slice.168, pred[2,8,128,384]{3,2,1,0:T(32,128)(4,1)S(1)} %get-tuple-element.15, f32[2,8,128]{2,1,0:T(8,128)S(1)} %negate_divide_fusion, pred[2,128,384]{2,1,0:T(8,128)(4,1)S(1)} %copy-done.14, ...), kind=kOutput, calls=%fused_computation.49 | convolution fusion | flops 814219264 | bytes 7749632 | tf_op jit(solution)/shard_map/transpose(jvp(bhqf,bkf->bhqk))/dot_general | solution.py:100
  58.2 1.3 multiply_reduce_fusion.1
  59.5 1.1 fusion.39
  62.3 0.9 copy-done.5
  63.9 1.0 fusion.120
  65.0 0.9 maximum_bitcast_fusion.10
  65.8 9.3 %all-to-all-start.1 = ((bf16[32,8,1024]{2,1,0:T(8,128)(2,1)}), bf16[32,8,1024]{2,1,0:T(8,128)(2,1)}, u32[]{:S(2)}, u32[]{:S(2)}) async-start(bf16[32,8,1024]{2,1,0:T(8,128)(2,1)} %maximum_bitcast_fusion.10), calls=%async_computation.1 | async-start | bytes 1048576 | tf_op jit(solution)/shard_map/all_to_all | solution.py:231
  75.2 1.8 %copy.109 = bf16[256,512]{0,1:T(8,128)(2,1)} copy(bf16[256,512]{1,0:T(8,128)(2,1)} %bitcast.226) | data formatting | bytes 524288 | tf_op jit(solution)/shard_map/jvp()/convert_element_type | solution.py:107
  77.0 1.8 %reshape.376 = bf16[32,8,512]{2,1,0:T(8,128)(2,1)} reshape(bf16[512,256]{1,0:T(8,128)(2,1)} %bitcast.222) | data formatting | bytes 524288 | tf_op jit(solution)/shard_map/reshape | solution.py:156
  78.8 1.7 %copy.110 = bf16[8,32,512]{2,1,0:T(8,128)(2,1)} copy(bf16[8,32,512]{2,0,1:T(8,128)(2,1)} %bitcast.223) | data formatting | bytes 524288 | tf_op jit(solution)/shard_map/transpose | solution.py:157
  80.5 1.8 %dot_general.103 = bf16[8,64,256]{2,1,0:T(8,128)(2,1)} reshape(bf16[8,32,512]{2,1,0:T(8,128)(2,1)} %copy.110) | data formatting | bytes 524288 | tf_op jit(solution)/shard_map/dot_general | solution.py:158
  82.3 1.8 %copy.107 = bf16[512,256]{1,0:T(8,128)(2,1)} copy(bf16[512,256]{0,1:T(8,128)(2,1)} %get-tuple-element.53) | data formatting | bytes 524288 | tf_op jit(solution)/shard_map/transpose | solution.py:156
  84.1 1.7 %reshape.375 = bf16[32,8,512]{2,1,0:T(8,128)(2,1)} reshape(bf16[512,256]{1,0:T(8,128)(2,1)} %copy.107) | data formatting | bytes 524288 | tf_op jit(solution)/shard_map/reshape | solution.py:156
  85.8 1.7 %copy.108 = bf16[8,32,512]{2,1,0:T(8,128)(2,1)} copy(bf16[8,32,512]{2,0,1:T(8,128)(2,1)} %bitcast.224) | data formatting | bytes 524288 | tf_op jit(solution)/shard_map/transpose | solution.py:157
  87.6 1.7 %dot_general.101 = bf16[8,64,256]{2,1,0:T(8,128)(2,1)} reshape(bf16[8,32,512]{2,1,0:T(8,128)(2,1)} %copy.108) | data formatting | bytes 524288 | tf_op jit(solution)/shard_map/dot_general | solution.py:158
  89.3 1.2 convolution_convert_fusion.3
  90.6 1.8 %convolution_convert_fusion = bf16[8,64,1536]{2,1,0:T(8,128)(2,1)S(1)} fusion(bf16[8,64,256]{2,1,0:T(8,128)(2,1)} %dot_general.101, bf16[256,1536,1]{1,0,2:T(8,128)(2,1)} %bitcast.214), kind=kOutput, calls=%fused_computation.22 | convolution fusion | flops 403439616 | bytes 2621440 | tf_op jit(solution)/shard_map/dot_general | solution.py:158
  92.4 1.6 pad_maximum_fusion
  94.0 5.8 %all-to-all-start.2 = ((bf16[8,64,2048]{2,1,0:T(8,128)(2,1)}), bf16[8,64,2048]{2,1,0:T(8,128)(2,1)}, u32[]{:S(2)}, u32[]{:S(2)}) async-start(bf16[8,64,2048]{2,1,0:T(8,128)(2,1)} %pad_maximum_fusion), calls=%async_computation.2 | async-start | bytes 4194304 | tf_op jit(solution)/shard_map/all_to_all | solution.py:166
  99.8 1.3 fusion.55
  101.1 2.2 %convolution_convert_fusion.9 = bf16[128,512]{1,0:T(8,128)(2,1)} fusion(bf16[512,512]{1,0:T(8,128)(2,1)} %param.14, f32[128,1024]{1,0:T(8,128)S(1)} %fusion.55, bf16[1,128,512]{2,1,0:T(8,128)(2,1)S(1)} %copy-done.10), kind=kOutput, calls=%fused_computation.66 | convolution fusion | flops 67371008 | bytes 1048576 | tf_op jit(solution)/shard_map/transpose(jvp())/dot_general | solution.py:49
  103.3 1.0 copy.103
  106.7 19.4 %all-to-all-done.2 = bf16[8,64,2048]{2,1,0:T(8,128)(2,1)} async-done(((bf16[8,64,2048]{2,1,0:T(8,128)(2,1)}), bf16[8,64,2048]{2,1,0:T(8,128)(2,1)}, u32[]{:S(2)}, u32[]{:S(2)}) %all-to-all-start.2) | async-done | bytes 2097184 | tf_op jit(solution)/shard_map/all_to_all | solution.py:166
  126.1 2.0 %reduce_sum.260 = bf16[64,2048]{1,0:T(8,128)(2,1)S(1)} reduce(bf16[8,64,2048]{2,1,0:T(8,128)(2,1)} %all-to-all-done.2, bf16[]{:T(256)} %constant.95.clone.1), dimensions={0}, to_apply=%region_23.24 | reduce | flops 917504 | bytes 2359298 | tf_op jit(solution)/shard_map/reduce_sum | solution.py:167
  128.1 0.9 reshape.377
  128.9 9.4 %all-to-all-start.3 = ((bf16[32,2,2048]{2,1,0:T(2,128)(2,1)}), bf16[32,2,2048]{2,1,0:T(2,128)(2,1)S(1)}, u32[]{:S(2)}, u32[]{:S(2)}) async-start(bf16[32,2,2048]{2,1,0:T(2,128)(2,1)} %reshape.377), calls=%async_computation.3 | async-start | bytes 524288 | tf_op jit(solution)/shard_map/all_to_all | solution.py:169
  139.5 8.6 %all-to-all-done.3 = bf16[32,2,2048]{2,1,0:T(2,128)(2,1)S(1)} async-done(((bf16[32,2,2048]{2,1,0:T(2,128)(2,1)}), bf16[32,2,2048]{2,1,0:T(2,128)(2,1)S(1)}, u32[]{:S(2)}, u32[]{:S(2)}) %all-to-all-start.3) | async-done | bytes 262176 | tf_op jit(solution)/shard_map/all_to_all | solution.py:169
  148.8 6.9 %all-to-all-start.4 = ((f32[8,2,2048]{2,1,0:T(2,128)}), f32[8,2,2048]{2,1,0:T(2,128)S(1)}, u32[]{:S(2)}, u32[]{:S(2)}) async-start(f32[8,2,2048]{2,1,0:T(2,128)} %broadcast_in_dim.161), calls=%async_computation.4 | async-start | bytes 262144 | tf_op jit(solution)/shard_map/all_to_all | solution.py:172
  156.5 4.6 %all-to-all-done.4 = f32[8,2,2048]{2,1,0:T(2,128)S(1)} async-done(((f32[8,2,2048]{2,1,0:T(2,128)}), f32[8,2,2048]{2,1,0:T(2,128)S(1)}, u32[]{:S(2)}, u32[]{:S(2)}) %all-to-all-start.4) | async-done | bytes 131104 | tf_op jit(solution)/shard_map/all_to_all | solution.py:172
  (124 shorter events, 19.1 us)
Async XLA Ops:
  0.6 41.7 %copy-start = (bf16[512,1536]{1,0:T(8,128)(2,1)S(1)}, bf16[512,1536]{1,0:T(8,128)(2,1)}, u32[]{:S(2)}) copy-start(bf16[512,1536]{1,0:T(8,128)(2,1)} %param.16) | copy-start | bytes 4718596
  0.6 7.9 %copy-start.1 = (bf16[1,128,512]{2,1,0:T(8,128)(2,1)S(1)}, bf16[1,128,512]{2,1,0:T(8,128)(2,1)}, u32[]{:S(2)}) copy-start(bf16[1,128,512]{2,1,0:T(8,128)(2,1)} %param.10) | copy-start | bytes 393220
  0.7 7.9 %copy-start.6 = (bf16[512,512]{1,0:T(8,128)(2,1)S(1)}, bf16[512,512]{1,0:T(8,128)(2,1)}, u32[]{:S(2)}) copy-start(bf16[512,512]{1,0:T(8,128)(2,1)} %param.14) | copy-start | bytes 1572868
  1.8 3.0 %copy-start.16 = (f32[128]{0:T(128)}, f32[128]{0:T(128)S(1)}, u32[]{:S(2)}) copy-start(f32[128]{0:T(128)S(1)} %broadcast_multiply_fusion.2) | copy-start | bytes 1540
  2.9 0.8 copy-start.24
  3.0 1.9 %copy-start.20 = (f32[128]{0:T(128)}, f32[128]{0:T(128)S(1)}, u32[]{:S(2)}) copy-start(f32[128]{0:T(128)S(1)} %fusion.98) | copy-start | bytes 1540
  4.9 3.9 %copy-start.22 = (s32[128]{0:T(128)}, s32[128]{0:T(128)S(1)}, u32[]{:S(2)}) copy-start(s32[128]{0:T(128)S(1)} %fusion.97) | copy-start | bytes 1540
  4.9 4.6 %copy-start.10 = (bf16[1,128,512]{2,1,0:T(8,128)(2,1)S(1)}, bf16[1,128,512]{2,1,0:T(8,128)(2,1)}, u32[]{:S(2)}) copy-start(bf16[1,128,512]{2,1,0:T(8,128)(2,1)} %param.11) | copy-start | bytes 393220
  8.8 0.7 copy-start.8
  10.5 31.4 %all-to-all-start = ((bf16[32,8,1024]{2,1,0:T(8,128)(2,1)}), bf16[32,8,1024]{2,1,0:T(8,128)(2,1)S(1)}, u32[]{:S(2)}, u32[]{:S(2)}) async-start(bf16[32,8,1024]{2,1,0:T(8,128)(2,1)} %fusion.42), calls=%async_computation | async-start | bytes 1048576 | tf_op jit(solution)/shard_map/all_to_all | solution.py:214
  42.3 1.6 copy-start.7
  43.8 0.9 copy-start.14
  43.8 0.9 copy-start.15
  59.4 1.1 copy-start.13
  61.8 1.4 copy-start.23
  62.3 0.9 copy-start.5
  65.8 28.1 %all-to-all-start.1 = ((bf16[32,8,1024]{2,1,0:T(8,128)(2,1)}), bf16[32,8,1024]{2,1,0:T(8,128)(2,1)}, u32[]{:S(2)}, u32[]{:S(2)}) async-start(bf16[32,8,1024]{2,1,0:T(8,128)(2,1)} %maximum_bitcast_fusion.10), calls=%async_computation.1 | async-start | bytes 1048576 | tf_op jit(solution)/shard_map/all_to_all | solution.py:231
  94.0 32.1 %all-to-all-start.2 = ((bf16[8,64,2048]{2,1,0:T(8,128)(2,1)}), bf16[8,64,2048]{2,1,0:T(8,128)(2,1)}, u32[]{:S(2)}, u32[]{:S(2)}) async-start(bf16[8,64,2048]{2,1,0:T(8,128)(2,1)} %pad_maximum_fusion), calls=%async_computation.2 | async-start | bytes 4194304 | tf_op jit(solution)/shard_map/all_to_all | solution.py:166
  101.1 3.9 %copy-start.3 = (f32[128,1024]{1,0:T(8,128)}, f32[128,1024]{1,0:T(8,128)S(1)}, u32[]{:S(2)}) copy-start(f32[128,1024]{1,0:T(8,128)S(1)} %fusion.55) | copy-start | bytes 1572868
  104.3 0.9 copy-start.12
  104.4 1.5 copy-start.2
  104.4 1.5 copy-start.17
  104.4 1.5 copy-start.19
  105.1 1.5 copy-start.25
  105.8 32.6 %copy-start.18 = (f32[128]{0:T(128)S(1)}, f32[128]{0:T(128)}, u32[]{:S(2)}) copy-start(f32[128]{0:T(128)} %copy-done.16) | copy-start | bytes 1540
  105.9 32.6 %copy-start.21 = (f32[128]{0:T(128)S(1)}, f32[128]{0:T(128)}, u32[]{:S(2)}) copy-start(f32[128]{0:T(128)} %copy-done.20) | copy-start | bytes 1540
  105.9 32.8 %copy-start.4 = (f32[128,1024]{1,0:T(8,128)S(1)}, f32[128,1024]{1,0:T(8,128)}, u32[]{:S(2)}) copy-start(f32[128,1024]{1,0:T(8,128)} %copy-done.3) | copy-start | bytes 1572868
  105.9 32.8 %copy-start.11 = (bf16[1,128,512]{2,1,0:T(8,128)(2,1)S(1)}, bf16[1,128,512]{2,1,0:T(8,128)(2,1)}, u32[]{:S(2)}) copy-start(bf16[1,128,512]{2,1,0:T(8,128)(2,1)} %param.11) | copy-start | bytes 393220
  106.6 49.1 %copy-start.9 = (bf16[128,512]{1,0:T(8,128)(2,1)S(1)}, bf16[128,512]{1,0:T(8,128)(2,1)}, u32[]{:S(2)}) copy-start(bf16[128,512]{1,0:T(8,128)(2,1)} %copy-done.8) | copy-start | bytes 393220
  128.9 19.1 %all-to-all-start.3 = ((bf16[32,2,2048]{2,1,0:T(2,128)(2,1)}), bf16[32,2,2048]{2,1,0:T(2,128)(2,1)S(1)}, u32[]{:S(2)}, u32[]{:S(2)}) async-start(bf16[32,2,2048]{2,1,0:T(2,128)(2,1)} %reshape.377), calls=%async_computation.3 | async-start | bytes 524288 | tf_op jit(solution)/shard_map/all_to_all | solution.py:169
  148.8 12.2 %all-to-all-start.4 = ((f32[8,2,2048]{2,1,0:T(2,128)}), f32[8,2,2048]{2,1,0:T(2,128)S(1)}, u32[]{:S(2)}, u32[]{:S(2)}) async-start(f32[8,2,2048]{2,1,0:T(2,128)} %broadcast_in_dim.161), calls=%async_computation.4 | async-start | bytes 262144 | tf_op jit(solution)/shard_map/all_to_all | solution.py:172

commit v10 on v9

--- a/solution.py
+++ b/solution.py
@@ -158,6 +158,13 @@
     return jnp.dot(flipped, right_part, preferred_element_type=jnp.float32)
 
 
+def dense_all_to_all(pieces, axis_name):
+    count = pieces.shape[0]
+    flat = pieces.reshape(count, -1, 128)
+    moved = lax.all_to_all(flat, axis_name, 0, 0, tiled=True)
+    return moved.reshape(pieces.shape)
+
+
 def reduce_weight_terms(partial, replicas, owners):
     rows, width = partial.shape
     per_replica = rows // replicas
@@ -166,10 +173,10 @@
     terms = lax.all_to_all(terms, "dp", 0, 0, tiled=True)
     terms = jnp.sum(terms.astype(jnp.float32), axis=0).astype(jnp.bfloat16)
     terms = terms.reshape(owners, per_device, width)
-    terms = lax.all_to_all(terms, "ev", 0, 0, tiled=True)
+    terms = dense_all_to_all(terms, "ev")
     piece = jnp.sum(terms.astype(jnp.float32), axis=0)
     copies = jnp.broadcast_to(piece[None], (replicas, per_device, width))
-    gathered = lax.all_to_all(copies, "dp", 0, 0, tiled=True)
+    gathered = dense_all_to_all(copies, "dp")
     return gathered.reshape(replicas * per_device, width)
 
 
@@ -211,7 +218,9 @@
     ).astype(jnp.bfloat16)
     both = jnp.concatenate([hidden, upstream], axis=1)
     outgoing = jnp.dot(placement, both, preferred_element_type=jnp.float32).astype(jnp.bfloat16)
-    landed = lax.all_to_all(outgoing, "ev", split_axis=0, concat_axis=0, tiled=True)
+    landed = dense_all_to_all(outgoing.reshape(owners, row_capacity, -1), "ev").reshape(
+        outgoing.shape
+    )
     landed_rows = landed[:, :features]
     landed_cotangent = landed[:, features:]
     row_presence = (
@@ -228,7 +237,9 @@
         cross_output_weight,
     )
     going_back = jnp.concatenate([result, back_rows.astype(jnp.bfloat16)], axis=1)
-    came_back = lax.all_to_all(going_back, "ev", split_axis=0, concat_axis=0, tiled=True)
+    came_back = dense_all_to_all(going_back.reshape(owners, row_capacity, -1), "ev").reshape(
+        going_back.shape
+    )
     picked = lax.dot_general(
         placement, came_back, (((0,), (0,)), ((), ())), preferred_element_type=jnp.float32
     )

time: 164 us -> 161 us (0.982)
  waiting for transfers between devices: 32.6 us -> 35.6 us
  other arithmetic: 23.6 us -> 20.9 us
  starting transfers between devices: 43.5 us -> 41.8 us
    another operation x0 -> x5, local copies, waits for them, and re-layouts: none -> 7.26 us  [the longest x3 3.91 us: dense_all_to_all(): flat = pieces.reshape(count, -1, 128)]
    select_n x6, local copies, waits for them, and re-layouts: 7.2 us -> 0.58 us  [pick_block(): picked = jnp.where(chosen == index, blocks[index], picked)]
    all_to_all x4, waiting for transfers between devices: 13.2 us -> 18.3 us  [dense_all_to_all(): moved = lax.all_to_all(flat, axis_name, 0, 0, tiled=True)]
    all_to_all x1, waiting for transfers between devices: 19.4 us -> 17.3 us  [reduce_weight_terms(): terms = lax.all_to_all(terms, 'dp', 0, 0, tiled=True)]
    all_to_all x4, starting transfers between devices: 37.7 us -> 35.9 us  [dense_all_to_all(): moved = lax.all_to_all(flat, axis_name, 0, 0, tiled=True)]
  transfers between devices with their start and end apart: 5 -> 5, of which waited for: 3 -> 4; matrix products, arithmetic and copies ran while one was open for 26% -> 22% of each run, Pallas kernels for 0% -> 0%
where the time goes in v10:
time: 161 us; the launch traced here: 159 us
  starting transfers between devices  41.8 us (26%)
  waiting for transfers between devices  35.6 us (22%)
  local copies, waits for them, and re-layouts  30.2 us (19%)
  matrix products  25.5 us (16%)
  other arithmetic  20.9 us (13%)
  between operations  5.25 us (3%)
    all_to_all x4, starting transfers between devices, dense_all_to_all(): moved = lax.all_to_all(flat, axis_name, 0, 0, tiled=True)  35.9 us
    all_to_all x4, waiting for transfers between devices, dense_all_to_all(): moved = lax.all_to_all(flat, axis_name, 0, 0, tiled=True)  18.3 us
    all_to_all x1, waiting for transfers between devices, reduce_weight_terms(): terms = lax.all_to_all(terms, 'dp', 0, 0, tiled=True)  17.3 us
    dot_general x3, matrix products, cross_account_inner(): jnp.einsum('bhqf,bkf->bhqk', masked_queries, key_rows) * HEAD_DIM ** (-0.5)  7.16 us
    all_to_all x1, starting transfers between devices, reduce_weight_terms(): terms = lax.all_to_all(terms, 'dp', 0, 0, tiled=True)  5.95 us
    dot_general x3, matrix products, cross_account_inner(): jnp.einsum('bhqk,bkf->bhqf', attention.astype(jnp.float32), value_rows)  4.31 us
    another operation x3, local copies, waits for them, and re-layouts, dense_all_to_all(): flat = pieces.reshape(count, -1, 128)  3.91 us
    dot_general x2, local copies, waits for them, and re-layouts, ordered_contract(): return jnp.dot(flipped, right_part, preferred_element_type=jnp.float32)  3.51 us
  transfers between devices with their start and end apart: 5, of which 4 were waited for; matrix products, arithmetic and copies ran while one was open for 22% of the time, Pallas kernels for 0%

profile of v10, /device:TPU:1, one launch (start us, length us, event | category | flops | bytes accessed | tf_op | source)
XLA Modules:
  0.0 159.2 jit_solution(2139785682042788202)
XLA Ops:
  0.7 1.2 convert_reduce_fusion.5
  1.9 1.1 fusion.60
  4.9 1.9 %convolution_convert_fusion.2 = bf16[128,1536]{1,0:T(8,128)(2,1)S(1)} fusion(bf16[512,1536]{1,0:T(8,128)(2,1)} %param.13, bf16[1,128,512]{2,1,0:T(8,128)(2,1)} %param.10, f32[512]{0:T(512)} %param.12, f32[128]{0:T(128)S(1)} %fusion.96, f32[128]{0:T(128)S(1)} %broadcast_multiply_fusion.2), kind=kOutput, calls=%fused_computation.25 | convolution fusion | flops 201850880 | bytes 2100224 | tf_op jit(solution)/shard_map/jvp()/dot_general | solution.py:38
  7.5 0.8 convert_reduce_fusion.3
  9.7 1.0 reshape_reshape.17
  10.8 12.1 %all-to-all-start = ((bf16[32,64,128]{2,1,0:T(8,128)(2,1)}), bf16[32,64,128]{2,1,0:T(8,128)(2,1)}, u32[]{:S(2)}, u32[]{:S(2)}) async-start(bf16[32,64,128]{2,1,0:T(8,128)(2,1)} %reshape_reshape.17), calls=%async_computation | async-start | bytes 1048576 | tf_op jit(solution)/shard_map/all_to_all | solution.py:164
  24.8 1.5 fusion.120
  28.7 1.3 convert_reduce_fusion.4
  32.4 5.1 %all-to-all-done = bf16[32,64,128]{2,1,0:T(8,128)(2,1)} async-done(((bf16[32,64,128]{2,1,0:T(8,128)(2,1)}), bf16[32,64,128]{2,1,0:T(8,128)(2,1)}, u32[]{:S(2)}, u32[]{:S(2)}) %all-to-all-start) | async-done | bytes 524320 | tf_op jit(solution)/shard_map/all_to_all | solution.py:164
  37.4 1.3 reshape_reshape.18
  39.1 1.4 convolution_convert_fusion.1
  41.5 1.4 fusion.122
  42.9 1.2 fusion.22
  44.1 2.0 %fusion.12 = (f32[2,8,128]{2,1,0:T(8,128)S(1)}, bf16[2,8,128,384]{3,2,1,0:T(8,128)(2,1)S(1)}) fusion(f32[2,8,128,384]{3,2,1,0:T(8,128)S(1)} %get-tuple-element.69, f32[2,8,128]{2,1,0:T(8,128)S(1)} %multiply_divide_fusion, f32[2,8,128]{2,1,0:T(8,128)S(1)} %get-tuple-element.68, pred[2,128,384]{2,1,0:T(8,128)(4,1)S(1)} %copy-done.14, ...), kind=kOutput, calls=%fused_computation.16 | convolution fusion | flops 811464704 | bytes 6168576 | tf_op jit(solution)/shard_map/transpose(jvp(bhqk,bkf->bhqf))/dot_general | solution.py:105
  46.1 3.0 %divide_convert_fusion = (bf16[2,8,128,384]{3,2,1,0:T(8,128)(2,1)S(1)}, f32[2,8,128]{2,1,0:T(8,128)S(1)}, f32[2,8,128]{2,1,0:T(8,128)S(1)}, pred[2,8,128,384]{3,2,1,0:T(32,128)(4,1)S(1)}) fusion(f32[2,8,128,384]{3,2,1,0:T(8,128)S(1)} %get-tuple-element.69, f32[2,8,128]{2,1,0:T(8,128)S(1)} %fusion.22, f32[2,8,128]{2,1,0:T(8,128)S(1)} %get-tuple-element.68, ...), kind=kLoop, calls=%fused_computation.19 | loop fusion | flops 10219520 | bytes 7217152 | tf_op jit(solution)/shard_map/jvp()/convert_element_type | solution.py:104
  49.1 3.0 %multiply_reduce_fusion = f32[2,128,512]{2,1,0:T(8,128)S(1)} fusion(f32[8,512]{1,0:T(8,128)S(1)} %copy-done.15, pred[2,8,128,384]{3,2,1,0:T(32,128)(4,1)S(1)} %get-tuple-element.15, f32[2,8,128]{2,1,0:T(8,128)S(1)} %negate_divide_fusion, pred[2,128,384]{2,1,0:T(8,128)(4,1)S(1)} %copy-done.14, bf16[1,384,512]{2,1,0:T(8,128)(2,1)S(1)} %get-tuple-element.78, ...), kind=kOutput, calls=%fused_computation.8 | convolution fusion | flops 815529984 | bytes 6963200 | tf_op jit(solution)/shard_map/transpose(jvp(bhqf,bkf->bhqk))/dot_general | solution.py:100
  52.1 2.8 %fusion.36 = f32[2,384,512]{2,1,0:T(8,128)S(1)} fusion(f32[8,512]{1,0:T(8,128)S(1)} %copy-done.15, f32[2,128,512]{2,1,0:T(8,128)S(1)} %slice.168, pred[2,8,128,384]{3,2,1,0:T(32,128)(4,1)S(1)} %get-tuple-element.15, f32[2,8,128]{2,1,0:T(8,128)S(1)} %negate_divide_fusion, pred[2,128,384]{2,1,0:T(8,128)(4,1)S(1)} %copy-done.14, ...), kind=kOutput, calls=%fused_computation.49 | convolution fusion | flops 814219264 | bytes 7749632 | tf_op jit(solution)/shard_map/transpose(jvp(bhqf,bkf->bhqk))/dot_general | solution.py:100
  54.9 1.3 multiply_reduce_fusion.1
  56.2 1.1 fusion.39
  59.1 0.9 copy-done.5
  60.7 1.0 fusion.118
  61.8 0.9 pad_maximum_fusion.1
  62.6 2.1 %reshape_reshape.19 = bf16[32,64,128]{2,1,0:T(8,128)(2,1)} reshape(bf16[256,1024]{1,0:T(8,128)(2,1)} %pad_maximum_fusion.1) | data formatting | bytes 1048576 | tf_op jit(solution)/shard_map/reshape;reshape | solution.py:163
  64.7 7.4 %all-to-all-start.1 = ((bf16[32,64,128]{2,1,0:T(8,128)(2,1)}), bf16[32,64,128]{2,1,0:T(8,128)(2,1)}, u32[]{:S(2)}, u32[]{:S(2)}) async-start(bf16[32,64,128]{2,1,0:T(8,128)(2,1)} %reshape_reshape.19), calls=%async_computation.1 | async-start | bytes 1048576 | tf_op jit(solution)/shard_map/all_to_all | solution.py:164
  72.1 1.8 %copy.81 = bf16[256,512]{0,1:T(8,128)(2,1)} copy(bf16[256,512]{1,0:T(8,128)(2,1)} %bitcast.212) | data formatting | bytes 524288 | tf_op jit(solution)/shard_map/jvp()/convert_element_type | solution.py:107
  73.9 1.7 %reshape.374 = bf16[32,8,512]{2,1,0:T(8,128)(2,1)} reshape(bf16[512,256]{1,0:T(8,128)(2,1)} %bitcast.208) | data formatting | bytes 524288 | tf_op jit(solution)/shard_map/reshape | solution.py:156
  75.6 1.7 %copy.82 = bf16[8,32,512]{2,1,0:T(8,128)(2,1)} copy(bf16[8,32,512]{2,0,1:T(8,128)(2,1)} %bitcast.209) | data formatting | bytes 524288 | tf_op jit(solution)/shard_map/transpose | solution.py:157
  77.4 1.7 %dot_general.103 = bf16[8,64,256]{2,1,0:T(8,128)(2,1)} reshape(bf16[8,32,512]{2,1,0:T(8,128)(2,1)} %copy.82) | data formatting | bytes 524288 | tf_op jit(solution)/shard_map/dot_general | solution.py:158
  79.1 1.8 %copy.79 = bf16[512,256]{1,0:T(8,128)(2,1)} copy(bf16[512,256]{0,1:T(8,128)(2,1)} %get-tuple-element.53) | data formatting | bytes 524288 | tf_op jit(solution)/shard_map/transpose | solution.py:156
  80.9 1.8 %reshape.373 = bf16[32,8,512]{2,1,0:T(8,128)(2,1)} reshape(bf16[512,256]{1,0:T(8,128)(2,1)} %copy.79) | data formatting | bytes 524288 | tf_op jit(solution)/shard_map/reshape | solution.py:156
  82.7 1.7 %copy.80 = bf16[8,32,512]{2,1,0:T(8,128)(2,1)} copy(bf16[8,32,512]{2,0,1:T(8,128)(2,1)} %bitcast.210) | data formatting | bytes 524288 | tf_op jit(solution)/shard_map/transpose | solution.py:157
  84.4 1.8 %dot_general.101 = bf16[8,64,256]{2,1,0:T(8,128)(2,1)} reshape(bf16[8,32,512]{2,1,0:T(8,128)(2,1)} %copy.80) | data formatting | bytes 524288 | tf_op jit(solution)/shard_map/dot_general | solution.py:158
  86.2 1.2 convolution_convert_fusion.3
  87.4 1.8 %convolution_convert_fusion = bf16[8,64,1536]{2,1,0:T(8,128)(2,1)S(1)} fusion(bf16[8,64,256]{2,1,0:T(8,128)(2,1)} %dot_general.101, bf16[256,1536,1]{1,0,2:T(8,128)(2,1)} %bitcast.200), kind=kOutput, calls=%fused_computation.22 | convolution fusion | flops 403439616 | bytes 2621440 | tf_op jit(solution)/shard_map/dot_general | solution.py:158
  89.2 1.6 %pad_maximum_fusion = bf16[8,64,2048]{2,1,0:T(8,128)(2,1)} fusion(bf16[8,64,512]{2,1,0:T(8,128)(2,1)S(1)} %convolution_convert_fusion.3, bf16[8,64,1536]{2,1,0:T(8,128)(2,1)S(1)} %convolution_convert_fusion), kind=kLoop, calls=%fused_computation.26 | loop fusion | flops 4194304 | bytes 4194304 | tf_op jit(solution)/shard_map/concatenate | solution.py:250
  90.8 6.0 %all-to-all-start.2 = ((bf16[8,64,2048]{2,1,0:T(8,128)(2,1)}), bf16[8,64,2048]{2,1,0:T(8,128)(2,1)}, u32[]{:S(2)}, u32[]{:S(2)}) async-start(bf16[8,64,2048]{2,1,0:T(8,128)(2,1)} %pad_maximum_fusion), calls=%async_computation.2 | async-start | bytes 4194304 | tf_op jit(solution)/shard_map/all_to_all | solution.py:173
  96.8 2.1 %reshape_reshape.20 = bf16[256,1024]{1,0:T(8,128)(2,1)} reshape(bf16[32,64,128]{2,1,0:T(8,128)(2,1)} %all-to-all-done.1) | data formatting | bytes 1048576 | tf_op jit(solution)/shard_map/reshape;reshape | solution.py:240
  98.9 1.3 fusion.82
  100.2 2.2 %convolution_convert_fusion.9 = bf16[128,512]{1,0:T(8,128)(2,1)} fusion(bf16[512,512]{1,0:T(8,128)(2,1)} %param.14, f32[128,1024]{1,0:T(8,128)S(1)} %fusion.82, bf16[1,128,512]{2,1,0:T(8,128)(2,1)S(1)} %copy-done.10), kind=kOutput, calls=%fused_computation.65 | convolution fusion | flops 67371008 | bytes 1048576 | tf_op jit(solution)/shard_map/transpose(jvp())/dot_general | solution.py:49
  102.4 1.0 copy.75
  105.7 17.3 %all-to-all-done.2 = bf16[8,64,2048]{2,1,0:T(8,128)(2,1)} async-done(((bf16[8,64,2048]{2,1,0:T(8,128)(2,1)}), bf16[8,64,2048]{2,1,0:T(8,128)(2,1)}, u32[]{:S(2)}, u32[]{:S(2)}) %all-to-all-start.2) | async-done | bytes 2097184 | tf_op jit(solution)/shard_map/all_to_all | solution.py:173
  123.1 2.0 %reduce_sum.260 = bf16[64,2048]{1,0:T(8,128)(2,1)S(1)} reduce(bf16[8,64,2048]{2,1,0:T(8,128)(2,1)} %all-to-all-done.2, bf16[]{:T(256)} %constant.95.clone.1), dimensions={0}, to_apply=%region_23.24 | reduce | flops 917504 | bytes 2359298 | tf_op jit(solution)/shard_map/reduce_sum | solution.py:174
  125.1 0.8 reshape_reshape.21
  125.9 9.4 %all-to-all-start.3 = ((bf16[32,32,128]{2,1,0:T(8,128)(2,1)}), bf16[32,32,128]{2,1,0:T(8,128)(2,1)S(1)}, u32[]{:S(2)}, u32[]{:S(2)}) async-start(bf16[32,32,128]{2,1,0:T(8,128)(2,1)} %reshape_reshape.21), calls=%async_computation.3 | async-start | bytes 524288 | tf_op jit(solution)/shard_map/all_to_all | solution.py:164
  135.6 0.8 fusion.79
  136.4 8.6 %all-to-all-done.3 = bf16[32,32,128]{2,1,0:T(8,128)(2,1)S(1)} async-done(((bf16[32,32,128]{2,1,0:T(8,128)(2,1)}), bf16[32,32,128]{2,1,0:T(8,128)(2,1)S(1)}, u32[]{:S(2)}, u32[]{:S(2)}) %all-to-all-start.3) | async-done | bytes 262176 | tf_op jit(solution)/shard_map/all_to_all | solution.py:164
  145.7 6.9 %all-to-all-start.4 = ((f32[8,32,128]{2,1,0:T(8,128)}), f32[8,32,128]{2,1,0:T(8,128)S(1)}, u32[]{:S(2)}, u32[]{:S(2)}) async-start(f32[8,32,128]{2,1,0:T(8,128)} %broadcast_in_dim.161), calls=%async_computation.4 | async-start | bytes 262144 | tf_op jit(solution)/shard_map/all_to_all | solution.py:164
  153.3 4.6 %all-to-all-done.4 = f32[8,32,128]{2,1,0:T(8,128)S(1)} async-done(((f32[8,32,128]{2,1,0:T(8,128)}), f32[8,32,128]{2,1,0:T(8,128)S(1)}, u32[]{:S(2)}, u32[]{:S(2)}) %all-to-all-start.4) | async-done | bytes 131104 | tf_op jit(solution)/shard_map/all_to_all | solution.py:164
  (128 shorter events, 15.6 us)
Async XLA Ops:
  0.6 38.4 %copy-start = (bf16[512,1536]{1,0:T(8,128)(2,1)S(1)}, bf16[512,1536]{1,0:T(8,128)(2,1)}, u32[]{:S(2)}) copy-start(bf16[512,1536]{1,0:T(8,128)(2,1)} %param.16) | copy-start | bytes 4718596
  0.6 7.9 %copy-start.1 = (bf16[1,128,512]{2,1,0:T(8,128)(2,1)S(1)}, bf16[1,128,512]{2,1,0:T(8,128)(2,1)}, u32[]{:S(2)}) copy-start(bf16[1,128,512]{2,1,0:T(8,128)(2,1)} %param.10) | copy-start | bytes 393220
  0.7 7.9 %copy-start.6 = (bf16[512,512]{1,0:T(8,128)(2,1)S(1)}, bf16[512,512]{1,0:T(8,128)(2,1)}, u32[]{:S(2)}) copy-start(bf16[512,512]{1,0:T(8,128)(2,1)} %param.14) | copy-start | bytes 1572868
  1.8 3.0 %copy-start.16 = (f32[128]{0:T(128)}, f32[128]{0:T(128)S(1)}, u32[]{:S(2)}) copy-start(f32[128]{0:T(128)S(1)} %broadcast_multiply_fusion.2) | copy-start | bytes 1540
  2.9 0.8 copy-start.24
  3.0 1.9 %copy-start.20 = (f32[128]{0:T(128)}, f32[128]{0:T(128)S(1)}, u32[]{:S(2)}) copy-start(f32[128]{0:T(128)S(1)} %fusion.96) | copy-start | bytes 1540
  4.9 3.9 %copy-start.22 = (s32[128]{0:T(128)}, s32[128]{0:T(128)S(1)}, u32[]{:S(2)}) copy-start(s32[128]{0:T(128)S(1)} %fusion.95) | copy-start | bytes 1540
  4.9 4.6 %copy-start.10 = (bf16[1,128,512]{2,1,0:T(8,128)(2,1)S(1)}, bf16[1,128,512]{2,1,0:T(8,128)(2,1)}, u32[]{:S(2)}) copy-start(bf16[1,128,512]{2,1,0:T(8,128)(2,1)} %param.11) | copy-start | bytes 393220
  8.8 0.7 copy-start.8
  10.8 26.7 %all-to-all-start = ((bf16[32,64,128]{2,1,0:T(8,128)(2,1)}), bf16[32,64,128]{2,1,0:T(8,128)(2,1)}, u32[]{:S(2)}, u32[]{:S(2)}) async-start(bf16[32,64,128]{2,1,0:T(8,128)(2,1)} %reshape_reshape.17), calls=%async_computation | async-start | bytes 1048576 | tf_op jit(solution)/shard_map/all_to_all | solution.py:164
  39.1 1.6 %copy-start.7 = (bf16[512,512]{1,0:T(8,128)(2,1)S(1)}, bf16[512,512]{1,0:T(8,128)(2,1)}, u32[]{:S(2)}) copy-start(bf16[512,512]{1,0:T(8,128)(2,1)} %param.17) | copy-start | bytes 1572868
  40.6 0.9 copy-start.14
  40.6 0.9 copy-start.15
  56.2 1.1 copy-start.13
  58.6 1.4 copy-start.23
  59.1 0.9 copy-start.5
  64.7 26.1 %all-to-all-start.1 = ((bf16[32,64,128]{2,1,0:T(8,128)(2,1)}), bf16[32,64,128]{2,1,0:T(8,128)(2,1)}, u32[]{:S(2)}, u32[]{:S(2)}) async-start(bf16[32,64,128]{2,1,0:T(8,128)(2,1)} %reshape_reshape.19), calls=%async_computation.1 | async-start | bytes 1048576 | tf_op jit(solution)/shard_map/all_to_all | solution.py:164
  90.8 32.3 %all-to-all-start.2 = ((bf16[8,64,2048]{2,1,0:T(8,128)(2,1)}), bf16[8,64,2048]{2,1,0:T(8,128)(2,1)}, u32[]{:S(2)}, u32[]{:S(2)}) async-start(bf16[8,64,2048]{2,1,0:T(8,128)(2,1)} %pad_maximum_fusion), calls=%async_computation.2 | async-start | bytes 4194304 | tf_op jit(solution)/shard_map/all_to_all | solution.py:173
  100.2 3.9 %copy-start.3 = (f32[128,1024]{1,0:T(8,128)}, f32[128,1024]{1,0:T(8,128)S(1)}, u32[]{:S(2)}) copy-start(f32[128,1024]{1,0:T(8,128)S(1)} %fusion.82) | copy-start | bytes 1572868
  103.4 0.9 copy-start.12
  103.4 1.5 copy-start.2
  103.4 1.5 copy-start.17
  103.4 1.5 copy-start.19
  104.2 1.5 copy-start.25
  104.9 30.4 %copy-start.18 = (f32[128]{0:T(128)S(1)}, f32[128]{0:T(128)}, u32[]{:S(2)}) copy-start(f32[128]{0:T(128)} %copy-done.16) | copy-start | bytes 1540
  104.9 30.4 %copy-start.21 = (f32[128]{0:T(128)S(1)}, f32[128]{0:T(128)}, u32[]{:S(2)}) copy-start(f32[128]{0:T(128)} %copy-done.20) | copy-start | bytes 1540
  104.9 30.6 %copy-start.4 = (f32[128,1024]{1,0:T(8,128)S(1)}, f32[128,1024]{1,0:T(8,128)}, u32[]{:S(2)}) copy-start(f32[128,1024]{1,0:T(8,128)} %copy-done.3) | copy-start | bytes 1572868
  104.9 30.6 %copy-start.11 = (bf16[1,128,512]{2,1,0:T(8,128)(2,1)S(1)}, bf16[1,128,512]{2,1,0:T(8,128)(2,1)}, u32[]{:S(2)}) copy-start(bf16[1,128,512]{2,1,0:T(8,128)(2,1)} %param.11) | copy-start | bytes 393220
  105.7 46.9 %copy-start.9 = (bf16[128,512]{1,0:T(8,128)(2,1)S(1)}, bf16[128,512]{1,0:T(8,128)(2,1)}, u32[]{:S(2)}) copy-start(bf16[128,512]{1,0:T(8,128)(2,1)} %copy-done.8) | copy-start | bytes 393220
  125.9 19.1 %all-to-all-start.3 = ((bf16[32,32,128]{2,1,0:T(8,128)(2,1)}), bf16[32,32,128]{2,1,0:T(8,128)(2,1)S(1)}, u32[]{:S(2)}, u32[]{:S(2)}) async-start(bf16[32,32,128]{2,1,0:T(8,128)(2,1)} %reshape_reshape.21), calls=%async_computation.3 | async-start | bytes 524288 | tf_op jit(solution)/shard_map/all_to_all | solution.py:164
  145.7 12.2 %all-to-all-start.4 = ((f32[8,32,128]{2,1,0:T(8,128)}), f32[8,32,128]{2,1,0:T(8,128)S(1)}, u32[]{:S(2)}, u32[]{:S(2)}) async-start(f32[8,32,128]{2,1,0:T(8,128)} %broadcast_in_dim.161), calls=%async_computation.4 | async-start | bytes 262144 | tf_op jit(solution)/shard_map/all_to_all | solution.py:164

commit v11 on v10

--- a/solution.py
+++ b/solution.py
@@ -165,19 +165,11 @@
     return moved.reshape(pieces.shape)
 
 
-def reduce_weight_terms(partial, replicas, owners):
+def replica_sums(partial, replicas):
     rows, width = partial.shape
-    per_replica = rows // replicas
-    per_device = per_replica // owners
-    terms = partial.astype(jnp.bfloat16).reshape(replicas, per_replica, width)
+    terms = partial.astype(jnp.bfloat16).reshape(replicas, rows // replicas, width)
     terms = lax.all_to_all(terms, "dp", 0, 0, tiled=True)
-    terms = jnp.sum(terms.astype(jnp.float32), axis=0).astype(jnp.bfloat16)
-    terms = terms.reshape(owners, per_device, width)
-    terms = dense_all_to_all(terms, "ev")
-    piece = jnp.sum(terms.astype(jnp.float32), axis=0)
-    copies = jnp.broadcast_to(piece[None], (replicas, per_device, width))
-    gathered = dense_all_to_all(copies, "dp")
-    return gathered.reshape(replicas * per_device, width)
+    return jnp.sum(terms.astype(jnp.float32), axis=0).astype(jnp.bfloat16)
 
 
 def on_device(
@@ -236,16 +228,6 @@
         cross_input_weight,
         cross_output_weight,
     )
-    going_back = jnp.concatenate([result, back_rows.astype(jnp.bfloat16)], axis=1)
-    came_back = dense_all_to_all(going_back.reshape(owners, row_capacity, -1), "ev").reshape(
-        going_back.shape
-    )
-    picked = lax.dot_general(
-        placement, came_back, (((0,), (0,)), ((), ())), preferred_element_type=jnp.float32
-    )
-    layer_out = (hidden.astype(jnp.float32) + picked[:, :features]).astype(jnp.bfloat16)
-    grad_hidden = (upstream.astype(jnp.float32) + picked[:, features:]).astype(jnp.bfloat16)
-    grad_rows = intra_pull(grad_hidden)[0]
     factor = (replicas * owners * local_rows) ** (-0.5)
     partial_sum = jnp.concatenate(
         [
@@ -254,7 +236,24 @@
         ],
         axis=1,
     )
-    portion = reduce_weight_terms(partial_sum, replicas, owners) * factor
+    weight_terms = replica_sums(partial_sum, replicas)
+    going_back = jnp.concatenate([result, back_rows.astype(jnp.bfloat16)], axis=1)
+    payload = jnp.concatenate(
+        [going_back.reshape(owners, -1, 128), weight_terms.reshape(owners, -1, 128)], axis=1
+    )
+    arrived = lax.all_to_all(payload, "ev", 0, 0, tiled=True)
+    split_at = going_back.size // owners // 128
+    came_back = arrived[:, :split_at].reshape(going_back.shape)
+    owner_terms = arrived[:, split_at:].reshape(owners, -1, weight_terms.shape[1])
+    piece = jnp.sum(owner_terms.astype(jnp.float32), axis=0)
+    copies = jnp.broadcast_to(piece[None], (replicas,) + piece.shape)
+    portion = dense_all_to_all(copies, "dp").reshape(-1, piece.shape[1]) * factor
+    picked = lax.dot_general(
+        placement, came_back, (((0,), (0,)), ((), ())), preferred_element_type=jnp.float32
+    )
+    layer_out = (hidden.astype(jnp.float32) + picked[:, :features]).astype(jnp.bfloat16)
+    grad_hidden = (upstream.astype(jnp.float32) + picked[:, features:]).astype(jnp.bfloat16)
+    grad_rows = intra_pull(grad_hidden)[0]
     return (
         layer_out[None],
         grad_rows[None],

time: 161 us -> 181 us (1.12)
  waiting for transfers between devices: 35.6 us -> 46.6 us
  matrix products: 25.5 us -> 34.3 us
  starting transfers between devices: 41.8 us -> 33.3 us
  other arithmetic: 20.9 us -> 28.7 us
    all_to_all x1 -> x2, waiting for transfers between devices: 17.3 us -> 41.4 us  [the longest x1 21.8 us: replica_sums(): terms = lax.all_to_all(terms, 'dp', 0, 0, tiled=True)]
    all_to_all x4 -> x2, starting transfers between devices: 35.9 us -> 20.1 us  [dense_all_to_all(): moved = lax.all_to_all(flat, axis_name, 0, 0, tiled=True)]
    all_to_all x4 -> x2, waiting for transfers between devices: 18.3 us -> 5.22 us  [dense_all_to_all(): moved = lax.all_to_all(flat, axis_name, 0, 0, tiled=True)]
    all_to_all x1 -> x2, starting transfers between devices: 5.95 us -> 13.2 us  [the longest x1 7.56 us: replica_sums(): terms = lax.all_to_all(terms, 'dp', 0, 0, tiled=True)]
    reduce_sum x2 -> x3, other arithmetic: 2.01 us -> 6.73 us  [the longest x1 2.98 us: cross_account_inner(): weights = jnp.where(allowed, jnp.exp(scores - highest), 0.0)]
    reshape x0 -> x3, local copies, waits for them, and re-layouts: none -> 4.06 us  [the longest x1 1.77 us: on_device(): weight_terms.reshape(owners, -1, 128)]
    convert_element_type x1 -> x0, other arithmetic: 3 us -> none  [cross_account_inner(): (weights / jnp.sum(weights, axis=-1, keepdims=True)).astype(jnp.bfloat16)]
    another operation x3 -> x1, local copies, waits for them, and re-layouts: 3.91 us -> 1.03 us  [dense_all_to_all(): flat = pieces.reshape(count, -1, 128)]
  transfers between devices with their start and end apart: 5 -> 4, of which waited for: 4 -> 4; matrix products, arithmetic and copies ran while one was open for 22% -> 8% of each run, Pallas kernels for 0% -> 0%
where the time goes in v11:
time: 181 us; the launch traced here: 179 us
  waiting for transfers between devices  46.6 us (26%)
  matrix products  34.3 us (19%)
  starting transfers between devices  33.3 us (18%)
  local copies, waits for them, and re-layouts  30.8 us (17%)
  other arithmetic  28.7 us (16%)
  between operations  5.31 us (3%)
    all_to_all x1, waiting for transfers between devices, replica_sums(): terms = lax.all_to_all(terms, 'dp', 0, 0, tiled=True)  21.8 us
    all_to_all x2, starting transfers between devices, dense_all_to_all(): moved = lax.all_to_all(flat, axis_name, 0, 0, tiled=True)  20.1 us
    all_to_all x1, waiting for transfers between devices, on_device(): arrived = lax.all_to_all(payload, 'ev', 0, 0, tiled=True)  19.6 us
    dot_general x3, matrix products, cross_account_inner(): jnp.einsum('bhqf,bkf->bhqk', masked_queries, key_rows) * HEAD_DIM ** (-0.5)  8.92 us
    all_to_all x1, starting transfers between devices, replica_sums(): terms = lax.all_to_all(terms, 'dp', 0, 0, tiled=True)  7.56 us
    dot_general x3, matrix products, cross_account_inner(): jnp.einsum('bhqk,bkf->bhqf', attention.astype(jnp.float32), value_rows)  6.16 us
    all_to_all x1, starting transfers between devices, on_device(): arrived = lax.all_to_all(payload, 'ev', 0, 0, tiled=True)  5.63 us
    all_to_all x2, waiting for transfers between devices, dense_all_to_all(): moved = lax.all_to_all(flat, axis_name, 0, 0, tiled=True)  5.22 us
  transfers between devices with their start and end apart: 4, of which 4 were waited for; matrix products, arithmetic and copies ran while one was open for 8% of the time, Pallas kernels for 0%

profile of v11, /device:TPU:1, one launch (start us, length us, event | category | flops | bytes accessed | tf_op | source)
XLA Modules:
  0.0 179.0 jit_solution(12619501692951299119)
XLA Ops:
  0.7 1.2 convert_reduce_fusion.5
  1.9 1.1 fusion.60
  5.4 1.9 %convolution_convert_fusion.2 = bf16[128,1536]{1,0:T(8,128)(2,1)S(1)} fusion(bf16[512,1536]{1,0:T(8,128)(2,1)} %param.13, bf16[1,128,512]{2,1,0:T(8,128)(2,1)} %param.10, f32[512]{0:T(512)} %param.12, f32[128]{0:T(128)S(1)} %fusion.96, f32[128]{0:T(128)S(1)} %broadcast_multiply_fusion.2), kind=kOutput, calls=%fused_computation.25 | convolution fusion | flops 201850880 | bytes 2100224 | tf_op jit(solution)/shard_map/jvp()/dot_general | solution.py:38
  10.3 1.0 reshape_reshape.8
  11.3 12.1 %all-to-all-start = ((bf16[32,64,128]{2,1,0:T(8,128)(2,1)}), bf16[32,64,128]{2,1,0:T(8,128)(2,1)}, u32[]{:S(2)}, u32[]{:S(2)}) async-start(bf16[32,64,128]{2,1,0:T(8,128)(2,1)} %reshape_reshape.8), calls=%async_computation | async-start | bytes 1048576 | tf_op jit(solution)/shard_map/all_to_all | solution.py:164
  25.3 1.5 fusion.120
  29.4 1.3 convert_reduce_fusion.4
  33.0 4.9 %all-to-all-done = bf16[32,64,128]{2,1,0:T(8,128)(2,1)} async-done(((bf16[32,64,128]{2,1,0:T(8,128)(2,1)}), bf16[32,64,128]{2,1,0:T(8,128)(2,1)}, u32[]{:S(2)}, u32[]{:S(2)}) %all-to-all-start) | async-done | bytes 524320 | tf_op jit(solution)/shard_map/all_to_all | solution.py:164
  38.0 1.3 reshape_reshape.9
  40.2 1.4 convolution_convert_fusion.1
  42.6 1.4 fusion.122
  44.0 1.2 fusion.22
  45.2 2.0 %fusion.12 = (f32[2,8,128]{2,1,0:T(8,128)S(1)}, bf16[2,8,128,384]{3,2,1,0:T(8,128)(2,1)S(1)}) fusion(f32[2,8,128,384]{3,2,1,0:T(8,128)S(1)} %get-tuple-element.69, f32[2,8,128]{2,1,0:T(8,128)S(1)} %multiply_divide_fusion, f32[2,8,128]{2,1,0:T(8,128)S(1)} %get-tuple-element.68, pred[2,128,384]{2,1,0:T(8,128)(4,1)S(1)} %copy-done.14, ...), kind=kOutput, calls=%fused_computation.16 | convolution fusion | flops 811464704 | bytes 6168576 | tf_op jit(solution)/shard_map/transpose(jvp(bhqk,bkf->bhqf))/dot_general | solution.py:105
  47.2 3.0 %fusion.116 = (f32[2,8,128]{2,1,0:T(8,128)S(1)}, bf16[2,8,128,384]{3,2,1,0:T(8,128)(2,1)S(1)}, f32[2,8,128]{2,1,0:T(8,128)S(1)}, pred[2,8,128,384]{3,2,1,0:T(32,128)(4,1)S(1)}) fusion(f32[2,8,128,384]{3,2,1,0:T(8,128)S(1)} %get-tuple-element.69, f32[2,8,128]{2,1,0:T(8,128)S(1)} %get-tuple-element.68, f32[2,8,128]{2,1,0:T(8,128)S(1)} %neg.25, ...), kind=kLoop, calls=%fused_computation.237 | loop fusion | flops 10219520 | bytes 7217152 | tf_op jit(solution)/shard_map/transpose(jvp())/reduce_sum | solution.py:103
  50.2 3.6 %multiply_reduce_fusion = f32[2,128,512]{2,1,0:T(8,128)} fusion(f32[8,512]{1,0:T(8,128)S(1)} %copy-done.16, pred[2,8,128,384]{3,2,1,0:T(32,128)(4,1)S(1)} %get-tuple-element.15, f32[2,8,128]{2,1,0:T(8,128)S(1)} %negate_divide_fusion, pred[2,128,384]{2,1,0:T(8,128)(4,1)S(1)} %copy-done.14, bf16[1,384,512]{2,1,0:T(8,128)(2,1)S(1)} %get-tuple-element.78, ...), kind=kOutput, calls=%fused_computation.8 | convolution fusion | flops 815529984 | bytes 6963200 | tf_op jit(solution)/shard_map/transpose(jvp(bhqf,bkf->bhqk))/dot_general | solution.py:100
  53.8 3.9 %fusion.36 = f32[2,384,512]{2,1,0:T(8,128)} fusion(f32[8,512]{1,0:T(8,128)S(1)} %copy-done.16, f32[2,128,512]{2,1,0:T(8,128)S(1)} %slice.176, pred[2,8,128,384]{3,2,1,0:T(32,128)(4,1)S(1)} %get-tuple-element.15, f32[2,8,128]{2,1,0:T(8,128)S(1)} %negate_divide_fusion, pred[2,128,384]{2,1,0:T(8,128)(4,1)S(1)} %copy-done.14, ...), kind=kOutput, calls=%fused_computation.49 | convolution fusion | flops 814219264 | bytes 7749632 | tf_op jit(solution)/shard_map/transpose(jvp(bhqf,bkf->bhqk))/dot_general | solution.py:100
  57.8 2.0 %multiply_reduce_fusion.1 = bf16[2,128,512]{2,1,0:T(8,128)(2,1)} fusion(bf16[2,8,128,384]{3,2,1,0:T(8,128)(2,1)S(1)} %get-tuple-element.13, f32[8,512]{1,0:T(8,128)S(1)} %copy-done.16, bf16[1,384,512]{2,1,0:T(8,128)(2,1)S(1)} %get-tuple-element.81, bf16[1,384,512]{2,1,0:T(8,128)(2,1)S(1)} %get-tuple-element.79), kind=kOutput, calls=%fused_computation.9 | convolution fusion | flops 807665664 | bytes 2637824 | tf_op jit(solution)/shard_map/jvp(bhqk,bkf->bhqf)/dot_general | solution.py:105
  59.7 2.2 %fusion.39 = f32[2,384,512]{2,1,0:T(8,128)} fusion(bf16[2,8,128,384]{3,2,1,0:T(8,128)(2,1)S(1)} %get-tuple-element.13, f32[2,128,512]{2,1,0:T(8,128)S(1)} %bitcast_convert_fusion, f32[8,512]{1,0:T(8,128)S(1)} %copy-done.16), kind=kOutput, calls=%fused_computation.50 | convolution fusion | flops 806354944 | bytes 3686400 | tf_op jit(solution)/shard_map/transpose(jvp(bhqk,bkf->bhqf))/dot_general | solution.py:105
  61.9 1.8 %copy.77 = bf16[256,512]{0,1:T(8,128)(2,1)} copy(bf16[256,512]{1,0:T(8,128)(2,1)} %bitcast.211) | data formatting | bytes 524288 | tf_op jit(solution)/shard_map/jvp()/convert_element_type | solution.py:107
  63.7 1.8 reshape.381
  65.5 1.7 copy.78
  67.2 1.7 dot_general.95
  69.0 2.1 %convolution_convert_fusion.3 = bf16[8,64,512]{2,1,0:T(8,128)(2,1)} fusion(bf16[8,64,256]{2,1,0:T(8,128)(2,1)} %dot_general.95, bf16[256,1024]{1,0:T(8,128)(2,1)S(1)} %reshape_reshape.9), kind=kOutput, calls=%fused_computation.51 | convolution fusion | flops 134479872 | bytes 1048576 | tf_op jit(solution)/shard_map/dot_general | solution.py:158
  71.1 1.7 slice_select_fusion.23
  75.2 1.7 fusion.118
  76.9 1.9 %copy.75 = bf16[512,256]{1,0:T(8,128)(2,1)} copy(bf16[512,256]{0,1:T(8,128)(2,1)} %get-tuple-element.53) | data formatting | bytes 524288 | tf_op jit(solution)/shard_map/transpose | solution.py:156
  78.7 1.7 reshape.380
  80.5 1.7 copy.76
  82.2 1.7 dot_general.93
  84.0 1.8 convolution_convert_fusion
  85.8 1.6 pad_maximum_fusion
  87.3 7.6 %all-to-all-start.1 = ((bf16[8,64,2048]{2,1,0:T(8,128)(2,1)}), bf16[8,64,2048]{2,1,0:T(8,128)(2,1)}, u32[]{:S(2)}, u32[]{:S(2)}) async-start(bf16[8,64,2048]{2,1,0:T(8,128)(2,1)} %pad_maximum_fusion), calls=%async_computation.1 | async-start | bytes 4194304 | tf_op jit(solution)/shard_map/all_to_all | solution.py:171
  94.9 1.1 add_convert_fusion.2
  96.1 1.2 convolution_convert_fusion.7
  98.2 1.3 reshape.379
  99.4 21.8 %all-to-all-done.1 = bf16[8,64,2048]{2,1,0:T(8,128)(2,1)} async-done(((bf16[8,64,2048]{2,1,0:T(8,128)(2,1)}), bf16[8,64,2048]{2,1,0:T(8,128)(2,1)}, u32[]{:S(2)}, u32[]{:S(2)}) %all-to-all-start.1) | async-done | bytes 2097184 | tf_op jit(solution)/shard_map/all_to_all | solution.py:171
  121.2 2.7 %reduce_sum.255 = bf16[64,2048]{1,0:T(8,128)(2,1)} reduce(bf16[8,64,2048]{2,1,0:T(8,128)(2,1)} %all-to-all-done.1, bf16[]{:T(256)} %constant.95.clone.1), dimensions={0}, to_apply=%region_18.19 | reduce | flops 917504 | bytes 2359298 | tf_op jit(solution)/shard_map/reduce_sum | solution.py:172
  123.9 1.8 reshape.382
  125.7 1.9 %pad_maximum_fusion.1 = bf16[32,96,128]{2,1,0:T(8,128)(2,1)} fusion(bf16[32,32,128]{2,1,0:T(8,128)(2,1)} %reshape.382, bf16[32,64,128]{2,1,0:T(8,128)(2,1)S(1)} %reshape.379), kind=kLoop, calls=%fused_computation.73 | loop fusion | flops 1572864 | bytes 1572864 | tf_op jit(solution)/shard_map/concatenate | solution.py:241
  127.6 5.6 %all-to-all-start.2 = ((bf16[32,96,128]{2,1,0:T(8,128)(2,1)}), bf16[32,96,128]{2,1,0:T(8,128)(2,1)}, u32[]{:S(2)}, u32[]{:S(2)}) async-start(bf16[32,96,128]{2,1,0:T(8,128)(2,1)} %pad_maximum_fusion.1), calls=%async_computation.2 | async-start | bytes 1572864 | tf_op jit(solution)/shard_map/all_to_all | solution.py:244
  133.3 19.6 %all-to-all-done.2 = bf16[32,96,128]{2,1,0:T(8,128)(2,1)} async-done(((bf16[32,96,128]{2,1,0:T(8,128)(2,1)}), bf16[32,96,128]{2,1,0:T(8,128)(2,1)}, u32[]{:S(2)}, u32[]{:S(2)}) %all-to-all-start.2) | async-done | bytes 786464 | tf_op jit(solution)/shard_map/all_to_all | solution.py:244
  152.9 1.1 slice.182
  154.0 1.0 reshape.383
  155.0 1.3 fusion.82
  156.4 2.0 %convolution_convert_fusion.9 = bf16[128,512]{1,0:T(8,128)(2,1)} fusion(bf16[512,512]{1,0:T(8,128)(2,1)} %param.14, f32[128,1024]{1,0:T(8,128)S(1)} %fusion.82, bf16[1,128,512]{2,1,0:T(8,128)(2,1)S(1)} %copy-done.10), kind=kOutput, calls=%fused_computation.65 | convolution fusion | flops 67371008 | bytes 1048576 | tf_op jit(solution)/shard_map/transpose(jvp())/dot_general | solution.py:49
  164.5 7.9 %all-to-all-start.3 = ((f32[8,32,128]{2,1,0:T(8,128)}), f32[8,32,128]{2,1,0:T(8,128)S(1)}, u32[]{:S(2)}, u32[]{:S(2)}) async-start(f32[8,32,128]{2,1,0:T(8,128)} %broadcast_in_dim.161), calls=%async_computation.3 | async-start | bytes 262144 | tf_op jit(solution)/shard_map/all_to_all | solution.py:164
  172.5 1.1 add_convert_fusion.1
  173.6 2.1 %fusion.63 = (f32[128]{0:T(128)S(1)}, f32[128,512]{1,0:T(8,128)S(1)}) fusion(bf16[1,128,512]{2,1,0:T(8,128)(2,1)S(1)} %copy-done.1, f32[128]{0:T(128)S(1)} %copy-done.18, f32[512]{0:T(512)} %param.12, bf16[128,1536]{0,1:T(8,128)(2,1)S(1)} %bitcast.204, bf16[512,1536]{1,0:T(8,128)(2,1)} %param.13), kind=kOutput, calls=%fused_computation.111 | convolution fusion | flops 201785216 | bytes 2362368 | tf_op jit(solution)/shard_map/transpose(jvp())/dot_general | solution.py:38
  (136 shorter events, 22.4 us)
Async XLA Ops:
  0.6 39.5 %copy-start = (bf16[512,1536]{1,0:T(8,128)(2,1)S(1)}, bf16[512,1536]{1,0:T(8,128)(2,1)}, u32[]{:S(2)}) copy-start(bf16[512,1536]{1,0:T(8,128)(2,1)} %param.16) | copy-start | bytes 4718596
  0.6 8.4 %copy-start.1 = (bf16[1,128,512]{2,1,0:T(8,128)(2,1)S(1)}, bf16[1,128,512]{2,1,0:T(8,128)(2,1)}, u32[]{:S(2)}) copy-start(bf16[1,128,512]{2,1,0:T(8,128)(2,1)} %param.10) | copy-start | bytes 393220
  0.7 8.4 %copy-start.3 = (bf16[512,512]{1,0:T(8,128)(2,1)S(1)}, bf16[512,512]{1,0:T(8,128)(2,1)}, u32[]{:S(2)}) copy-start(bf16[512,512]{1,0:T(8,128)(2,1)} %param.14) | copy-start | bytes 1572868
  1.8 5.7 %copy-start.17 = (f32[128]{0:T(128)}, f32[128]{0:T(128)S(1)}, u32[]{:S(2)}) copy-start(f32[128]{0:T(128)S(1)} %broadcast_multiply_fusion.2) | copy-start | bytes 1540
  2.9 0.6 copy-start.28
  3.0 4.6 %copy-start.21 = (f32[128]{0:T(128)}, f32[128]{0:T(128)S(1)}, u32[]{:S(2)}) copy-start(f32[128]{0:T(128)S(1)} %fusion.96) | copy-start | bytes 1540
  5.4 3.9 %copy-start.23 = (s32[128]{0:T(128)}, s32[128]{0:T(128)S(1)}, u32[]{:S(2)}) copy-start(s32[128]{0:T(128)S(1)} %fusion.95) | copy-start | bytes 1540
  5.4 4.6 %copy-start.10 = (bf16[1,128,512]{2,1,0:T(8,128)(2,1)S(1)}, bf16[1,128,512]{2,1,0:T(8,128)(2,1)}, u32[]{:S(2)}) copy-start(bf16[1,128,512]{2,1,0:T(8,128)(2,1)} %param.11) | copy-start | bytes 393220
  9.3 0.7 copy-start.8
  11.3 26.7 %all-to-all-start = ((bf16[32,64,128]{2,1,0:T(8,128)(2,1)}), bf16[32,64,128]{2,1,0:T(8,128)(2,1)}, u32[]{:S(2)}, u32[]{:S(2)}) async-start(bf16[32,64,128]{2,1,0:T(8,128)(2,1)} %reshape_reshape.8), calls=%async_computation | async-start | bytes 1048576 | tf_op jit(solution)/shard_map/all_to_all | solution.py:164
  39.6 0.6 copy-start.19
  40.2 1.4 copy-start.24
  40.2 1.6 copy-start.4
  41.7 0.9 copy-start.14
  41.7 0.9 copy-start.16
  69.0 3.9 %copy-start.7 = (f32[2,384,512]{2,1,0:T(8,128)S(1)}, f32[2,384,512]{2,1,0:T(8,128)}, u32[]{:S(2)}) copy-start(f32[2,384,512]{2,1,0:T(8,128)} %fusion.36) | copy-start | bytes 4718596
  73.3 1.0 copy-start.15
  73.7 0.8 copy-start.27
  74.4 0.8 copy-start.20
  74.4 0.8 copy-start.25
  74.5 2.4 %copy-start.2 = (bf16[2,128,1536]{2,1,0:T(8,128)(2,1)}, bf16[2,128,1536]{2,1,0:T(8,128)(2,1)S(1)}, u32[]{:S(2)}) copy-start(bf16[2,128,1536]{2,1,0:T(8,128)(2,1)S(1)} %add_convert_fusion) | copy-start | bytes 2359300
  76.9 8.9 %copy-start.6 = (bf16[8,64,512]{2,1,0:T(8,128)(2,1)S(1)}, bf16[8,64,512]{2,1,0:T(8,128)(2,1)}, u32[]{:S(2)}) copy-start(bf16[8,64,512]{2,1,0:T(8,128)(2,1)} %convolution_convert_fusion.3) | copy-start | bytes 1572868
  87.3 7.6 %copy-start.26 = (f32[256]{0:T(256)S(1)}, f32[256]{0:T(256)}, u32[]{:S(2)}) copy-start(f32[256]{0:T(256)} %get-tuple-element.8) | copy-start | bytes 3076
  87.3 8.7 %copy-start.5 = (bf16[512,512]{1,0:T(8,128)(2,1)S(1)}, bf16[512,512]{1,0:T(8,128)(2,1)}, u32[]{:S(2)}) copy-start(bf16[512,512]{1,0:T(8,128)(2,1)} %param.17) | copy-start | bytes 1572868
  87.3 33.9 %all-to-all-start.1 = ((bf16[8,64,2048]{2,1,0:T(8,128)(2,1)}), bf16[8,64,2048]{2,1,0:T(8,128)(2,1)}, u32[]{:S(2)}, u32[]{:S(2)}) async-start(bf16[8,64,2048]{2,1,0:T(8,128)(2,1)} %pad_maximum_fusion), calls=%async_computation.1 | async-start | bytes 4194304 | tf_op jit(solution)/shard_map/all_to_all | solution.py:171
  127.6 25.3 %all-to-all-start.2 = ((bf16[32,96,128]{2,1,0:T(8,128)(2,1)}), bf16[32,96,128]{2,1,0:T(8,128)(2,1)}, u32[]{:S(2)}, u32[]{:S(2)}) async-start(bf16[32,96,128]{2,1,0:T(8,128)(2,1)} %pad_maximum_fusion.1), calls=%async_computation.2 | async-start | bytes 1572864 | tf_op jit(solution)/shard_map/all_to_all | solution.py:244
  159.4 1.5 copy-start.12
  160.4 12.1 %copy-start.13 = (f32[1,1,8,128,64]{3,4,2,1,0:T(8,128)S(1)}, f32[1,1,8,128,64]{3,4,2,1,0:T(8,128)}, u32[]{:S(2)}) copy-start(f32[1,1,8,128,64]{3,4,2,1,0:T(8,128)} %convolution_bitcast_fusion.2) | copy-start | bytes 786436
  160.7 12.9 %copy-start.18 = (f32[128]{0:T(128)S(1)}, f32[128]{0:T(128)}, u32[]{:S(2)}) copy-start(f32[128]{0:T(128)} %copy-done.17) | copy-start | bytes 1540
  160.9 14.8 %copy-start.29 = (f32[128]{0:T(128)S(1)}, f32[128]{0:T(128)}, u32[]{:S(2)}) copy-start(f32[128]{0:T(128)} %copy-done.28) | copy-start | bytes 1540
  160.9 14.8 %copy-start.22 = (f32[128]{0:T(128)S(1)}, f32[128]{0:T(128)}, u32[]{:S(2)}) copy-start(f32[128]{0:T(128)} %copy-done.21) | copy-start | bytes 1540
  160.9 15.0 %copy-start.11 = (bf16[1,128,512]{2,1,0:T(8,128)(2,1)S(1)}, bf16[1,128,512]{2,1,0:T(8,128)(2,1)}, u32[]{:S(2)}) copy-start(bf16[1,128,512]{2,1,0:T(8,128)(2,1)} %param.11) | copy-start | bytes 393220
  161.9 14.9 %copy-start.9 = (bf16[128,512]{1,0:T(8,128)(2,1)S(1)}, bf16[128,512]{1,0:T(8,128)(2,1)}, u32[]{:S(2)}) copy-start(bf16[128,512]{1,0:T(8,128)(2,1)} %copy-done.8) | copy-start | bytes 393220
  164.5 13.2 %all-to-all-start.3 = ((f32[8,32,128]{2,1,0:T(8,128)}), f32[8,32,128]{2,1,0:T(8,128)S(1)}, u32[]{:S(2)}, u32[]{:S(2)}) async-start(f32[8,32,128]{2,1,0:T(8,128)} %broadcast_in_dim.161), calls=%async_computation.3 | async-start | bytes 262144 | tf_op jit(solution)/shard_map/all_to_all | solution.py:164

commit v12 on v10

--- a/solution.py
+++ b/solution.py
@@ -167,17 +167,16 @@
 
 def reduce_weight_terms(partial, replicas, owners):
     rows, width = partial.shape
-    per_replica = rows // replicas
-    per_device = per_replica // owners
-    terms = partial.astype(jnp.bfloat16).reshape(replicas, per_replica, width)
+    per_device = rows // replicas // owners
+    lanes = per_device * width // 128
+    terms = partial.astype(jnp.bfloat16).reshape(replicas, owners, lanes, 128)
     terms = lax.all_to_all(terms, "dp", 0, 0, tiled=True)
     terms = jnp.sum(terms.astype(jnp.float32), axis=0).astype(jnp.bfloat16)
-    terms = terms.reshape(owners, per_device, width)
-    terms = dense_all_to_all(terms, "ev")
-    piece = jnp.sum(terms.astype(jnp.float32), axis=0)
-    copies = jnp.broadcast_to(piece[None], (replicas, per_device, width))
-    gathered = dense_all_to_all(copies, "dp")
-    return gathered.reshape(replicas * per_device, width)
+    terms = lax.all_to_all(terms, "ev", 0, 0, tiled=True)
+    piece = jnp.sum(terms.astype(jnp.float32), axis=0).astype(jnp.bfloat16)
+    copies = jnp.broadcast_to(piece[None], (replicas,) + piece.shape)
+    gathered = lax.all_to_all(copies, "dp", 0, 0, tiled=True)
+    return gathered.reshape(replicas * per_device, width).astype(jnp.float32)
 
 
 def on_device(

time: 161 us -> 165 us (1.025)
  local copies, waits for them, and re-layouts: 30.2 us -> 34.1 us
    all_to_all x4 -> x2, starting transfers between devices: 35.9 us -> 19.5 us  [dense_all_to_all(): moved = lax.all_to_all(flat, axis_name, 0, 0, tiled=True)]
    all_to_all x0 -> x2, starting transfers between devices: none -> 16.3 us  [the longest x1 9.43 us: reduce_weight_terms(): terms = lax.all_to_all(terms, 'ev', 0, 0, tiled=True)]
    all_to_all x4 -> x2, waiting for transfers between devices: 18.3 us -> 5.06 us  [dense_all_to_all(): moved = lax.all_to_all(flat, axis_name, 0, 0, tiled=True)]
    all_to_all x0 -> x2, waiting for transfers between devices: none -> 12.8 us  [the longest x1 8.59 us: reduce_weight_terms(): terms = lax.all_to_all(terms, 'ev', 0, 0, tiled=True)]
    convert_element_type x0 -> x1, local copies, waits for them, and re-layouts: none -> 4.2 us  [reduce_weight_terms(): terms = partial.astype(jnp.bfloat16).reshape(replicas, owners, lanes, 128)]
    reshape x0 -> x2, local copies, waits for them, and re-layouts: none -> 3.51 us  [ordered_contract(): flipped = jnp.swapaxes(flipped, 0, 1).reshape(features, rows)]
    dot_general x2 -> x0, local copies, waits for them, and re-layouts: 3.51 us -> none  [ordered_contract(): return jnp.dot(flipped, right_part, preferred_element_type=jnp.float32)]
    another operation x3 -> x2, local copies, waits for them, and re-layouts: 3.91 us -> 3.12 us  [dense_all_to_all(): flat = pieces.reshape(count, -1, 128)]
  transfers between devices with their start and end apart: 5 -> 5, of which waited for: 4 -> 4; matrix products, arithmetic and copies ran while one was open for 22% -> 24% of each run, Pallas kernels for 0% -> 0%
where the time goes in v12:
time: 165 us; the launch traced here: 163 us
  starting transfers between devices  41.8 us (25%)
  waiting for transfers between devices  35.2 us (21%)
  local copies, waits for them, and re-layouts  34.1 us (21%)
  matrix products  25.5 us (15%)
  other arithmetic  21.5 us (13%)
  between operations  5.24 us (3%)
    all_to_all x2, starting transfers between devices, dense_all_to_all(): moved = lax.all_to_all(flat, axis_name, 0, 0, tiled=True)  19.5 us
    all_to_all x1, waiting for transfers between devices, reduce_weight_terms(): terms = lax.all_to_all(terms, 'dp', 0, 0, tiled=True)  17.4 us
    all_to_all x1, starting transfers between devices, reduce_weight_terms(): terms = lax.all_to_all(terms, 'ev', 0, 0, tiled=True)  9.43 us
    all_to_all x1, waiting for transfers between devices, reduce_weight_terms(): terms = lax.all_to_all(terms, 'ev', 0, 0, tiled=True)  8.59 us
    dot_general x3, matrix products, cross_account_inner(): jnp.einsum('bhqf,bkf->bhqk', masked_queries, key_rows) * HEAD_DIM ** (-0.5)  7.17 us
    all_to_all x1, starting transfers between devices, reduce_weight_terms(): gathered = lax.all_to_all(copies, 'dp', 0, 0, tiled=True)  6.92 us
    all_to_all x1, starting transfers between devices, reduce_weight_terms(): terms = lax.all_to_all(terms, 'dp', 0, 0, tiled=True)  5.94 us
    all_to_all x2, waiting for transfers between devices, dense_all_to_all(): moved = lax.all_to_all(flat, axis_name, 0, 0, tiled=True)  5.06 us
  transfers between devices with their start and end apart: 5, of which 4 were waited for; matrix products, arithmetic and copies ran while one was open for 24% of the time, Pallas kernels for 0%

profile of v12, /device:TPU:1, one launch (start us, length us, event | category | flops | bytes accessed | tf_op | source)
XLA Modules:
  0.0 163.3 jit_solution(13679364780769193233)
XLA Ops:
  0.7 1.2 convert_reduce_fusion.4
  1.9 1.1 fusion.60
  5.4 1.9 %convolution_convert_fusion.2 = bf16[128,1536]{1,0:T(8,128)(2,1)S(1)} fusion(bf16[512,1536]{1,0:T(8,128)(2,1)} %param.13, bf16[1,128,512]{2,1,0:T(8,128)(2,1)} %param.10, f32[512]{0:T(512)} %param.12, f32[128]{0:T(128)S(1)} %fusion.95, f32[128]{0:T(128)S(1)} %broadcast_multiply_fusion.1), kind=kOutput, calls=%fused_computation.25 | convolution fusion | flops 201850880 | bytes 2100224 | tf_op jit(solution)/shard_map/jvp()/dot_general | solution.py:38
  8.0 0.8 convert_reduce_fusion.2
  10.3 1.0 reshape_reshape.13
  11.3 12.2 %all-to-all-start = ((bf16[32,64,128]{2,1,0:T(8,128)(2,1)}), bf16[32,64,128]{2,1,0:T(8,128)(2,1)}, u32[]{:S(2)}, u32[]{:S(2)}) async-start(bf16[32,64,128]{2,1,0:T(8,128)(2,1)} %reshape_reshape.13), calls=%async_computation | async-start | bytes 1048576 | tf_op jit(solution)/shard_map/all_to_all | solution.py:164
  25.3 1.5 fusion.119
  29.3 1.3 convert_reduce_fusion.3
  32.9 5.1 %all-to-all-done = bf16[32,64,128]{2,1,0:T(8,128)(2,1)} async-done(((bf16[32,64,128]{2,1,0:T(8,128)(2,1)}), bf16[32,64,128]{2,1,0:T(8,128)(2,1)}, u32[]{:S(2)}, u32[]{:S(2)}) %all-to-all-start) | async-done | bytes 524320 | tf_op jit(solution)/shard_map/all_to_all | solution.py:164
  38.0 1.3 reshape_reshape.14
  39.6 1.4 convolution_convert_fusion.1
  42.0 1.4 fusion.121
  43.4 1.2 fusion.22
  44.7 2.0 %fusion.12 = (f32[2,8,128]{2,1,0:T(8,128)S(1)}, bf16[2,8,128,384]{3,2,1,0:T(8,128)(2,1)S(1)}) fusion(f32[2,8,128,384]{3,2,1,0:T(8,128)S(1)} %get-tuple-element.69, f32[2,8,128]{2,1,0:T(8,128)S(1)} %multiply_divide_fusion, f32[2,8,128]{2,1,0:T(8,128)S(1)} %get-tuple-element.68, pred[2,128,384]{2,1,0:T(8,128)(4,1)S(1)} %copy-done.14, ...), kind=kOutput, calls=%fused_computation.16 | convolution fusion | flops 811464704 | bytes 6168576 | tf_op jit(solution)/shard_map/transpose(jvp(bhqk,bkf->bhqf))/dot_general | solution.py:105
  46.7 3.0 %divide_convert_fusion = (bf16[2,8,128,384]{3,2,1,0:T(8,128)(2,1)S(1)}, f32[2,8,128]{2,1,0:T(8,128)S(1)}, f32[2,8,128]{2,1,0:T(8,128)S(1)}, pred[2,8,128,384]{3,2,1,0:T(32,128)(4,1)S(1)}) fusion(f32[2,8,128,384]{3,2,1,0:T(8,128)S(1)} %get-tuple-element.69, f32[2,8,128]{2,1,0:T(8,128)S(1)} %fusion.22, f32[2,8,128]{2,1,0:T(8,128)S(1)} %get-tuple-element.68, ...), kind=kLoop, calls=%fused_computation.19 | loop fusion | flops 10219520 | bytes 7217152 | tf_op jit(solution)/shard_map/jvp()/convert_element_type | solution.py:104
  49.7 3.0 %multiply_reduce_fusion = f32[2,128,512]{2,1,0:T(8,128)S(1)} fusion(f32[8,512]{1,0:T(8,128)S(1)} %copy-done.15, pred[2,8,128,384]{3,2,1,0:T(32,128)(4,1)S(1)} %get-tuple-element.15, f32[2,8,128]{2,1,0:T(8,128)S(1)} %negate_divide_fusion, pred[2,128,384]{2,1,0:T(8,128)(4,1)S(1)} %copy-done.14, bf16[1,384,512]{2,1,0:T(8,128)(2,1)S(1)} %get-tuple-element.78, ...), kind=kOutput, calls=%fused_computation.8 | convolution fusion | flops 815529984 | bytes 6963200 | tf_op jit(solution)/shard_map/transpose(jvp(bhqf,bkf->bhqk))/dot_general | solution.py:100
  52.7 2.8 %fusion.36 = f32[2,384,512]{2,1,0:T(8,128)S(1)} fusion(f32[8,512]{1,0:T(8,128)S(1)} %copy-done.15, f32[2,128,512]{2,1,0:T(8,128)S(1)} %slice.168, pred[2,8,128,384]{3,2,1,0:T(32,128)(4,1)S(1)} %get-tuple-element.15, f32[2,8,128]{2,1,0:T(8,128)S(1)} %negate_divide_fusion, pred[2,128,384]{2,1,0:T(8,128)(4,1)S(1)} %copy-done.14, ...), kind=kOutput, calls=%fused_computation.49 | convolution fusion | flops 814219264 | bytes 7749632 | tf_op jit(solution)/shard_map/transpose(jvp(bhqf,bkf->bhqk))/dot_general | solution.py:100
  55.5 1.3 multiply_reduce_fusion.1
  56.8 1.1 fusion.39
  59.7 0.9 copy-done.5
  61.2 1.0 fusion.117
  62.3 0.9 pad_maximum_fusion.1
  63.2 2.1 %reshape_reshape.15 = bf16[32,64,128]{2,1,0:T(8,128)(2,1)} reshape(bf16[256,1024]{1,0:T(8,128)(2,1)} %pad_maximum_fusion.1) | data formatting | bytes 1048576 | tf_op jit(solution)/shard_map/reshape;reshape | solution.py:163
  65.3 7.4 %all-to-all-start.1 = ((bf16[32,64,128]{2,1,0:T(8,128)(2,1)}), bf16[32,64,128]{2,1,0:T(8,128)(2,1)}, u32[]{:S(2)}, u32[]{:S(2)}) async-start(bf16[32,64,128]{2,1,0:T(8,128)(2,1)} %reshape_reshape.15), calls=%async_computation.1 | async-start | bytes 1048576 | tf_op jit(solution)/shard_map/all_to_all | solution.py:164
  72.7 1.8 %copy.75 = bf16[256,512]{0,1:T(8,128)(2,1)} copy(bf16[256,512]{1,0:T(8,128)(2,1)} %bitcast.207) | data formatting | bytes 524288 | tf_op jit(solution)/shard_map/jvp()/convert_element_type | solution.py:107
  74.5 1.8 %reshape.371 = bf16[32,8,512]{2,1,0:T(8,128)(2,1)} reshape(bf16[512,256]{1,0:T(8,128)(2,1)} %bitcast.203) | data formatting | bytes 524288 | tf_op jit(solution)/shard_map/reshape | solution.py:156
  76.2 1.7 %copy.76 = bf16[8,32,512]{2,1,0:T(8,128)(2,1)} copy(bf16[8,32,512]{2,0,1:T(8,128)(2,1)} %bitcast.204) | data formatting | bytes 524288 | tf_op jit(solution)/shard_map/transpose | solution.py:157
  77.9 1.7 %reshape.372 = bf16[512,256]{1,0:T(8,128)(2,1)} reshape(bf16[8,32,512]{2,1,0:T(8,128)(2,1)} %copy.76) | data formatting | bytes 524288 | tf_op jit(solution)/shard_map/reshape | solution.py:157
  79.7 1.8 %copy.73 = bf16[512,256]{1,0:T(8,128)(2,1)} copy(bf16[512,256]{0,1:T(8,128)(2,1)} %get-tuple-element.53) | data formatting | bytes 524288 | tf_op jit(solution)/shard_map/transpose | solution.py:156
  81.5 1.8 %reshape.369 = bf16[32,8,512]{2,1,0:T(8,128)(2,1)} reshape(bf16[512,256]{1,0:T(8,128)(2,1)} %copy.73) | data formatting | bytes 524288 | tf_op jit(solution)/shard_map/reshape | solution.py:156
  83.3 1.7 %copy.74 = bf16[8,32,512]{2,1,0:T(8,128)(2,1)} copy(bf16[8,32,512]{2,0,1:T(8,128)(2,1)} %bitcast.205) | data formatting | bytes 524288 | tf_op jit(solution)/shard_map/transpose | solution.py:157
  85.0 1.8 %reshape.370 = bf16[512,256]{1,0:T(8,128)(2,1)} reshape(bf16[8,32,512]{2,1,0:T(8,128)(2,1)} %copy.74) | data formatting | bytes 524288 | tf_op jit(solution)/shard_map/reshape | solution.py:157
  86.7 1.2 convolution_convert_fusion.3
  88.0 1.8 %convolution_convert_fusion = bf16[512,1536]{1,0:T(8,128)(2,1)S(1)} fusion(bf16[512,256]{1,0:T(8,128)(2,1)} %reshape.370, bf16[256,1536]{1,0:T(8,128)(2,1)} %bitcast.195), kind=kOutput, calls=%fused_computation.22 | convolution fusion | flops 403439616 | bytes 2621440 | tf_op jit(solution)/shard_map/dot_general | solution.py:158
  89.8 1.6 pad_maximum_fusion
  91.4 4.2 %convert_element_type.203 = bf16[8,32,32,128]{3,2,1,0:T(8,128)(2,1)} reshape(bf16[512,2048]{1,0:T(8,128)(2,1)} %pad_maximum_fusion) | data formatting | bytes 4194304 | tf_op jit(solution)/shard_map/convert_element_type | solution.py:172
  95.6 5.9 %all-to-all-start.2 = ((bf16[8,32,32,128]{3,2,1,0:T(8,128)(2,1)}), bf16[8,32,32,128]{3,2,1,0:T(8,128)(2,1)}, u32[]{:S(2)}, u32[]{:S(2)}) async-start(bf16[8,32,32,128]{3,2,1,0:T(8,128)(2,1)} %convert_element_type.203), calls=%async_computation.2 | async-start | bytes 4194304 | tf_op jit(solution)/shard_map/all_to_all | solution.py:173
  101.5 2.1 %reshape_reshape.16 = bf16[256,1024]{1,0:T(8,128)(2,1)} reshape(bf16[32,64,128]{2,1,0:T(8,128)(2,1)} %all-to-all-done.1) | data formatting | bytes 1048576 | tf_op jit(solution)/shard_map/reshape;reshape | solution.py:239
  103.6 1.3 fusion.81
  104.9 2.2 %convolution_convert_fusion.9 = bf16[128,512]{1,0:T(8,128)(2,1)} fusion(bf16[512,512]{1,0:T(8,128)(2,1)} %param.14, f32[128,1024]{1,0:T(8,128)S(1)} %fusion.81, bf16[1,128,512]{2,1,0:T(8,128)(2,1)S(1)} %copy-done.10), kind=kOutput, calls=%fused_computation.65 | convolution fusion | flops 67371008 | bytes 1048576 | tf_op jit(solution)/shard_map/transpose(jvp())/dot_general | solution.py:49
  107.1 1.0 copy.69
  110.4 17.4 %all-to-all-done.2 = bf16[8,32,32,128]{3,2,1,0:T(8,128)(2,1)} async-done(((bf16[8,32,32,128]{3,2,1,0:T(8,128)(2,1)}), bf16[8,32,32,128]{3,2,1,0:T(8,128)(2,1)}, u32[]{:S(2)}, u32[]{:S(2)}) %all-to-all-start.2) | async-done | bytes 2097184 | tf_op jit(solution)/shard_map/all_to_all | solution.py:173
  127.8 2.6 %reduce_sum.263 = bf16[32,32,128]{2,1,0:T(8,128)(2,1)} reduce(bf16[8,32,32,128]{3,2,1,0:T(8,128)(2,1)} %all-to-all-done.2, bf16[]{:T(256)} %constant.96.clone.1), dimensions={0}, to_apply=%region_23.24 | reduce | flops 917504 | bytes 2359298 | tf_op jit(solution)/shard_map/reduce_sum | solution.py:174
  130.4 9.4 %all-to-all-start.3 = ((bf16[32,32,128]{2,1,0:T(8,128)(2,1)}), bf16[32,32,128]{2,1,0:T(8,128)(2,1)S(1)}, u32[]{:S(2)}, u32[]{:S(2)}) async-start(bf16[32,32,128]{2,1,0:T(8,128)(2,1)} %reduce_sum.263), calls=%async_computation.3 | async-start | bytes 524288 | tf_op jit(solution)/shard_map/all_to_all | solution.py:175
  140.1 0.8 fusion.78
  140.9 8.6 %all-to-all-done.3 = bf16[32,32,128]{2,1,0:T(8,128)(2,1)S(1)} async-done(((bf16[32,32,128]{2,1,0:T(8,128)(2,1)}), bf16[32,32,128]{2,1,0:T(8,128)(2,1)S(1)}, u32[]{:S(2)}, u32[]{:S(2)}) %all-to-all-start.3) | async-done | bytes 262176 | tf_op jit(solution)/shard_map/all_to_all | solution.py:175
  150.2 6.9 %all-to-all-start.4 = ((bf16[8,32,128]{2,1,0:T(8,128)(2,1)}), bf16[8,32,128]{2,1,0:T(8,128)(2,1)S(1)}, u32[]{:S(2)}, u32[]{:S(2)}) async-start(bf16[8,32,128]{2,1,0:T(8,128)(2,1)} %broadcast_in_dim.161), calls=%async_computation.4 | async-start | bytes 131072 | tf_op jit(solution)/shard_map/all_to_all | solution.py:178
  157.8 4.2 %all-to-all-done.4 = bf16[8,32,128]{2,1,0:T(8,128)(2,1)S(1)} async-done(((bf16[8,32,128]{2,1,0:T(8,128)(2,1)}), bf16[8,32,128]{2,1,0:T(8,128)(2,1)S(1)}, u32[]{:S(2)}, u32[]{:S(2)}) %all-to-all-start.4) | async-done | bytes 65568 | tf_op jit(solution)/shard_map/all_to_all | solution.py:178
  (128 shorter events, 16.1 us)
Async XLA Ops:
  0.6 39.0 %copy-start = (bf16[512,1536]{1,0:T(8,128)(2,1)S(1)}, bf16[512,1536]{1,0:T(8,128)(2,1)}, u32[]{:S(2)}) copy-start(bf16[512,1536]{1,0:T(8,128)(2,1)} %param.16) | copy-start | bytes 4718596
  0.6 8.4 %copy-start.1 = (bf16[1,128,512]{2,1,0:T(8,128)(2,1)S(1)}, bf16[1,128,512]{2,1,0:T(8,128)(2,1)}, u32[]{:S(2)}) copy-start(bf16[1,128,512]{2,1,0:T(8,128)(2,1)} %param.10) | copy-start | bytes 393220
  0.7 8.4 %copy-start.6 = (bf16[512,512]{1,0:T(8,128)(2,1)S(1)}, bf16[512,512]{1,0:T(8,128)(2,1)}, u32[]{:S(2)}) copy-start(bf16[512,512]{1,0:T(8,128)(2,1)} %param.14) | copy-start | bytes 1572868
  1.8 5.7 %copy-start.16 = (f32[128]{0:T(128)}, f32[128]{0:T(128)S(1)}, u32[]{:S(2)}) copy-start(f32[128]{0:T(128)S(1)} %broadcast_multiply_fusion.1) | copy-start | bytes 1540
  2.9 0.6 copy-start.24
  3.0 4.6 %copy-start.20 = (f32[128]{0:T(128)}, f32[128]{0:T(128)S(1)}, u32[]{:S(2)}) copy-start(f32[128]{0:T(128)S(1)} %fusion.95) | copy-start | bytes 1540
  5.4 3.9 %copy-start.22 = (s32[128]{0:T(128)}, s32[128]{0:T(128)S(1)}, u32[]{:S(2)}) copy-start(s32[128]{0:T(128)S(1)} %fusion.94) | copy-start | bytes 1540
  5.4 4.6 %copy-start.10 = (bf16[1,128,512]{2,1,0:T(8,128)(2,1)S(1)}, bf16[1,128,512]{2,1,0:T(8,128)(2,1)}, u32[]{:S(2)}) copy-start(bf16[1,128,512]{2,1,0:T(8,128)(2,1)} %param.11) | copy-start | bytes 393220
  9.3 0.7 copy-start.8
  11.3 26.7 %all-to-all-start = ((bf16[32,64,128]{2,1,0:T(8,128)(2,1)}), bf16[32,64,128]{2,1,0:T(8,128)(2,1)}, u32[]{:S(2)}, u32[]{:S(2)}) async-start(bf16[32,64,128]{2,1,0:T(8,128)(2,1)} %reshape_reshape.13), calls=%async_computation | async-start | bytes 1048576 | tf_op jit(solution)/shard_map/all_to_all | solution.py:164
  39.6 1.6 copy-start.7
  41.1 0.9 copy-start.14
  41.1 0.9 copy-start.15
  56.8 1.1 copy-start.13
  59.2 1.4 copy-start.23
  59.7 0.9 copy-start.5
  65.3 30.3 %all-to-all-start.1 = ((bf16[32,64,128]{2,1,0:T(8,128)(2,1)}), bf16[32,64,128]{2,1,0:T(8,128)(2,1)}, u32[]{:S(2)}, u32[]{:S(2)}) async-start(bf16[32,64,128]{2,1,0:T(8,128)(2,1)} %reshape_reshape.15), calls=%async_computation.1 | async-start | bytes 1048576 | tf_op jit(solution)/shard_map/all_to_all | solution.py:164
  95.6 32.2 %all-to-all-start.2 = ((bf16[8,32,32,128]{3,2,1,0:T(8,128)(2,1)}), bf16[8,32,32,128]{3,2,1,0:T(8,128)(2,1)}, u32[]{:S(2)}, u32[]{:S(2)}) async-start(bf16[8,32,32,128]{3,2,1,0:T(8,128)(2,1)} %convert_element_type.203), calls=%async_computation.2 | async-start | bytes 4194304 | tf_op jit(solution)/shard_map/all_to_all | solution.py:173
  104.9 3.9 %copy-start.3 = (f32[128,1024]{1,0:T(8,128)}, f32[128,1024]{1,0:T(8,128)S(1)}, u32[]{:S(2)}) copy-start(f32[128,1024]{1,0:T(8,128)S(1)} %fusion.81) | copy-start | bytes 1572868
  108.1 0.9 copy-start.12
  108.1 1.5 copy-start.2
  108.1 1.5 copy-start.17
  108.2 1.5 copy-start.19
  108.9 1.5 copy-start.25
  109.5 30.3 %copy-start.18 = (f32[128]{0:T(128)S(1)}, f32[128]{0:T(128)}, u32[]{:S(2)}) copy-start(f32[128]{0:T(128)} %copy-done.16) | copy-start | bytes 1540
  109.5 30.4 %copy-start.21 = (f32[128]{0:T(128)S(1)}, f32[128]{0:T(128)}, u32[]{:S(2)}) copy-start(f32[128]{0:T(128)} %copy-done.20) | copy-start | bytes 1540
  109.6 30.6 %copy-start.4 = (f32[128,1024]{1,0:T(8,128)S(1)}, f32[128,1024]{1,0:T(8,128)}, u32[]{:S(2)}) copy-start(f32[128,1024]{1,0:T(8,128)} %copy-done.3) | copy-start | bytes 1572868
  109.6 30.6 %copy-start.11 = (bf16[1,128,512]{2,1,0:T(8,128)(2,1)S(1)}, bf16[1,128,512]{2,1,0:T(8,128)(2,1)}, u32[]{:S(2)}) copy-start(bf16[1,128,512]{2,1,0:T(8,128)(2,1)} %param.11) | copy-start | bytes 393220
  109.7 47.5 %copy-start.9 = (bf16[128,512]{1,0:T(8,128)(2,1)S(1)}, bf16[128,512]{1,0:T(8,128)(2,1)}, u32[]{:S(2)}) copy-start(bf16[128,512]{1,0:T(8,128)(2,1)} %copy-done.8) | copy-start | bytes 393220
  130.4 19.1 %all-to-all-start.3 = ((bf16[32,32,128]{2,1,0:T(8,128)(2,1)}), bf16[32,32,128]{2,1,0:T(8,128)(2,1)S(1)}, u32[]{:S(2)}, u32[]{:S(2)}) async-start(bf16[32,32,128]{2,1,0:T(8,128)(2,1)} %reduce_sum.263), calls=%async_computation.3 | async-start | bytes 524288 | tf_op jit(solution)/shard_map/all_to_all | solution.py:175
  150.2 11.8 %all-to-all-start.4 = ((bf16[8,32,128]{2,1,0:T(8,128)(2,1)}), bf16[8,32,128]{2,1,0:T(8,128)(2,1)S(1)}, u32[]{:S(2)}, u32[]{:S(2)}) async-start(bf16[8,32,128]{2,1,0:T(8,128)(2,1)} %broadcast_in_dim.161), calls=%async_computation.4 | async-start | bytes 131072 | tf_op jit(solution)/shard_map/all_to_all | solution.py:178

commit v13 on v10

--- a/solution.py
+++ b/solution.py
@@ -38,14 +38,19 @@
     packed_rows = jnp.dot(normed, input_weight, preferred_element_type=jnp.float32).astype(
         jnp.bfloat16
     )
-    parts = heads_first(packed_rows, block_groups)
-    queries, key_rows, value_rows = parts[0], parts[1], parts[2]
-    scores = jnp.einsum("bhqd,bhkd->bhqk", queries, key_rows) * HEAD_DIM ** (-0.5)
+    by_block = packed_rows.astype(jnp.float32).reshape(block_groups, EVENTS_PER_BLOCK, -1)
+    queries = by_block[:, :, :features]
+    key_rows = by_block[:, :, features : 2 * features]
+    value_rows = by_block[:, :, 2 * features :]
+    mask = head_mask(features)
+    masked_queries = queries[:, None, :, :] * mask[None, :, None, :]
+    scores = jnp.einsum("bhqf,bkf->bhqk", masked_queries, key_rows) * HEAD_DIM ** (-0.5)
     highest = jnp.max(scores, axis=-1, keepdims=True)
     weights = jnp.exp(scores - highest)
     attention = (weights / jnp.sum(weights, axis=-1, keepdims=True)).astype(jnp.bfloat16)
-    merged_rows = jnp.einsum("bhqk,bhkd->bhqd", attention.astype(jnp.float32), value_rows)
-    merged_rows = rows_first(merged_rows, row_total)
+    per_head = jnp.einsum("bhqk,bkf->bhqf", attention.astype(jnp.float32), value_rows)
+    merged_rows = jnp.sum(per_head * mask[None, :, None, :], axis=1)
+    merged_rows = merged_rows.astype(jnp.bfloat16).reshape(row_total, features)
     branch = jnp.dot(merged_rows, output_weight, preferred_element_type=jnp.float32)
     return (source.astype(jnp.float32) + branch).astype(jnp.bfloat16)
 

time: 161 us -> 159 us (0.988)
  matrix products: 25.5 us -> 28.7 us
  other arithmetic: 20.9 us -> 18.5 us
  waiting for transfers between devices: 35.6 us -> 33.6 us
    dot_general x6, matrix products: 1.55 us -> 7.71 us  [the longest x3 4.27 us: intra_branch(): jnp.einsum('bhqf,bkf->bhqk', masked_queries, key_rows) * HEAD_DIM ** (-0.5)]
    all_to_all x1, waiting for transfers between devices: 17.3 us -> 12.5 us  [reduce_weight_terms(): terms = lax.all_to_all(terms, 'dp', 0, 0, tiled=True)]
    all_to_all x4, waiting for transfers between devices: 18.3 us -> 21.1 us  [dense_all_to_all(): moved = lax.all_to_all(flat, axis_name, 0, 0, tiled=True)]
    dot_general x2, matrix products: 2.46 us -> 0.54 us  [intra_branch(): jnp.dot(merged_rows, output_weight, preferred_element_type=jnp.float32)]
    reduce_sum x0 -> x1, local copies, waits for them, and re-layouts: none -> 1.78 us  [intra_branch(): masked_queries = queries[:, None, :, :] * mask[None, :, None, :]]
  transfers between devices with their start and end apart: 5 -> 5, of which waited for: 4 -> 4; matrix products, arithmetic and copies ran while one was open for 22% -> 23% of each run, Pallas kernels for 0% -> 0%
where the time goes in v13:
time: 159 us; the launch traced here: 157 us
  starting transfers between devices  41.9 us (26%)
  waiting for transfers between devices  33.6 us (21%)
  local copies, waits for them, and re-layouts  29.2 us (18%)
  matrix products  28.7 us (18%)
  other arithmetic  18.5 us (12%)
  between operations  5.22 us (3%)
    all_to_all x4, starting transfers between devices, dense_all_to_all(): moved = lax.all_to_all(flat, axis_name, 0, 0, tiled=True)  35.8 us
    all_to_all x4, waiting for transfers between devices, dense_all_to_all(): moved = lax.all_to_all(flat, axis_name, 0, 0, tiled=True)  21.1 us
    all_to_all x1, waiting for transfers between devices, reduce_weight_terms(): terms = lax.all_to_all(terms, 'dp', 0, 0, tiled=True)  12.5 us
    dot_general x3, matrix products, cross_account_inner(): jnp.einsum('bhqf,bkf->bhqk', masked_queries, key_rows) * HEAD_DIM ** (-0.5)  7.18 us
    all_to_all x1, starting transfers between devices, reduce_weight_terms(): terms = lax.all_to_all(terms, 'dp', 0, 0, tiled=True)  6.08 us
    dot_general x3, matrix products, cross_account_inner(): jnp.einsum('bhqk,bkf->bhqf', attention.astype(jnp.float32), value_rows)  4.33 us
    dot_general x3, matrix products, intra_branch(): jnp.einsum('bhqf,bkf->bhqk', masked_queries, key_rows) * HEAD_DIM ** (-0.5)  4.27 us
    another operation x3, local copies, waits for them, and re-layouts, dense_all_to_all(): flat = pieces.reshape(count, -1, 128)  3.89 us
  transfers between devices with their start and end apart: 5, of which 4 were waited for; matrix products, arithmetic and copies ran while one was open for 23% of the time, Pallas kernels for 0%

profile of v13, /device:TPU:1, one launch (start us, length us, event | category | flops | bytes accessed | tf_op | source)
XLA Modules:
  0.0 157.2 jit_solution(17863713493138067944)
XLA Ops:
  0.7 1.1 convert_reduce_fusion.5
  1.8 1.1 fusion.94
  2.9 0.8 dynamic-slice.1
  4.8 2.0 %fusion.22 = bf16[1,128,1536]{2,1,0:T(8,128)(2,1)S(1)} fusion(bf16[512,1536]{1,0:T(8,128)(2,1)} %param.13, bf16[1,128,512]{2,1,0:T(8,128)(2,1)} %param.10, f32[512]{0:T(512)} %param.12, f32[128]{0:T(128)S(1)} %fusion.132, f32[128]{0:T(128)S(1)} %broadcast_multiply_fusion.2), kind=kOutput, calls=%fused_computation.34 | convolution fusion | flops 201850880 | bytes 2100224 | tf_op jit(solution)/shard_map/jvp()/dot_general | solution.py:38
  6.9 0.8 copy-done.12
  10.0 1.0 reshape_reshape.17
  11.0 12.0 %all-to-all-start = ((bf16[32,64,128]{2,1,0:T(8,128)(2,1)}), bf16[32,64,128]{2,1,0:T(8,128)(2,1)S(1)}, u32[]{:S(2)}, u32[]{:S(2)}) async-start(bf16[32,64,128]{2,1,0:T(8,128)(2,1)} %reshape_reshape.17), calls=%async_computation | async-start | bytes 1048576 | tf_op jit(solution)/shard_map/all_to_all | solution.py:169
  29.7 7.9 %all-to-all-done = bf16[32,64,128]{2,1,0:T(8,128)(2,1)S(1)} async-done(((bf16[32,64,128]{2,1,0:T(8,128)(2,1)}), bf16[32,64,128]{2,1,0:T(8,128)(2,1)S(1)}, u32[]{:S(2)}, u32[]{:S(2)}) %all-to-all-start) | async-done | bytes 524320 | tf_op jit(solution)/shard_map/all_to_all | solution.py:169
  39.7 1.4 fusion.159
  41.0 1.2 fusion.31
  42.3 2.0 %fusion.12 = (f32[2,8,128]{2,1,0:T(8,128)S(1)}, bf16[2,8,128,384]{3,2,1,0:T(8,128)(2,1)S(1)}) fusion(f32[2,8,128,384]{3,2,1,0:T(8,128)S(1)} %get-tuple-element.69, f32[2,8,128]{2,1,0:T(8,128)S(1)} %multiply_divide_fusion, f32[2,8,128]{2,1,0:T(8,128)S(1)} %get-tuple-element.68, pred[2,128,384]{2,1,0:T(8,128)(4,1)S(1)} %broadcast_or_fusion, ...), kind=kOutput, calls=%fused_computation.16 | convolution fusion | flops 811464704 | bytes 6168576 | tf_op jit(solution)/shard_map/transpose(jvp(bhqk,bkf->bhqf))/dot_general | solution.py:110
  44.3 3.0 %divide_convert_fusion = (bf16[2,8,128,384]{3,2,1,0:T(8,128)(2,1)S(1)}, f32[2,8,128]{2,1,0:T(8,128)S(1)}, f32[2,8,128]{2,1,0:T(8,128)S(1)}, pred[2,8,128,384]{3,2,1,0:T(32,128)(4,1)S(1)}) fusion(f32[2,8,128,384]{3,2,1,0:T(8,128)S(1)} %get-tuple-element.69, f32[2,8,128]{2,1,0:T(8,128)S(1)} %fusion.31, f32[2,8,128]{2,1,0:T(8,128)S(1)} %get-tuple-element.68, ...), kind=kLoop, calls=%fused_computation.19 | loop fusion | flops 10219520 | bytes 7217152 | tf_op jit(solution)/shard_map/jvp()/convert_element_type | solution.py:109
  47.3 3.0 %multiply_reduce_fusion = f32[2,128,512]{2,1,0:T(8,128)S(1)} fusion(f32[8,512]{1,0:T(8,128)S(1)} %fusion.126, pred[2,8,128,384]{3,2,1,0:T(32,128)(4,1)S(1)} %get-tuple-element.15, f32[2,8,128]{2,1,0:T(8,128)S(1)} %negate_divide_fusion, pred[2,128,384]{2,1,0:T(8,128)(4,1)S(1)} %broadcast_or_fusion, bf16[1,384,512]{2,1,0:T(8,128)(2,1)S(1)} %get-tuple-element.77, ...), kind=kOutput, calls=%fused_computation.8 | convolution fusion | flops 815529984 | bytes 6963200 | tf_op jit(solution)/shard_map/transpose(jvp(bhqf,bkf->bhqk))/dot_general | solution.py:105
  50.4 2.8 %fusion.45 = f32[2,384,512]{2,1,0:T(8,128)S(1)} fusion(f32[8,512]{1,0:T(8,128)S(1)} %fusion.126, f32[2,128,512]{2,1,0:T(8,128)S(1)} %slice.169, pred[2,8,128,384]{3,2,1,0:T(32,128)(4,1)S(1)} %get-tuple-element.15, f32[2,8,128]{2,1,0:T(8,128)S(1)} %negate_divide_fusion, pred[2,128,384]{2,1,0:T(8,128)(4,1)S(1)} %broadcast_or_fusion, ...), kind=kOutput, calls=%fused_computation.60 | convolution fusion | flops 814219264 | bytes 7749632 | tf_op jit(solution)/shard_map/transpose(jvp(bhqf,bkf->bhqk))/dot_general | solution.py:105
  53.2 1.3 multiply_reduce_fusion.1
  54.5 1.1 fusion.48
  58.2 1.0 fusion.155
  59.3 0.9 pad_maximum_fusion.1
  60.2 2.1 %reshape_reshape.19 = bf16[32,64,128]{2,1,0:T(8,128)(2,1)} reshape(bf16[256,1024]{1,0:T(8,128)(2,1)} %pad_maximum_fusion.1) | data formatting | bytes 1048576 | tf_op jit(solution)/shard_map/reshape;reshape | solution.py:168
  62.2 7.4 %all-to-all-start.1 = ((bf16[32,64,128]{2,1,0:T(8,128)(2,1)}), bf16[32,64,128]{2,1,0:T(8,128)(2,1)}, u32[]{:S(2)}, u32[]{:S(2)}) async-start(bf16[32,64,128]{2,1,0:T(8,128)(2,1)} %reshape_reshape.19), calls=%async_computation.1 | async-start | bytes 1048576 | tf_op jit(solution)/shard_map/all_to_all | solution.py:169
  70.2 1.8 %copy.71 = bf16[256,512]{0,1:T(8,128)(2,1)} copy(bf16[256,512]{1,0:T(8,128)(2,1)} %bitcast.188) | data formatting | bytes 524288 | tf_op jit(solution)/shard_map/jvp()/convert_element_type | solution.py:112
  72.0 1.8 %reshape.368 = bf16[32,8,512]{2,1,0:T(8,128)(2,1)} reshape(bf16[512,256]{1,0:T(8,128)(2,1)} %bitcast.184) | data formatting | bytes 524288 | tf_op jit(solution)/shard_map/reshape | solution.py:161
  73.8 1.7 %copy.72 = bf16[8,32,512]{2,1,0:T(8,128)(2,1)} copy(bf16[8,32,512]{2,0,1:T(8,128)(2,1)} %bitcast.185) | data formatting | bytes 524288 | tf_op jit(solution)/shard_map/transpose | solution.py:162
  75.5 1.8 %dot_general.106 = bf16[8,64,256]{2,1,0:T(8,128)(2,1)} reshape(bf16[8,32,512]{2,1,0:T(8,128)(2,1)} %copy.72) | data formatting | bytes 524288 | tf_op jit(solution)/shard_map/dot_general | solution.py:163
  77.3 1.8 %copy.69 = bf16[512,256]{1,0:T(8,128)(2,1)} copy(bf16[512,256]{0,1:T(8,128)(2,1)} %get-tuple-element.53) | data formatting | bytes 524288 | tf_op jit(solution)/shard_map/transpose | solution.py:161
  79.1 1.7 %reshape.367 = bf16[32,8,512]{2,1,0:T(8,128)(2,1)} reshape(bf16[512,256]{1,0:T(8,128)(2,1)} %copy.69) | data formatting | bytes 524288 | tf_op jit(solution)/shard_map/reshape | solution.py:161
  80.8 1.7 %copy.70 = bf16[8,32,512]{2,1,0:T(8,128)(2,1)} copy(bf16[8,32,512]{2,0,1:T(8,128)(2,1)} %bitcast.186) | data formatting | bytes 524288 | tf_op jit(solution)/shard_map/transpose | solution.py:162
  82.5 1.7 %dot_general.104 = bf16[8,64,256]{2,1,0:T(8,128)(2,1)} reshape(bf16[8,32,512]{2,1,0:T(8,128)(2,1)} %copy.70) | data formatting | bytes 524288 | tf_op jit(solution)/shard_map/dot_general | solution.py:163
  84.3 1.2 convolution_convert_fusion.3
  85.5 1.5 convolution_convert_fusion
  87.1 1.6 %pad_maximum_fusion = bf16[8,64,2048]{2,1,0:T(8,128)(2,1)} fusion(bf16[8,64,512]{2,1,0:T(8,128)(2,1)S(1)} %convolution_convert_fusion.3, bf16[8,64,1536]{2,1,0:T(8,128)(2,1)S(1)} %convolution_convert_fusion), kind=kLoop, calls=%fused_computation.35 | loop fusion | flops 4194304 | bytes 4194304 | tf_op jit(solution)/shard_map/concatenate | solution.py:255
  88.7 6.1 %all-to-all-start.2 = ((bf16[8,64,2048]{2,1,0:T(8,128)(2,1)}), bf16[8,64,2048]{2,1,0:T(8,128)(2,1)}, u32[]{:S(2)}, u32[]{:S(2)}) async-start(bf16[8,64,2048]{2,1,0:T(8,128)(2,1)} %pad_maximum_fusion), calls=%async_computation.2 | async-start | bytes 4194304 | tf_op jit(solution)/shard_map/all_to_all | solution.py:178
  94.8 2.1 %reshape_reshape.20 = bf16[256,1024]{1,0:T(8,128)(2,1)} reshape(bf16[32,64,128]{2,1,0:T(8,128)(2,1)} %all-to-all-done.1) | data formatting | bytes 1048576 | tf_op jit(solution)/shard_map/reshape;reshape | solution.py:245
  96.9 1.3 fusion.117
  98.6 1.5 convert_reduce_fusion.3
  100.7 2.1 %multiply_reduce_fusion.2 = f32[128,512]{1,0:T(8,128)} fusion(f32[8,512]{1,0:T(8,128)S(1)} %copy-done.17, f32[8,128,128]{1,2,0:T(8,128)S(1)} %get-tuple-element.5, pred[8,128,128]{1,2,0:T(32,128)(4,1)S(1)} %get-tuple-element.7, f32[8,128]{1,0:T(8,128)S(1)} %negate_divide_fusion.1, bf16[1,128,1536]{2,1,0:T(8,128)(2,1)} %copy-done.11), kind=kOutput, calls=%fused_computation.36 | convolution fusion | flops 135593984 | bytes 1069056 | tf_op jit(solution)/shard_map/transpose(jvp(bhqf,bkf->bhqk))/dot_general | solution.py:47
  102.8 1.8 %copy.68 = f32[128,512]{0,1:T(8,128)} copy(f32[128,512]{1,0:T(8,128)} %multiply_reduce_fusion.2) | data formatting | bytes 524288 | tf_op jit(solution)/shard_map/transpose(jvp())/reduce_sum | solution.py:46
  104.6 1.7 %fusion.60 = f32[1,128,512]{1,2,0:T(8,128)S(1)} fusion(f32[8,512]{1,0:T(8,128)S(1)} %copy-done.17, f32[128,512]{1,0:T(8,128)} %copy-done.12, f32[8,128,128]{1,2,0:T(8,128)S(1)} %get-tuple-element.5, pred[8,128,128]{1,2,0:T(32,128)(4,1)} %copy-done.27, f32[8,128]{1,0:T(8,128)S(1)} %negate_divide_fusion.1), kind=kOutput, calls=%fused_computation.70 | convolution fusion | flops 135135232 | bytes 1200128 | tf_op jit(solution)/shard_map/transpose(jvp(bhqf,bkf->bhqk))/dot_general | solution.py:47
  106.3 1.4 fusion.63
  107.8 0.7 fusion.97
  108.6 12.5 %all-to-all-done.2 = bf16[8,64,2048]{2,1,0:T(8,128)(2,1)} async-done(((bf16[8,64,2048]{2,1,0:T(8,128)(2,1)}), bf16[8,64,2048]{2,1,0:T(8,128)(2,1)}, u32[]{:S(2)}, u32[]{:S(2)}) %all-to-all-start.2) | async-done | bytes 2097184 | tf_op jit(solution)/shard_map/all_to_all | solution.py:178
  121.1 2.0 %reduce_sum.284 = bf16[64,2048]{1,0:T(8,128)(2,1)S(1)} reduce(bf16[8,64,2048]{2,1,0:T(8,128)(2,1)} %all-to-all-done.2, bf16[]{:T(256)} %constant.97.clone.1), dimensions={0}, to_apply=%region_25.26 | reduce | flops 917504 | bytes 2359298 | tf_op jit(solution)/shard_map/reduce_sum | solution.py:179
  123.1 0.8 reshape_reshape.21
  123.9 9.4 %all-to-all-start.3 = ((bf16[32,32,128]{2,1,0:T(8,128)(2,1)}), bf16[32,32,128]{2,1,0:T(8,128)(2,1)S(1)}, u32[]{:S(2)}, u32[]{:S(2)}) async-start(bf16[32,32,128]{2,1,0:T(8,128)(2,1)} %reshape_reshape.21), calls=%async_computation.3 | async-start | bytes 524288 | tf_op jit(solution)/shard_map/all_to_all | solution.py:169
  133.5 0.8 fusion.113
  134.4 8.6 %all-to-all-done.3 = bf16[32,32,128]{2,1,0:T(8,128)(2,1)S(1)} async-done(((bf16[32,32,128]{2,1,0:T(8,128)(2,1)}), bf16[32,32,128]{2,1,0:T(8,128)(2,1)S(1)}, u32[]{:S(2)}, u32[]{:S(2)}) %all-to-all-start.3) | async-done | bytes 262176 | tf_op jit(solution)/shard_map/all_to_all | solution.py:169
  143.7 6.9 %all-to-all-start.4 = ((f32[8,32,128]{2,1,0:T(8,128)}), f32[8,32,128]{2,1,0:T(8,128)S(1)}, u32[]{:S(2)}, u32[]{:S(2)}) async-start(f32[8,32,128]{2,1,0:T(8,128)} %broadcast_in_dim.162), calls=%async_computation.4 | async-start | bytes 262144 | tf_op jit(solution)/shard_map/all_to_all | solution.py:169
  151.3 4.6 %all-to-all-done.4 = f32[8,32,128]{2,1,0:T(8,128)S(1)} async-done(((f32[8,32,128]{2,1,0:T(8,128)}), f32[8,32,128]{2,1,0:T(8,128)S(1)}, u32[]{:S(2)}, u32[]{:S(2)}) %all-to-all-start.4) | async-done | bytes 131104 | tf_op jit(solution)/shard_map/all_to_all | solution.py:169
  (130 shorter events, 15.4 us)
Async XLA Ops:
  0.6 37.5 %copy-start = (bf16[512,1536]{1,0:T(8,128)(2,1)S(1)}, bf16[512,1536]{1,0:T(8,128)(2,1)}, u32[]{:S(2)}) copy-start(bf16[512,1536]{1,0:T(8,128)(2,1)} %param.16) | copy-start | bytes 4718596
  2.9 5.9 %copy-start.25 = (f32[128]{0:T(128)}, f32[128]{0:T(128)S(1)}, u32[]{:S(2)}) copy-start(f32[128]{0:T(128)S(1)} %fusion.94) | copy-start | bytes 1540
  2.9 51.5 %copy-start.16 = (f32[8,512]{1,0:T(8,128)}, f32[8,512]{1,0:T(8,128)S(1)}, u32[]{:S(2)}) copy-start(f32[8,512]{1,0:T(8,128)S(1)} %fusion.126) | copy-start | bytes 49156
  4.8 4.2 %copy-start.18 = (s32[128]{0:T(128)}, s32[128]{0:T(128)S(1)}, u32[]{:S(2)}) copy-start(s32[128]{0:T(128)S(1)} %fusion.131) | copy-start | bytes 1540
  4.8 3.9 %copy-start.1 = (bf16[1,128,512]{2,1,0:T(8,128)(2,1)S(1)}, bf16[1,128,512]{2,1,0:T(8,128)(2,1)}, u32[]{:S(2)}) copy-start(bf16[1,128,512]{2,1,0:T(8,128)(2,1)} %param.10) | copy-start | bytes 393220
  4.8 4.0 %copy-start.2 = (bf16[512,512]{1,0:T(8,128)(2,1)S(1)}, bf16[512,512]{1,0:T(8,128)(2,1)}, u32[]{:S(2)}) copy-start(bf16[512,512]{1,0:T(8,128)(2,1)} %param.14) | copy-start | bytes 1572868
  6.8 2.2 %copy-start.11 = (bf16[1,128,1536]{2,1,0:T(8,128)(2,1)}, bf16[1,128,1536]{2,1,0:T(8,128)(2,1)S(1)}, u32[]{:S(2)}) copy-start(bf16[1,128,1536]{2,1,0:T(8,128)(2,1)S(1)} %fusion.22) | copy-start | bytes 1179652
  6.8 2.9 %copy-start.6 = (bf16[1,128,512]{2,1,0:T(8,128)(2,1)S(1)}, bf16[1,128,512]{2,1,0:T(8,128)(2,1)}, u32[]{:S(2)}) copy-start(bf16[1,128,512]{2,1,0:T(8,128)(2,1)} %param.11) | copy-start | bytes 393220
  6.8 0.8 copy-start.12
  8.2 16.6 %copy-start.21 = (s32[1,1,2,2]{3,2,1,0:T(2,128)S(1)}, s32[1,1,2,2]{3,2,1,0:T(2,128)}, u32[]{:S(2)}) copy-start(s32[1,1,2,2]{3,2,1,0:T(2,128)} %param.19) | copy-start | bytes 52
  8.3 19.7 %copy-start.15 = (s32[1,4096]{1,0:T(1,128)S(1)}, s32[1,4096]{1,0:T(1,128)}, u32[]{:S(2)}) copy-start(s32[1,4096]{1,0:T(1,128)} %param.18) | copy-start | bytes 49156
  8.8 29.4 %copy-start.22 = (f32[512]{0:T(512)S(1)}, f32[512]{0:T(512)}, u32[]{:S(2)}) copy-start(f32[512]{0:T(512)} %param.15) | copy-start | bytes 6148
  9.0 0.7 copy-start.8
  11.0 26.5 %all-to-all-start = ((bf16[32,64,128]{2,1,0:T(8,128)(2,1)}), bf16[32,64,128]{2,1,0:T(8,128)(2,1)S(1)}, u32[]{:S(2)}, u32[]{:S(2)}) async-start(bf16[32,64,128]{2,1,0:T(8,128)(2,1)} %reshape_reshape.17), calls=%async_computation | async-start | bytes 1048576 | tf_op jit(solution)/shard_map/all_to_all | solution.py:169
  38.2 1.0 copy-start.4
  54.4 1.4 copy-start.10
  56.8 0.7 copy-start.23
  62.2 26.5 %all-to-all-start.1 = ((bf16[32,64,128]{2,1,0:T(8,128)(2,1)}), bf16[32,64,128]{2,1,0:T(8,128)(2,1)}, u32[]{:S(2)}, u32[]{:S(2)}) async-start(bf16[32,64,128]{2,1,0:T(8,128)(2,1)} %reshape_reshape.19), calls=%async_computation.1 | async-start | bytes 1048576 | tf_op jit(solution)/shard_map/all_to_all | solution.py:169
  88.7 8.2 %copy-start.19 = (s32[128]{0:T(128)S(1)}, s32[128]{0:T(128)}, u32[]{:S(2)}) copy-start(s32[128]{0:T(128)} %copy-done.18) | copy-start | bytes 1540
  88.7 9.5 %copy-start.3 = (bf16[512,512]{1,0:T(8,128)(2,1)S(1)}, bf16[512,512]{1,0:T(8,128)(2,1)}, u32[]{:S(2)}) copy-start(bf16[512,512]{1,0:T(8,128)(2,1)} %param.14) | copy-start | bytes 1572868
  88.7 9.5 %copy-start.7 = (bf16[1,128,512]{2,1,0:T(8,128)(2,1)S(1)}, bf16[1,128,512]{2,1,0:T(8,128)(2,1)}, u32[]{:S(2)}) copy-start(bf16[1,128,512]{2,1,0:T(8,128)(2,1)} %param.11) | copy-start | bytes 393220
  88.7 9.8 %copy-start.17 = (f32[8,512]{1,0:T(8,128)S(1)}, f32[8,512]{1,0:T(8,128)}, u32[]{:S(2)}) copy-start(f32[8,512]{1,0:T(8,128)} %copy-done.16) | copy-start | bytes 49156
  88.7 9.8 %copy-start.20 = (f32[8,128]{1,0:T(8,128)S(1)}, f32[8,128]{1,0:T(8,128)}, u32[]{:S(2)}) copy-start(f32[8,128]{1,0:T(8,128)} %multiply_divide_fusion.1) | copy-start | bytes 12292
  88.7 32.4 %all-to-all-start.2 = ((bf16[8,64,2048]{2,1,0:T(8,128)(2,1)}), bf16[8,64,2048]{2,1,0:T(8,128)(2,1)}, u32[]{:S(2)}, u32[]{:S(2)}) async-start(bf16[8,64,2048]{2,1,0:T(8,128)(2,1)} %pad_maximum_fusion), calls=%async_computation.2 | async-start | bytes 4194304 | tf_op jit(solution)/shard_map/all_to_all | solution.py:178
  98.5 1.7 %copy-start.14 = (f32[128,512]{1,0:T(8,128)}, f32[128,512]{1,0:T(8,128)S(1)}, u32[]{:S(2)}) copy-start(f32[128,512]{1,0:T(8,128)S(1)} %fusion.67) | copy-start | bytes 786436
  100.1 0.7 copy-start.27
  100.7 7.0 %copy-start.24 = (f32[512]{0:T(512)S(1)}, f32[512]{0:T(512)}, u32[]{:S(2)}) copy-start(f32[512]{0:T(512)} %param.12) | copy-start | bytes 6148
  104.6 3.2 %copy-start.5 = (bf16[512,1536]{1,0:T(8,128)(2,1)S(1)}, bf16[512,1536]{1,0:T(8,128)(2,1)}, u32[]{:S(2)}) copy-start(bf16[512,1536]{1,0:T(8,128)(2,1)} %param.13) | copy-start | bytes 4718596
  104.6 3.2 %copy-start.13 = (f32[128,512]{0,1:T(8,128)S(1)}, f32[128,512]{0,1:T(8,128)}, u32[]{:S(2)}) copy-start(f32[128,512]{0,1:T(8,128)} %copy.68) | copy-start | bytes 786436
  106.3 2.2 %copy-start.26 = (f32[128]{0:T(128)S(1)}, f32[128]{0:T(128)}, u32[]{:S(2)}) copy-start(f32[128]{0:T(128)} %copy-done.25) | copy-start | bytes 1540
  108.5 42.1 %copy-start.9 = (bf16[128,512]{1,0:T(8,128)(2,1)S(1)}, bf16[128,512]{1,0:T(8,128)(2,1)}, u32[]{:S(2)}) copy-start(bf16[128,512]{1,0:T(8,128)(2,1)} %copy-done.8) | copy-start | bytes 393220
  123.9 19.1 %all-to-all-start.3 = ((bf16[32,32,128]{2,1,0:T(8,128)(2,1)}), bf16[32,32,128]{2,1,0:T(8,128)(2,1)S(1)}, u32[]{:S(2)}, u32[]{:S(2)}) async-start(bf16[32,32,128]{2,1,0:T(8,128)(2,1)} %reshape_reshape.21), calls=%async_computation.3 | async-start | bytes 524288 | tf_op jit(solution)/shard_map/all_to_all | solution.py:169
  143.7 12.2 %all-to-all-start.4 = ((f32[8,32,128]{2,1,0:T(8,128)}), f32[8,32,128]{2,1,0:T(8,128)S(1)}, u32[]{:S(2)}, u32[]{:S(2)}) async-start(f32[8,32,128]{2,1,0:T(8,128)} %broadcast_in_dim.162), calls=%async_computation.4 | async-start | bytes 262144 | tf_op jit(solution)/shard_map/all_to_all | solution.py:169

commit v14 on v13

--- a/solution.py
+++ b/solution.py
@@ -210,13 +210,12 @@
         rows_here,
     )
     targets = owner_map[0]
-    onehot = (targets[:, None] == jnp.arange(owners, dtype=jnp.int32)[None, :]).astype(jnp.int32)
-    row_counts = jnp.sum(onehot.reshape(owners, local_rows, owners), axis=1)
-    inbound_rows = lax.dynamic_index_in_dim(row_counts, own_index, axis=1, keepdims=False)
-    own_onehot = lax.dynamic_slice_in_dim(onehot, own_index * local_rows, local_rows, 0)
+    own_dest = lax.dynamic_slice_in_dim(targets, own_index * local_rows, local_rows, 0)
+    owner_ids = jnp.arange(owners, dtype=jnp.int32)
+    own_onehot = (own_dest[:, None] == owner_ids[None, :]).astype(jnp.int32)
     before = jnp.cumsum(own_onehot, axis=0) - own_onehot
     slot_ids = jnp.sum(before * own_onehot, axis=1)
-    own_dest = lax.dynamic_slice_in_dim(targets, own_index * local_rows, local_rows, 0)
+    inbound_rows = jnp.sum((targets == own_index).astype(jnp.int32).reshape(owners, local_rows), axis=1)
     position = own_dest * row_capacity + slot_ids
     placement = (
         jnp.arange(buffer_rows, dtype=jnp.int32)[:, None] == position[None, :]

time: 159 us -> 158 us (level)
  no operation moved by 1% of the time
where the time goes in v14:
time: 158 us; the launch traced here: 157 us
  starting transfers between devices  41.9 us (27%)
  waiting for transfers between devices  34.3 us (22%)
  local copies, waits for them, and re-layouts  28.9 us (18%)
  matrix products  28.7 us (18%)
  other arithmetic  18.1 us (11%)
  between operations  5.22 us (3%)
    all_to_all x4, starting transfers between devices, dense_all_to_all(): moved = lax.all_to_all(flat, axis_name, 0, 0, tiled=True)  35.8 us
    all_to_all x4, waiting for transfers between devices, dense_all_to_all(): moved = lax.all_to_all(flat, axis_name, 0, 0, tiled=True)  21.8 us
    all_to_all x1, waiting for transfers between devices, reduce_weight_terms(): terms = lax.all_to_all(terms, 'dp', 0, 0, tiled=True)  12.5 us
    dot_general x3, matrix products, cross_account_inner(): jnp.einsum('bhqf,bkf->bhqk', masked_queries, key_rows) * HEAD_DIM ** (-0.5)  7.15 us
    all_to_all x1, starting transfers between devices, reduce_weight_terms(): terms = lax.all_to_all(terms, 'dp', 0, 0, tiled=True)  6.08 us
    dot_general x3, matrix products, cross_account_inner(): jnp.einsum('bhqk,bkf->bhqf', attention.astype(jnp.float32), value_rows)  4.33 us
    dot_general x3, matrix products, intra_branch(): jnp.einsum('bhqf,bkf->bhqk', masked_queries, key_rows) * HEAD_DIM ** (-0.5)  4.26 us
    another operation x3, local copies, waits for them, and re-layouts, dense_all_to_all(): flat = pieces.reshape(count, -1, 128)  3.89 us
  transfers between devices with their start and end apart: 5, of which 4 were waited for; matrix products, arithmetic and copies ran while one was open for 23% of the time, Pallas kernels for 0%

profile of v14, /device:TPU:1, one launch (start us, length us, event | category | flops | bytes accessed | tf_op | source)
XLA Modules:
  0.0 157.1 jit_solution(3259621349489490679)
XLA Ops:
  0.7 1.1 convert_reduce_fusion.4
  1.8 1.1 fusion.94
  4.7 2.0 %fusion.22 = bf16[1,128,1536]{2,1,0:T(8,128)(2,1)S(1)} fusion(bf16[512,1536]{1,0:T(8,128)(2,1)} %param.13, bf16[1,128,512]{2,1,0:T(8,128)(2,1)} %param.10, f32[512]{0:T(512)} %param.12, f32[128]{0:T(128)S(1)} %fusion.131, f32[128]{0:T(128)S(1)} %broadcast_multiply_fusion.2), kind=kOutput, calls=%fused_computation.34 | convolution fusion | flops 201850880 | bytes 2100224 | tf_op jit(solution)/shard_map/jvp()/dot_general | solution.py:38
  6.8 0.8 copy-done.12
  9.9 1.0 reshape_reshape.17
  10.9 12.0 %all-to-all-start = ((bf16[32,64,128]{2,1,0:T(8,128)(2,1)}), bf16[32,64,128]{2,1,0:T(8,128)(2,1)S(1)}, u32[]{:S(2)}, u32[]{:S(2)}) async-start(bf16[32,64,128]{2,1,0:T(8,128)(2,1)} %reshape_reshape.17), calls=%async_computation | async-start | bytes 1048576 | tf_op jit(solution)/shard_map/all_to_all | solution.py:169
  28.9 8.6 %all-to-all-done = bf16[32,64,128]{2,1,0:T(8,128)(2,1)S(1)} async-done(((bf16[32,64,128]{2,1,0:T(8,128)(2,1)}), bf16[32,64,128]{2,1,0:T(8,128)(2,1)S(1)}, u32[]{:S(2)}, u32[]{:S(2)}) %all-to-all-start) | async-done | bytes 524320 | tf_op jit(solution)/shard_map/all_to_all | solution.py:169
  39.5 1.4 fusion.159
  40.9 1.2 fusion.31
  42.2 2.0 %fusion.12 = (f32[2,8,128]{2,1,0:T(8,128)S(1)}, bf16[2,8,128,384]{3,2,1,0:T(8,128)(2,1)S(1)}) fusion(f32[2,8,128,384]{3,2,1,0:T(8,128)S(1)} %get-tuple-element.69, f32[2,8,128]{2,1,0:T(8,128)S(1)} %multiply_divide_fusion, f32[2,8,128]{2,1,0:T(8,128)S(1)} %get-tuple-element.68, pred[2,128,384]{2,1,0:T(8,128)(4,1)S(1)} %broadcast_or_fusion, ...), kind=kOutput, calls=%fused_computation.16 | convolution fusion | flops 811464704 | bytes 6168576 | tf_op jit(solution)/shard_map/transpose(jvp(bhqk,bkf->bhqf))/dot_general | solution.py:110
  44.2 3.0 %divide_convert_fusion = (bf16[2,8,128,384]{3,2,1,0:T(8,128)(2,1)S(1)}, f32[2,8,128]{2,1,0:T(8,128)S(1)}, f32[2,8,128]{2,1,0:T(8,128)S(1)}, pred[2,8,128,384]{3,2,1,0:T(32,128)(4,1)S(1)}) fusion(f32[2,8,128,384]{3,2,1,0:T(8,128)S(1)} %get-tuple-element.69, f32[2,8,128]{2,1,0:T(8,128)S(1)} %fusion.31, f32[2,8,128]{2,1,0:T(8,128)S(1)} %get-tuple-element.68, ...), kind=kLoop, calls=%fused_computation.19 | loop fusion | flops 10219520 | bytes 7217152 | tf_op jit(solution)/shard_map/jvp()/convert_element_type | solution.py:109
  47.2 3.0 %multiply_reduce_fusion = f32[2,128,512]{2,1,0:T(8,128)S(1)} fusion(f32[8,512]{1,0:T(8,128)S(1)} %fusion.125, pred[2,8,128,384]{3,2,1,0:T(32,128)(4,1)S(1)} %get-tuple-element.15, f32[2,8,128]{2,1,0:T(8,128)S(1)} %negate_divide_fusion, pred[2,128,384]{2,1,0:T(8,128)(4,1)S(1)} %broadcast_or_fusion, bf16[1,384,512]{2,1,0:T(8,128)(2,1)S(1)} %get-tuple-element.77, ...), kind=kOutput, calls=%fused_computation.8 | convolution fusion | flops 815529984 | bytes 6963200 | tf_op jit(solution)/shard_map/transpose(jvp(bhqf,bkf->bhqk))/dot_general | solution.py:105
  50.2 2.8 %fusion.45 = f32[2,384,512]{2,1,0:T(8,128)S(1)} fusion(f32[8,512]{1,0:T(8,128)S(1)} %fusion.125, f32[2,128,512]{2,1,0:T(8,128)S(1)} %slice.169, pred[2,8,128,384]{3,2,1,0:T(32,128)(4,1)S(1)} %get-tuple-element.15, f32[2,8,128]{2,1,0:T(8,128)S(1)} %negate_divide_fusion, pred[2,128,384]{2,1,0:T(8,128)(4,1)S(1)} %broadcast_or_fusion, ...), kind=kOutput, calls=%fused_computation.60 | convolution fusion | flops 814219264 | bytes 7749632 | tf_op jit(solution)/shard_map/transpose(jvp(bhqf,bkf->bhqk))/dot_general | solution.py:105
  53.0 1.3 multiply_reduce_fusion.1
  54.3 1.1 fusion.48
  57.4 0.7 fusion.85
  58.1 1.0 fusion.155
  59.2 0.9 pad_maximum_fusion.1
  60.0 2.1 %reshape_reshape.19 = bf16[32,64,128]{2,1,0:T(8,128)(2,1)} reshape(bf16[256,1024]{1,0:T(8,128)(2,1)} %pad_maximum_fusion.1) | data formatting | bytes 1048576 | tf_op jit(solution)/shard_map/reshape;reshape | solution.py:168
  62.1 7.4 %all-to-all-start.1 = ((bf16[32,64,128]{2,1,0:T(8,128)(2,1)}), bf16[32,64,128]{2,1,0:T(8,128)(2,1)}, u32[]{:S(2)}, u32[]{:S(2)}) async-start(bf16[32,64,128]{2,1,0:T(8,128)(2,1)} %reshape_reshape.19), calls=%async_computation.1 | async-start | bytes 1048576 | tf_op jit(solution)/shard_map/all_to_all | solution.py:169
  70.1 1.8 %copy.59 = bf16[256,512]{0,1:T(8,128)(2,1)} copy(bf16[256,512]{1,0:T(8,128)(2,1)} %bitcast.189) | data formatting | bytes 524288 | tf_op jit(solution)/shard_map/jvp()/convert_element_type | solution.py:112
  71.9 1.8 %reshape.367 = bf16[32,8,512]{2,1,0:T(8,128)(2,1)} reshape(bf16[512,256]{1,0:T(8,128)(2,1)} %bitcast.185) | data formatting | bytes 524288 | tf_op jit(solution)/shard_map/reshape | solution.py:161
  73.6 1.7 %copy.60 = bf16[8,32,512]{2,1,0:T(8,128)(2,1)} copy(bf16[8,32,512]{2,0,1:T(8,128)(2,1)} %bitcast.186) | data formatting | bytes 524288 | tf_op jit(solution)/shard_map/transpose | solution.py:162
  75.4 1.8 %dot_general.106 = bf16[8,64,256]{2,1,0:T(8,128)(2,1)} reshape(bf16[8,32,512]{2,1,0:T(8,128)(2,1)} %copy.60) | data formatting | bytes 524288 | tf_op jit(solution)/shard_map/dot_general | solution.py:163
  77.1 1.8 %copy.57 = bf16[512,256]{1,0:T(8,128)(2,1)} copy(bf16[512,256]{0,1:T(8,128)(2,1)} %get-tuple-element.53) | data formatting | bytes 524288 | tf_op jit(solution)/shard_map/transpose | solution.py:161
  78.9 1.7 %reshape.366 = bf16[32,8,512]{2,1,0:T(8,128)(2,1)} reshape(bf16[512,256]{1,0:T(8,128)(2,1)} %copy.57) | data formatting | bytes 524288 | tf_op jit(solution)/shard_map/reshape | solution.py:161
  80.7 1.7 %copy.58 = bf16[8,32,512]{2,1,0:T(8,128)(2,1)} copy(bf16[8,32,512]{2,0,1:T(8,128)(2,1)} %bitcast.187) | data formatting | bytes 524288 | tf_op jit(solution)/shard_map/transpose | solution.py:162
  82.4 1.7 %dot_general.104 = bf16[8,64,256]{2,1,0:T(8,128)(2,1)} reshape(bf16[8,32,512]{2,1,0:T(8,128)(2,1)} %copy.58) | data formatting | bytes 524288 | tf_op jit(solution)/shard_map/dot_general | solution.py:163
  84.2 1.2 convolution_convert_fusion.3
  85.4 1.5 convolution_convert_fusion
  86.9 1.6 %pad_maximum_fusion = bf16[8,64,2048]{2,1,0:T(8,128)(2,1)} fusion(bf16[8,64,512]{2,1,0:T(8,128)(2,1)S(1)} %convolution_convert_fusion.3, bf16[8,64,1536]{2,1,0:T(8,128)(2,1)S(1)} %convolution_convert_fusion), kind=kLoop, calls=%fused_computation.35 | loop fusion | flops 4194304 | bytes 4194304 | tf_op jit(solution)/shard_map/concatenate | solution.py:254
  88.6 6.1 %all-to-all-start.2 = ((bf16[8,64,2048]{2,1,0:T(8,128)(2,1)}), bf16[8,64,2048]{2,1,0:T(8,128)(2,1)}, u32[]{:S(2)}, u32[]{:S(2)}) async-start(bf16[8,64,2048]{2,1,0:T(8,128)(2,1)} %pad_maximum_fusion), calls=%async_computation.2 | async-start | bytes 4194304 | tf_op jit(solution)/shard_map/all_to_all | solution.py:178
  94.7 2.1 %reshape_reshape.20 = bf16[256,1024]{1,0:T(8,128)(2,1)} reshape(bf16[32,64,128]{2,1,0:T(8,128)(2,1)} %all-to-all-done.1) | data formatting | bytes 1048576 | tf_op jit(solution)/shard_map/reshape;reshape | solution.py:244
  96.7 1.3 fusion.117
  98.4 1.5 convert_reduce_fusion.3
  100.6 2.1 %multiply_reduce_fusion.2 = f32[128,512]{1,0:T(8,128)} fusion(f32[8,512]{1,0:T(8,128)S(1)} %copy-done.17, f32[8,128,128]{1,2,0:T(8,128)S(1)} %get-tuple-element.5, pred[8,128,128]{1,2,0:T(32,128)(4,1)S(1)} %get-tuple-element.7, f32[8,128]{1,0:T(8,128)S(1)} %negate_divide_fusion.1, bf16[1,128,1536]{2,1,0:T(8,128)(2,1)} %copy-done.11), kind=kOutput, calls=%fused_computation.36 | convolution fusion | flops 135593984 | bytes 1069056 | tf_op jit(solution)/shard_map/transpose(jvp(bhqf,bkf->bhqk))/dot_general | solution.py:47
  102.7 1.8 %copy.56 = f32[128,512]{0,1:T(8,128)} copy(f32[128,512]{1,0:T(8,128)} %multiply_reduce_fusion.2) | data formatting | bytes 524288 | tf_op jit(solution)/shard_map/transpose(jvp())/reduce_sum | solution.py:46
  104.5 1.7 %fusion.60 = f32[1,128,512]{1,2,0:T(8,128)S(1)} fusion(f32[8,512]{1,0:T(8,128)S(1)} %copy-done.17, f32[128,512]{1,0:T(8,128)} %copy-done.12, f32[8,128,128]{1,2,0:T(8,128)S(1)} %get-tuple-element.5, pred[8,128,128]{1,2,0:T(32,128)(4,1)} %copy-done.27, f32[8,128]{1,0:T(8,128)S(1)} %negate_divide_fusion.1), kind=kOutput, calls=%fused_computation.70 | convolution fusion | flops 135135232 | bytes 1200128 | tf_op jit(solution)/shard_map/transpose(jvp(bhqf,bkf->bhqk))/dot_general | solution.py:47
  106.2 1.4 fusion.63
  107.7 0.7 fusion.97
  108.4 12.5 %all-to-all-done.2 = bf16[8,64,2048]{2,1,0:T(8,128)(2,1)} async-done(((bf16[8,64,2048]{2,1,0:T(8,128)(2,1)}), bf16[8,64,2048]{2,1,0:T(8,128)(2,1)}, u32[]{:S(2)}, u32[]{:S(2)}) %all-to-all-start.2) | async-done | bytes 2097184 | tf_op jit(solution)/shard_map/all_to_all | solution.py:178
  121.0 2.0 %reduce_sum.284 = bf16[64,2048]{1,0:T(8,128)(2,1)S(1)} reduce(bf16[8,64,2048]{2,1,0:T(8,128)(2,1)} %all-to-all-done.2, bf16[]{:T(256)} %constant.93.clone.1), dimensions={0}, to_apply=%region_25.26 | reduce | flops 917504 | bytes 2359298 | tf_op jit(solution)/shard_map/reduce_sum | solution.py:179
  122.9 0.8 reshape_reshape.21
  123.8 9.4 %all-to-all-start.3 = ((bf16[32,32,128]{2,1,0:T(8,128)(2,1)}), bf16[32,32,128]{2,1,0:T(8,128)(2,1)S(1)}, u32[]{:S(2)}, u32[]{:S(2)}) async-start(bf16[32,32,128]{2,1,0:T(8,128)(2,1)} %reshape_reshape.21), calls=%async_computation.3 | async-start | bytes 524288 | tf_op jit(solution)/shard_map/all_to_all | solution.py:169
  133.4 0.8 fusion.113
  134.2 8.6 %all-to-all-done.3 = bf16[32,32,128]{2,1,0:T(8,128)(2,1)S(1)} async-done(((bf16[32,32,128]{2,1,0:T(8,128)(2,1)}), bf16[32,32,128]{2,1,0:T(8,128)(2,1)S(1)}, u32[]{:S(2)}, u32[]{:S(2)}) %all-to-all-start.3) | async-done | bytes 262176 | tf_op jit(solution)/shard_map/all_to_all | solution.py:169
  143.5 6.9 %all-to-all-start.4 = ((f32[8,32,128]{2,1,0:T(8,128)}), f32[8,32,128]{2,1,0:T(8,128)S(1)}, u32[]{:S(2)}, u32[]{:S(2)}) async-start(f32[8,32,128]{2,1,0:T(8,128)} %broadcast_in_dim.87), calls=%async_computation.4 | async-start | bytes 262144 | tf_op jit(solution)/shard_map/all_to_all | solution.py:169
  151.2 4.6 %all-to-all-done.4 = f32[8,32,128]{2,1,0:T(8,128)S(1)} async-done(((f32[8,32,128]{2,1,0:T(8,128)}), f32[8,32,128]{2,1,0:T(8,128)S(1)}, u32[]{:S(2)}, u32[]{:S(2)}) %all-to-all-start.4) | async-done | bytes 131104 | tf_op jit(solution)/shard_map/all_to_all | solution.py:169
  (130 shorter events, 14.7 us)
Async XLA Ops:
  0.6 37.4 %copy-start = (bf16[512,1536]{1,0:T(8,128)(2,1)S(1)}, bf16[512,1536]{1,0:T(8,128)(2,1)}, u32[]{:S(2)}) copy-start(bf16[512,1536]{1,0:T(8,128)(2,1)} %param.16) | copy-start | bytes 4718596
  2.9 5.8 %copy-start.25 = (f32[128]{0:T(128)}, f32[128]{0:T(128)S(1)}, u32[]{:S(2)}) copy-start(f32[128]{0:T(128)S(1)} %fusion.94) | copy-start | bytes 1540
  2.9 51.4 %copy-start.16 = (f32[8,512]{1,0:T(8,128)}, f32[8,512]{1,0:T(8,128)S(1)}, u32[]{:S(2)}) copy-start(f32[8,512]{1,0:T(8,128)S(1)} %fusion.125) | copy-start | bytes 49156
  4.7 4.2 %copy-start.18 = (s32[128]{0:T(128)}, s32[128]{0:T(128)S(1)}, u32[]{:S(2)}) copy-start(s32[128]{0:T(128)S(1)} %fusion.130) | copy-start | bytes 1540
  4.7 3.9 %copy-start.1 = (bf16[1,128,512]{2,1,0:T(8,128)(2,1)S(1)}, bf16[1,128,512]{2,1,0:T(8,128)(2,1)}, u32[]{:S(2)}) copy-start(bf16[1,128,512]{2,1,0:T(8,128)(2,1)} %param.10) | copy-start | bytes 393220
  4.7 4.0 %copy-start.2 = (bf16[512,512]{1,0:T(8,128)(2,1)S(1)}, bf16[512,512]{1,0:T(8,128)(2,1)}, u32[]{:S(2)}) copy-start(bf16[512,512]{1,0:T(8,128)(2,1)} %param.14) | copy-start | bytes 1572868
  6.7 2.2 %copy-start.11 = (bf16[1,128,1536]{2,1,0:T(8,128)(2,1)}, bf16[1,128,1536]{2,1,0:T(8,128)(2,1)S(1)}, u32[]{:S(2)}) copy-start(bf16[1,128,1536]{2,1,0:T(8,128)(2,1)S(1)} %fusion.22) | copy-start | bytes 1179652
  6.7 2.9 %copy-start.6 = (bf16[1,128,512]{2,1,0:T(8,128)(2,1)S(1)}, bf16[1,128,512]{2,1,0:T(8,128)(2,1)}, u32[]{:S(2)}) copy-start(bf16[1,128,512]{2,1,0:T(8,128)(2,1)} %param.11) | copy-start | bytes 393220
  6.7 0.8 copy-start.12
  8.1 14.8 %copy-start.15 = (s32[1,4096]{1,0:T(1,128)S(1)}, s32[1,4096]{1,0:T(1,128)}, u32[]{:S(2)}) copy-start(s32[1,4096]{1,0:T(1,128)} %param.18) | copy-start | bytes 49156
  8.1 16.7 %copy-start.21 = (s32[1,1,2,2]{3,2,1,0:T(2,128)S(1)}, s32[1,1,2,2]{3,2,1,0:T(2,128)}, u32[]{:S(2)}) copy-start(s32[1,1,2,2]{3,2,1,0:T(2,128)} %param.19) | copy-start | bytes 52
  8.7 29.4 %copy-start.22 = (f32[512]{0:T(512)S(1)}, f32[512]{0:T(512)}, u32[]{:S(2)}) copy-start(f32[512]{0:T(512)} %param.15) | copy-start | bytes 6148
  8.9 0.7 copy-start.8
  10.9 26.5 %all-to-all-start = ((bf16[32,64,128]{2,1,0:T(8,128)(2,1)}), bf16[32,64,128]{2,1,0:T(8,128)(2,1)S(1)}, u32[]{:S(2)}, u32[]{:S(2)}) async-start(bf16[32,64,128]{2,1,0:T(8,128)(2,1)} %reshape_reshape.17), calls=%async_computation | async-start | bytes 1048576 | tf_op jit(solution)/shard_map/all_to_all | solution.py:169
  38.0 1.0 copy-start.4
  54.3 1.4 copy-start.10
  56.7 0.7 copy-start.23
  62.1 26.5 %all-to-all-start.1 = ((bf16[32,64,128]{2,1,0:T(8,128)(2,1)}), bf16[32,64,128]{2,1,0:T(8,128)(2,1)}, u32[]{:S(2)}, u32[]{:S(2)}) async-start(bf16[32,64,128]{2,1,0:T(8,128)(2,1)} %reshape_reshape.19), calls=%async_computation.1 | async-start | bytes 1048576 | tf_op jit(solution)/shard_map/all_to_all | solution.py:169
  88.5 8.2 %copy-start.19 = (s32[128]{0:T(128)S(1)}, s32[128]{0:T(128)}, u32[]{:S(2)}) copy-start(s32[128]{0:T(128)} %copy-done.18) | copy-start | bytes 1540
  88.5 9.5 %copy-start.3 = (bf16[512,512]{1,0:T(8,128)(2,1)S(1)}, bf16[512,512]{1,0:T(8,128)(2,1)}, u32[]{:S(2)}) copy-start(bf16[512,512]{1,0:T(8,128)(2,1)} %param.14) | copy-start | bytes 1572868
  88.6 9.5 %copy-start.7 = (bf16[1,128,512]{2,1,0:T(8,128)(2,1)S(1)}, bf16[1,128,512]{2,1,0:T(8,128)(2,1)}, u32[]{:S(2)}) copy-start(bf16[1,128,512]{2,1,0:T(8,128)(2,1)} %param.11) | copy-start | bytes 393220
  88.6 9.8 %copy-start.17 = (f32[8,512]{1,0:T(8,128)S(1)}, f32[8,512]{1,0:T(8,128)}, u32[]{:S(2)}) copy-start(f32[8,512]{1,0:T(8,128)} %copy-done.16) | copy-start | bytes 49156
  88.6 9.8 %copy-start.20 = (f32[8,128]{1,0:T(8,128)S(1)}, f32[8,128]{1,0:T(8,128)}, u32[]{:S(2)}) copy-start(f32[8,128]{1,0:T(8,128)} %multiply_divide_fusion.1) | copy-start | bytes 12292
  88.6 32.4 %all-to-all-start.2 = ((bf16[8,64,2048]{2,1,0:T(8,128)(2,1)}), bf16[8,64,2048]{2,1,0:T(8,128)(2,1)}, u32[]{:S(2)}, u32[]{:S(2)}) async-start(bf16[8,64,2048]{2,1,0:T(8,128)(2,1)} %pad_maximum_fusion), calls=%async_computation.2 | async-start | bytes 4194304 | tf_op jit(solution)/shard_map/all_to_all | solution.py:178
  98.4 1.7 %copy-start.14 = (f32[128,512]{1,0:T(8,128)}, f32[128,512]{1,0:T(8,128)S(1)}, u32[]{:S(2)}) copy-start(f32[128,512]{1,0:T(8,128)S(1)} %fusion.67) | copy-start | bytes 786436
  99.9 0.7 copy-start.27
  100.6 7.0 %copy-start.24 = (f32[512]{0:T(512)S(1)}, f32[512]{0:T(512)}, u32[]{:S(2)}) copy-start(f32[512]{0:T(512)} %param.12) | copy-start | bytes 6148
  104.5 3.2 %copy-start.5 = (bf16[512,1536]{1,0:T(8,128)(2,1)S(1)}, bf16[512,1536]{1,0:T(8,128)(2,1)}, u32[]{:S(2)}) copy-start(bf16[512,1536]{1,0:T(8,128)(2,1)} %param.13) | copy-start | bytes 4718596
  104.5 3.2 %copy-start.13 = (f32[128,512]{0,1:T(8,128)S(1)}, f32[128,512]{0,1:T(8,128)}, u32[]{:S(2)}) copy-start(f32[128,512]{0,1:T(8,128)} %copy.56) | copy-start | bytes 786436
  106.2 2.2 %copy-start.26 = (f32[128]{0:T(128)S(1)}, f32[128]{0:T(128)}, u32[]{:S(2)}) copy-start(f32[128]{0:T(128)} %copy-done.25) | copy-start | bytes 1540
  108.4 42.1 %copy-start.9 = (bf16[128,512]{1,0:T(8,128)(2,1)S(1)}, bf16[128,512]{1,0:T(8,128)(2,1)}, u32[]{:S(2)}) copy-start(bf16[128,512]{1,0:T(8,128)(2,1)} %copy-done.8) | copy-start | bytes 393220
  123.8 19.1 %all-to-all-start.3 = ((bf16[32,32,128]{2,1,0:T(8,128)(2,1)}), bf16[32,32,128]{2,1,0:T(8,128)(2,1)S(1)}, u32[]{:S(2)}, u32[]{:S(2)}) async-start(bf16[32,32,128]{2,1,0:T(8,128)(2,1)} %reshape_reshape.21), calls=%async_computation.3 | async-start | bytes 524288 | tf_op jit(solution)/shard_map/all_to_all | solution.py:169
  143.5 12.2 %all-to-all-start.4 = ((f32[8,32,128]{2,1,0:T(8,128)}), f32[8,32,128]{2,1,0:T(8,128)S(1)}, u32[]{:S(2)}, u32[]{:S(2)}) async-start(f32[8,32,128]{2,1,0:T(8,128)} %broadcast_in_dim.87), calls=%async_computation.4 | async-start | bytes 262144 | tf_op jit(solution)/shard_map/all_to_all | solution.py:169

commit v15 on v13

--- a/solution.py
+++ b/solution.py
@@ -179,10 +179,10 @@
     terms = jnp.sum(terms.astype(jnp.float32), axis=0).astype(jnp.bfloat16)
     terms = terms.reshape(owners, per_device, width)
     terms = dense_all_to_all(terms, "ev")
-    piece = jnp.sum(terms.astype(jnp.float32), axis=0)
+    piece = jnp.sum(terms.astype(jnp.float32), axis=0).astype(jnp.bfloat16)
     copies = jnp.broadcast_to(piece[None], (replicas, per_device, width))
     gathered = dense_all_to_all(copies, "dp")
-    return gathered.reshape(replicas * per_device, width)
+    return gathered.reshape(replicas * per_device, width).astype(jnp.float32)
 
 
 def on_device(

time: 159 us -> 158 us (level)
  no operation moved by 1% of the time
where the time goes in v15:
time: 158 us; the launch traced here: 157 us
  starting transfers between devices  41.9 us (27%)
  waiting for transfers between devices  33.2 us (21%)
  local copies, waits for them, and re-layouts  29.2 us (18%)
  matrix products  28.7 us (18%)
  other arithmetic  18.6 us (12%)
  between operations  5.22 us (3%)
    all_to_all x4, starting transfers between devices, dense_all_to_all(): moved = lax.all_to_all(flat, axis_name, 0, 0, tiled=True)  35.8 us
    all_to_all x4, waiting for transfers between devices, dense_all_to_all(): moved = lax.all_to_all(flat, axis_name, 0, 0, tiled=True)  20.7 us
    all_to_all x1, waiting for transfers between devices, reduce_weight_terms(): terms = lax.all_to_all(terms, 'dp', 0, 0, tiled=True)  12.5 us
    dot_general x3, matrix products, cross_account_inner(): jnp.einsum('bhqf,bkf->bhqk', masked_queries, key_rows) * HEAD_DIM ** (-0.5)  7.18 us
    all_to_all x1, starting transfers between devices, reduce_weight_terms(): terms = lax.all_to_all(terms, 'dp', 0, 0, tiled=True)  6.08 us
    dot_general x3, matrix products, cross_account_inner(): jnp.einsum('bhqk,bkf->bhqf', attention.astype(jnp.float32), value_rows)  4.33 us
    dot_general x3, matrix products, intra_branch(): jnp.einsum('bhqf,bkf->bhqk', masked_queries, key_rows) * HEAD_DIM ** (-0.5)  4.27 us
    another operation x3, local copies, waits for them, and re-layouts, dense_all_to_all(): flat = pieces.reshape(count, -1, 128)  3.89 us
  transfers between devices with their start and end apart: 5, of which 4 were waited for; matrix products, arithmetic and copies ran while one was open for 23% of the time, Pallas kernels for 0%

profile of v15, /device:TPU:1, one launch (start us, length us, event | category | flops | bytes accessed | tf_op | source)
XLA Modules:
  0.0 156.8 jit_solution(8072191395042482330)
XLA Ops:
  0.7 1.1 convert_reduce_fusion.4
  1.8 1.1 fusion.94
  2.9 0.8 dynamic-slice.1
  4.8 2.0 %fusion.22 = bf16[1,128,1536]{2,1,0:T(8,128)(2,1)S(1)} fusion(bf16[512,1536]{1,0:T(8,128)(2,1)} %param.13, bf16[1,128,512]{2,1,0:T(8,128)(2,1)} %param.10, f32[512]{0:T(512)} %param.12, f32[128]{0:T(128)S(1)} %fusion.132, f32[128]{0:T(128)S(1)} %broadcast_multiply_fusion.1), kind=kOutput, calls=%fused_computation.34 | convolution fusion | flops 201850880 | bytes 2100224 | tf_op jit(solution)/shard_map/jvp()/dot_general | solution.py:38
  6.9 0.8 copy-done.12
  10.0 1.0 reshape_reshape.17
  11.0 12.0 %all-to-all-start = ((bf16[32,64,128]{2,1,0:T(8,128)(2,1)}), bf16[32,64,128]{2,1,0:T(8,128)(2,1)S(1)}, u32[]{:S(2)}, u32[]{:S(2)}) async-start(bf16[32,64,128]{2,1,0:T(8,128)(2,1)} %reshape_reshape.17), calls=%async_computation | async-start | bytes 1048576 | tf_op jit(solution)/shard_map/all_to_all | solution.py:169
  29.7 7.9 %all-to-all-done = bf16[32,64,128]{2,1,0:T(8,128)(2,1)S(1)} async-done(((bf16[32,64,128]{2,1,0:T(8,128)(2,1)}), bf16[32,64,128]{2,1,0:T(8,128)(2,1)S(1)}, u32[]{:S(2)}, u32[]{:S(2)}) %all-to-all-start) | async-done | bytes 524320 | tf_op jit(solution)/shard_map/all_to_all | solution.py:169
  39.7 1.4 fusion.159
  41.0 1.2 fusion.31
  42.3 2.0 %fusion.12 = (f32[2,8,128]{2,1,0:T(8,128)S(1)}, bf16[2,8,128,384]{3,2,1,0:T(8,128)(2,1)S(1)}) fusion(f32[2,8,128,384]{3,2,1,0:T(8,128)S(1)} %get-tuple-element.69, f32[2,8,128]{2,1,0:T(8,128)S(1)} %multiply_divide_fusion, f32[2,8,128]{2,1,0:T(8,128)S(1)} %get-tuple-element.68, pred[2,128,384]{2,1,0:T(8,128)(4,1)S(1)} %broadcast_or_fusion, ...), kind=kOutput, calls=%fused_computation.16 | convolution fusion | flops 811464704 | bytes 6168576 | tf_op jit(solution)/shard_map/transpose(jvp(bhqk,bkf->bhqf))/dot_general | solution.py:110
  44.3 3.0 %divide_convert_fusion = (bf16[2,8,128,384]{3,2,1,0:T(8,128)(2,1)S(1)}, f32[2,8,128]{2,1,0:T(8,128)S(1)}, f32[2,8,128]{2,1,0:T(8,128)S(1)}, pred[2,8,128,384]{3,2,1,0:T(32,128)(4,1)S(1)}) fusion(f32[2,8,128,384]{3,2,1,0:T(8,128)S(1)} %get-tuple-element.69, f32[2,8,128]{2,1,0:T(8,128)S(1)} %fusion.31, f32[2,8,128]{2,1,0:T(8,128)S(1)} %get-tuple-element.68, ...), kind=kLoop, calls=%fused_computation.19 | loop fusion | flops 10219520 | bytes 7217152 | tf_op jit(solution)/shard_map/jvp()/convert_element_type | solution.py:109
  47.3 3.0 %multiply_reduce_fusion = f32[2,128,512]{2,1,0:T(8,128)S(1)} fusion(f32[8,512]{1,0:T(8,128)S(1)} %fusion.126, pred[2,8,128,384]{3,2,1,0:T(32,128)(4,1)S(1)} %get-tuple-element.15, f32[2,8,128]{2,1,0:T(8,128)S(1)} %negate_divide_fusion, pred[2,128,384]{2,1,0:T(8,128)(4,1)S(1)} %broadcast_or_fusion, bf16[1,384,512]{2,1,0:T(8,128)(2,1)S(1)} %get-tuple-element.77, ...), kind=kOutput, calls=%fused_computation.8 | convolution fusion | flops 815529984 | bytes 6963200 | tf_op jit(solution)/shard_map/transpose(jvp(bhqf,bkf->bhqk))/dot_general | solution.py:105
  50.4 2.8 %fusion.45 = f32[2,384,512]{2,1,0:T(8,128)S(1)} fusion(f32[8,512]{1,0:T(8,128)S(1)} %fusion.126, f32[2,128,512]{2,1,0:T(8,128)S(1)} %slice.169, pred[2,8,128,384]{3,2,1,0:T(32,128)(4,1)S(1)} %get-tuple-element.15, f32[2,8,128]{2,1,0:T(8,128)S(1)} %negate_divide_fusion, pred[2,128,384]{2,1,0:T(8,128)(4,1)S(1)} %broadcast_or_fusion, ...), kind=kOutput, calls=%fused_computation.60 | convolution fusion | flops 814219264 | bytes 7749632 | tf_op jit(solution)/shard_map/transpose(jvp(bhqf,bkf->bhqk))/dot_general | solution.py:105
  53.2 1.3 multiply_reduce_fusion.1
  54.5 1.1 fusion.48
  58.2 1.0 fusion.155
  59.3 0.9 pad_maximum_fusion.1
  60.2 2.1 %reshape_reshape.19 = bf16[32,64,128]{2,1,0:T(8,128)(2,1)} reshape(bf16[256,1024]{1,0:T(8,128)(2,1)} %pad_maximum_fusion.1) | data formatting | bytes 1048576 | tf_op jit(solution)/shard_map/reshape;reshape | solution.py:168
  62.2 7.4 %all-to-all-start.1 = ((bf16[32,64,128]{2,1,0:T(8,128)(2,1)}), bf16[32,64,128]{2,1,0:T(8,128)(2,1)}, u32[]{:S(2)}, u32[]{:S(2)}) async-start(bf16[32,64,128]{2,1,0:T(8,128)(2,1)} %reshape_reshape.19), calls=%async_computation.1 | async-start | bytes 1048576 | tf_op jit(solution)/shard_map/all_to_all | solution.py:169
  70.2 1.8 %copy.71 = bf16[256,512]{0,1:T(8,128)(2,1)} copy(bf16[256,512]{1,0:T(8,128)(2,1)} %bitcast.188) | data formatting | bytes 524288 | tf_op jit(solution)/shard_map/jvp()/convert_element_type | solution.py:112
  72.0 1.8 %reshape.369 = bf16[32,8,512]{2,1,0:T(8,128)(2,1)} reshape(bf16[512,256]{1,0:T(8,128)(2,1)} %bitcast.184) | data formatting | bytes 524288 | tf_op jit(solution)/shard_map/reshape | solution.py:161
  73.8 1.7 %copy.72 = bf16[8,32,512]{2,1,0:T(8,128)(2,1)} copy(bf16[8,32,512]{2,0,1:T(8,128)(2,1)} %bitcast.185) | data formatting | bytes 524288 | tf_op jit(solution)/shard_map/transpose | solution.py:162
  75.5 1.8 %dot_general.106 = bf16[8,64,256]{2,1,0:T(8,128)(2,1)} reshape(bf16[8,32,512]{2,1,0:T(8,128)(2,1)} %copy.72) | data formatting | bytes 524288 | tf_op jit(solution)/shard_map/dot_general | solution.py:163
  77.3 1.8 %copy.69 = bf16[512,256]{1,0:T(8,128)(2,1)} copy(bf16[512,256]{0,1:T(8,128)(2,1)} %get-tuple-element.53) | data formatting | bytes 524288 | tf_op jit(solution)/shard_map/transpose | solution.py:161
  79.1 1.7 %reshape.368 = bf16[32,8,512]{2,1,0:T(8,128)(2,1)} reshape(bf16[512,256]{1,0:T(8,128)(2,1)} %copy.69) | data formatting | bytes 524288 | tf_op jit(solution)/shard_map/reshape | solution.py:161
  80.8 1.7 %copy.70 = bf16[8,32,512]{2,1,0:T(8,128)(2,1)} copy(bf16[8,32,512]{2,0,1:T(8,128)(2,1)} %bitcast.186) | data formatting | bytes 524288 | tf_op jit(solution)/shard_map/transpose | solution.py:162
  82.5 1.7 %dot_general.104 = bf16[8,64,256]{2,1,0:T(8,128)(2,1)} reshape(bf16[8,32,512]{2,1,0:T(8,128)(2,1)} %copy.70) | data formatting | bytes 524288 | tf_op jit(solution)/shard_map/dot_general | solution.py:163
  84.3 1.2 convolution_convert_fusion.3
  85.5 1.5 convolution_convert_fusion
  87.1 1.6 %pad_maximum_fusion = bf16[8,64,2048]{2,1,0:T(8,128)(2,1)} fusion(bf16[8,64,512]{2,1,0:T(8,128)(2,1)S(1)} %convolution_convert_fusion.3, bf16[8,64,1536]{2,1,0:T(8,128)(2,1)S(1)} %convolution_convert_fusion), kind=kLoop, calls=%fused_computation.35 | loop fusion | flops 4194304 | bytes 4194304 | tf_op jit(solution)/shard_map/concatenate | solution.py:255
  88.7 6.1 %all-to-all-start.2 = ((bf16[8,64,2048]{2,1,0:T(8,128)(2,1)}), bf16[8,64,2048]{2,1,0:T(8,128)(2,1)}, u32[]{:S(2)}, u32[]{:S(2)}) async-start(bf16[8,64,2048]{2,1,0:T(8,128)(2,1)} %pad_maximum_fusion), calls=%async_computation.2 | async-start | bytes 4194304 | tf_op jit(solution)/shard_map/all_to_all | solution.py:178
  94.8 2.1 %reshape_reshape.20 = bf16[256,1024]{1,0:T(8,128)(2,1)} reshape(bf16[32,64,128]{2,1,0:T(8,128)(2,1)} %all-to-all-done.1) | data formatting | bytes 1048576 | tf_op jit(solution)/shard_map/reshape;reshape | solution.py:245
  96.9 1.3 fusion.117
  98.6 1.5 convert_reduce_fusion.2
  100.7 2.1 %multiply_reduce_fusion.2 = f32[128,512]{1,0:T(8,128)} fusion(f32[8,512]{1,0:T(8,128)S(1)} %copy-done.17, f32[8,128,128]{1,2,0:T(8,128)S(1)} %get-tuple-element.5, pred[8,128,128]{1,2,0:T(32,128)(4,1)S(1)} %get-tuple-element.7, f32[8,128]{1,0:T(8,128)S(1)} %negate_divide_fusion.1, bf16[1,128,1536]{2,1,0:T(8,128)(2,1)} %copy-done.11), kind=kOutput, calls=%fused_computation.36 | convolution fusion | flops 135593984 | bytes 1069056 | tf_op jit(solution)/shard_map/transpose(jvp(bhqf,bkf->bhqk))/dot_general | solution.py:47
  102.8 1.8 %copy.68 = f32[128,512]{0,1:T(8,128)} copy(f32[128,512]{1,0:T(8,128)} %multiply_reduce_fusion.2) | data formatting | bytes 524288 | tf_op jit(solution)/shard_map/transpose(jvp())/reduce_sum | solution.py:46
  104.6 1.7 %fusion.60 = f32[1,128,512]{1,2,0:T(8,128)S(1)} fusion(f32[8,512]{1,0:T(8,128)S(1)} %copy-done.17, f32[128,512]{1,0:T(8,128)} %copy-done.12, f32[8,128,128]{1,2,0:T(8,128)S(1)} %get-tuple-element.5, pred[8,128,128]{1,2,0:T(32,128)(4,1)} %copy-done.27, f32[8,128]{1,0:T(8,128)S(1)} %negate_divide_fusion.1), kind=kOutput, calls=%fused_computation.70 | convolution fusion | flops 135135232 | bytes 1200128 | tf_op jit(solution)/shard_map/transpose(jvp(bhqf,bkf->bhqk))/dot_general | solution.py:47
  106.3 1.4 fusion.63
  107.8 0.7 fusion.97
  108.6 12.5 %all-to-all-done.2 = bf16[8,64,2048]{2,1,0:T(8,128)(2,1)} async-done(((bf16[8,64,2048]{2,1,0:T(8,128)(2,1)}), bf16[8,64,2048]{2,1,0:T(8,128)(2,1)}, u32[]{:S(2)}, u32[]{:S(2)}) %all-to-all-start.2) | async-done | bytes 2097184 | tf_op jit(solution)/shard_map/all_to_all | solution.py:178
  121.1 2.0 %reduce_sum.287 = bf16[64,2048]{1,0:T(8,128)(2,1)S(1)} reduce(bf16[8,64,2048]{2,1,0:T(8,128)(2,1)} %all-to-all-done.2, bf16[]{:T(256)} %constant.98.clone.1), dimensions={0}, to_apply=%region_25.26 | reduce | flops 917504 | bytes 2359298 | tf_op jit(solution)/shard_map/reduce_sum | solution.py:179
  123.1 0.8 reshape_reshape.21
  123.9 9.4 %all-to-all-start.3 = ((bf16[32,32,128]{2,1,0:T(8,128)(2,1)}), bf16[32,32,128]{2,1,0:T(8,128)(2,1)S(1)}, u32[]{:S(2)}, u32[]{:S(2)}) async-start(bf16[32,32,128]{2,1,0:T(8,128)(2,1)} %reshape_reshape.21), calls=%async_computation.3 | async-start | bytes 524288 | tf_op jit(solution)/shard_map/all_to_all | solution.py:169
  133.5 0.8 fusion.113
  134.4 8.6 %all-to-all-done.3 = bf16[32,32,128]{2,1,0:T(8,128)(2,1)S(1)} async-done(((bf16[32,32,128]{2,1,0:T(8,128)(2,1)}), bf16[32,32,128]{2,1,0:T(8,128)(2,1)S(1)}, u32[]{:S(2)}, u32[]{:S(2)}) %all-to-all-start.3) | async-done | bytes 262176 | tf_op jit(solution)/shard_map/all_to_all | solution.py:169
  143.7 6.9 %all-to-all-start.4 = ((bf16[8,32,128]{2,1,0:T(8,128)(2,1)}), bf16[8,32,128]{2,1,0:T(8,128)(2,1)S(1)}, u32[]{:S(2)}, u32[]{:S(2)}) async-start(bf16[8,32,128]{2,1,0:T(8,128)(2,1)} %broadcast_in_dim.162), calls=%async_computation.4 | async-start | bytes 131072 | tf_op jit(solution)/shard_map/all_to_all | solution.py:169
  151.3 4.2 %all-to-all-done.4 = bf16[8,32,128]{2,1,0:T(8,128)(2,1)S(1)} async-done(((bf16[8,32,128]{2,1,0:T(8,128)(2,1)}), bf16[8,32,128]{2,1,0:T(8,128)(2,1)S(1)}, u32[]{:S(2)}, u32[]{:S(2)}) %all-to-all-start.4) | async-done | bytes 65568 | tf_op jit(solution)/shard_map/all_to_all | solution.py:169
  (130 shorter events, 15.4 us)
Async XLA Ops:
  0.6 37.5 %copy-start = (bf16[512,1536]{1,0:T(8,128)(2,1)S(1)}, bf16[512,1536]{1,0:T(8,128)(2,1)}, u32[]{:S(2)}) copy-start(bf16[512,1536]{1,0:T(8,128)(2,1)} %param.16) | copy-start | bytes 4718596
  2.9 5.9 %copy-start.25 = (f32[128]{0:T(128)}, f32[128]{0:T(128)S(1)}, u32[]{:S(2)}) copy-start(f32[128]{0:T(128)S(1)} %fusion.94) | copy-start | bytes 1540
  2.9 51.5 %copy-start.16 = (f32[8,512]{1,0:T(8,128)}, f32[8,512]{1,0:T(8,128)S(1)}, u32[]{:S(2)}) copy-start(f32[8,512]{1,0:T(8,128)S(1)} %fusion.126) | copy-start | bytes 49156
  4.8 4.2 %copy-start.18 = (s32[128]{0:T(128)}, s32[128]{0:T(128)S(1)}, u32[]{:S(2)}) copy-start(s32[128]{0:T(128)S(1)} %fusion.131) | copy-start | bytes 1540
  4.8 3.9 %copy-start.1 = (bf16[1,128,512]{2,1,0:T(8,128)(2,1)S(1)}, bf16[1,128,512]{2,1,0:T(8,128)(2,1)}, u32[]{:S(2)}) copy-start(bf16[1,128,512]{2,1,0:T(8,128)(2,1)} %param.10) | copy-start | bytes 393220
  4.8 4.0 %copy-start.2 = (bf16[512,512]{1,0:T(8,128)(2,1)S(1)}, bf16[512,512]{1,0:T(8,128)(2,1)}, u32[]{:S(2)}) copy-start(bf16[512,512]{1,0:T(8,128)(2,1)} %param.14) | copy-start | bytes 1572868
  6.8 2.2 %copy-start.11 = (bf16[1,128,1536]{2,1,0:T(8,128)(2,1)}, bf16[1,128,1536]{2,1,0:T(8,128)(2,1)S(1)}, u32[]{:S(2)}) copy-start(bf16[1,128,1536]{2,1,0:T(8,128)(2,1)S(1)} %fusion.22) | copy-start | bytes 1179652
  6.8 2.9 %copy-start.6 = (bf16[1,128,512]{2,1,0:T(8,128)(2,1)S(1)}, bf16[1,128,512]{2,1,0:T(8,128)(2,1)}, u32[]{:S(2)}) copy-start(bf16[1,128,512]{2,1,0:T(8,128)(2,1)} %param.11) | copy-start | bytes 393220
  6.8 0.8 copy-start.12
  8.2 16.6 %copy-start.21 = (s32[1,1,2,2]{3,2,1,0:T(2,128)S(1)}, s32[1,1,2,2]{3,2,1,0:T(2,128)}, u32[]{:S(2)}) copy-start(s32[1,1,2,2]{3,2,1,0:T(2,128)} %param.19) | copy-start | bytes 52
  8.3 19.7 %copy-start.15 = (s32[1,4096]{1,0:T(1,128)S(1)}, s32[1,4096]{1,0:T(1,128)}, u32[]{:S(2)}) copy-start(s32[1,4096]{1,0:T(1,128)} %param.18) | copy-start | bytes 49156
  8.8 29.4 %copy-start.22 = (f32[512]{0:T(512)S(1)}, f32[512]{0:T(512)}, u32[]{:S(2)}) copy-start(f32[512]{0:T(512)} %param.15) | copy-start | bytes 6148
  9.0 0.7 copy-start.8
  11.0 26.5 %all-to-all-start = ((bf16[32,64,128]{2,1,0:T(8,128)(2,1)}), bf16[32,64,128]{2,1,0:T(8,128)(2,1)S(1)}, u32[]{:S(2)}, u32[]{:S(2)}) async-start(bf16[32,64,128]{2,1,0:T(8,128)(2,1)} %reshape_reshape.17), calls=%async_computation | async-start | bytes 1048576 | tf_op jit(solution)/shard_map/all_to_all | solution.py:169
  38.2 1.0 copy-start.4
  54.4 1.4 copy-start.10
  56.8 0.7 copy-start.23
  62.2 26.5 %all-to-all-start.1 = ((bf16[32,64,128]{2,1,0:T(8,128)(2,1)}), bf16[32,64,128]{2,1,0:T(8,128)(2,1)}, u32[]{:S(2)}, u32[]{:S(2)}) async-start(bf16[32,64,128]{2,1,0:T(8,128)(2,1)} %reshape_reshape.19), calls=%async_computation.1 | async-start | bytes 1048576 | tf_op jit(solution)/shard_map/all_to_all | solution.py:169
  88.7 8.2 %copy-start.19 = (s32[128]{0:T(128)S(1)}, s32[128]{0:T(128)}, u32[]{:S(2)}) copy-start(s32[128]{0:T(128)} %copy-done.18) | copy-start | bytes 1540
  88.7 9.5 %copy-start.3 = (bf16[512,512]{1,0:T(8,128)(2,1)S(1)}, bf16[512,512]{1,0:T(8,128)(2,1)}, u32[]{:S(2)}) copy-start(bf16[512,512]{1,0:T(8,128)(2,1)} %param.14) | copy-start | bytes 1572868
  88.7 9.5 %copy-start.7 = (bf16[1,128,512]{2,1,0:T(8,128)(2,1)S(1)}, bf16[1,128,512]{2,1,0:T(8,128)(2,1)}, u32[]{:S(2)}) copy-start(bf16[1,128,512]{2,1,0:T(8,128)(2,1)} %param.11) | copy-start | bytes 393220
  88.7 9.8 %copy-start.17 = (f32[8,512]{1,0:T(8,128)S(1)}, f32[8,512]{1,0:T(8,128)}, u32[]{:S(2)}) copy-start(f32[8,512]{1,0:T(8,128)} %copy-done.16) | copy-start | bytes 49156
  88.7 9.8 %copy-start.20 = (f32[8,128]{1,0:T(8,128)S(1)}, f32[8,128]{1,0:T(8,128)}, u32[]{:S(2)}) copy-start(f32[8,128]{1,0:T(8,128)} %multiply_divide_fusion.1) | copy-start | bytes 12292
  88.7 32.4 %all-to-all-start.2 = ((bf16[8,64,2048]{2,1,0:T(8,128)(2,1)}), bf16[8,64,2048]{2,1,0:T(8,128)(2,1)}, u32[]{:S(2)}, u32[]{:S(2)}) async-start(bf16[8,64,2048]{2,1,0:T(8,128)(2,1)} %pad_maximum_fusion), calls=%async_computation.2 | async-start | bytes 4194304 | tf_op jit(solution)/shard_map/all_to_all | solution.py:178
  98.5 1.7 %copy-start.14 = (f32[128,512]{1,0:T(8,128)}, f32[128,512]{1,0:T(8,128)S(1)}, u32[]{:S(2)}) copy-start(f32[128,512]{1,0:T(8,128)S(1)} %fusion.67) | copy-start | bytes 786436
  100.1 0.7 copy-start.27
  100.7 7.0 %copy-start.24 = (f32[512]{0:T(512)S(1)}, f32[512]{0:T(512)}, u32[]{:S(2)}) copy-start(f32[512]{0:T(512)} %param.12) | copy-start | bytes 6148
  104.6 3.2 %copy-start.5 = (bf16[512,1536]{1,0:T(8,128)(2,1)S(1)}, bf16[512,1536]{1,0:T(8,128)(2,1)}, u32[]{:S(2)}) copy-start(bf16[512,1536]{1,0:T(8,128)(2,1)} %param.13) | copy-start | bytes 4718596
  104.6 3.2 %copy-start.13 = (f32[128,512]{0,1:T(8,128)S(1)}, f32[128,512]{0,1:T(8,128)}, u32[]{:S(2)}) copy-start(f32[128,512]{0,1:T(8,128)} %copy.68) | copy-start | bytes 786436
  106.3 2.2 %copy-start.26 = (f32[128]{0:T(128)S(1)}, f32[128]{0:T(128)}, u32[]{:S(2)}) copy-start(f32[128]{0:T(128)} %copy-done.25) | copy-start | bytes 1540
  108.5 42.1 %copy-start.9 = (bf16[128,512]{1,0:T(8,128)(2,1)S(1)}, bf16[128,512]{1,0:T(8,128)(2,1)}, u32[]{:S(2)}) copy-start(bf16[128,512]{1,0:T(8,128)(2,1)} %copy-done.8) | copy-start | bytes 393220
  123.9 19.1 %all-to-all-start.3 = ((bf16[32,32,128]{2,1,0:T(8,128)(2,1)}), bf16[32,32,128]{2,1,0:T(8,128)(2,1)S(1)}, u32[]{:S(2)}, u32[]{:S(2)}) async-start(bf16[32,32,128]{2,1,0:T(8,128)(2,1)} %reshape_reshape.21), calls=%async_computation.3 | async-start | bytes 524288 | tf_op jit(solution)/shard_map/all_to_all | solution.py:169
  143.7 11.8 %all-to-all-start.4 = ((bf16[8,32,128]{2,1,0:T(8,128)(2,1)}), bf16[8,32,128]{2,1,0:T(8,128)(2,1)S(1)}, u32[]{:S(2)}, u32[]{:S(2)}) async-start(bf16[8,32,128]{2,1,0:T(8,128)(2,1)} %broadcast_in_dim.162), calls=%async_computation.4 | async-start | bytes 131072 | tf_op jit(solution)/shard_map/all_to_all | solution.py:169

commit v16 on v13

--- a/solution.py
+++ b/solution.py
@@ -223,9 +223,7 @@
     ).astype(jnp.bfloat16)
     both = jnp.concatenate([hidden, upstream], axis=1)
     outgoing = jnp.dot(placement, both, preferred_element_type=jnp.float32).astype(jnp.bfloat16)
-    landed = dense_all_to_all(outgoing.reshape(owners, row_capacity, -1), "ev").reshape(
-        outgoing.shape
-    )
+    landed = lax.all_to_all(outgoing, "ev", split_axis=0, concat_axis=0, tiled=True)
     landed_rows = landed[:, :features]
     landed_cotangent = landed[:, features:]
     row_presence = (
@@ -242,9 +240,7 @@
         cross_output_weight,
     )
     going_back = jnp.concatenate([result, back_rows.astype(jnp.bfloat16)], axis=1)
-    came_back = dense_all_to_all(going_back.reshape(owners, row_capacity, -1), "ev").reshape(
-        going_back.shape
-    )
+    came_back = lax.all_to_all(going_back, "ev", split_axis=0, concat_axis=0, tiled=True)
     picked = lax.dot_general(
         placement, came_back, (((0,), (0,)), ((), ())), preferred_element_type=jnp.float32
     )

time: 159 us -> 156 us (0.981)
  local copies, waits for them, and re-layouts: 29.2 us -> 23.8 us
  waiting for transfers between devices: 33.6 us -> 35.6 us
    all_to_all x4 -> x2, starting transfers between devices: 35.8 us -> 16.4 us  [dense_all_to_all(): moved = lax.all_to_all(flat, axis_name, 0, 0, tiled=True)]
    all_to_all x0 -> x2, starting transfers between devices: none -> 19.4 us  [the longest x1 12 us: on_device(): lax.all_to_all(outgoing, 'ev', split_axis=0, concat_axis=0, tiled=True)]
    all_to_all x4 -> x2, waiting for transfers between devices: 21.1 us -> 13.2 us  [dense_all_to_all(): moved = lax.all_to_all(flat, axis_name, 0, 0, tiled=True)]
    all_to_all x0 -> x2, waiting for transfers between devices: none -> 7.77 us  [the longest x1 7.77 us: on_device(): lax.all_to_all(outgoing, 'ev', split_axis=0, concat_axis=0, tiled=True)]
    another operation x3 -> x1, local copies, waits for them, and re-layouts: 3.89 us -> 0.82 us  [dense_all_to_all(): flat = pieces.reshape(count, -1, 128)]
    another operation x2 -> x0, local copies, waits for them, and re-layouts: 2.31 us -> none  [the longest x1 2.08 us: on_device(): dense_all_to_all(going_back.reshape(owners, row_capacity, -1), 'ev')]
    all_to_all x1, waiting for transfers between devices: 12.5 us -> 14.6 us  [reduce_weight_terms(): terms = lax.all_to_all(terms, 'dp', 0, 0, tiled=True)]
  transfers between devices with their start and end apart: 5 -> 5, of which waited for: 4 -> 4; matrix products, arithmetic and copies ran while one was open for 23% -> 22% of each run, Pallas kernels for 0% -> 0%
where the time goes in v16:
time: 156 us; the launch traced here: 155 us
  starting transfers between devices  41.9 us (27%)
  waiting for transfers between devices  35.6 us (23%)
  matrix products  29.5 us (19%)
  local copies, waits for them, and re-layouts  23.8 us (15%)
  other arithmetic  18.7 us (12%)
  between operations  5.35 us (3%)
    all_to_all x2, starting transfers between devices, dense_all_to_all(): moved = lax.all_to_all(flat, axis_name, 0, 0, tiled=True)  16.4 us
    all_to_all x1, waiting for transfers between devices, reduce_weight_terms(): terms = lax.all_to_all(terms, 'dp', 0, 0, tiled=True)  14.6 us
    all_to_all x2, waiting for transfers between devices, dense_all_to_all(): moved = lax.all_to_all(flat, axis_name, 0, 0, tiled=True)  13.2 us
    all_to_all x1, starting transfers between devices, on_device(): lax.all_to_all(outgoing, 'ev', split_axis=0, concat_axis=0, tiled=True)  12 us
    all_to_all x1, waiting for transfers between devices, on_device(): lax.all_to_all(outgoing, 'ev', split_axis=0, concat_axis=0, tiled=True)  7.77 us
    all_to_all x1, starting transfers between devices, on_device(): lax.all_to_all(going_back, 'ev', split_axis=0, concat_axis=0, tiled=True)  7.39 us
    dot_general x3, matrix products, cross_account_inner(): jnp.einsum('bhqf,bkf->bhqk', masked_queries, key_rows) * HEAD_DIM ** (-0.5)  7.18 us
    all_to_all x1, starting transfers between devices, reduce_weight_terms(): terms = lax.all_to_all(terms, 'dp', 0, 0, tiled=True)  6.08 us
  transfers between devices with their start and end apart: 5, of which 4 were waited for; matrix products, arithmetic and copies ran while one was open for 22% of the time, Pallas kernels for 0%

profile of v16, /device:TPU:1, one launch (start us, length us, event | category | flops | bytes accessed | tf_op | source)
XLA Modules:
  0.0 154.9 jit_solution(12868773223984764037)
XLA Ops:
  0.7 1.1 convert_reduce_fusion.5
  1.8 1.1 fusion.97
  2.9 0.8 dynamic-slice.1
  4.8 2.0 %fusion.22 = bf16[1,128,1536]{2,1,0:T(8,128)(2,1)S(1)} fusion(bf16[512,1536]{1,0:T(8,128)(2,1)} %param.13, bf16[1,128,512]{2,1,0:T(8,128)(2,1)} %param.10, f32[512]{0:T(512)} %param.12, f32[128]{0:T(128)S(1)} %fusion.134, f32[128]{0:T(128)S(1)} %broadcast_multiply_fusion.2), kind=kOutput, calls=%fused_computation.34 | convolution fusion | flops 201850880 | bytes 2100224 | tf_op jit(solution)/shard_map/jvp()/dot_general | solution.py:38
  6.9 0.8 copy-done.12
  9.7 1.1 fusion.51
  10.8 12.0 %all-to-all-start = ((bf16[32,8,1024]{2,1,0:T(8,128)(2,1)}), bf16[32,8,1024]{2,1,0:T(8,128)(2,1)S(1)}, u32[]{:S(2)}, u32[]{:S(2)}) async-start(bf16[32,8,1024]{2,1,0:T(8,128)(2,1)} %fusion.51), calls=%async_computation | async-start | bytes 1048576 | tf_op jit(solution)/shard_map/all_to_all | solution.py:226
  29.5 7.8 %all-to-all-done = bf16[32,8,1024]{2,1,0:T(8,128)(2,1)S(1)} async-done(((bf16[32,8,1024]{2,1,0:T(8,128)(2,1)}), bf16[32,8,1024]{2,1,0:T(8,128)(2,1)S(1)}, u32[]{:S(2)}, u32[]{:S(2)}) %all-to-all-start) | async-done | bytes 524320 | tf_op jit(solution)/shard_map/all_to_all | solution.py:226
  39.2 1.4 fusion.161
  40.6 1.2 fusion.31
  41.8 2.0 %fusion.12 = (f32[2,8,128]{2,1,0:T(8,128)S(1)}, bf16[2,8,128,384]{3,2,1,0:T(8,128)(2,1)S(1)}) fusion(f32[2,8,128,384]{3,2,1,0:T(8,128)S(1)} %get-tuple-element.69, f32[2,8,128]{2,1,0:T(8,128)S(1)} %multiply_divide_fusion, f32[2,8,128]{2,1,0:T(8,128)S(1)} %get-tuple-element.68, pred[2,128,384]{2,1,0:T(8,128)(4,1)S(1)} %broadcast_or_fusion, ...), kind=kOutput, calls=%fused_computation.16 | convolution fusion | flops 811464704 | bytes 6168576 | tf_op jit(solution)/shard_map/transpose(jvp(bhqk,bkf->bhqf))/dot_general | solution.py:110
  43.8 3.0 %divide_convert_fusion = (bf16[2,8,128,384]{3,2,1,0:T(8,128)(2,1)S(1)}, f32[2,8,128]{2,1,0:T(8,128)S(1)}, f32[2,8,128]{2,1,0:T(8,128)S(1)}, pred[2,8,128,384]{3,2,1,0:T(32,128)(4,1)S(1)}) fusion(f32[2,8,128,384]{3,2,1,0:T(8,128)S(1)} %get-tuple-element.69, f32[2,8,128]{2,1,0:T(8,128)S(1)} %fusion.31, f32[2,8,128]{2,1,0:T(8,128)S(1)} %get-tuple-element.68, ...), kind=kLoop, calls=%fused_computation.19 | loop fusion | flops 10219520 | bytes 7217152 | tf_op jit(solution)/shard_map/jvp()/convert_element_type | solution.py:109
  46.9 3.0 %multiply_reduce_fusion = f32[2,128,512]{2,1,0:T(8,128)S(1)} fusion(f32[8,512]{1,0:T(8,128)S(1)} %fusion.128, pred[2,8,128,384]{3,2,1,0:T(32,128)(4,1)S(1)} %get-tuple-element.15, f32[2,8,128]{2,1,0:T(8,128)S(1)} %negate_divide_fusion, pred[2,128,384]{2,1,0:T(8,128)(4,1)S(1)} %broadcast_or_fusion, bf16[1,384,512]{2,1,0:T(8,128)(2,1)S(1)} %get-tuple-element.77, ...), kind=kOutput, calls=%fused_computation.8 | convolution fusion | flops 815529984 | bytes 6963200 | tf_op jit(solution)/shard_map/transpose(jvp(bhqf,bkf->bhqk))/dot_general | solution.py:105
  49.9 2.8 %fusion.45 = f32[2,384,512]{2,1,0:T(8,128)S(1)} fusion(f32[8,512]{1,0:T(8,128)S(1)} %fusion.128, f32[2,128,512]{2,1,0:T(8,128)S(1)} %slice.169, pred[2,8,128,384]{3,2,1,0:T(32,128)(4,1)S(1)} %get-tuple-element.15, f32[2,8,128]{2,1,0:T(8,128)S(1)} %negate_divide_fusion, pred[2,128,384]{2,1,0:T(8,128)(4,1)S(1)} %broadcast_or_fusion, ...), kind=kOutput, calls=%fused_computation.60 | convolution fusion | flops 814219264 | bytes 7749632 | tf_op jit(solution)/shard_map/transpose(jvp(bhqf,bkf->bhqk))/dot_general | solution.py:105
  52.7 1.3 multiply_reduce_fusion.1
  54.0 1.1 fusion.48
  57.3 0.7 fusion.86
  58.0 1.0 fusion.157
  59.0 0.9 maximum_bitcast_fusion.10
  59.9 7.4 %all-to-all-start.1 = ((bf16[32,8,1024]{2,1,0:T(8,128)(2,1)}), bf16[32,8,1024]{2,1,0:T(8,128)(2,1)}, u32[]{:S(2)}, u32[]{:S(2)}) async-start(bf16[32,8,1024]{2,1,0:T(8,128)(2,1)} %maximum_bitcast_fusion.10), calls=%async_computation.1 | async-start | bytes 1048576 | tf_op jit(solution)/shard_map/all_to_all | solution.py:243
  67.9 1.8 %copy.71 = bf16[256,512]{0,1:T(8,128)(2,1)} copy(bf16[256,512]{1,0:T(8,128)(2,1)} %bitcast.202) | data formatting | bytes 524288 | tf_op jit(solution)/shard_map/jvp()/convert_element_type | solution.py:112
  69.7 1.8 %reshape.372 = bf16[32,8,512]{2,1,0:T(8,128)(2,1)} reshape(bf16[512,256]{1,0:T(8,128)(2,1)} %bitcast.198) | data formatting | bytes 524288 | tf_op jit(solution)/shard_map/reshape | solution.py:161
  71.5 1.7 %copy.72 = bf16[8,32,512]{2,1,0:T(8,128)(2,1)} copy(bf16[8,32,512]{2,0,1:T(8,128)(2,1)} %bitcast.199) | data formatting | bytes 524288 | tf_op jit(solution)/shard_map/transpose | solution.py:162
  73.2 1.8 %dot_general.106 = bf16[8,64,256]{2,1,0:T(8,128)(2,1)} reshape(bf16[8,32,512]{2,1,0:T(8,128)(2,1)} %copy.72) | data formatting | bytes 524288 | tf_op jit(solution)/shard_map/dot_general | solution.py:163
  75.0 1.8 %copy.69 = bf16[512,256]{1,0:T(8,128)(2,1)} copy(bf16[512,256]{0,1:T(8,128)(2,1)} %get-tuple-element.53) | data formatting | bytes 524288 | tf_op jit(solution)/shard_map/transpose | solution.py:161
  76.8 1.7 %reshape.371 = bf16[32,8,512]{2,1,0:T(8,128)(2,1)} reshape(bf16[512,256]{1,0:T(8,128)(2,1)} %copy.69) | data formatting | bytes 524288 | tf_op jit(solution)/shard_map/reshape | solution.py:161
  78.5 1.7 %copy.70 = bf16[8,32,512]{2,1,0:T(8,128)(2,1)} copy(bf16[8,32,512]{2,0,1:T(8,128)(2,1)} %bitcast.200) | data formatting | bytes 524288 | tf_op jit(solution)/shard_map/transpose | solution.py:162
  80.3 1.7 %dot_general.104 = bf16[8,64,256]{2,1,0:T(8,128)(2,1)} reshape(bf16[8,32,512]{2,1,0:T(8,128)(2,1)} %copy.70) | data formatting | bytes 524288 | tf_op jit(solution)/shard_map/dot_general | solution.py:163
  82.0 1.2 convolution_convert_fusion.3
  83.3 1.5 convolution_convert_fusion
  84.8 1.6 %pad_maximum_fusion = bf16[8,64,2048]{2,1,0:T(8,128)(2,1)} fusion(bf16[8,64,512]{2,1,0:T(8,128)(2,1)S(1)} %convolution_convert_fusion.3, bf16[8,64,1536]{2,1,0:T(8,128)(2,1)S(1)} %convolution_convert_fusion), kind=kLoop, calls=%fused_computation.35 | loop fusion | flops 4194304 | bytes 4194304 | tf_op jit(solution)/shard_map/concatenate | solution.py:251
  86.4 6.1 %all-to-all-start.2 = ((bf16[8,64,2048]{2,1,0:T(8,128)(2,1)}), bf16[8,64,2048]{2,1,0:T(8,128)(2,1)}, u32[]{:S(2)}, u32[]{:S(2)}) async-start(bf16[8,64,2048]{2,1,0:T(8,128)(2,1)} %pad_maximum_fusion), calls=%async_computation.2 | async-start | bytes 4194304 | tf_op jit(solution)/shard_map/all_to_all | solution.py:178
  92.5 1.3 fusion.87
  94.2 1.5 convert_reduce_fusion.3
  96.4 2.1 %multiply_reduce_fusion.2 = f32[128,512]{1,0:T(8,128)} fusion(f32[8,512]{1,0:T(8,128)S(1)} %copy-done.17, f32[8,128,128]{1,2,0:T(8,128)S(1)} %get-tuple-element.5, pred[8,128,128]{1,2,0:T(32,128)(4,1)S(1)} %get-tuple-element.7, f32[8,128]{1,0:T(8,128)S(1)} %negate_divide_fusion.1, bf16[1,128,1536]{2,1,0:T(8,128)(2,1)} %copy-done.11), kind=kOutput, calls=%fused_computation.36 | convolution fusion | flops 135593984 | bytes 1069056 | tf_op jit(solution)/shard_map/transpose(jvp(bhqf,bkf->bhqk))/dot_general | solution.py:47
  98.5 1.8 %copy.68 = f32[128,512]{0,1:T(8,128)} copy(f32[128,512]{1,0:T(8,128)} %multiply_reduce_fusion.2) | data formatting | bytes 524288 | tf_op jit(solution)/shard_map/transpose(jvp())/reduce_sum | solution.py:46
  100.3 1.7 %fusion.61 = f32[1,128,512]{1,2,0:T(8,128)S(1)} fusion(f32[8,512]{1,0:T(8,128)S(1)} %copy-done.17, f32[128,512]{1,0:T(8,128)} %copy-done.12, f32[8,128,128]{1,2,0:T(8,128)S(1)} %get-tuple-element.5, pred[8,128,128]{1,2,0:T(32,128)(4,1)} %copy-done.27, f32[8,128]{1,0:T(8,128)S(1)} %negate_divide_fusion.1), kind=kOutput, calls=%fused_computation.71 | convolution fusion | flops 135135232 | bytes 1200128 | tf_op jit(solution)/shard_map/transpose(jvp(bhqf,bkf->bhqk))/dot_general | solution.py:47
  102.0 1.4 fusion.64
  103.4 0.7 fusion.100
  104.2 14.6 %all-to-all-done.2 = bf16[8,64,2048]{2,1,0:T(8,128)(2,1)} async-done(((bf16[8,64,2048]{2,1,0:T(8,128)(2,1)}), bf16[8,64,2048]{2,1,0:T(8,128)(2,1)}, u32[]{:S(2)}, u32[]{:S(2)}) %all-to-all-start.2) | async-done | bytes 2097184 | tf_op jit(solution)/shard_map/all_to_all | solution.py:178
  118.8 2.0 %reduce_sum.284 = bf16[64,2048]{1,0:T(8,128)(2,1)S(1)} reduce(bf16[8,64,2048]{2,1,0:T(8,128)(2,1)} %all-to-all-done.2, bf16[]{:T(256)} %constant.97.clone.1), dimensions={0}, to_apply=%region_25.26 | reduce | flops 917504 | bytes 2359298 | tf_op jit(solution)/shard_map/reduce_sum | solution.py:179
  120.8 0.8 reshape_reshape.2
  121.6 9.4 %all-to-all-start.3 = ((bf16[32,32,128]{2,1,0:T(8,128)(2,1)}), bf16[32,32,128]{2,1,0:T(8,128)(2,1)S(1)}, u32[]{:S(2)}, u32[]{:S(2)}) async-start(bf16[32,32,128]{2,1,0:T(8,128)(2,1)} %reshape_reshape.2), calls=%async_computation.3 | async-start | bytes 524288 | tf_op jit(solution)/shard_map/all_to_all | solution.py:169
  131.3 0.8 fusion.116
  132.1 8.6 %all-to-all-done.3 = bf16[32,32,128]{2,1,0:T(8,128)(2,1)S(1)} async-done(((bf16[32,32,128]{2,1,0:T(8,128)(2,1)}), bf16[32,32,128]{2,1,0:T(8,128)(2,1)S(1)}, u32[]{:S(2)}, u32[]{:S(2)}) %all-to-all-start.3) | async-done | bytes 262176 | tf_op jit(solution)/shard_map/all_to_all | solution.py:169
  141.4 6.9 %all-to-all-start.4 = ((f32[8,32,128]{2,1,0:T(8,128)}), f32[8,32,128]{2,1,0:T(8,128)S(1)}, u32[]{:S(2)}, u32[]{:S(2)}) async-start(f32[8,32,128]{2,1,0:T(8,128)} %broadcast_in_dim.162), calls=%async_computation.4 | async-start | bytes 262144 | tf_op jit(solution)/shard_map/all_to_all | solution.py:169
  148.3 0.7 fusion.117
  149.0 4.6 %all-to-all-done.4 = f32[8,32,128]{2,1,0:T(8,128)S(1)} async-done(((f32[8,32,128]{2,1,0:T(8,128)}), f32[8,32,128]{2,1,0:T(8,128)S(1)}, u32[]{:S(2)}, u32[]{:S(2)}) %all-to-all-start.4) | async-done | bytes 131104 | tf_op jit(solution)/shard_map/all_to_all | solution.py:169
  (126 shorter events, 13.8 us)
Async XLA Ops:
  0.6 37.0 %copy-start = (bf16[512,1536]{1,0:T(8,128)(2,1)S(1)}, bf16[512,1536]{1,0:T(8,128)(2,1)}, u32[]{:S(2)}) copy-start(bf16[512,1536]{1,0:T(8,128)(2,1)} %param.16) | copy-start | bytes 4718596
  2.9 0.8 copy-start.25
  2.9 51.0 %copy-start.16 = (f32[8,512]{1,0:T(8,128)}, f32[8,512]{1,0:T(8,128)S(1)}, u32[]{:S(2)}) copy-start(f32[8,512]{1,0:T(8,128)S(1)} %fusion.128) | copy-start | bytes 49156
  4.8 4.2 %copy-start.18 = (s32[128]{0:T(128)}, s32[128]{0:T(128)S(1)}, u32[]{:S(2)}) copy-start(s32[128]{0:T(128)S(1)} %fusion.133) | copy-start | bytes 1540
  4.8 3.9 %copy-start.1 = (bf16[1,128,512]{2,1,0:T(8,128)(2,1)S(1)}, bf16[1,128,512]{2,1,0:T(8,128)(2,1)}, u32[]{:S(2)}) copy-start(bf16[1,128,512]{2,1,0:T(8,128)(2,1)} %param.10) | copy-start | bytes 393220
  4.8 3.9 %copy-start.2 = (bf16[512,512]{1,0:T(8,128)(2,1)S(1)}, bf16[512,512]{1,0:T(8,128)(2,1)}, u32[]{:S(2)}) copy-start(bf16[512,512]{1,0:T(8,128)(2,1)} %param.14) | copy-start | bytes 1572868
  6.8 2.2 %copy-start.11 = (bf16[1,128,1536]{2,1,0:T(8,128)(2,1)}, bf16[1,128,1536]{2,1,0:T(8,128)(2,1)S(1)}, u32[]{:S(2)}) copy-start(bf16[1,128,1536]{2,1,0:T(8,128)(2,1)S(1)} %fusion.22) | copy-start | bytes 1179652
  6.8 2.9 %copy-start.6 = (bf16[1,128,512]{2,1,0:T(8,128)(2,1)S(1)}, bf16[1,128,512]{2,1,0:T(8,128)(2,1)}, u32[]{:S(2)}) copy-start(bf16[1,128,512]{2,1,0:T(8,128)(2,1)} %param.11) | copy-start | bytes 393220
  6.8 0.8 copy-start.12
  8.1 16.5 %copy-start.21 = (s32[1,1,2,2]{3,2,1,0:T(2,128)S(1)}, s32[1,1,2,2]{3,2,1,0:T(2,128)}, u32[]{:S(2)}) copy-start(s32[1,1,2,2]{3,2,1,0:T(2,128)} %param.19) | copy-start | bytes 52
  8.1 19.7 %copy-start.15 = (s32[1,4096]{1,0:T(1,128)S(1)}, s32[1,4096]{1,0:T(1,128)}, u32[]{:S(2)}) copy-start(s32[1,4096]{1,0:T(1,128)} %param.18) | copy-start | bytes 49156
  8.3 29.4 %copy-start.22 = (f32[512]{0:T(512)S(1)}, f32[512]{0:T(512)}, u32[]{:S(2)}) copy-start(f32[512]{0:T(512)} %param.15) | copy-start | bytes 6148
  9.0 0.7 copy-start.8
  10.8 26.6 %all-to-all-start = ((bf16[32,8,1024]{2,1,0:T(8,128)(2,1)}), bf16[32,8,1024]{2,1,0:T(8,128)(2,1)S(1)}, u32[]{:S(2)}, u32[]{:S(2)}) async-start(bf16[32,8,1024]{2,1,0:T(8,128)(2,1)} %fusion.51), calls=%async_computation | async-start | bytes 1048576 | tf_op jit(solution)/shard_map/all_to_all | solution.py:226
  37.7 1.0 copy-start.4
  54.0 1.1 copy-start.10
  56.6 0.7 copy-start.23
  59.9 26.5 %all-to-all-start.1 = ((bf16[32,8,1024]{2,1,0:T(8,128)(2,1)}), bf16[32,8,1024]{2,1,0:T(8,128)(2,1)}, u32[]{:S(2)}, u32[]{:S(2)}) async-start(bf16[32,8,1024]{2,1,0:T(8,128)(2,1)} %maximum_bitcast_fusion.10), calls=%async_computation.1 | async-start | bytes 1048576 | tf_op jit(solution)/shard_map/all_to_all | solution.py:243
  86.4 6.1 %copy-start.19 = (s32[128]{0:T(128)S(1)}, s32[128]{0:T(128)}, u32[]{:S(2)}) copy-start(s32[128]{0:T(128)} %copy-done.18) | copy-start | bytes 1540
  86.4 7.4 %copy-start.3 = (bf16[512,512]{1,0:T(8,128)(2,1)S(1)}, bf16[512,512]{1,0:T(8,128)(2,1)}, u32[]{:S(2)}) copy-start(bf16[512,512]{1,0:T(8,128)(2,1)} %param.14) | copy-start | bytes 1572868
  86.4 7.4 %copy-start.7 = (bf16[1,128,512]{2,1,0:T(8,128)(2,1)S(1)}, bf16[1,128,512]{2,1,0:T(8,128)(2,1)}, u32[]{:S(2)}) copy-start(bf16[1,128,512]{2,1,0:T(8,128)(2,1)} %param.11) | copy-start | bytes 393220
  86.4 7.8 %copy-start.17 = (f32[8,512]{1,0:T(8,128)S(1)}, f32[8,512]{1,0:T(8,128)}, u32[]{:S(2)}) copy-start(f32[8,512]{1,0:T(8,128)} %copy-done.16) | copy-start | bytes 49156
  86.4 7.8 %copy-start.20 = (f32[8,128]{1,0:T(8,128)S(1)}, f32[8,128]{1,0:T(8,128)}, u32[]{:S(2)}) copy-start(f32[8,128]{1,0:T(8,128)} %multiply_divide_fusion.1) | copy-start | bytes 12292
  86.4 32.4 %all-to-all-start.2 = ((bf16[8,64,2048]{2,1,0:T(8,128)(2,1)}), bf16[8,64,2048]{2,1,0:T(8,128)(2,1)}, u32[]{:S(2)}, u32[]{:S(2)}) async-start(bf16[8,64,2048]{2,1,0:T(8,128)(2,1)} %pad_maximum_fusion), calls=%async_computation.2 | async-start | bytes 4194304 | tf_op jit(solution)/shard_map/all_to_all | solution.py:178
  94.2 1.7 %copy-start.14 = (f32[128,512]{1,0:T(8,128)}, f32[128,512]{1,0:T(8,128)S(1)}, u32[]{:S(2)}) copy-start(f32[128,512]{1,0:T(8,128)S(1)} %fusion.68) | copy-start | bytes 786436
  95.7 0.7 copy-start.27
  96.4 7.0 %copy-start.24 = (f32[512]{0:T(512)S(1)}, f32[512]{0:T(512)}, u32[]{:S(2)}) copy-start(f32[512]{0:T(512)} %param.12) | copy-start | bytes 6148
  100.3 3.1 %copy-start.5 = (bf16[512,1536]{1,0:T(8,128)(2,1)S(1)}, bf16[512,1536]{1,0:T(8,128)(2,1)}, u32[]{:S(2)}) copy-start(bf16[512,1536]{1,0:T(8,128)(2,1)} %param.13) | copy-start | bytes 4718596
  100.3 3.2 %copy-start.13 = (f32[128,512]{0,1:T(8,128)S(1)}, f32[128,512]{0,1:T(8,128)}, u32[]{:S(2)}) copy-start(f32[128,512]{0,1:T(8,128)} %copy.68) | copy-start | bytes 786436
  101.9 2.2 %copy-start.26 = (f32[128]{0:T(128)S(1)}, f32[128]{0:T(128)}, u32[]{:S(2)}) copy-start(f32[128]{0:T(128)} %copy-done.25) | copy-start | bytes 1540
  104.2 44.2 %copy-start.9 = (bf16[128,512]{1,0:T(8,128)(2,1)S(1)}, bf16[128,512]{1,0:T(8,128)(2,1)}, u32[]{:S(2)}) copy-start(bf16[128,512]{1,0:T(8,128)(2,1)} %copy-done.8) | copy-start | bytes 393220
  121.6 19.1 %all-to-all-start.3 = ((bf16[32,32,128]{2,1,0:T(8,128)(2,1)}), bf16[32,32,128]{2,1,0:T(8,128)(2,1)S(1)}, u32[]{:S(2)}, u32[]{:S(2)}) async-start(bf16[32,32,128]{2,1,0:T(8,128)(2,1)} %reshape_reshape.2), calls=%async_computation.3 | async-start | bytes 524288 | tf_op jit(solution)/shard_map/all_to_all | solution.py:169
  141.4 12.2 %all-to-all-start.4 = ((f32[8,32,128]{2,1,0:T(8,128)}), f32[8,32,128]{2,1,0:T(8,128)S(1)}, u32[]{:S(2)}, u32[]{:S(2)}) async-start(f32[8,32,128]{2,1,0:T(8,128)} %broadcast_in_dim.162), calls=%async_computation.4 | async-start | bytes 262144 | tf_op jit(solution)/shard_map/all_to_all | solution.py:169
